TPU v7x, 32 devices: a whole 2x2x4 slice. The times are simulated.
32 devices in a mesh: groups: 2 (over x), ex: 16 (over z, y, core).
Axes of the slice: x: 2, y: 2, z: 4, core: 2. Of those that a mesh axis runs over, the one named last changes fastest.
Arguments:
- grads: bfloat16 [1024, 65536], P(('groups', 'ex')), parts along dimension 0, may hold values from -6 to 6
- proj: bfloat16 [65536, 1024], P('ex'), may hold values from -0.0234375 to 0.0234375
- target_ids: int32 [24, 128], replicated, may hold values from 0 to 511, as said below
- target_counts: int32 [24], replicated, may hold values from 1 to 128, as said below
Outputs:
- scores: float32 [1024, 24], P(('groups', 'ex')), parts along dimension 0
- sketch: float32 [1024, 1024], P(('groups', 'ex')), parts along dimension 0
There are 2 independent parts, one for each index of `groups`. A program takes and returns all parts, laid end to end along the dimension named above; an argument that names none is the same for every part. Nothing has to cross between parts.
Inputs may be any that keep to these rules, and one draw needn't show every extreme that they name: `target_ids`: indices of examples of this part; slots at or past a domain's count are ignored. `target_counts`: some domain fills all 128 slots.
All inputs are finite; a program needn't handle non-finite values.
Results may differ from a plain program's by a relative error of at most 0.0003.
Values may be sent and summed in bfloat16 or wider, within the bound.
No kernel may reach another device: no remote copies, remote signals or barrier semaphores. Data moves between devices by JAX's collectives and lax.ppermute only.
A program may use at most 128 MiB of HBM per device.

v0:
```python
import jax
import jax.numpy as jnp
from jax import lax
from jax.sharding import PartitionSpec as P


def partner(array, axis, bit):
    return lax.ppermute(array, axis, [(i, i ^ 1 << bit) for i in range(lax.axis_size(axis))])


def on_device(grads, proj, target_ids, target_counts):
    count_ex = lax.axis_size("ex")
    top_bits = count_ex.bit_length() - 1
    position = lax.axis_index("ex")
    ex_rows = grads.shape[0]
    examples = ex_rows * count_ex
    sketch_width = proj.shape[1]
    block_rows = proj.shape[0]
    outer_count = count_ex // 8
    set_width = outer_count * block_rows
    proj_set = proj
    for level in range(3, top_bits):
        partner_rows = partner(proj_set, "ex", level)
        high_side = position // 2**level % 2 == 1
        lower_rows = jnp.where(high_side, partner_rows, proj_set)
        upper_rows = jnp.where(high_side, proj_set, partner_rows)
        proj_set = jnp.concatenate([lower_rows, upper_rows], axis=0)
    pieces = (
        grads.reshape(ex_rows, outer_count, 8, block_rows)
        .transpose(2, 0, 1, 3)
        .reshape(8, ex_rows, set_width)
    )
    for level in range(2, -1, -1):
        shaped = pieces.reshape(2 ** (2 - level), 2, 2**level, ex_rows, set_width)
        high_side = position // 2**level % 2 == 1
        low_half = shaped[:, 0]
        high_half = shaped[:, 1]
        kept_half = jnp.where(high_side, high_half, low_half)
        sent_half = jnp.where(high_side, low_half, high_half)
        received = partner(sent_half, "ex", level)
        new_low = jnp.where(high_side, received, kept_half)
        new_high = jnp.where(high_side, kept_half, received)
        pieces = jnp.stack([new_low, new_high], axis=1).reshape(8, ex_rows, set_width)
    group_rows = pieces.reshape(8 * ex_rows, set_width)
    partial_value = jnp.dot(group_rows, proj_set, preferred_element_type=jnp.float32).reshape(
        8, ex_rows, sketch_width
    )
    for level in range(2, -1, -1):
        shaped = partial_value.reshape(2, 2**level, ex_rows, sketch_width)
        high_side = position // 2**level % 2 == 1
        kept_half = jnp.where(high_side, shaped[1], shaped[0])
        sent_half = jnp.where(high_side, shaped[0], shaped[1])
        partial_value = kept_half + partner(sent_half, "ex", level)
    sketch = partial_value.reshape(ex_rows, sketch_width)
    gram_local = jnp.dot(sketch.T, sketch, precision=lax.Precision.HIGHEST)
    slot_count = target_ids.shape[1]
    live_slot = jnp.arange(slot_count, dtype=jnp.int32)[None, :] < target_counts[:, None]
    own_index = position * ex_rows + jnp.arange(ex_rows, dtype=jnp.int32)
    matches = (target_ids[:, :, None] == own_index[None, None, :]) & live_slot[:, :, None]
    weight = jnp.sum(matches.astype(jnp.float32), axis=1) / target_counts[:, None].astype(
        jnp.float32
    )
    domain_local = jnp.dot(weight, sketch, precision=lax.Precision.HIGHEST)
    gram_matrix, domain = lax.psum((gram_local, domain_local), "ex")
    hessian = gram_matrix / jnp.float32(examples) + 0.1 * jnp.eye(sketch_width, dtype=jnp.float32)
    factor = jnp.linalg.cholesky(hessian)
    middle = lax.linalg.triangular_solve(factor, domain.T, left_side=True, lower=True)
    solved = lax.linalg.triangular_solve(
        factor, middle, left_side=True, lower=True, transpose_a=True
    )
    scores = jnp.dot(sketch, solved, precision=lax.Precision.HIGHEST)
    return (scores, sketch)


def solution(mesh):
    placed = (P(("groups", "ex"), None), P("ex", None), P(), P())
    return jax.shard_map(
        on_device,
        mesh=mesh,
        in_specs=placed,
        out_specs=(P(("groups", "ex"), None), P(("groups", "ex"), None)),
        check_vma=False,
    )
```

profile of v0, /device:TPU:0, one launch (start us, length us, event | category | flops | bytes accessed | tf_op | source)
XLA Modules:
  0.0 965.4 jit_solution(13928558609386680264)
XLA Ops:
  7.2 4.5 copy.87
  11.7 6.3 copy.89
  18.1 8.0 reshape_reshape.11
  31.6 45.7 %collective-permute-done = bf16[1,4,32,8192]{3,2,1,0:T(8,128)(2,1)} collective-permute-done((bf16[1,4,32,8192]{3,2,1,0:T(8,128)(2,1)S(1)}, bf16[1,4,32,8192]{3,2,1,0:T(8,128)(2,1)}, u32[]{:S(2)}, u32[]{:S(2)}) %collective-permute-start) | collective-permute-done | bytes 2097184 | tf_op jit(solution)/shard_map/ppermute | solution.py:8
  87.8 42.9 %collective-permute-done.1 = bf16[2,2,32,8192]{3,2,1,0:T(8,128)(2,1)} collective-permute-done((bf16[2,2,32,8192]{3,2,1,0:T(8,128)(2,1)}, bf16[2,2,32,8192]{3,2,1,0:T(8,128)(2,1)}, u32[]{:S(2)}, u32[]{:S(2)}) %collective-permute-start.1) | collective-permute-done | bytes 2097184 | tf_op jit(solution)/shard_map/ppermute | solution.py:8
  144.5 302.7 %collective-permute-done.3 = bf16[4096,1024]{1,0:T(8,128)(2,1)} collective-permute-done((bf16[4096,1024]{1,0:T(8,128)(2,1)}, bf16[4096,1024]{1,0:T(8,128)(2,1)}, u32[]{:S(2)}, u32[]{:S(2)}) %collective-permute-start.3) | collective-permute-done | bytes 8388640 | tf_op jit(solution)/shard_map/ppermute | solution.py:8
  447.2 9.1 broadcast_select_fusion.1
  456.3 7.3 fusion
  464.4 12.1 %collective-permute-done.4 = f32[4,32,1024]{2,1,0:T(8,128)S(1)} collective-permute-done((f32[4,32,1024]{2,1,0:T(8,128)S(1)}, f32[4,32,1024]{2,1,0:T(8,128)S(1)}, u32[]{:S(2)}, u32[]{:S(2)}) %collective-permute-start.4) | collective-permute-done | bytes 524320 | tf_op jit(solution)/shard_map/ppermute | solution.py:8
  477.6 5.7 collective-permute-done.5
  484.9 5.0 fusion.115
  490.9 114.5 %all-reduce.4.cloned.1.call-done = (f32[1024,1024]{0,1:T(8,128)}, f32[1024,24]{0,1:T(8,128)}) async-done(((f32[1024,1024]{0,1:T(8,128)}, f32[1024,24]{0,1:T(8,128)}), (f32[1024,1024]{0,1:T(8,128)}, f32[1024,24]{0,1:T(8,128)})) %all-reduce.4.cloned.1.call-update) | async-done | bytes 4292624 | tf_op jit(solution)/shard_map/psum | solution.py:64
  605.4 5.0 select_add_fusion
  610.4 5.7 copy.61
  622.6 11.7 %cholesky.222 = f32[128,128]{1,0:T(8,128)S(1)} custom-call(f32[128,128]{1,0:T(8,128)S(1)} %cholesky.577), custom_call_target="Cholesky" | custom-call | tf_op jit(solution)/shard_map/jit(cholesky)/cholesky | solution.py:66
  634.3 9.8 %custom-call.64 = f32[1,128,128]{1,2,0:T(8,128)S(1)} custom-call(f32[1,128,128]{2,1,0:T(8,128)S(1)} %get-tuple-element.57), custom_call_target="InvertDiagBlocksLowerTriangular" | custom-call | tf_op jit(solution)/shard_map/jit(cholesky)/cholesky | solution.py:66
  647.2 11.7 %cholesky.243 = f32[128,128]{1,0:T(8,128)S(1)} custom-call(f32[128,128]{1,0:T(8,128)S(1)} %cholesky.581), custom_call_target="Cholesky" | custom-call | tf_op jit(solution)/shard_map/jit(cholesky)/cholesky | solution.py:66
  659.5 9.8 %custom-call.65 = f32[1,128,128]{1,2,0:T(8,128)S(1)} custom-call(f32[1,128,128]{2,1,0:T(8,128)S(1)} %get-tuple-element.55), custom_call_target="InvertDiagBlocksLowerTriangular" | custom-call | tf_op jit(solution)/shard_map/jit(cholesky)/cholesky | solution.py:66
  674.9 11.7 %cholesky.466 = f32[128,128]{1,0:T(8,128)S(1)} custom-call(f32[128,128]{1,0:T(8,128)S(1)} %cholesky.586), custom_call_target="Cholesky" | custom-call | tf_op jit(solution)/shard_map/jit(cholesky)/cholesky | solution.py:66
  687.4 9.8 %custom-call.66 = f32[1,128,128]{1,2,0:T(8,128)S(1)} custom-call(f32[1,128,128]{2,1,0:T(8,128)S(1)} %get-tuple-element.53), custom_call_target="InvertDiagBlocksLowerTriangular" | custom-call | tf_op jit(solution)/shard_map/jit(cholesky)/cholesky | solution.py:66
  701.8 11.7 %cholesky.485 = f32[128,128]{1,0:T(8,128)S(1)} custom-call(f32[128,128]{1,0:T(8,128)S(1)} %cholesky.591), custom_call_target="Cholesky" | custom-call | tf_op jit(solution)/shard_map/jit(cholesky)/cholesky | solution.py:66
  714.3 9.8 %custom-call.67 = f32[1,128,128]{1,2,0:T(8,128)S(1)} custom-call(f32[1,128,128]{2,1,0:T(8,128)S(1)} %get-tuple-element.51), custom_call_target="InvertDiagBlocksLowerTriangular" | custom-call | tf_op jit(solution)/shard_map/jit(cholesky)/cholesky | solution.py:66
  728.4 12.1 %cholesky.504 = f32[128,128]{1,0:T(8,128)S(1)} custom-call(f32[128,128]{1,0:T(8,128)S(1)} %cholesky.596), custom_call_target="Cholesky" | custom-call | tf_op jit(solution)/shard_map/jit(cholesky)/cholesky | solution.py:66
  741.3 9.8 %custom-call.68 = f32[1,128,128]{1,2,0:T(8,128)S(1)} custom-call(f32[1,128,128]{2,1,0:T(8,128)S(1)} %get-tuple-element.49), custom_call_target="InvertDiagBlocksLowerTriangular" | custom-call | tf_op jit(solution)/shard_map/jit(cholesky)/cholesky | solution.py:66
  755.3 11.7 %cholesky.524 = f32[128,128]{1,0:T(8,128)S(1)} custom-call(f32[128,128]{1,0:T(8,128)S(1)} %cholesky.601), custom_call_target="Cholesky" | custom-call | tf_op jit(solution)/shard_map/jit(cholesky)/cholesky | solution.py:66
  767.8 9.8 %custom-call.69 = f32[1,128,128]{1,2,0:T(8,128)S(1)} custom-call(f32[1,128,128]{2,1,0:T(8,128)S(1)} %get-tuple-element.47), custom_call_target="InvertDiagBlocksLowerTriangular" | custom-call | tf_op jit(solution)/shard_map/jit(cholesky)/cholesky | solution.py:66
  781.4 11.7 %cholesky.544 = f32[128,128]{1,0:T(8,128)S(1)} custom-call(f32[128,128]{1,0:T(8,128)S(1)} %cholesky.606), custom_call_target="Cholesky" | custom-call | tf_op jit(solution)/shard_map/jit(cholesky)/cholesky | solution.py:66
  793.9 9.8 %custom-call.70 = f32[1,128,128]{1,2,0:T(8,128)S(1)} custom-call(f32[1,128,128]{2,1,0:T(8,128)S(1)} %get-tuple-element.45), custom_call_target="InvertDiagBlocksLowerTriangular" | custom-call | tf_op jit(solution)/shard_map/jit(cholesky)/cholesky | solution.py:66
  806.8 11.7 %cholesky.562 = f32[128,128]{1,0:T(8,128)S(1)} custom-call(f32[128,128]{1,0:T(8,128)S(1)} %convolution_subtract_fusion.6), custom_call_target="Cholesky" | custom-call | tf_op jit(solution)/shard_map/jit(cholesky)/cholesky | solution.py:66
  829.0 4.9 select_select_fusion
  833.8 23.7 %while.1 = (s32[]{:T(128)}, f32[1024,1024]{0,1:T(8,128)}, s32[8,2]{0,1:T(2,128)S(1)}, f32[8,128,128]{2,1,0:T(8,128)S(1)}, s32[]{:T(128)}) while((s32[]{:T(128)}, f32[1024,1024]{0,1:T(8,128)}, s32[8,2]{0,1:T(2,128)S(1)}, f32[8,128,128]{2,1,0:T(8,128)S(1)}, s32[]{:T(128)}) %tuple.60), condition=%wide.while_cond, body=%wide.while_body.sunk | while | flops 2 | bytes 393321 | solution.py:68
  857.6 78.8 %custom-call.71 = f32[8,128,128]{1,2,0:T(8,128)S(1)} custom-call(f32[8,128,128]{2,1,0:T(8,128)S(1)} %get-tuple-element.9), custom_call_target="InvertDiagBlocksLowerTriangular" | custom-call | tf_op jit(solution)/shard_map/triangular_solve | solution.py:68
  (198 shorter events, 123.8 us)
Async XLA Ops:
  7.2 598.2 %all-reduce.4.cloned.1.call-start = ((), (), s32[]{:S(2)}) async-start(), calls=%async_computation | async-start | bytes 8585216 | tf_op jit(solution)/shard_map/psum | solution.py:64
  28.5 48.8 %collective-permute-start = (bf16[1,4,32,8192]{3,2,1,0:T(8,128)(2,1)S(1)}, bf16[1,4,32,8192]{3,2,1,0:T(8,128)(2,1)}, u32[]{:S(2)}, u32[]{:S(2)}) collective-permute-start(bf16[1,4,32,8192]{3,2,1,0:T(8,128)(2,1)S(1)} %select_bitcast_fusion.3), channel_id=1, source_target_pairs={{0,4},{1,5},{2,6},{3,7},{4,0},{5,1},{6,2},{7,3},{8,12},{9,13},{10,... | collective-permute-start | bytes 6291464 | tf_op jit(solution)/shard_map/ppermute | solution.py:8
  80.6 1.4 copy-start.2
  83.5 47.1 %collective-permute-start.1 = (bf16[2,2,32,8192]{3,2,1,0:T(8,128)(2,1)}, bf16[2,2,32,8192]{3,2,1,0:T(8,128)(2,1)}, u32[]{:S(2)}, u32[]{:S(2)}) collective-permute-start(bf16[2,2,32,8192]{3,2,1,0:T(8,128)(2,1)} %fusion.7), channel_id=1, source_target_pairs={{0,2},{1,3},{2,0},{3,1},{4,6},{5,7},{6,4},{7,5},{8,10},{9,11},{10,... | collective-permute-start | bytes 6291464 | tf_op jit(solution)/shard_map/ppermute | solution.py:8
  85.2 362.0 %collective-permute-start.3 = (bf16[4096,1024]{1,0:T(8,128)(2,1)}, bf16[4096,1024]{1,0:T(8,128)(2,1)}, u32[]{:S(2)}, u32[]{:S(2)}) collective-permute-start(bf16[4096,1024]{1,0:T(8,128)(2,1)} %param.5), channel_id=1, source_target_pairs={{0,8},{1,9},{2,10},{3,11},{4,12},{5,13},{6,14},{7,15},{8,0},{9,1},... | collective-permute-start | bytes 25165832 | tf_op jit(solution)/shard_map/ppermute | solution.py:8
  134.3 2.0 copy-start.1
  136.5 4.4 collective-permute-start.2
  463.6 14.0 %copy-start.7 = (s32[24]{0:T(128)S(1)}, s32[24]{0:T(128)}, u32[]{:S(2)}) copy-start(s32[24]{0:T(128)} %param.7) | copy-start | bytes 292
  463.6 19.9 %copy-start.6 = (s32[24,128]{1,0:T(8,128)S(1)}, s32[24,128]{1,0:T(8,128)}, u32[]{:S(2)}) copy-start(s32[24,128]{1,0:T(8,128)} %param.6) | copy-start | bytes 36868
  463.7 12.8 %collective-permute-start.4 = (f32[4,32,1024]{2,1,0:T(8,128)S(1)}, f32[4,32,1024]{2,1,0:T(8,128)S(1)}, u32[]{:S(2)}, u32[]{:S(2)}) collective-permute-start(f32[4,32,1024]{2,1,0:T(8,128)S(1)} %bitcast.197), channel_id=1, source_target_pairs={{0,4},{1,5},{2,6},{3,7},{4,0},{5,1},{6,2},{7,3},{8,12},{9,13},{10,... | collective-permute-start | bytes 1572872 | tf_op jit(solution)/shard_map/ppermute | solution.py:8
  476.6 6.7 collective-permute-start.5
  483.4 1.4 collective-permute-start.6
  484.8 472.7 %copy-start.4 = (f32[32,1024]{1,0:T(8,128)}, f32[32,1024]{1,0:T(8,128)S(1)}, u32[]{:S(2)}) copy-start(f32[32,1024]{1,0:T(8,128)S(1)} %add_bitcast_fusion) | copy-start | bytes 393220
  620.6 1.9 copy-start.3
  670.5 2.0 copy-start
  829.0 107.4 %copy-start.5 = (f32[1024,24]{0,1:T(8,128)S(1)}, f32[1024,24]{0,1:T(8,128)}, u32[]{:S(2)}) copy-start(f32[1024,24]{0,1:T(8,128)} %get-tuple-element.31) | copy-start | bytes 294916
Sparse Core Ops, SparseCore 0:
  491.0 114.3 all-reduce.3
where the time goes:
time: 973 us; the launch traced here: 965 us
  waiting for transfers between devices  529 us (54%)
  other arithmetic  285 us (29%)
  local copies, waits for them, and re-layouts  61.4 us (6%)
  matrix products  60.4 us (6%)
  between operations  20.4 us (2%)
    ppermute x7, waiting for transfers between devices, partner(): lax.ppermute(array, axis, [(i, i ^ 1 << bit) for i in range(lax.axis_size...  414 us
    another operation x30, other arithmetic, on_device(): factor = jnp.linalg.cholesky(hessian)  168 us
    psum x1, waiting for transfers between devices, on_device(): gram_matrix, domain = lax.psum((gram_local, domain_local), 'ex')  114 us
    another operation x3, other arithmetic, on_device(): lax.linalg.triangular_solve(factor, middle, left_side=True, lower=True, t...  83.7 us
    another operation x14, matrix products, on_device(): factor = jnp.linalg.cholesky(hessian)  25.9 us
    another operation x40, local copies, waits for them, and re-layouts  23.5 us
  transfers between devices with their start and end apart: 8, of which 8 were waited for; matrix products, arithmetic and copies ran while one was open for 1% of the time, Pallas kernels for 0%

commit v1 on v0

v1 whole, which is shorter than its diff:
```python
import jax
import jax.numpy as jnp
from jax import lax
from jax.sharding import PartitionSpec as P


def partner(array, axis, bit):
    return lax.ppermute(array, axis, [(i, i ^ 1 << bit) for i in range(lax.axis_size(axis))])


def reduce_scatter(partial_value, bits, position):
    value = partial_value
    for level in range(bits):
        value = value.reshape((-1, 2) + value.shape[1:])
        own_bit = position // 2**level % 2
        kept = lax.dynamic_index_in_dim(value, own_bit, axis=1, keepdims=False)
        sent = lax.dynamic_index_in_dim(value, 1 - own_bit, axis=1, keepdims=False)
        value = kept + partner(sent, "ex", level)
    return value[0]


def all_gather(block, bits, position):
    value = block[None]
    for level in range(bits - 1, -1, -1):
        received = partner(value, "ex", level)
        high_side = position // 2**level % 2 == 1
        low = jnp.where(high_side, received, value)
        high = jnp.where(high_side, value, received)
        value = jnp.stack([low, high], axis=1).reshape((-1,) + value.shape[1:])
    return value


def on_device(grads, proj, target_ids, target_counts):
    count_ex = lax.axis_size("ex")
    bits = count_ex.bit_length() - 1
    position = lax.axis_index("ex")
    ex_rows = grads.shape[0]
    examples = ex_rows * count_ex
    sketch_width = proj.shape[1]
    with jax.named_scope("gradient_exchange"):
        columns = lax.all_to_all(grads, "ex", split_axis=1, concat_axis=0, tiled=True)
    with jax.named_scope("partial_projection"):
        partial_value = jnp.dot(columns, proj, preferred_element_type=jnp.float32)
    with jax.named_scope("sketch_reduce"):
        sketch = reduce_scatter(
            partial_value.reshape(count_ex, ex_rows, sketch_width), bits, position
        )
    with jax.named_scope("sketch_gather"):
        sketch_all = all_gather(sketch, bits, position).reshape(examples, sketch_width)
    slot_count = target_ids.shape[1]
    live_slot = jnp.arange(slot_count, dtype=jnp.int32)[None, :] < target_counts[:, None]
    example_index = jnp.arange(examples, dtype=jnp.int32)
    matches = (target_ids[:, :, None] == example_index[None, None, :]) & live_slot[:, :, None]
    weight = jnp.sum(matches.astype(jnp.float32), axis=1) / target_counts[:, None].astype(
        jnp.float32
    )
    if examples < sketch_width:
        with jax.named_scope("kernel_matrix"):
            kernel = jnp.dot(sketch_all, sketch_all.T, precision=lax.Precision.HIGHEST)
        with jax.named_scope("kernel_solve"):
            system = kernel / jnp.float32(examples) + 0.1 * jnp.eye(examples, dtype=jnp.float32)
            factor = jnp.linalg.cholesky(system)
            middle = lax.linalg.triangular_solve(factor, weight.T, left_side=True, lower=True)
            coeffs = lax.linalg.triangular_solve(
                factor, middle, left_side=True, lower=True, transpose_a=True
            )
        own_kernel = lax.dynamic_slice_in_dim(kernel, position * ex_rows, ex_rows, axis=0)
        scores = jnp.dot(own_kernel, coeffs, precision=lax.Precision.HIGHEST)
    else:
        with jax.named_scope("gram_solve"):
            gram_matrix = jnp.dot(sketch_all.T, sketch_all, precision=lax.Precision.HIGHEST)
            domain = jnp.dot(weight, sketch_all, precision=lax.Precision.HIGHEST)
            hessian = gram_matrix / jnp.float32(examples) + 0.1 * jnp.eye(
                sketch_width, dtype=jnp.float32
            )
            factor = jnp.linalg.cholesky(hessian)
            middle = lax.linalg.triangular_solve(factor, domain.T, left_side=True, lower=True)
            solved = lax.linalg.triangular_solve(
                factor, middle, left_side=True, lower=True, transpose_a=True
            )
        scores = jnp.dot(sketch, solved, precision=lax.Precision.HIGHEST)
    return (scores, sketch)


def solution(mesh):
    placed = (P(("groups", "ex"), None), P("ex", None), P(), P())
    return jax.shard_map(
        on_device,
        mesh=mesh,
        in_specs=placed,
        out_specs=(P(("groups", "ex"), None), P(("groups", "ex"), None)),
        check_vma=False,
    )
```

time: 973 us -> 328 us (0.34)
  waiting for transfers between devices: 529 us -> 134 us
  other arithmetic: 285 us -> 123 us
  local copies, waits for them, and re-layouts: 61.4 us -> 16.5 us
  matrix products: 60.4 us -> 17.5 us
  starting transfers between devices: 9.15 us -> 29.1 us
  between operations: 20.4 us -> 4.07 us
    ppermute x7 -> x8, waiting for transfers between devices: 414 us -> 56.3 us  [partner(): lax.ppermute(array, axis, [(i, i ^ 1 << bit) for i in range(lax.axis_size...]
    psum x1 -> x0, waiting for transfers between devices: 114 us -> none  [on_device(): gram_matrix, domain = lax.psum((gram_local, domain_local), 'ex')]
    another operation x34 -> x21, other arithmetic: 175 us -> 79.5 us  [the longest x14 78.7 us: on_device(): factor = jnp.linalg.cholesky(system)]
    all_to_all x0 -> x1, waiting for transfers between devices: none -> 77.7 us  [on_device(): lax.all_to_all(grads, 'ex', split_axis=1, concat_axis=0, tiled=True)]
    another operation x3, other arithmetic: 83.7 us -> 40.2 us  [on_device(): lax.linalg.triangular_solve(factor, middle, left_side=True, lower=True, t...]
    another operation x29 -> x13, matrix products: 35.7 us -> 3.56 us  [the longest x6 2.12 us: on_device(): factor = jnp.linalg.cholesky(system)]
    another operation x67 -> x18, local copies, waits for them, and re-layouts: 37.5 us -> 10.9 us
    select_n x8 -> x0, other arithmetic: 16.6 us -> none  [the longest x1 9.05 us: on_device(): lower_rows = jnp.where(high_side, partner_rows, proj_set)]
  transfers between devices with their start and end apart: 8 -> 9, of which waited for: 8 -> 9; matrix products, arithmetic and copies ran while one was open for 1% -> 1% of each run, Pallas kernels for 0% -> 0%
where the time goes in v1:
time: 328 us; the launch traced here: 325 us
  waiting for transfers between devices  134 us (41%)
  other arithmetic  123 us (38%)
  starting transfers between devices  29.1 us (9%)
  matrix products  17.5 us (5%)
  local copies, waits for them, and re-layouts  16.5 us (5%)
  between operations  4.07 us (1%)
    another operation x14, other arithmetic, on_device(): factor = jnp.linalg.cholesky(system)  78.7 us
    all_to_all x1, waiting for transfers between devices, on_device(): lax.all_to_all(grads, 'ex', split_axis=1, concat_axis=0, tiled=True)  77.7 us
    ppermute x8, waiting for transfers between devices, partner(): lax.ppermute(array, axis, [(i, i ^ 1 << bit) for i in range(lax.axis_size...  56.3 us
    another operation x3, other arithmetic, on_device(): lax.linalg.triangular_solve(factor, middle, left_side=True, lower=True, t...  40.2 us
    ppermute x8, starting transfers between devices, partner(): lax.ppermute(array, axis, [(i, i ^ 1 << bit) for i in range(lax.axis_size...  21.7 us
    another operation x12, local copies, waits for them, and re-layouts  10.5 us
    dot_general x1, matrix products, on_device(): partial_value = jnp.dot(columns, proj, preferred_element_type=jnp.float32)  8.14 us
    all_to_all x1, starting transfers between devices, on_device(): lax.all_to_all(grads, 'ex', split_axis=1, concat_axis=0, tiled=True)  7.44 us
  transfers between devices with their start and end apart: 9, of which 9 were waited for; matrix products, arithmetic and copies ran while one was open for 1% of the time, Pallas kernels for 0%

profile of v1, /device:TPU:0, one launch (start us, length us, event | category | flops | bytes accessed | tf_op | source)
XLA Modules:
  0.0 324.7 jit_solution(8416492365125750362)
XLA Ops:
  0.6 4.7 %copy.26 = bf16[4,16,8,4096]{3,2,0,1:T(8,128)(2,1)} copy(bf16[4,16,8,4096]{3,2,1,0:T(8,128)(2,1)} %bitcast.121) | data formatting | bytes 8388608 | tf_op jit(solution)/shard_map/gradient_exchange/all_to_all | solution.py:41
  5.3 7.4 %all-to-all-start = ((bf16[32,16,4096]{2,0,1:T(8,128)(2,1)}), bf16[32,16,4096]{2,0,1:T(8,128)(2,1)}, u32[]{:S(2)}, u32[]{:S(2)}) async-start(bf16[32,16,4096]{2,0,1:T(8,128)(2,1)} %bitcast.119), calls=%async_computation | async-start | bytes 8388608 | tf_op jit(solution)/shard_map/gradient_exchange/all_to_all | solution.py:41
  12.7 77.7 %all-to-all-done = bf16[32,16,4096]{2,0,1:T(8,128)(2,1)} async-done(((bf16[32,16,4096]{2,0,1:T(8,128)(2,1)}), bf16[32,16,4096]{2,0,1:T(8,128)(2,1)}, u32[]{:S(2)}, u32[]{:S(2)}) %all-to-all-start) | async-done | bytes 4194336 | tf_op jit(solution)/shard_map/gradient_exchange/all_to_all | solution.py:41
  90.4 8.1 %fusion = f32[8,2,32,1024]{3,2,1,0:T(8,128)S(1)} fusion(bf16[8,2,32,4096]{3,2,1,0:T(8,128)(2,1)} %bitcast.1, bf16[4096,1024]{1,0:T(8,128)(2,1)} %param.5), kind=kOutput, calls=%fused_computation.2 | convolution fusion | flops 4294967296 | bytes 14680064 | tf_op jit(solution)/shard_map/partial_projection/dot_general | solution.py:43
  98.7 0.8 collective-permute-start
  99.5 2.4 collective-permute-done
  101.9 1.4 bitcast_add_fusion
  103.3 6.3 %collective-permute-start.1 = (f32[4,32,1024]{2,1,0:T(8,128)S(1)}, f32[4,32,1024]{2,1,0:T(8,128)S(1)}, u32[]{:S(2)}, u32[]{:S(2)}) collective-permute-start(f32[4,32,1024]{2,1,0:T(8,128)S(1)} %dynamic-slice_bitcast_fusion.1), channel_id=1, source_target_pairs={{0,2},{1,3},{2,0},{3,1},{4,6},{5,7},{6,4},{7,5},{8,10},{9,11},{10,... | collective-permute-start | bytes 1572872 | tf_op jit(solution)/shard_map/sketch_reduce/ppermute | solution.py:8
  109.6 12.4 %collective-permute-done.1 = f32[4,32,1024]{2,1,0:T(8,128)S(1)} collective-permute-done((f32[4,32,1024]{2,1,0:T(8,128)S(1)}, f32[4,32,1024]{2,1,0:T(8,128)S(1)}, u32[]{:S(2)}, u32[]{:S(2)}) %collective-permute-start.1) | collective-permute-done | bytes 524320 | tf_op jit(solution)/shard_map/sketch_reduce/ppermute | solution.py:8
  122.2 11.4 %collective-permute-start.2 = (f32[2,32,1024]{2,1,0:T(8,128)S(1)}, f32[2,32,1024]{2,1,0:T(8,128)S(1)}, u32[]{:S(2)}, u32[]{:S(2)}) collective-permute-start(f32[2,32,1024]{2,1,0:T(8,128)S(1)} %dynamic-slice_bitcast_fusion.2), channel_id=1, source_target_pairs={{0,4},{1,5},{2,6},{3,7},{4,0},{5,1},{6,2},{7,3},{8,12},{9,13},{10,... | collective-permute-start | bytes 786440 | tf_op jit(solution)/shard_map/sketch_reduce/ppermute | solution.py:8
  133.6 6.3 %collective-permute-done.2 = f32[2,32,1024]{2,1,0:T(8,128)S(1)} collective-permute-done((f32[2,32,1024]{2,1,0:T(8,128)S(1)}, f32[2,32,1024]{2,1,0:T(8,128)S(1)}, u32[]{:S(2)}, u32[]{:S(2)}) %collective-permute-start.2) | collective-permute-done | bytes 262176 | tf_op jit(solution)/shard_map/sketch_reduce/ppermute | solution.py:8
  139.9 2.7 collective-permute-start.3
  142.6 5.7 %collective-permute-done.3 = f32[1,32,1024]{2,1,0:T(8,128)S(1)} collective-permute-done((f32[1,32,1024]{2,1,0:T(8,128)S(1)}, f32[1,32,1024]{2,1,0:T(8,128)S(1)}, u32[]{:S(2)}, u32[]{:S(2)}) %collective-permute-start.3) | collective-permute-done | bytes 131104 | tf_op jit(solution)/shard_map/sketch_reduce/ppermute | solution.py:8
  148.7 7.9 %collective-permute-done.4 = f32[1,32,1024]{2,1,0:T(8,128)S(1)} collective-permute-done((f32[1,32,1024]{2,1,0:T(8,128)S(1)}, f32[1,32,1024]{2,1,0:T(8,128)S(1)}, u32[]{:S(2)}, u32[]{:S(2)}) %collective-permute-start.4) | collective-permute-done | bytes 131104 | tf_op jit(solution)/shard_map/sketch_gather/ppermute | solution.py:8
  156.7 8.2 %collective-permute-done.5 = f32[2,32,1024]{2,1,0:T(8,128)S(1)} collective-permute-done((f32[2,32,1024]{2,1,0:T(8,128)S(1)}, f32[2,32,1024]{2,1,0:T(8,128)S(1)}, u32[]{:S(2)}, u32[]{:S(2)}) %collective-permute-start.5) | collective-permute-done | bytes 262176 | tf_op jit(solution)/shard_map/sketch_gather/ppermute | solution.py:8
  165.1 13.0 %collective-permute-done.6 = f32[4,32,1024]{2,1,0:T(8,128)S(1)} collective-permute-done((f32[4,32,1024]{2,1,0:T(8,128)S(1)}, f32[4,32,1024]{2,1,0:T(8,128)S(1)}, u32[]{:S(2)}, u32[]{:S(2)}) %collective-permute-start.6) | collective-permute-done | bytes 524320 | tf_op jit(solution)/shard_map/sketch_gather/ppermute | solution.py:8
  178.9 1.7 convert_reduce_fusion
  181.9 3.5 %fusion.61 = f32[512,512]{1,0:T(8,128)S(1)} fusion(f32[512,1024]{1,0:T(8,128)S(1)} %bitcast.118), kind=kOutput, calls=%fused_computation.127 | convolution fusion | flops 3221225472 | bytes 3145728 | tf_op jit(solution)/shard_map/kernel_matrix/dot_general | solution.py:59
  186.1 11.7 %cholesky.103 = f32[128,128]{1,0:T(8,128)S(1)} custom-call(f32[128,128]{1,0:T(8,128)S(1)} %cholesky.263), custom_call_target="Cholesky" | custom-call | tf_op jit(solution)/shard_map/kernel_solve/jit(cholesky)/cholesky | solution.py:62
  198.0 9.8 %custom-call.32 = f32[1,128,128]{1,2,0:T(8,128)S(1)} custom-call(f32[1,128,128]{2,1,0:T(8,128)S(1)} %get-tuple-element.37), custom_call_target="InvertDiagBlocksLowerTriangular" | custom-call | tf_op jit(solution)/shard_map/kernel_solve/jit(cholesky)/cholesky | solution.py:62
  208.5 11.9 %cholesky.215 = f32[128,128]{1,0:T(8,128)S(1)} custom-call(f32[128,128]{1,0:T(8,128)S(1)} %cholesky.267), custom_call_target="Cholesky" | custom-call | tf_op jit(solution)/shard_map/kernel_solve/jit(cholesky)/cholesky | solution.py:62
  220.5 9.8 %custom-call.33 = f32[1,128,128]{1,2,0:T(8,128)S(1)} custom-call(f32[1,128,128]{2,1,0:T(8,128)S(1)} %get-tuple-element.34), custom_call_target="InvertDiagBlocksLowerTriangular" | custom-call | tf_op jit(solution)/shard_map/kernel_solve/jit(cholesky)/cholesky | solution.py:62
  230.9 11.7 %cholesky.236 = f32[128,128]{1,0:T(8,128)S(1)} custom-call(f32[128,128]{1,0:T(8,128)S(1)} %cholesky.272), custom_call_target="Cholesky" | custom-call | tf_op jit(solution)/shard_map/kernel_solve/jit(cholesky)/cholesky | solution.py:62
  242.7 9.8 %custom-call.34 = f32[1,128,128]{1,2,0:T(8,128)S(1)} custom-call(f32[1,128,128]{2,1,0:T(8,128)S(1)} %get-tuple-element.31), custom_call_target="InvertDiagBlocksLowerTriangular" | custom-call | tf_op jit(solution)/shard_map/kernel_solve/jit(cholesky)/cholesky | solution.py:62
  253.4 11.7 %cholesky.253 = f32[128,128]{1,0:T(8,128)S(1)} custom-call(f32[128,128]{1,0:T(8,128)S(1)} %convolution_subtract_fusion.2), custom_call_target="Cholesky" | custom-call | tf_op jit(solution)/shard_map/kernel_solve/jit(cholesky)/cholesky | solution.py:62
  269.8 10.5 %while.1 = (s32[]{:T(128)}, f32[512,512]{1,0:T(8,128)S(1)}, s32[4,2]{0,1:T(2,128)S(1)}, f32[4,128,128]{2,1,0:T(8,128)}, s32[]{:T(128)}) while((s32[]{:T(128)}, f32[512,512]{1,0:T(8,128)S(1)}, s32[4,2]{0,1:T(2,128)S(1)}, f32[4,128,128]{2,1,0:T(8,128)}, s32[]{:T(128)}) %tuple.35), condition=%wide.while_cond, body=%wide.while_body.sunk | while | flops 2 | bytes 132205 | solution.py:64
  270.5 2.0 bitcast_dynamic-update-slice_fusion.2
  273.1 2.0 bitcast_dynamic-update-slice_fusion.2
  275.7 2.0 bitcast_dynamic-update-slice_fusion.2
  278.3 2.0 bitcast_dynamic-update-slice_fusion.2
  280.3 40.1 %custom-call.35 = f32[4,128,128]{1,2,0:T(8,128)S(1)} custom-call(f32[4,128,128]{2,1,0:T(8,128)} %get-tuple-element.9), custom_call_target="InvertDiagBlocksLowerTriangular" | custom-call | tf_op jit(solution)/shard_map/kernel_solve/triangular_solve | solution.py:64
  323.4 0.8 fusion.20
  (77 shorter events, 13.7 us)
Async XLA Ops:
  5.3 85.1 %all-to-all-start = ((bf16[32,16,4096]{2,0,1:T(8,128)(2,1)}), bf16[32,16,4096]{2,0,1:T(8,128)(2,1)}, u32[]{:S(2)}, u32[]{:S(2)}) async-start(bf16[32,16,4096]{2,0,1:T(8,128)(2,1)} %bitcast.119), calls=%async_computation | async-start | bytes 8388608 | tf_op jit(solution)/shard_map/gradient_exchange/all_to_all | solution.py:41
  98.7 3.3 %collective-permute-start = (f32[8,32,1024]{2,1,0:T(8,128)S(1)}, f32[8,32,1024]{2,1,0:T(8,128)}, u32[]{:S(2)}, u32[]{:S(2)}) collective-permute-start(f32[8,32,1024]{2,1,0:T(8,128)S(1)} %dynamic-slice_bitcast_fusion), channel_id=1, source_target_pairs={{0,1},{1,0},{2,3},{3,2},{4,5},{5,4},{6,7},{7,6},{8,9},{9,8},{10,11... | collective-permute-start | bytes 3145736 | tf_op jit(solution)/shard_map/sketch_reduce/ppermute | solution.py:8
  103.3 18.7 %collective-permute-start.1 = (f32[4,32,1024]{2,1,0:T(8,128)S(1)}, f32[4,32,1024]{2,1,0:T(8,128)S(1)}, u32[]{:S(2)}, u32[]{:S(2)}) collective-permute-start(f32[4,32,1024]{2,1,0:T(8,128)S(1)} %dynamic-slice_bitcast_fusion.1), channel_id=1, source_target_pairs={{0,2},{1,3},{2,0},{3,1},{4,6},{5,7},{6,4},{7,5},{8,10},{9,11},{10,... | collective-permute-start | bytes 1572872 | tf_op jit(solution)/shard_map/sketch_reduce/ppermute | solution.py:8
  122.2 17.7 %collective-permute-start.2 = (f32[2,32,1024]{2,1,0:T(8,128)S(1)}, f32[2,32,1024]{2,1,0:T(8,128)S(1)}, u32[]{:S(2)}, u32[]{:S(2)}) collective-permute-start(f32[2,32,1024]{2,1,0:T(8,128)S(1)} %dynamic-slice_bitcast_fusion.2), channel_id=1, source_target_pairs={{0,4},{1,5},{2,6},{3,7},{4,0},{5,1},{6,2},{7,3},{8,12},{9,13},{10,... | collective-permute-start | bytes 786440 | tf_op jit(solution)/shard_map/sketch_reduce/ppermute | solution.py:8
  139.9 8.4 %collective-permute-start.3 = (f32[1,32,1024]{2,1,0:T(8,128)S(1)}, f32[1,32,1024]{2,1,0:T(8,128)S(1)}, u32[]{:S(2)}, u32[]{:S(2)}) collective-permute-start(f32[1,32,1024]{2,1,0:T(8,128)S(1)} %constant_dynamic-slice_fusion.1), channel_id=1, source_target_pairs={{0,8},{1,9},{2,10},{3,11},{4,12},{5,13},{6,14},{7,15},{8,0},{9,1},... | collective-permute-start | bytes 393224 | tf_op jit(solution)/shard_map/sketch_reduce/ppermute | solution.py:8
  148.3 29.9 %copy-start = (f32[1,32,1024]{2,1,0:T(8,128)}, f32[1,32,1024]{2,1,0:T(8,128)S(1)}, u32[]{:S(2)}) copy-start(f32[1,32,1024]{2,1,0:T(8,128)S(1)} %dynamic-slice_add_fusion) | copy-start | bytes 393220
  148.4 8.2 %collective-permute-start.4 = (f32[1,32,1024]{2,1,0:T(8,128)S(1)}, f32[1,32,1024]{2,1,0:T(8,128)S(1)}, u32[]{:S(2)}, u32[]{:S(2)}) collective-permute-start(f32[1,32,1024]{2,1,0:T(8,128)S(1)} %dynamic-slice_add_fusion), channel_id=1, source_target_pairs={{0,8},{1,9},{2,10},{3,11},{4,12},{5,13},{6,14},{7,15},{8,0},{9,1},... | collective-permute-start | bytes 393224 | tf_op jit(solution)/shard_map/sketch_gather/ppermute | solution.py:8
  156.6 8.3 %collective-permute-start.5 = (f32[2,32,1024]{2,1,0:T(8,128)S(1)}, f32[2,32,1024]{2,1,0:T(8,128)S(1)}, u32[]{:S(2)}, u32[]{:S(2)}) collective-permute-start(f32[2,32,1024]{2,1,0:T(8,128)S(1)} %maximum_bitcast_fusion), channel_id=1, source_target_pairs={{0,4},{1,5},{2,6},{3,7},{4,0},{5,1},{6,2},{7,3},{8,12},{9,13},{10,... | collective-permute-start | bytes 786440 | tf_op jit(solution)/shard_map/sketch_gather/ppermute | solution.py:8
  165.0 13.1 %collective-permute-start.6 = (f32[4,32,1024]{2,1,0:T(8,128)S(1)}, f32[4,32,1024]{2,1,0:T(8,128)S(1)}, u32[]{:S(2)}, u32[]{:S(2)}) collective-permute-start(f32[4,32,1024]{2,1,0:T(8,128)S(1)} %bitcast.124), channel_id=1, source_target_pairs={{0,2},{1,3},{2,0},{3,1},{4,6},{5,7},{6,4},{7,5},{8,10},{9,11},{10,... | collective-permute-start | bytes 1572872 | tf_op jit(solution)/shard_map/sketch_gather/ppermute | solution.py:8
  178.2 0.7 copy-start.2
  178.2 0.7 copy-start.1
  178.4 2.7 collective-permute-start.7

commit v2 on v1

--- a/solution.py
+++ b/solution.py
@@ -2,6 +2,60 @@
 import jax.numpy as jnp
 from jax import lax
 from jax.sharding import PartitionSpec as P
+import functools
+from jax.experimental import pallas as pl
+from jax.experimental.pallas import tpu as pltpu
+
+HI = lax.Precision.HIGHEST
+
+def _invert_block(block):
+    size = block.shape[0]
+    lane = lax.broadcasted_iota(jnp.int32, block.shape, 1)
+    sub = lax.broadcasted_iota(jnp.int32, block.shape, 0)
+    lane_row = lax.broadcasted_iota(jnp.int32, (1, size), 1)
+    sub_col = lax.broadcasted_iota(jnp.int32, (size, 1), 0)
+
+    def step(k, a):
+        row = jnp.sum(jnp.where(sub == k, a, 0.0), axis=0, keepdims=True)
+        col = jnp.sum(jnp.where(lane == k, a, 0.0), axis=1, keepdims=True)
+        pivot = jnp.sum(jnp.where(lane_row == k, row, 0.0), axis=1, keepdims=True)
+        scaled = jnp.where(lane_row == k, 1.0, row) / pivot
+        col = jnp.where(sub_col == k, 0.0, col)
+        a = jnp.where(lane == k, 0.0, a) - col * scaled
+        return jnp.where(sub == k, scaled, a)
+
+    return lax.fori_loop(0, size, step, block)
+
+
+def _solve_kernel(m_ref, w_ref, y_ref, a_ref, *, block):
+    n = m_ref.shape[0]
+    a_ref[:, :n] = m_ref[...]
+    a_ref[:, n:] = w_ref[...]
+    blocks = n // block
+    for j in range(blocks):
+        lo = j * block
+        inverse = _invert_block(a_ref[lo:lo + block, lo:lo + block])
+        pivot_rows = jnp.dot(inverse, a_ref[lo:lo + block, lo:], precision=HI,
+                             preferred_element_type=jnp.float32)
+        for i in range(blocks):
+            if i == j:
+                continue
+            r = i * block
+            a_ref[r:r + block, lo:] = a_ref[r:r + block, lo:] - jnp.dot(
+                a_ref[r:r + block, lo:lo + block], pivot_rows, precision=HI,
+                preferred_element_type=jnp.float32)
+        a_ref[lo:lo + block, lo:] = pivot_rows
+    y_ref[...] = a_ref[:, n:]
+
+
+def spd_solve(system, rhs, block=128, interpret=False):
+    n = system.shape[0]
+    return pl.pallas_call(
+        functools.partial(_solve_kernel, block=block),
+        out_shape=jax.ShapeDtypeStruct(rhs.shape, jnp.float32),
+        scratch_shapes=[pltpu.VMEM((n, n + rhs.shape[1]), jnp.float32)],
+        interpret=interpret,
+    )(system, rhs)
 
 
 def partner(array, axis, bit):
@@ -54,16 +108,14 @@
     weight = jnp.sum(matches.astype(jnp.float32), axis=1) / target_counts[:, None].astype(
         jnp.float32
     )
-    if examples < sketch_width:
+    if examples < sketch_width and examples % 128 == 0:
         with jax.named_scope("kernel_matrix"):
             kernel = jnp.dot(sketch_all, sketch_all.T, precision=lax.Precision.HIGHEST)
         with jax.named_scope("kernel_solve"):
             system = kernel / jnp.float32(examples) + 0.1 * jnp.eye(examples, dtype=jnp.float32)
-            factor = jnp.linalg.cholesky(system)
-            middle = lax.linalg.triangular_solve(factor, weight.T, left_side=True, lower=True)
-            coeffs = lax.linalg.triangular_solve(
-                factor, middle, left_side=True, lower=True, transpose_a=True
-            )
+            lanes = -(-weight.shape[0] // 128) * 128
+            rhs = jnp.pad(weight.T, ((0, 0), (0, lanes - weight.shape[0])))
+            coeffs = spd_solve(system, rhs, block=min(128, examples))[:, : weight.shape[0]]
         own_kernel = lax.dynamic_slice_in_dim(kernel, position * ex_rows, ex_rows, axis=0)
         scores = jnp.dot(own_kernel, coeffs, precision=lax.Precision.HIGHEST)
     else:

time: 328 us -> 256 us (0.78); the launches traced: 325 us -> 256 us
  other arithmetic: 123 us -> 3.83 us
  Pallas kernels: 0 us -> 67.4 us
  local copies, waits for them, and re-layouts: 16.5 us -> 6.43 us
    another operation x17 -> x0, other arithmetic: 119 us -> none  [the longest x14 78.7 us: on_device(): factor = jnp.linalg.cholesky(system)]
    pallas_call x0 -> x1, Pallas kernels: none -> 67.4 us  [spd_solve(): pl.pallas_call(functools.partial(_solve_kernel, block=block), out_shape=j...]
    another operation x17 -> x0, local copies, waits for them, and re-layouts: 10.6 us -> none
    another operation x20 -> x0, matrix products: 5.02 us -> none  [the longest x6 2.12 us: on_device(): factor = jnp.linalg.cholesky(system)]
  transfers between devices with their start and end apart: 9 -> 9, of which waited for: 9 -> 8; matrix products, arithmetic and copies ran while one was open for 1% -> 1% of each run, Pallas kernels for 0% -> 0%
where the time goes in v2:
time: 256 us
  waiting for transfers between devices  134 us (52%)
  Pallas kernels  67.4 us (26%)
  starting transfers between devices  29.1 us (11%)
  matrix products  14.8 us (6%)
  local copies, waits for them, and re-layouts  6.43 us (3%)
  other arithmetic  3.83 us (1%)
    all_to_all x1, waiting for transfers between devices, on_device(): lax.all_to_all(grads, 'ex', split_axis=1, concat_axis=0, tiled=True)  77.7 us
    pallas_call x1, Pallas kernels, spd_solve(): pl.pallas_call(functools.partial(_solve_kernel, block=block), out_shape=j...  67.4 us
    ppermute x8, waiting for transfers between devices, partner(): lax.ppermute(array, axis, [(i, i ^ 1 << bit) for i in range(lax.axis_size...  56 us
    ppermute x8, starting transfers between devices, partner(): lax.ppermute(array, axis, [(i, i ^ 1 << bit) for i in range(lax.axis_size...  21.7 us
    dot_general x1, matrix products, on_device(): partial_value = jnp.dot(columns, proj, preferred_element_type=jnp.float32)  8.14 us
    all_to_all x1, starting transfers between devices, on_device(): lax.all_to_all(grads, 'ex', split_axis=1, concat_axis=0, tiled=True)  7.44 us
  transfers between devices with their start and end apart: 9, of which 8 were waited for; matrix products, arithmetic and copies ran while one was open for 1% of the time, Pallas kernels for 0%

profile of v2, /device:TPU:0, one launch (start us, length us, event | category | flops | bytes accessed | tf_op | source)
XLA Modules:
  0.0 256.1 jit_solution(4509795096111854018)
XLA Ops:
  0.6 4.7 %copy.29 = bf16[4,16,8,4096]{3,2,0,1:T(8,128)(2,1)} copy(bf16[4,16,8,4096]{3,2,1,0:T(8,128)(2,1)} %bitcast.66) | data formatting | bytes 8388608 | tf_op jit(solution)/shard_map/gradient_exchange/all_to_all | solution.py:95
  5.3 7.4 %all-to-all-start = ((bf16[32,16,4096]{2,0,1:T(8,128)(2,1)}), bf16[32,16,4096]{2,0,1:T(8,128)(2,1)}, u32[]{:S(2)}, u32[]{:S(2)}) async-start(bf16[32,16,4096]{2,0,1:T(8,128)(2,1)} %bitcast.64), calls=%async_computation | async-start | bytes 8388608 | tf_op jit(solution)/shard_map/gradient_exchange/all_to_all | solution.py:95
  12.7 77.7 %all-to-all-done = bf16[32,16,4096]{2,0,1:T(8,128)(2,1)} async-done(((bf16[32,16,4096]{2,0,1:T(8,128)(2,1)}), bf16[32,16,4096]{2,0,1:T(8,128)(2,1)}, u32[]{:S(2)}, u32[]{:S(2)}) %all-to-all-start) | async-done | bytes 4194336 | tf_op jit(solution)/shard_map/gradient_exchange/all_to_all | solution.py:95
  90.4 8.1 %fusion = f32[8,2,32,1024]{3,2,1,0:T(8,128)S(1)} fusion(bf16[8,2,32,4096]{3,2,1,0:T(8,128)(2,1)} %bitcast.1, bf16[4096,1024]{1,0:T(8,128)(2,1)} %param.5), kind=kOutput, calls=%fused_computation | convolution fusion | flops 4294967296 | bytes 14680064 | tf_op jit(solution)/shard_map/partial_projection/dot_general | solution.py:97
  98.6 0.1 dynamic-slice_bitcast_fusion
  98.7 0.8 collective-permute-start
  99.5 2.4 collective-permute-done
  101.9 1.4 bitcast_add_fusion
  103.3 6.3 %collective-permute-start.1 = (f32[4,32,1024]{2,1,0:T(8,128)S(1)}, f32[4,32,1024]{2,1,0:T(8,128)S(1)}, u32[]{:S(2)}, u32[]{:S(2)}) collective-permute-start(f32[4,32,1024]{2,1,0:T(8,128)S(1)} %dynamic-slice_bitcast_fusion.1), channel_id=1, source_target_pairs={{0,2},{1,3},{2,0},{3,1},{4,6},{5,7},{6,4},{7,5},{8,10},{9,11},{10,... | collective-permute-start | bytes 1572872 | tf_op jit(solution)/shard_map/sketch_reduce/ppermute | solution.py:62
  109.6 12.4 %collective-permute-done.1 = f32[4,32,1024]{2,1,0:T(8,128)S(1)} collective-permute-done((f32[4,32,1024]{2,1,0:T(8,128)S(1)}, f32[4,32,1024]{2,1,0:T(8,128)S(1)}, u32[]{:S(2)}, u32[]{:S(2)}) %collective-permute-start.1) | collective-permute-done | bytes 524320 | tf_op jit(solution)/shard_map/sketch_reduce/ppermute | solution.py:62
  122.2 11.4 %collective-permute-start.2 = (f32[2,32,1024]{2,1,0:T(8,128)S(1)}, f32[2,32,1024]{2,1,0:T(8,128)S(1)}, u32[]{:S(2)}, u32[]{:S(2)}) collective-permute-start(f32[2,32,1024]{2,1,0:T(8,128)S(1)} %dynamic-slice_bitcast_fusion.2), channel_id=1, source_target_pairs={{0,4},{1,5},{2,6},{3,7},{4,0},{5,1},{6,2},{7,3},{8,12},{9,13},{10,... | collective-permute-start | bytes 786440 | tf_op jit(solution)/shard_map/sketch_reduce/ppermute | solution.py:62
  133.6 6.3 %collective-permute-done.2 = f32[2,32,1024]{2,1,0:T(8,128)S(1)} collective-permute-done((f32[2,32,1024]{2,1,0:T(8,128)S(1)}, f32[2,32,1024]{2,1,0:T(8,128)S(1)}, u32[]{:S(2)}, u32[]{:S(2)}) %collective-permute-start.2) | collective-permute-done | bytes 262176 | tf_op jit(solution)/shard_map/sketch_reduce/ppermute | solution.py:62
  139.9 2.7 %collective-permute-start.3 = (f32[1,32,1024]{2,1,0:T(8,128)S(1)}, f32[1,32,1024]{2,1,0:T(8,128)S(1)}, u32[]{:S(2)}, u32[]{:S(2)}) collective-permute-start(f32[1,32,1024]{2,1,0:T(8,128)S(1)} %constant_dynamic-slice_fusion), channel_id=1, source_target_pairs={{0,8},{1,9},{2,10},{3,11},{4,12},{5,13},{6,14},{7,15},{8,0},{9,1},... | collective-permute-start | bytes 393224 | tf_op jit(solution)/shard_map/sketch_reduce/ppermute | solution.py:62
  142.6 5.7 %collective-permute-done.3 = f32[1,32,1024]{2,1,0:T(8,128)S(1)} collective-permute-done((f32[1,32,1024]{2,1,0:T(8,128)S(1)}, f32[1,32,1024]{2,1,0:T(8,128)S(1)}, u32[]{:S(2)}, u32[]{:S(2)}) %collective-permute-start.3) | collective-permute-done | bytes 131104 | tf_op jit(solution)/shard_map/sketch_reduce/ppermute | solution.py:62
  148.4 0.3 collective-permute-start.4
  148.7 7.9 %collective-permute-done.4 = f32[1,32,1024]{2,1,0:T(8,128)S(1)} collective-permute-done((f32[1,32,1024]{2,1,0:T(8,128)S(1)}, f32[1,32,1024]{2,1,0:T(8,128)S(1)}, u32[]{:S(2)}, u32[]{:S(2)}) %collective-permute-start.4) | collective-permute-done | bytes 131104 | tf_op jit(solution)/shard_map/sketch_gather/ppermute | solution.py:62
  156.6 0.1 collective-permute-start.5
  156.7 8.2 %collective-permute-done.5 = f32[2,32,1024]{2,1,0:T(8,128)S(1)} collective-permute-done((f32[2,32,1024]{2,1,0:T(8,128)S(1)}, f32[2,32,1024]{2,1,0:T(8,128)S(1)}, u32[]{:S(2)}, u32[]{:S(2)}) %collective-permute-start.5) | collective-permute-done | bytes 262176 | tf_op jit(solution)/shard_map/sketch_gather/ppermute | solution.py:62
  165.1 13.0 %collective-permute-done.6 = f32[4,32,1024]{2,1,0:T(8,128)S(1)} collective-permute-done((f32[4,32,1024]{2,1,0:T(8,128)S(1)}, f32[4,32,1024]{2,1,0:T(8,128)S(1)}, u32[]{:S(2)}, u32[]{:S(2)}) %collective-permute-start.6) | collective-permute-done | bytes 524320 | tf_op jit(solution)/shard_map/sketch_gather/ppermute | solution.py:62
  178.1 0.1 select_bitcast_fusion.3
  178.4 0.1 collective-permute-start.7
  178.5 0.4 copy-done.2
  178.9 0.1 iota_compare_fusion.2
  179.0 1.6 convert_reduce_fusion
  180.5 0.1 copy.24
  180.7 0.7 pad.4.w_ref
  181.4 0.2 select_bitcast_fusion.1
  181.7 0.1 pad_maximum_fusion
  181.8 0.2 copy.23
  182.1 4.5 %select_add_fusion = (f32[512,512]{1,0:T(8,128)}, f32[512,512]{1,0:T(8,128)S(1)}) fusion(f32[512,1024]{1,0:T(8,128)S(1)} %bitcast.63), kind=kOutput, calls=%fused_computation.9 | convolution fusion | flops 3222274048 | bytes 4194304 | tf_op jit(solution)/shard_map/kernel_matrix/dot_general | solution.py:113
  186.6 67.4 %kernel_solve.1 = f32[512,128]{1,0:T(8,128)} custom-call(f32[512,512]{1,0:T(8,128)} %get-tuple-element.10.m_ref, f32[512,128]{1,0:T(8,128)} %pad.4.w_ref), custom_call_target="tpu_custom_call" | custom-call | tf_op jit(solution)/shard_map/kernel_solve/pallas_call | solution.py:53
  254.0 2.1 fusion.3
  (21 shorter events, 0.6 us)
Async XLA Ops:
  5.3 85.1 %all-to-all-start = ((bf16[32,16,4096]{2,0,1:T(8,128)(2,1)}), bf16[32,16,4096]{2,0,1:T(8,128)(2,1)}, u32[]{:S(2)}, u32[]{:S(2)}) async-start(bf16[32,16,4096]{2,0,1:T(8,128)(2,1)} %bitcast.64), calls=%async_computation | async-start | bytes 8388608 | tf_op jit(solution)/shard_map/gradient_exchange/all_to_all | solution.py:95
  98.7 3.3 %collective-permute-start = (f32[8,32,1024]{2,1,0:T(8,128)S(1)}, f32[8,32,1024]{2,1,0:T(8,128)}, u32[]{:S(2)}, u32[]{:S(2)}) collective-permute-start(f32[8,32,1024]{2,1,0:T(8,128)S(1)} %dynamic-slice_bitcast_fusion), channel_id=1, source_target_pairs={{0,1},{1,0},{2,3},{3,2},{4,5},{5,4},{6,7},{7,6},{8,9},{9,8},{10,11... | collective-permute-start | bytes 3145736 | tf_op jit(solution)/shard_map/sketch_reduce/ppermute | solution.py:62
  103.3 18.7 %collective-permute-start.1 = (f32[4,32,1024]{2,1,0:T(8,128)S(1)}, f32[4,32,1024]{2,1,0:T(8,128)S(1)}, u32[]{:S(2)}, u32[]{:S(2)}) collective-permute-start(f32[4,32,1024]{2,1,0:T(8,128)S(1)} %dynamic-slice_bitcast_fusion.1), channel_id=1, source_target_pairs={{0,2},{1,3},{2,0},{3,1},{4,6},{5,7},{6,4},{7,5},{8,10},{9,11},{10,... | collective-permute-start | bytes 1572872 | tf_op jit(solution)/shard_map/sketch_reduce/ppermute | solution.py:62
  122.2 17.7 %collective-permute-start.2 = (f32[2,32,1024]{2,1,0:T(8,128)S(1)}, f32[2,32,1024]{2,1,0:T(8,128)S(1)}, u32[]{:S(2)}, u32[]{:S(2)}) collective-permute-start(f32[2,32,1024]{2,1,0:T(8,128)S(1)} %dynamic-slice_bitcast_fusion.2), channel_id=1, source_target_pairs={{0,4},{1,5},{2,6},{3,7},{4,0},{5,1},{6,2},{7,3},{8,12},{9,13},{10,... | collective-permute-start | bytes 786440 | tf_op jit(solution)/shard_map/sketch_reduce/ppermute | solution.py:62
  139.9 8.4 %collective-permute-start.3 = (f32[1,32,1024]{2,1,0:T(8,128)S(1)}, f32[1,32,1024]{2,1,0:T(8,128)S(1)}, u32[]{:S(2)}, u32[]{:S(2)}) collective-permute-start(f32[1,32,1024]{2,1,0:T(8,128)S(1)} %constant_dynamic-slice_fusion), channel_id=1, source_target_pairs={{0,8},{1,9},{2,10},{3,11},{4,12},{5,13},{6,14},{7,15},{8,0},{9,1},... | collective-permute-start | bytes 393224 | tf_op jit(solution)/shard_map/sketch_reduce/ppermute | solution.py:62
  148.3 29.9 %copy-start = (f32[1,32,1024]{2,1,0:T(8,128)}, f32[1,32,1024]{2,1,0:T(8,128)S(1)}, u32[]{:S(2)}) copy-start(f32[1,32,1024]{2,1,0:T(8,128)S(1)} %dynamic-slice_add_fusion) | copy-start | bytes 393220
  148.4 8.2 %collective-permute-start.4 = (f32[1,32,1024]{2,1,0:T(8,128)S(1)}, f32[1,32,1024]{2,1,0:T(8,128)S(1)}, u32[]{:S(2)}, u32[]{:S(2)}) collective-permute-start(f32[1,32,1024]{2,1,0:T(8,128)S(1)} %dynamic-slice_add_fusion), channel_id=1, source_target_pairs={{0,8},{1,9},{2,10},{3,11},{4,12},{5,13},{6,14},{7,15},{8,0},{9,1},... | collective-permute-start | bytes 393224 | tf_op jit(solution)/shard_map/sketch_gather/ppermute | solution.py:62
  156.6 8.3 %collective-permute-start.5 = (f32[2,32,1024]{2,1,0:T(8,128)S(1)}, f32[2,32,1024]{2,1,0:T(8,128)S(1)}, u32[]{:S(2)}, u32[]{:S(2)}) collective-permute-start(f32[2,32,1024]{2,1,0:T(8,128)S(1)} %maximum_bitcast_fusion), channel_id=1, source_target_pairs={{0,4},{1,5},{2,6},{3,7},{4,0},{5,1},{6,2},{7,3},{8,12},{9,13},{10,... | collective-permute-start | bytes 786440 | tf_op jit(solution)/shard_map/sketch_gather/ppermute | solution.py:62
  165.0 13.1 %collective-permute-start.6 = (f32[4,32,1024]{2,1,0:T(8,128)S(1)}, f32[4,32,1024]{2,1,0:T(8,128)S(1)}, u32[]{:S(2)}, u32[]{:S(2)}) collective-permute-start(f32[4,32,1024]{2,1,0:T(8,128)S(1)} %bitcast.69), channel_id=1, source_target_pairs={{0,2},{1,3},{2,0},{3,1},{4,6},{5,7},{6,4},{7,5},{8,10},{9,11},{10,... | collective-permute-start | bytes 1572872 | tf_op jit(solution)/shard_map/sketch_gather/ppermute | solution.py:62
  178.2 0.7 copy-start.2
  178.2 0.7 copy-start.1
  178.4 3.0 %collective-permute-start.7 = (f32[8,32,1024]{2,1,0:T(8,128)S(1)}, f32[8,32,1024]{2,1,0:T(8,128)S(1)}, u32[]{:S(2)}, u32[]{:S(2)}) collective-permute-start(f32[8,32,1024]{2,1,0:T(8,128)S(1)} %bitcast.65), channel_id=1, source_target_pairs={{0,1},{1,0},{2,3},{3,2},{4,5},{5,4},{6,7},{7,6},{8,9},{9,8},{10,11... | collective-permute-start | bytes 3145736 | tf_op jit(solution)/shard_map/sketch_gather/ppermute | solution.py:62

commit v3 on v2

--- a/solution.py
+++ b/solution.py
@@ -15,16 +15,33 @@
     lane_row = lax.broadcasted_iota(jnp.int32, (1, size), 1)
     sub_col = lax.broadcasted_iota(jnp.int32, (size, 1), 0)
 
-    def step(k, a):
-        row = jnp.sum(jnp.where(sub == k, a, 0.0), axis=0, keepdims=True)
-        col = jnp.sum(jnp.where(lane == k, a, 0.0), axis=1, keepdims=True)
-        pivot = jnp.sum(jnp.where(lane_row == k, row, 0.0), axis=1, keepdims=True)
-        scaled = jnp.where(lane_row == k, 1.0, row) / pivot
-        col = jnp.where(sub_col == k, 0.0, col)
-        a = jnp.where(lane == k, 0.0, a) - col * scaled
-        return jnp.where(sub == k, scaled, a)
+    def pick(row, k):
+        return jnp.sum(jnp.where(lane_row == k, row, 0.0), axis=1, keepdims=True)
 
-    return lax.fori_loop(0, size, step, block)
+    def step(h, a):
+        k = 2 * h
+        row0 = jnp.sum(jnp.where(sub == k, a, 0.0), axis=0, keepdims=True)
+        row1 = jnp.sum(jnp.where(sub == k + 1, a, 0.0), axis=0, keepdims=True)
+        col0 = jnp.sum(jnp.where(lane == k, a, 0.0), axis=1, keepdims=True)
+        col1 = jnp.sum(jnp.where(lane == k + 1, a, 0.0), axis=1, keepdims=True)
+        p00 = pick(row0, k)
+        p01 = pick(row0, k + 1)
+        p10 = pick(row1, k)
+        p11 = pick(row1, k + 1)
+        det = p00 * p11 - p01 * p10
+        ident0 = jnp.where(lane_row == k, 1.0, jnp.where(lane_row == k + 1, 0.0, row0))
+        ident1 = jnp.where(lane_row == k, 0.0, jnp.where(lane_row == k + 1, 1.0, row1))
+        scaled0 = (p11 * ident0 - p01 * ident1) / det
+        scaled1 = (p00 * ident1 - p10 * ident0) / det
+        pivot_rows = (sub_col == k) | (sub_col == k + 1)
+        col0 = jnp.where(pivot_rows, 0.0, col0)
+        col1 = jnp.where(pivot_rows, 0.0, col1)
+        pivot_cols = (lane == k) | (lane == k + 1)
+        a = jnp.where(pivot_cols, 0.0, a) - col0 * scaled0 - col1 * scaled1
+        a = jnp.where(sub == k, scaled0, a)
+        return jnp.where(sub == k + 1, scaled1, a)
+
+    return lax.fori_loop(0, size // 2, step, block)
 
 
 def _solve_kernel(m_ref, w_ref, y_ref, a_ref, *, block):

time: 256 us -> 235 us (0.918)
  Pallas kernels: 67.4 us -> 45.9 us
    pallas_call x1, Pallas kernels: 67.4 us -> 45.9 us  [spd_solve(): pl.pallas_call(functools.partial(_solve_kernel, block=block), out_shape=j...]
where the time goes in v3:
time: 235 us
  waiting for transfers between devices  134 us (57%)
  Pallas kernels  45.9 us (20%)
  starting transfers between devices  29.1 us (12%)
  matrix products  14.8 us (6%)
  local copies, waits for them, and re-layouts  6.43 us (3%)
  other arithmetic  3.83 us (2%)
    all_to_all x1, waiting for transfers between devices, on_device(): lax.all_to_all(grads, 'ex', split_axis=1, concat_axis=0, tiled=True)  77.7 us
    ppermute x8, waiting for transfers between devices, partner(): lax.ppermute(array, axis, [(i, i ^ 1 << bit) for i in range(lax.axis_size...  56 us
    pallas_call x1, Pallas kernels, spd_solve(): pl.pallas_call(functools.partial(_solve_kernel, block=block), out_shape=j...  45.9 us
    ppermute x8, starting transfers between devices, partner(): lax.ppermute(array, axis, [(i, i ^ 1 << bit) for i in range(lax.axis_size...  21.7 us
    dot_general x1, matrix products, on_device(): partial_value = jnp.dot(columns, proj, preferred_element_type=jnp.float32)  8.14 us
    all_to_all x1, starting transfers between devices, on_device(): lax.all_to_all(grads, 'ex', split_axis=1, concat_axis=0, tiled=True)  7.44 us
  transfers between devices with their start and end apart: 9, of which 8 were waited for; matrix products, arithmetic and copies ran while one was open for 1% of the time, Pallas kernels for 0%

profile of v3, /device:TPU:0, one launch (start us, length us, event | category | flops | bytes accessed | tf_op | source)
XLA Modules:
  0.0 234.6 jit_solution(12359638168212335924)
XLA Ops:
  0.6 4.7 %copy.29 = bf16[4,16,8,4096]{3,2,0,1:T(8,128)(2,1)} copy(bf16[4,16,8,4096]{3,2,1,0:T(8,128)(2,1)} %bitcast.66) | data formatting | bytes 8388608 | tf_op jit(solution)/shard_map/gradient_exchange/all_to_all | solution.py:112
  5.3 7.4 %all-to-all-start = ((bf16[32,16,4096]{2,0,1:T(8,128)(2,1)}), bf16[32,16,4096]{2,0,1:T(8,128)(2,1)}, u32[]{:S(2)}, u32[]{:S(2)}) async-start(bf16[32,16,4096]{2,0,1:T(8,128)(2,1)} %bitcast.64), calls=%async_computation | async-start | bytes 8388608 | tf_op jit(solution)/shard_map/gradient_exchange/all_to_all | solution.py:112
  12.7 77.7 %all-to-all-done = bf16[32,16,4096]{2,0,1:T(8,128)(2,1)} async-done(((bf16[32,16,4096]{2,0,1:T(8,128)(2,1)}), bf16[32,16,4096]{2,0,1:T(8,128)(2,1)}, u32[]{:S(2)}, u32[]{:S(2)}) %all-to-all-start) | async-done | bytes 4194336 | tf_op jit(solution)/shard_map/gradient_exchange/all_to_all | solution.py:112
  90.4 8.1 %fusion = f32[8,2,32,1024]{3,2,1,0:T(8,128)S(1)} fusion(bf16[8,2,32,4096]{3,2,1,0:T(8,128)(2,1)} %bitcast.1, bf16[4096,1024]{1,0:T(8,128)(2,1)} %param.5), kind=kOutput, calls=%fused_computation | convolution fusion | flops 4294967296 | bytes 14680064 | tf_op jit(solution)/shard_map/partial_projection/dot_general | solution.py:114
  98.6 0.1 dynamic-slice_bitcast_fusion
  98.7 0.8 collective-permute-start
  99.5 2.4 %collective-permute-done = f32[8,32,1024]{2,1,0:T(8,128)} collective-permute-done((f32[8,32,1024]{2,1,0:T(8,128)S(1)}, f32[8,32,1024]{2,1,0:T(8,128)}, u32[]{:S(2)}, u32[]{:S(2)}) %collective-permute-start) | collective-permute-done | bytes 1048608 | tf_op jit(solution)/shard_map/sketch_reduce/ppermute | solution.py:79
  101.9 1.4 bitcast_add_fusion
  103.3 6.3 %collective-permute-start.1 = (f32[4,32,1024]{2,1,0:T(8,128)S(1)}, f32[4,32,1024]{2,1,0:T(8,128)S(1)}, u32[]{:S(2)}, u32[]{:S(2)}) collective-permute-start(f32[4,32,1024]{2,1,0:T(8,128)S(1)} %dynamic-slice_bitcast_fusion.1), channel_id=1, source_target_pairs={{0,2},{1,3},{2,0},{3,1},{4,6},{5,7},{6,4},{7,5},{8,10},{9,11},{10,... | collective-permute-start | bytes 1572872 | tf_op jit(solution)/shard_map/sketch_reduce/ppermute | solution.py:79
  109.6 12.4 %collective-permute-done.1 = f32[4,32,1024]{2,1,0:T(8,128)S(1)} collective-permute-done((f32[4,32,1024]{2,1,0:T(8,128)S(1)}, f32[4,32,1024]{2,1,0:T(8,128)S(1)}, u32[]{:S(2)}, u32[]{:S(2)}) %collective-permute-start.1) | collective-permute-done | bytes 524320 | tf_op jit(solution)/shard_map/sketch_reduce/ppermute | solution.py:79
  122.2 11.4 %collective-permute-start.2 = (f32[2,32,1024]{2,1,0:T(8,128)S(1)}, f32[2,32,1024]{2,1,0:T(8,128)S(1)}, u32[]{:S(2)}, u32[]{:S(2)}) collective-permute-start(f32[2,32,1024]{2,1,0:T(8,128)S(1)} %dynamic-slice_bitcast_fusion.2), channel_id=1, source_target_pairs={{0,4},{1,5},{2,6},{3,7},{4,0},{5,1},{6,2},{7,3},{8,12},{9,13},{10,... | collective-permute-start | bytes 786440 | tf_op jit(solution)/shard_map/sketch_reduce/ppermute | solution.py:79
  133.6 6.3 %collective-permute-done.2 = f32[2,32,1024]{2,1,0:T(8,128)S(1)} collective-permute-done((f32[2,32,1024]{2,1,0:T(8,128)S(1)}, f32[2,32,1024]{2,1,0:T(8,128)S(1)}, u32[]{:S(2)}, u32[]{:S(2)}) %collective-permute-start.2) | collective-permute-done | bytes 262176 | tf_op jit(solution)/shard_map/sketch_reduce/ppermute | solution.py:79
  139.9 2.7 %collective-permute-start.3 = (f32[1,32,1024]{2,1,0:T(8,128)S(1)}, f32[1,32,1024]{2,1,0:T(8,128)S(1)}, u32[]{:S(2)}, u32[]{:S(2)}) collective-permute-start(f32[1,32,1024]{2,1,0:T(8,128)S(1)} %constant_dynamic-slice_fusion), channel_id=1, source_target_pairs={{0,8},{1,9},{2,10},{3,11},{4,12},{5,13},{6,14},{7,15},{8,0},{9,1},... | collective-permute-start | bytes 393224 | tf_op jit(solution)/shard_map/sketch_reduce/ppermute | solution.py:79
  142.6 5.7 %collective-permute-done.3 = f32[1,32,1024]{2,1,0:T(8,128)S(1)} collective-permute-done((f32[1,32,1024]{2,1,0:T(8,128)S(1)}, f32[1,32,1024]{2,1,0:T(8,128)S(1)}, u32[]{:S(2)}, u32[]{:S(2)}) %collective-permute-start.3) | collective-permute-done | bytes 131104 | tf_op jit(solution)/shard_map/sketch_reduce/ppermute | solution.py:79
  148.4 0.3 collective-permute-start.4
  148.7 7.9 %collective-permute-done.4 = f32[1,32,1024]{2,1,0:T(8,128)S(1)} collective-permute-done((f32[1,32,1024]{2,1,0:T(8,128)S(1)}, f32[1,32,1024]{2,1,0:T(8,128)S(1)}, u32[]{:S(2)}, u32[]{:S(2)}) %collective-permute-start.4) | collective-permute-done | bytes 131104 | tf_op jit(solution)/shard_map/sketch_gather/ppermute | solution.py:79
  156.6 0.1 collective-permute-start.5
  156.7 8.2 %collective-permute-done.5 = f32[2,32,1024]{2,1,0:T(8,128)S(1)} collective-permute-done((f32[2,32,1024]{2,1,0:T(8,128)S(1)}, f32[2,32,1024]{2,1,0:T(8,128)S(1)}, u32[]{:S(2)}, u32[]{:S(2)}) %collective-permute-start.5) | collective-permute-done | bytes 262176 | tf_op jit(solution)/shard_map/sketch_gather/ppermute | solution.py:79
  165.1 13.0 %collective-permute-done.6 = f32[4,32,1024]{2,1,0:T(8,128)S(1)} collective-permute-done((f32[4,32,1024]{2,1,0:T(8,128)S(1)}, f32[4,32,1024]{2,1,0:T(8,128)S(1)}, u32[]{:S(2)}, u32[]{:S(2)}) %collective-permute-start.6) | collective-permute-done | bytes 524320 | tf_op jit(solution)/shard_map/sketch_gather/ppermute | solution.py:79
  178.1 0.1 select_bitcast_fusion.3
  178.4 0.1 collective-permute-start.7
  178.5 0.4 copy-done.2
  178.9 0.1 iota_compare_fusion.2
  179.0 1.6 convert_reduce_fusion
  180.5 0.1 copy.24
  180.7 0.7 pad.4.w_ref
  181.4 0.2 select_bitcast_fusion.1
  181.7 0.1 pad_maximum_fusion
  181.8 0.2 copy.23
  182.1 4.5 %select_add_fusion = (f32[512,512]{1,0:T(8,128)}, f32[512,512]{1,0:T(8,128)S(1)}) fusion(f32[512,1024]{1,0:T(8,128)S(1)} %bitcast.63), kind=kOutput, calls=%fused_computation.9 | convolution fusion | flops 3222274048 | bytes 4194304 | tf_op jit(solution)/shard_map/kernel_matrix/dot_general | solution.py:130
  186.6 45.9 %kernel_solve.1 = f32[512,128]{1,0:T(8,128)} custom-call(f32[512,512]{1,0:T(8,128)} %get-tuple-element.10.m_ref, f32[512,128]{1,0:T(8,128)} %pad.4.w_ref), custom_call_target="tpu_custom_call" | custom-call | tf_op jit(solution)/shard_map/kernel_solve/pallas_call | solution.py:70
  232.5 2.1 fusion.3
  (21 shorter events, 0.6 us)
Async XLA Ops:
  5.3 85.1 %all-to-all-start = ((bf16[32,16,4096]{2,0,1:T(8,128)(2,1)}), bf16[32,16,4096]{2,0,1:T(8,128)(2,1)}, u32[]{:S(2)}, u32[]{:S(2)}) async-start(bf16[32,16,4096]{2,0,1:T(8,128)(2,1)} %bitcast.64), calls=%async_computation | async-start | bytes 8388608 | tf_op jit(solution)/shard_map/gradient_exchange/all_to_all | solution.py:112
  98.7 3.3 %collective-permute-start = (f32[8,32,1024]{2,1,0:T(8,128)S(1)}, f32[8,32,1024]{2,1,0:T(8,128)}, u32[]{:S(2)}, u32[]{:S(2)}) collective-permute-start(f32[8,32,1024]{2,1,0:T(8,128)S(1)} %dynamic-slice_bitcast_fusion), channel_id=1, source_target_pairs={{0,1},{1,0},{2,3},{3,2},{4,5},{5,4},{6,7},{7,6},{8,9},{9,8},{10,11... | collective-permute-start | bytes 3145736 | tf_op jit(solution)/shard_map/sketch_reduce/ppermute | solution.py:79
  103.3 18.7 %collective-permute-start.1 = (f32[4,32,1024]{2,1,0:T(8,128)S(1)}, f32[4,32,1024]{2,1,0:T(8,128)S(1)}, u32[]{:S(2)}, u32[]{:S(2)}) collective-permute-start(f32[4,32,1024]{2,1,0:T(8,128)S(1)} %dynamic-slice_bitcast_fusion.1), channel_id=1, source_target_pairs={{0,2},{1,3},{2,0},{3,1},{4,6},{5,7},{6,4},{7,5},{8,10},{9,11},{10,... | collective-permute-start | bytes 1572872 | tf_op jit(solution)/shard_map/sketch_reduce/ppermute | solution.py:79
  122.2 17.7 %collective-permute-start.2 = (f32[2,32,1024]{2,1,0:T(8,128)S(1)}, f32[2,32,1024]{2,1,0:T(8,128)S(1)}, u32[]{:S(2)}, u32[]{:S(2)}) collective-permute-start(f32[2,32,1024]{2,1,0:T(8,128)S(1)} %dynamic-slice_bitcast_fusion.2), channel_id=1, source_target_pairs={{0,4},{1,5},{2,6},{3,7},{4,0},{5,1},{6,2},{7,3},{8,12},{9,13},{10,... | collective-permute-start | bytes 786440 | tf_op jit(solution)/shard_map/sketch_reduce/ppermute | solution.py:79
  139.9 8.4 %collective-permute-start.3 = (f32[1,32,1024]{2,1,0:T(8,128)S(1)}, f32[1,32,1024]{2,1,0:T(8,128)S(1)}, u32[]{:S(2)}, u32[]{:S(2)}) collective-permute-start(f32[1,32,1024]{2,1,0:T(8,128)S(1)} %constant_dynamic-slice_fusion), channel_id=1, source_target_pairs={{0,8},{1,9},{2,10},{3,11},{4,12},{5,13},{6,14},{7,15},{8,0},{9,1},... | collective-permute-start | bytes 393224 | tf_op jit(solution)/shard_map/sketch_reduce/ppermute | solution.py:79
  148.3 29.9 %copy-start = (f32[1,32,1024]{2,1,0:T(8,128)}, f32[1,32,1024]{2,1,0:T(8,128)S(1)}, u32[]{:S(2)}) copy-start(f32[1,32,1024]{2,1,0:T(8,128)S(1)} %dynamic-slice_add_fusion) | copy-start | bytes 393220
  148.4 8.2 %collective-permute-start.4 = (f32[1,32,1024]{2,1,0:T(8,128)S(1)}, f32[1,32,1024]{2,1,0:T(8,128)S(1)}, u32[]{:S(2)}, u32[]{:S(2)}) collective-permute-start(f32[1,32,1024]{2,1,0:T(8,128)S(1)} %dynamic-slice_add_fusion), channel_id=1, source_target_pairs={{0,8},{1,9},{2,10},{3,11},{4,12},{5,13},{6,14},{7,15},{8,0},{9,1},... | collective-permute-start | bytes 393224 | tf_op jit(solution)/shard_map/sketch_gather/ppermute | solution.py:79
  156.6 8.3 %collective-permute-start.5 = (f32[2,32,1024]{2,1,0:T(8,128)S(1)}, f32[2,32,1024]{2,1,0:T(8,128)S(1)}, u32[]{:S(2)}, u32[]{:S(2)}) collective-permute-start(f32[2,32,1024]{2,1,0:T(8,128)S(1)} %maximum_bitcast_fusion), channel_id=1, source_target_pairs={{0,4},{1,5},{2,6},{3,7},{4,0},{5,1},{6,2},{7,3},{8,12},{9,13},{10,... | collective-permute-start | bytes 786440 | tf_op jit(solution)/shard_map/sketch_gather/ppermute | solution.py:79
  165.0 13.1 %collective-permute-start.6 = (f32[4,32,1024]{2,1,0:T(8,128)S(1)}, f32[4,32,1024]{2,1,0:T(8,128)S(1)}, u32[]{:S(2)}, u32[]{:S(2)}) collective-permute-start(f32[4,32,1024]{2,1,0:T(8,128)S(1)} %bitcast.69), channel_id=1, source_target_pairs={{0,2},{1,3},{2,0},{3,1},{4,6},{5,7},{6,4},{7,5},{8,10},{9,11},{10,... | collective-permute-start | bytes 1572872 | tf_op jit(solution)/shard_map/sketch_gather/ppermute | solution.py:79
  178.2 0.7 copy-start.2
  178.2 0.7 copy-start.1
  178.4 3.0 %collective-permute-start.7 = (f32[8,32,1024]{2,1,0:T(8,128)S(1)}, f32[8,32,1024]{2,1,0:T(8,128)S(1)}, u32[]{:S(2)}, u32[]{:S(2)}) collective-permute-start(f32[8,32,1024]{2,1,0:T(8,128)S(1)} %bitcast.65), channel_id=1, source_target_pairs={{0,1},{1,0},{2,3},{3,2},{4,5},{5,4},{6,7},{7,6},{8,9},{9,8},{10,11... | collective-permute-start | bytes 3145736 | tf_op jit(solution)/shard_map/sketch_gather/ppermute | solution.py:79

commit v4 on v2

--- a/solution.py
+++ b/solution.py
@@ -15,16 +15,47 @@
     lane_row = lax.broadcasted_iota(jnp.int32, (1, size), 1)
     sub_col = lax.broadcasted_iota(jnp.int32, (size, 1), 0)
 
-    def step(k, a):
-        row = jnp.sum(jnp.where(sub == k, a, 0.0), axis=0, keepdims=True)
-        col = jnp.sum(jnp.where(lane == k, a, 0.0), axis=1, keepdims=True)
-        pivot = jnp.sum(jnp.where(lane_row == k, row, 0.0), axis=1, keepdims=True)
-        scaled = jnp.where(lane_row == k, 1.0, row) / pivot
-        col = jnp.where(sub_col == k, 0.0, col)
-        a = jnp.where(lane == k, 0.0, a) - col * scaled
-        return jnp.where(sub == k, scaled, a)
+    def pick(row, k):
+        return jnp.sum(jnp.where(lane_row == k, row, 0.0), axis=1, keepdims=True)
 
-    return lax.fori_loop(0, size, step, block)
+    def pair_pivot(first, second, k):
+        p00 = pick(first, k)
+        p01 = pick(first, k + 1)
+        p10 = pick(second, k)
+        p11 = pick(second, k + 1)
+        det = p00 * p11 - p01 * p10
+        ident0 = jnp.where(lane_row == k, 1.0, jnp.where(lane_row == k + 1, 0.0, first))
+        ident1 = jnp.where(lane_row == k, 0.0, jnp.where(lane_row == k + 1, 1.0, second))
+        scaled0 = (p11 * ident0 - p01 * ident1) / det
+        scaled1 = (p00 * ident1 - p10 * ident0) / det
+        return scaled0, scaled1
+
+    def eliminate(row, k, scaled0, scaled1):
+        f0 = pick(row, k)
+        f1 = pick(row, k + 1)
+        kept = jnp.where((lane_row == k) | (lane_row == k + 1), 0.0, row)
+        return kept - f0 * scaled0 - f1 * scaled1
+
+    def step(h, a):
+        k = 4 * h
+        rows = [jnp.sum(jnp.where(sub == k + t, a, 0.0), axis=0, keepdims=True) for t in range(4)]
+        cols = [jnp.sum(jnp.where(lane == k + t, a, 0.0), axis=1, keepdims=True) for t in range(4)]
+        s0, s1 = pair_pivot(rows[0], rows[1], k)
+        r2 = eliminate(rows[2], k, s0, s1)
+        r3 = eliminate(rows[3], k, s0, s1)
+        s2, s3 = pair_pivot(r2, r3, k + 2)
+        s0 = eliminate(s0, k + 2, s2, s3)
+        s1 = eliminate(s1, k + 2, s2, s3)
+        slab = (s0, s1, s2, s3)
+        pivot_rows = (sub_col >= k) & (sub_col < k + 4)
+        a = jnp.where((lane >= k) & (lane < k + 4), 0.0, a)
+        for t in range(4):
+            a = a - jnp.where(pivot_rows, 0.0, cols[t]) * slab[t]
+        for t in range(4):
+            a = jnp.where(sub == k + t, slab[t], a)
+        return a
+
+    return lax.fori_loop(0, size // 4, step, block)
 
 
 def _solve_kernel(m_ref, w_ref, y_ref, a_ref, *, block):

time: 256 us -> 231 us (0.902)
  Pallas kernels: 67.4 us -> 42 us
    pallas_call x1, Pallas kernels: 67.4 us -> 42 us  [spd_solve(): pl.pallas_call(functools.partial(_solve_kernel, block=block), out_shape=j...]
where the time goes in v4:
time: 231 us
  waiting for transfers between devices  134 us (58%)
  Pallas kernels  42 us (18%)
  starting transfers between devices  29.1 us (13%)
  matrix products  14.8 us (6%)
  local copies, waits for them, and re-layouts  6.43 us (3%)
  other arithmetic  3.83 us (2%)
    all_to_all x1, waiting for transfers between devices, on_device(): lax.all_to_all(grads, 'ex', split_axis=1, concat_axis=0, tiled=True)  77.7 us
    ppermute x8, waiting for transfers between devices, partner(): lax.ppermute(array, axis, [(i, i ^ 1 << bit) for i in range(lax.axis_size...  56 us
    pallas_call x1, Pallas kernels, spd_solve(): pl.pallas_call(functools.partial(_solve_kernel, block=block), out_shape=j...  42 us
    ppermute x8, starting transfers between devices, partner(): lax.ppermute(array, axis, [(i, i ^ 1 << bit) for i in range(lax.axis_size...  21.7 us
    dot_general x1, matrix products, on_device(): partial_value = jnp.dot(columns, proj, preferred_element_type=jnp.float32)  8.14 us
    all_to_all x1, starting transfers between devices, on_device(): lax.all_to_all(grads, 'ex', split_axis=1, concat_axis=0, tiled=True)  7.44 us
    all_to_all x1, local copies, waits for them, and re-layouts, on_device(): lax.all_to_all(grads, 'ex', split_axis=1, concat_axis=0, tiled=True)  4.65 us
  transfers between devices with their start and end apart: 9, of which 8 were waited for; matrix products, arithmetic and copies ran while one was open for 1% of the time, Pallas kernels for 0%

profile of v4, /device:TPU:0, one launch (start us, length us, event | category | flops | bytes accessed | tf_op | source)
XLA Modules:
  0.0 230.7 jit_solution(7328823462901898088)
XLA Ops:
  0.6 4.7 %copy.29 = bf16[4,16,8,4096]{3,2,0,1:T(8,128)(2,1)} copy(bf16[4,16,8,4096]{3,2,1,0:T(8,128)(2,1)} %bitcast.66) | data formatting | bytes 8388608 | tf_op jit(solution)/shard_map/gradient_exchange/all_to_all | solution.py:126
  5.3 7.4 %all-to-all-start = ((bf16[32,16,4096]{2,0,1:T(8,128)(2,1)}), bf16[32,16,4096]{2,0,1:T(8,128)(2,1)}, u32[]{:S(2)}, u32[]{:S(2)}) async-start(bf16[32,16,4096]{2,0,1:T(8,128)(2,1)} %bitcast.64), calls=%async_computation | async-start | bytes 8388608 | tf_op jit(solution)/shard_map/gradient_exchange/all_to_all | solution.py:126
  12.7 77.7 %all-to-all-done = bf16[32,16,4096]{2,0,1:T(8,128)(2,1)} async-done(((bf16[32,16,4096]{2,0,1:T(8,128)(2,1)}), bf16[32,16,4096]{2,0,1:T(8,128)(2,1)}, u32[]{:S(2)}, u32[]{:S(2)}) %all-to-all-start) | async-done | bytes 4194336 | tf_op jit(solution)/shard_map/gradient_exchange/all_to_all | solution.py:126
  90.4 8.1 %fusion = f32[8,2,32,1024]{3,2,1,0:T(8,128)S(1)} fusion(bf16[8,2,32,4096]{3,2,1,0:T(8,128)(2,1)} %bitcast.1, bf16[4096,1024]{1,0:T(8,128)(2,1)} %param.5), kind=kOutput, calls=%fused_computation | convolution fusion | flops 4294967296 | bytes 14680064 | tf_op jit(solution)/shard_map/partial_projection/dot_general | solution.py:128
  98.6 0.1 dynamic-slice_bitcast_fusion
  98.7 0.8 collective-permute-start
  99.5 2.4 %collective-permute-done = f32[8,32,1024]{2,1,0:T(8,128)} collective-permute-done((f32[8,32,1024]{2,1,0:T(8,128)S(1)}, f32[8,32,1024]{2,1,0:T(8,128)}, u32[]{:S(2)}, u32[]{:S(2)}) %collective-permute-start) | collective-permute-done | bytes 1048608 | tf_op jit(solution)/shard_map/sketch_reduce/ppermute | solution.py:93
  101.9 1.4 bitcast_add_fusion
  103.3 6.3 %collective-permute-start.1 = (f32[4,32,1024]{2,1,0:T(8,128)S(1)}, f32[4,32,1024]{2,1,0:T(8,128)S(1)}, u32[]{:S(2)}, u32[]{:S(2)}) collective-permute-start(f32[4,32,1024]{2,1,0:T(8,128)S(1)} %dynamic-slice_bitcast_fusion.1), channel_id=1, source_target_pairs={{0,2},{1,3},{2,0},{3,1},{4,6},{5,7},{6,4},{7,5},{8,10},{9,11},{10,... | collective-permute-start | bytes 1572872 | tf_op jit(solution)/shard_map/sketch_reduce/ppermute | solution.py:93
  109.6 12.4 %collective-permute-done.1 = f32[4,32,1024]{2,1,0:T(8,128)S(1)} collective-permute-done((f32[4,32,1024]{2,1,0:T(8,128)S(1)}, f32[4,32,1024]{2,1,0:T(8,128)S(1)}, u32[]{:S(2)}, u32[]{:S(2)}) %collective-permute-start.1) | collective-permute-done | bytes 524320 | tf_op jit(solution)/shard_map/sketch_reduce/ppermute | solution.py:93
  122.2 11.4 %collective-permute-start.2 = (f32[2,32,1024]{2,1,0:T(8,128)S(1)}, f32[2,32,1024]{2,1,0:T(8,128)S(1)}, u32[]{:S(2)}, u32[]{:S(2)}) collective-permute-start(f32[2,32,1024]{2,1,0:T(8,128)S(1)} %dynamic-slice_bitcast_fusion.2), channel_id=1, source_target_pairs={{0,4},{1,5},{2,6},{3,7},{4,0},{5,1},{6,2},{7,3},{8,12},{9,13},{10,... | collective-permute-start | bytes 786440 | tf_op jit(solution)/shard_map/sketch_reduce/ppermute | solution.py:93
  133.6 6.3 %collective-permute-done.2 = f32[2,32,1024]{2,1,0:T(8,128)S(1)} collective-permute-done((f32[2,32,1024]{2,1,0:T(8,128)S(1)}, f32[2,32,1024]{2,1,0:T(8,128)S(1)}, u32[]{:S(2)}, u32[]{:S(2)}) %collective-permute-start.2) | collective-permute-done | bytes 262176 | tf_op jit(solution)/shard_map/sketch_reduce/ppermute | solution.py:93
  139.9 2.7 %collective-permute-start.3 = (f32[1,32,1024]{2,1,0:T(8,128)S(1)}, f32[1,32,1024]{2,1,0:T(8,128)S(1)}, u32[]{:S(2)}, u32[]{:S(2)}) collective-permute-start(f32[1,32,1024]{2,1,0:T(8,128)S(1)} %constant_dynamic-slice_fusion), channel_id=1, source_target_pairs={{0,8},{1,9},{2,10},{3,11},{4,12},{5,13},{6,14},{7,15},{8,0},{9,1},... | collective-permute-start | bytes 393224 | tf_op jit(solution)/shard_map/sketch_reduce/ppermute | solution.py:93
  142.6 5.7 %collective-permute-done.3 = f32[1,32,1024]{2,1,0:T(8,128)S(1)} collective-permute-done((f32[1,32,1024]{2,1,0:T(8,128)S(1)}, f32[1,32,1024]{2,1,0:T(8,128)S(1)}, u32[]{:S(2)}, u32[]{:S(2)}) %collective-permute-start.3) | collective-permute-done | bytes 131104 | tf_op jit(solution)/shard_map/sketch_reduce/ppermute | solution.py:93
  148.4 0.3 collective-permute-start.4
  148.7 7.9 %collective-permute-done.4 = f32[1,32,1024]{2,1,0:T(8,128)S(1)} collective-permute-done((f32[1,32,1024]{2,1,0:T(8,128)S(1)}, f32[1,32,1024]{2,1,0:T(8,128)S(1)}, u32[]{:S(2)}, u32[]{:S(2)}) %collective-permute-start.4) | collective-permute-done | bytes 131104 | tf_op jit(solution)/shard_map/sketch_gather/ppermute | solution.py:93
  156.6 0.1 collective-permute-start.5
  156.7 8.2 %collective-permute-done.5 = f32[2,32,1024]{2,1,0:T(8,128)S(1)} collective-permute-done((f32[2,32,1024]{2,1,0:T(8,128)S(1)}, f32[2,32,1024]{2,1,0:T(8,128)S(1)}, u32[]{:S(2)}, u32[]{:S(2)}) %collective-permute-start.5) | collective-permute-done | bytes 262176 | tf_op jit(solution)/shard_map/sketch_gather/ppermute | solution.py:93
  165.1 13.0 %collective-permute-done.6 = f32[4,32,1024]{2,1,0:T(8,128)S(1)} collective-permute-done((f32[4,32,1024]{2,1,0:T(8,128)S(1)}, f32[4,32,1024]{2,1,0:T(8,128)S(1)}, u32[]{:S(2)}, u32[]{:S(2)}) %collective-permute-start.6) | collective-permute-done | bytes 524320 | tf_op jit(solution)/shard_map/sketch_gather/ppermute | solution.py:93
  178.1 0.1 select_bitcast_fusion.3
  178.4 0.1 collective-permute-start.7
  178.5 0.4 copy-done.2
  178.9 0.1 iota_compare_fusion.2
  179.0 1.6 convert_reduce_fusion
  180.5 0.1 copy.24
  180.7 0.7 pad.4.w_ref
  181.4 0.2 select_bitcast_fusion.1
  181.7 0.1 pad_maximum_fusion
  181.8 0.2 copy.23
  182.1 4.5 %select_add_fusion = (f32[512,512]{1,0:T(8,128)}, f32[512,512]{1,0:T(8,128)S(1)}) fusion(f32[512,1024]{1,0:T(8,128)S(1)} %bitcast.63), kind=kOutput, calls=%fused_computation.9 | convolution fusion | flops 3222274048 | bytes 4194304 | tf_op jit(solution)/shard_map/kernel_matrix/dot_general | solution.py:144
  186.6 42.0 %kernel_solve.1 = f32[512,128]{1,0:T(8,128)} custom-call(f32[512,512]{1,0:T(8,128)} %get-tuple-element.10.m_ref, f32[512,128]{1,0:T(8,128)} %pad.4.w_ref), custom_call_target="tpu_custom_call" | custom-call | tf_op jit(solution)/shard_map/kernel_solve/pallas_call | solution.py:84
  228.5 2.1 fusion.3
  (21 shorter events, 0.6 us)
Async XLA Ops:
  5.3 85.1 %all-to-all-start = ((bf16[32,16,4096]{2,0,1:T(8,128)(2,1)}), bf16[32,16,4096]{2,0,1:T(8,128)(2,1)}, u32[]{:S(2)}, u32[]{:S(2)}) async-start(bf16[32,16,4096]{2,0,1:T(8,128)(2,1)} %bitcast.64), calls=%async_computation | async-start | bytes 8388608 | tf_op jit(solution)/shard_map/gradient_exchange/all_to_all | solution.py:126
  98.7 3.3 %collective-permute-start = (f32[8,32,1024]{2,1,0:T(8,128)S(1)}, f32[8,32,1024]{2,1,0:T(8,128)}, u32[]{:S(2)}, u32[]{:S(2)}) collective-permute-start(f32[8,32,1024]{2,1,0:T(8,128)S(1)} %dynamic-slice_bitcast_fusion), channel_id=1, source_target_pairs={{0,1},{1,0},{2,3},{3,2},{4,5},{5,4},{6,7},{7,6},{8,9},{9,8},{10,11... | collective-permute-start | bytes 3145736 | tf_op jit(solution)/shard_map/sketch_reduce/ppermute | solution.py:93
  103.3 18.7 %collective-permute-start.1 = (f32[4,32,1024]{2,1,0:T(8,128)S(1)}, f32[4,32,1024]{2,1,0:T(8,128)S(1)}, u32[]{:S(2)}, u32[]{:S(2)}) collective-permute-start(f32[4,32,1024]{2,1,0:T(8,128)S(1)} %dynamic-slice_bitcast_fusion.1), channel_id=1, source_target_pairs={{0,2},{1,3},{2,0},{3,1},{4,6},{5,7},{6,4},{7,5},{8,10},{9,11},{10,... | collective-permute-start | bytes 1572872 | tf_op jit(solution)/shard_map/sketch_reduce/ppermute | solution.py:93
  122.2 17.7 %collective-permute-start.2 = (f32[2,32,1024]{2,1,0:T(8,128)S(1)}, f32[2,32,1024]{2,1,0:T(8,128)S(1)}, u32[]{:S(2)}, u32[]{:S(2)}) collective-permute-start(f32[2,32,1024]{2,1,0:T(8,128)S(1)} %dynamic-slice_bitcast_fusion.2), channel_id=1, source_target_pairs={{0,4},{1,5},{2,6},{3,7},{4,0},{5,1},{6,2},{7,3},{8,12},{9,13},{10,... | collective-permute-start | bytes 786440 | tf_op jit(solution)/shard_map/sketch_reduce/ppermute | solution.py:93
  139.9 8.4 %collective-permute-start.3 = (f32[1,32,1024]{2,1,0:T(8,128)S(1)}, f32[1,32,1024]{2,1,0:T(8,128)S(1)}, u32[]{:S(2)}, u32[]{:S(2)}) collective-permute-start(f32[1,32,1024]{2,1,0:T(8,128)S(1)} %constant_dynamic-slice_fusion), channel_id=1, source_target_pairs={{0,8},{1,9},{2,10},{3,11},{4,12},{5,13},{6,14},{7,15},{8,0},{9,1},... | collective-permute-start | bytes 393224 | tf_op jit(solution)/shard_map/sketch_reduce/ppermute | solution.py:93
  148.3 29.9 %copy-start = (f32[1,32,1024]{2,1,0:T(8,128)}, f32[1,32,1024]{2,1,0:T(8,128)S(1)}, u32[]{:S(2)}) copy-start(f32[1,32,1024]{2,1,0:T(8,128)S(1)} %dynamic-slice_add_fusion) | copy-start | bytes 393220
  148.4 8.2 %collective-permute-start.4 = (f32[1,32,1024]{2,1,0:T(8,128)S(1)}, f32[1,32,1024]{2,1,0:T(8,128)S(1)}, u32[]{:S(2)}, u32[]{:S(2)}) collective-permute-start(f32[1,32,1024]{2,1,0:T(8,128)S(1)} %dynamic-slice_add_fusion), channel_id=1, source_target_pairs={{0,8},{1,9},{2,10},{3,11},{4,12},{5,13},{6,14},{7,15},{8,0},{9,1},... | collective-permute-start | bytes 393224 | tf_op jit(solution)/shard_map/sketch_gather/ppermute | solution.py:93
  156.6 8.3 %collective-permute-start.5 = (f32[2,32,1024]{2,1,0:T(8,128)S(1)}, f32[2,32,1024]{2,1,0:T(8,128)S(1)}, u32[]{:S(2)}, u32[]{:S(2)}) collective-permute-start(f32[2,32,1024]{2,1,0:T(8,128)S(1)} %maximum_bitcast_fusion), channel_id=1, source_target_pairs={{0,4},{1,5},{2,6},{3,7},{4,0},{5,1},{6,2},{7,3},{8,12},{9,13},{10,... | collective-permute-start | bytes 786440 | tf_op jit(solution)/shard_map/sketch_gather/ppermute | solution.py:93
  165.0 13.1 %collective-permute-start.6 = (f32[4,32,1024]{2,1,0:T(8,128)S(1)}, f32[4,32,1024]{2,1,0:T(8,128)S(1)}, u32[]{:S(2)}, u32[]{:S(2)}) collective-permute-start(f32[4,32,1024]{2,1,0:T(8,128)S(1)} %bitcast.69), channel_id=1, source_target_pairs={{0,2},{1,3},{2,0},{3,1},{4,6},{5,7},{6,4},{7,5},{8,10},{9,11},{10,... | collective-permute-start | bytes 1572872 | tf_op jit(solution)/shard_map/sketch_gather/ppermute | solution.py:93
  178.2 0.7 copy-start.2
  178.2 0.7 copy-start.1
  178.4 3.0 %collective-permute-start.7 = (f32[8,32,1024]{2,1,0:T(8,128)S(1)}, f32[8,32,1024]{2,1,0:T(8,128)S(1)}, u32[]{:S(2)}, u32[]{:S(2)}) collective-permute-start(f32[8,32,1024]{2,1,0:T(8,128)S(1)} %bitcast.65), channel_id=1, source_target_pairs={{0,1},{1,0},{2,3},{3,2},{4,5},{5,4},{6,7},{7,6},{8,9},{9,8},{10,11... | collective-permute-start | bytes 3145736 | tf_op jit(solution)/shard_map/sketch_gather/ppermute | solution.py:93

commit v5 on v4

--- a/solution.py
+++ b/solution.py
@@ -93,26 +93,39 @@
     return lax.ppermute(array, axis, [(i, i ^ 1 << bit) for i in range(lax.axis_size(axis))])
 
 
-def reduce_scatter(partial_value, bits, position):
-    value = partial_value
-    for level in range(bits):
-        value = value.reshape((-1, 2) + value.shape[1:])
+def reduce_scatter(partial_value, order, position):
+    bits = len(order)
+    value = partial_value.reshape((2,) * bits + partial_value.shape[1:])
+    remaining = list(range(bits - 1, -1, -1))
+    for level in order:
+        axis = remaining.index(level)
         own_bit = position // 2**level % 2
-        kept = lax.dynamic_index_in_dim(value, own_bit, axis=1, keepdims=False)
-        sent = lax.dynamic_index_in_dim(value, 1 - own_bit, axis=1, keepdims=False)
+        kept = lax.dynamic_index_in_dim(value, own_bit, axis=axis, keepdims=False)
+        sent = lax.dynamic_index_in_dim(value, 1 - own_bit, axis=axis, keepdims=False)
         value = kept + partner(sent, "ex", level)
-    return value[0]
-
-
-def all_gather(block, bits, position):
-    value = block[None]
-    for level in range(bits - 1, -1, -1):
+        remaining.remove(level)
+    return value
+
+
+def all_gather(block, order, position):
+    value = block
+    present = []
+    for level in reversed(order):
         received = partner(value, "ex", level)
         high_side = position // 2**level % 2 == 1
         low = jnp.where(high_side, received, value)
         high = jnp.where(high_side, value, received)
-        value = jnp.stack([low, high], axis=1).reshape((-1,) + value.shape[1:])
-    return value
+        present.append(level)
+        present.sort(reverse=True)
+        value = jnp.stack([low, high], axis=present.index(level))
+    return value.reshape((-1,) + block.shape[1:])
+
+
+def bit_orders(bits):
+    first = list(range(bits))
+    if bits < 3:
+        return [first]
+    return [first, [0, 2, 1] + list(range(3, bits))]
 
 
 def on_device(grads, proj, target_ids, target_counts):
@@ -126,12 +139,23 @@
         columns = lax.all_to_all(grads, "ex", split_axis=1, concat_axis=0, tiled=True)
     with jax.named_scope("partial_projection"):
         partial_value = jnp.dot(columns, proj, preferred_element_type=jnp.float32)
-    with jax.named_scope("sketch_reduce"):
-        sketch = reduce_scatter(
-            partial_value.reshape(count_ex, ex_rows, sketch_width), bits, position
-        )
-    with jax.named_scope("sketch_gather"):
-        sketch_all = all_gather(sketch, bits, position).reshape(examples, sketch_width)
+    orders = bit_orders(bits)
+    width = sketch_width // len(orders)
+    owned, gathered = [], []
+    for half, order in enumerate(orders):
+        with jax.named_scope("sketch_reduce"):
+            part = reduce_scatter(
+                partial_value[:, half * width:(half + 1) * width].reshape(
+                    count_ex, ex_rows, width
+                ),
+                order,
+                position,
+            )
+        with jax.named_scope("sketch_gather"):
+            gathered.append(all_gather(part, order, position))
+        owned.append(part)
+    sketch = jnp.concatenate(owned, axis=1)
+    sketch_all = jnp.concatenate(gathered, axis=1)
     slot_count = target_ids.shape[1]
     live_slot = jnp.arange(slot_count, dtype=jnp.int32)[None, :] < target_counts[:, None]
     example_index = jnp.arange(examples, dtype=jnp.int32)

time: 231 us -> 211 us (0.913)
  waiting for transfers between devices: 134 us -> 104 us
  starting transfers between devices: 29.1 us -> 38.2 us
    ppermute x8 -> x16, waiting for transfers between devices: 56 us -> 26.3 us  [partner(): lax.ppermute(array, axis, [(i, i ^ 1 << bit) for i in range(lax.axis_size...]
    ppermute x8 -> x16, starting transfers between devices: 21.7 us -> 30.8 us  [partner(): lax.ppermute(array, axis, [(i, i ^ 1 << bit) for i in range(lax.axis_size...]
  transfers between devices with their start and end apart: 9 -> 17, of which waited for: 8 -> 12; matrix products, arithmetic and copies ran while one was open for 1% -> 3% of each run, Pallas kernels for 0% -> 0%
where the time goes in v5:
time: 211 us
  waiting for transfers between devices  104 us (49%)
  Pallas kernels  42 us (20%)
  starting transfers between devices  38.2 us (18%)
  matrix products  14.8 us (7%)
  local copies, waits for them, and re-layouts  7.09 us (3%)
  other arithmetic  4.18 us (2%)
    all_to_all x1, waiting for transfers between devices, on_device(): lax.all_to_all(grads, 'ex', split_axis=1, concat_axis=0, tiled=True)  77.7 us
    pallas_call x1, Pallas kernels, spd_solve(): pl.pallas_call(functools.partial(_solve_kernel, block=block), out_shape=j...  42 us
    ppermute x16, starting transfers between devices, partner(): lax.ppermute(array, axis, [(i, i ^ 1 << bit) for i in range(lax.axis_size...  30.8 us
    ppermute x16, waiting for transfers between devices, partner(): lax.ppermute(array, axis, [(i, i ^ 1 << bit) for i in range(lax.axis_size...  26.3 us
    dot_general x1, matrix products, on_device(): partial_value = jnp.dot(columns, proj, preferred_element_type=jnp.float32)  8.14 us
    all_to_all x1, starting transfers between devices, on_device(): lax.all_to_all(grads, 'ex', split_axis=1, concat_axis=0, tiled=True)  7.44 us
    all_to_all x1, local copies, waits for them, and re-layouts, on_device(): lax.all_to_all(grads, 'ex', split_axis=1, concat_axis=0, tiled=True)  4.72 us
    dot_general x1, matrix products, on_device(): kernel = jnp.dot(sketch_all, sketch_all.T, precision=lax.Precision.HIGHEST)  4.55 us
  transfers between devices with their start and end apart: 17, of which 12 were waited for; matrix products, arithmetic and copies ran while one was open for 3% of the time, Pallas kernels for 0%

profile of v5, /device:TPU:0, one launch (start us, length us, event | category | flops | bytes accessed | tf_op | source)
XLA Modules:
  0.0 211.2 jit_solution(5921730115359283317)
XLA Ops:
  0.6 4.7 %copy.70 = bf16[4,16,8,4096]{3,2,0,1:T(8,128)(2,1)} copy(bf16[4,16,8,4096]{3,2,1,0:T(8,128)(2,1)} %bitcast.88) | data formatting | bytes 8388608 | tf_op jit(solution)/shard_map/gradient_exchange/all_to_all | solution.py:139
  5.3 7.4 %all-to-all-start = ((bf16[32,16,4096]{2,0,1:T(8,128)(2,1)}), bf16[32,16,4096]{2,0,1:T(8,128)(2,1)}, u32[]{:S(2)}, u32[]{:S(2)}) async-start(bf16[32,16,4096]{2,0,1:T(8,128)(2,1)} %bitcast.87), calls=%async_computation | async-start | bytes 8388608 | tf_op jit(solution)/shard_map/gradient_exchange/all_to_all | solution.py:139
  12.8 77.7 %all-to-all-done = bf16[32,16,4096]{2,0,1:T(8,128)(2,1)} async-done(((bf16[32,16,4096]{2,0,1:T(8,128)(2,1)}), bf16[32,16,4096]{2,0,1:T(8,128)(2,1)}, u32[]{:S(2)}, u32[]{:S(2)}) %all-to-all-start) | async-done | bytes 4194336 | tf_op jit(solution)/shard_map/gradient_exchange/all_to_all | solution.py:139
  90.5 8.1 %fusion.11 = f32[512,1024]{1,0:T(8,128)S(1)} fusion(bf16[512,4096]{1,0:T(8,128)(2,1)} %bitcast.1, bf16[4096,1024]{1,0:T(8,128)(2,1)} %param.5), kind=kOutput, calls=%fused_computation.63 | convolution fusion | flops 4294967296 | bytes 14680064 | tf_op jit(solution)/shard_map/partial_projection/dot_general | solution.py:141
  99.1 0.8 collective-permute-start.8
  100.1 0.9 copy.72
  101.1 1.5 convert_reduce_fusion
  102.9 14.7 %collective-permute-start.9 = (f32[2,2,32,512]{3,2,1,0:T(8,128)S(1)}, f32[2,2,32,512]{3,2,1,0:T(8,128)S(1)}, u32[]{:S(2)}, u32[]{:S(2)}) collective-permute-start(f32[2,2,32,512]{3,2,1,0:T(8,128)S(1)} %dynamic-slice_bitcast_fusion), channel_id=1, source_target_pairs={{0,4},{1,5},{2,6},{3,7},{4,0},{5,1},{6,2},{7,3},{8,12},{9,13},{10,... | collective-permute-start | bytes 786440 | tf_op jit(solution)/shard_map/sketch_reduce/ppermute | solution.py:93
  117.7 3.0 %collective-permute-start.1 = (f32[2,2,32,512]{3,2,1,0:T(8,128)S(1)}, f32[2,2,32,512]{3,2,1,0:T(8,128)S(1)}, u32[]{:S(2)}, u32[]{:S(2)}) collective-permute-start(f32[2,2,32,512]{3,2,1,0:T(8,128)S(1)} %dynamic-slice_bitcast_fusion.1), channel_id=1, source_target_pairs={{0,2},{1,3},{2,0},{3,1},{4,6},{5,7},{6,4},{7,5},{8,10},{9,11},{10,... | collective-permute-start | bytes 786440 | tf_op jit(solution)/shard_map/sketch_reduce/ppermute | solution.py:93
  120.7 3.5 %collective-permute-done.9 = f32[2,2,32,512]{3,2,1,0:T(8,128)S(1)} collective-permute-done((f32[2,2,32,512]{3,2,1,0:T(8,128)S(1)}, f32[2,2,32,512]{3,2,1,0:T(8,128)S(1)}, u32[]{:S(2)}, u32[]{:S(2)}) %collective-permute-start.9) | collective-permute-done | bytes 262176 | tf_op jit(solution)/shard_map/sketch_reduce/ppermute | solution.py:93
  124.3 3.2 %collective-permute-start.10 = (f32[2,32,512]{2,1,0:T(8,128)S(1)}, f32[2,32,512]{2,1,0:T(8,128)S(1)}, u32[]{:S(2)}, u32[]{:S(2)}) collective-permute-start(f32[2,32,512]{2,1,0:T(8,128)S(1)} %dynamic-slice_bitcast_fusion.2), channel_id=1, source_target_pairs={{0,2},{1,3},{2,0},{3,1},{4,6},{5,7},{6,4},{7,5},{8,10},{9,11},{10,... | collective-permute-start | bytes 393224 | tf_op jit(solution)/shard_map/sketch_reduce/ppermute | solution.py:93
  127.5 1.8 collective-permute-start.2
  129.3 1.6 collective-permute-done.10
  131.0 3.0 %collective-permute-start.11 = (f32[32,512]{1,0:T(8,128)S(1)}, f32[32,512]{1,0:T(8,128)S(1)}, u32[]{:S(2)}, u32[]{:S(2)}) collective-permute-start(f32[32,512]{1,0:T(8,128)S(1)} %dynamic-slice_bitcast_fusion.4), channel_id=1, source_target_pairs={{0,8},{1,9},{2,10},{3,11},{4,12},{5,13},{6,14},{7,15},{8,0},{9,1},... | collective-permute-start | bytes 196616 | tf_op jit(solution)/shard_map/sketch_reduce/ppermute | solution.py:93
  134.2 4.0 %collective-permute-done.11 = f32[32,512]{1,0:T(8,128)S(1)} collective-permute-done((f32[32,512]{1,0:T(8,128)S(1)}, f32[32,512]{1,0:T(8,128)S(1)}, u32[]{:S(2)}, u32[]{:S(2)}) %collective-permute-start.11) | collective-permute-done | bytes 65568 | tf_op jit(solution)/shard_map/sketch_reduce/ppermute | solution.py:93
  138.2 1.0 collective-permute-start.12
  139.3 2.5 %collective-permute-done.3 = f32[32,512]{1,0:T(8,128)S(1)} collective-permute-done((f32[32,512]{1,0:T(8,128)S(1)}, f32[32,512]{1,0:T(8,128)S(1)}, u32[]{:S(2)}, u32[]{:S(2)}) %collective-permute-start.3) | collective-permute-done | bytes 65568 | tf_op jit(solution)/shard_map/sketch_reduce/ppermute | solution.py:93
  141.9 2.3 %collective-permute-done.12 = f32[32,512]{1,0:T(8,128)S(1)} collective-permute-done((f32[32,512]{1,0:T(8,128)S(1)}, f32[32,512]{1,0:T(8,128)S(1)}, u32[]{:S(2)}, u32[]{:S(2)}) %collective-permute-start.12) | collective-permute-done | bytes 65568 | tf_op jit(solution)/shard_map/sketch_gather/ppermute | solution.py:93
  144.2 0.9 collective-permute-start.13
  145.1 2.5 %collective-permute-done.4 = f32[32,512]{1,0:T(8,128)S(1)} collective-permute-done((f32[32,512]{1,0:T(8,128)S(1)}, f32[32,512]{1,0:T(8,128)S(1)}, u32[]{:S(2)}, u32[]{:S(2)}) %collective-permute-start.4) | collective-permute-done | bytes 65568 | tf_op jit(solution)/shard_map/sketch_gather/ppermute | solution.py:93
  148.0 1.2 collective-permute-done.13
  149.3 0.6 collective-permute-start.14
  149.9 2.9 %collective-permute-done.5 = f32[2,32,512]{2,1,0:T(8,128)S(1)} collective-permute-done((f32[2,32,512]{2,1,0:T(8,128)S(1)}, f32[2,32,512]{2,1,0:T(8,128)S(1)}, u32[]{:S(2)}, u32[]{:S(2)}) %collective-permute-start.5) | collective-permute-done | bytes 131104 | tf_op jit(solution)/shard_map/sketch_gather/ppermute | solution.py:93
  152.8 0.9 collective-permute-start.6
  153.7 2.0 collective-permute-done.14
  155.9 3.4 %collective-permute-done.6 = f32[2,2,32,512]{3,2,1,0:T(8,128)S(1)} collective-permute-done((f32[2,2,32,512]{3,2,1,0:T(8,128)S(1)}, f32[2,2,32,512]{3,2,1,0:T(8,128)S(1)}, u32[]{:S(2)}, u32[]{:S(2)}) %collective-permute-start.6) | collective-permute-done | bytes 262176 | tf_op jit(solution)/shard_map/sketch_gather/ppermute | solution.py:93
  159.3 0.9 pad_maximum_fusion.2
  160.2 0.7 pad.4.w_ref
  161.0 0.7 pad_maximum_fusion.8
  162.5 4.5 %select_add_fusion = (f32[512,512]{1,0:T(8,128)}, f32[512,512]{1,0:T(8,128)S(1)}) fusion(f32[512,512]{1,0:T(8,128)S(1)} %bitcast.91, f32[512,512]{1,0:T(8,128)S(1)} %bitcast.92), kind=kOutput, calls=%fused_computation.10 | convolution fusion | flops 3222798336 | bytes 4194304 | tf_op jit(solution)/shard_map/kernel_matrix/dot_general | solution.py:168
  167.1 42.0 %kernel_solve.1 = f32[512,128]{1,0:T(8,128)} custom-call(f32[512,512]{1,0:T(8,128)} %get-tuple-element.24.m_ref, f32[512,128]{1,0:T(8,128)} %pad.4.w_ref), custom_call_target="tpu_custom_call" | custom-call | tf_op jit(solution)/shard_map/kernel_solve/pallas_call | solution.py:84
  209.0 2.1 %fusion.5 = f32[32,24]{0,1:T(8,128)} fusion(f32[512,128]{1,0:T(8,128)} %kernel_solve.1, f32[512,512]{1,0:T(8,128)S(1)} %get-tuple-element.25, s32[]{:T(128)S(6)} %select_n.227), kind=kOutput, calls=%fused_computation.22 | convolution fusion | flops 4718592 | bytes 330756 | tf_op jit(solution)/shard_map/dot_general | solution.py:175
  (53 shorter events, 3.1 us)
Async XLA Ops:
  5.3 85.1 %all-to-all-start = ((bf16[32,16,4096]{2,0,1:T(8,128)(2,1)}), bf16[32,16,4096]{2,0,1:T(8,128)(2,1)}, u32[]{:S(2)}, u32[]{:S(2)}) async-start(bf16[32,16,4096]{2,0,1:T(8,128)(2,1)} %bitcast.87), calls=%async_computation | async-start | bytes 8388608 | tf_op jit(solution)/shard_map/gradient_exchange/all_to_all | solution.py:139
  98.6 1.4 copy-start.1
  98.8 2.2 %copy-start = (s32[24,128]{1,0:T(8,128)S(1)}, s32[24,128]{1,0:T(8,128)}, u32[]{:S(2)}) copy-start(s32[24,128]{1,0:T(8,128)} %param.6) | copy-start | bytes 36868
  99.1 3.6 %collective-permute-start.8 = (f32[2,2,2,32,512]{4,3,2,0,1:T(8,128)S(1)}, f32[2,2,2,32,512]{4,3,2,0,1:T(8,128)S(1)}, u32[]{:S(2)}, u32[]{:S(2)}) collective-permute-start(f32[2,2,2,32,512]{4,3,2,0,1:T(8,128)S(1)} %bitcast.93), channel_id=1, source_target_pairs={{0,1},{1,0},{2,3},{3,2},{4,5},{5,4},{6,7},{7,6},{8,9},{9,8},{10,11... | collective-permute-start | bytes 1572872 | tf_op jit(solution)/shard_map/sketch_reduce/ppermute | solution.py:93
  100.9 16.7 %collective-permute-start = (f32[2,2,2,32,512]{4,3,1,0,2:T(8,128)}, f32[2,2,2,32,512]{4,3,1,0,2:T(8,128)S(1)}, u32[]{:S(2)}, u32[]{:S(2)}) collective-permute-start(f32[2,2,2,32,512]{4,3,1,0,2:T(8,128)} %bitcast.86), channel_id=1, source_target_pairs={{0,1},{1,0},{2,3},{3,2},{4,5},{5,4},{6,7},{7,6},{8,9},{9,8},{10,11... | collective-permute-start | bytes 1572872 | tf_op jit(solution)/shard_map/sketch_reduce/ppermute | solution.py:93
  102.9 21.3 %collective-permute-start.9 = (f32[2,2,32,512]{3,2,1,0:T(8,128)S(1)}, f32[2,2,32,512]{3,2,1,0:T(8,128)S(1)}, u32[]{:S(2)}, u32[]{:S(2)}) collective-permute-start(f32[2,2,32,512]{3,2,1,0:T(8,128)S(1)} %dynamic-slice_bitcast_fusion), channel_id=1, source_target_pairs={{0,4},{1,5},{2,6},{3,7},{4,0},{5,1},{6,2},{7,3},{8,12},{9,13},{10,... | collective-permute-start | bytes 786440 | tf_op jit(solution)/shard_map/sketch_reduce/ppermute | solution.py:93
  117.7 9.7 %collective-permute-start.1 = (f32[2,2,32,512]{3,2,1,0:T(8,128)S(1)}, f32[2,2,32,512]{3,2,1,0:T(8,128)S(1)}, u32[]{:S(2)}, u32[]{:S(2)}) collective-permute-start(f32[2,2,32,512]{3,2,1,0:T(8,128)S(1)} %dynamic-slice_bitcast_fusion.1), channel_id=1, source_target_pairs={{0,2},{1,3},{2,0},{3,1},{4,6},{5,7},{6,4},{7,5},{8,10},{9,11},{10,... | collective-permute-start | bytes 786440 | tf_op jit(solution)/shard_map/sketch_reduce/ppermute | solution.py:93
  124.3 6.7 %collective-permute-start.10 = (f32[2,32,512]{2,1,0:T(8,128)S(1)}, f32[2,32,512]{2,1,0:T(8,128)S(1)}, u32[]{:S(2)}, u32[]{:S(2)}) collective-permute-start(f32[2,32,512]{2,1,0:T(8,128)S(1)} %dynamic-slice_bitcast_fusion.2), channel_id=1, source_target_pairs={{0,2},{1,3},{2,0},{3,1},{4,6},{5,7},{6,4},{7,5},{8,10},{9,11},{10,... | collective-permute-start | bytes 393224 | tf_op jit(solution)/shard_map/sketch_reduce/ppermute | solution.py:93
  127.5 6.4 %collective-permute-start.2 = (f32[2,32,512]{2,1,0:T(8,128)S(1)}, f32[2,32,512]{2,1,0:T(8,128)S(1)}, u32[]{:S(2)}, u32[]{:S(2)}) collective-permute-start(f32[2,32,512]{2,1,0:T(8,128)S(1)} %dynamic-slice_bitcast_fusion.3), channel_id=1, source_target_pairs={{0,4},{1,5},{2,6},{3,7},{4,0},{5,1},{6,2},{7,3},{8,12},{9,13},{10,... | collective-permute-start | bytes 393224 | tf_op jit(solution)/shard_map/sketch_reduce/ppermute | solution.py:93
  131.0 7.2 %collective-permute-start.11 = (f32[32,512]{1,0:T(8,128)S(1)}, f32[32,512]{1,0:T(8,128)S(1)}, u32[]{:S(2)}, u32[]{:S(2)}) collective-permute-start(f32[32,512]{1,0:T(8,128)S(1)} %dynamic-slice_bitcast_fusion.4), channel_id=1, source_target_pairs={{0,8},{1,9},{2,10},{3,11},{4,12},{5,13},{6,14},{7,15},{8,0},{9,1},... | collective-permute-start | bytes 196616 | tf_op jit(solution)/shard_map/sketch_reduce/ppermute | solution.py:93
  134.0 7.8 %collective-permute-start.3 = (f32[32,512]{1,0:T(8,128)S(1)}, f32[32,512]{1,0:T(8,128)S(1)}, u32[]{:S(2)}, u32[]{:S(2)}) collective-permute-start(f32[32,512]{1,0:T(8,128)S(1)} %dynamic-slice_bitcast_fusion.5), channel_id=1, source_target_pairs={{0,8},{1,9},{2,10},{3,11},{4,12},{5,13},{6,14},{7,15},{8,0},{9,1},... | collective-permute-start | bytes 196616 | tf_op jit(solution)/shard_map/sketch_reduce/ppermute | solution.py:93
  138.2 5.9 %collective-permute-start.12 = (f32[32,512]{1,0:T(8,128)S(1)}, f32[32,512]{1,0:T(8,128)S(1)}, u32[]{:S(2)}, u32[]{:S(2)}) collective-permute-start(f32[32,512]{1,0:T(8,128)S(1)} %bitcast_add_fusion.6), channel_id=1, source_target_pairs={{0,8},{1,9},{2,10},{3,11},{4,12},{5,13},{6,14},{7,15},{8,0},{9,1},... | collective-permute-start | bytes 196616 | tf_op jit(solution)/shard_map/sketch_gather/ppermute | solution.py:93
  141.8 5.8 %collective-permute-start.4 = (f32[32,512]{1,0:T(8,128)S(1)}, f32[32,512]{1,0:T(8,128)S(1)}, u32[]{:S(2)}, u32[]{:S(2)}) collective-permute-start(f32[32,512]{1,0:T(8,128)S(1)} %bitcast_add_fusion.7), channel_id=1, source_target_pairs={{0,8},{1,9},{2,10},{3,11},{4,12},{5,13},{6,14},{7,15},{8,0},{9,1},... | collective-permute-start | bytes 196616 | tf_op jit(solution)/shard_map/sketch_gather/ppermute | solution.py:93
  144.2 5.0 %collective-permute-start.13 = (f32[2,32,512]{2,1,0:T(8,128)S(1)}, f32[2,32,512]{2,1,0:T(8,128)S(1)}, u32[]{:S(2)}, u32[]{:S(2)}) collective-permute-start(f32[2,32,512]{2,1,0:T(8,128)S(1)} %pad_maximum_fusion.7), channel_id=1, source_target_pairs={{0,2},{1,3},{2,0},{3,1},{4,6},{5,7},{6,4},{7,5},{8,10},{9,11},{10,... | collective-permute-start | bytes 393224 | tf_op jit(solution)/shard_map/sketch_gather/ppermute | solution.py:93
  147.7 5.1 %collective-permute-start.5 = (f32[2,32,512]{2,1,0:T(8,128)S(1)}, f32[2,32,512]{2,1,0:T(8,128)S(1)}, u32[]{:S(2)}, u32[]{:S(2)}) collective-permute-start(f32[2,32,512]{2,1,0:T(8,128)S(1)} %pad_maximum_fusion.6), channel_id=1, source_target_pairs={{0,4},{1,5},{2,6},{3,7},{4,0},{5,1},{6,2},{7,3},{8,12},{9,13},{10,... | collective-permute-start | bytes 393224 | tf_op jit(solution)/shard_map/sketch_gather/ppermute | solution.py:93
  149.3 6.4 %collective-permute-start.14 = (f32[2,2,32,512]{3,2,0,1:T(8,128)S(1)}, f32[2,2,32,512]{3,2,0,1:T(8,128)S(1)}, u32[]{:S(2)}, u32[]{:S(2)}) collective-permute-start(f32[2,2,32,512]{3,2,0,1:T(8,128)S(1)} %pad_maximum_fusion.5), channel_id=1, source_target_pairs={{0,4},{1,5},{2,6},{3,7},{4,0},{5,1},{6,2},{7,3},{8,12},{9,13},{10,... | collective-permute-start | bytes 786440 | tf_op jit(solution)/shard_map/sketch_gather/ppermute | solution.py:93
  152.8 6.4 %collective-permute-start.6 = (f32[2,2,32,512]{3,2,1,0:T(8,128)S(1)}, f32[2,2,32,512]{3,2,1,0:T(8,128)S(1)}, u32[]{:S(2)}, u32[]{:S(2)}) collective-permute-start(f32[2,2,32,512]{3,2,1,0:T(8,128)S(1)} %pad_maximum_fusion.4), channel_id=1, source_target_pairs={{0,2},{1,3},{2,0},{3,1},{4,6},{5,7},{6,4},{7,5},{8,10},{9,11},{10,... | collective-permute-start | bytes 786440 | tf_op jit(solution)/shard_map/sketch_gather/ppermute | solution.py:93
  155.8 5.8 %collective-permute-start.15 = (f32[2,2,2,32,512]{4,3,0,2,1:T(8,128)S(1)}, f32[2,2,2,32,512]{4,3,0,2,1:T(8,128)S(1)}, u32[]{:S(2)}, u32[]{:S(2)}) collective-permute-start(f32[2,2,2,32,512]{4,3,0,2,1:T(8,128)S(1)} %pad_maximum_fusion.3), channel_id=1, source_target_pairs={{0,1},{1,0},{2,3},{3,2},{4,5},{5,4},{6,7},{7,6},{8,9},{9,8},{10,11... | collective-permute-start | bytes 1572872 | tf_op jit(solution)/shard_map/sketch_gather/ppermute | solution.py:93
  160.2 2.1 %collective-permute-start.7 = (f32[2,2,2,32,512]{4,3,2,1,0:T(8,128)}, f32[2,2,2,32,512]{4,3,2,1,0:T(8,128)S(1)}, u32[]{:S(2)}, u32[]{:S(2)}) collective-permute-start(f32[2,2,2,32,512]{4,3,2,1,0:T(8,128)} %pad_maximum_fusion.2), channel_id=1, source_target_pairs={{0,1},{1,0},{2,3},{3,2},{4,5},{5,4},{6,7},{7,6},{8,9},{9,8},{10,11... | collective-permute-start | bytes 1572872 | tf_op jit(solution)/shard_map/sketch_gather/ppermute | solution.py:93

commit v6 on v5

--- a/solution.py
+++ b/solution.py
@@ -137,17 +137,18 @@
     sketch_width = proj.shape[1]
     with jax.named_scope("gradient_exchange"):
         columns = lax.all_to_all(grads, "ex", split_axis=1, concat_axis=0, tiled=True)
-    with jax.named_scope("partial_projection"):
-        partial_value = jnp.dot(columns, proj, preferred_element_type=jnp.float32)
     orders = bit_orders(bits)
     width = sketch_width // len(orders)
     owned, gathered = [], []
     for half, order in enumerate(orders):
+        with jax.named_scope("partial_projection"):
+            partial_value = jnp.dot(
+                columns, proj[:, half * width:(half + 1) * width],
+                preferred_element_type=jnp.float32,
+            )
         with jax.named_scope("sketch_reduce"):
             part = reduce_scatter(
-                partial_value[:, half * width:(half + 1) * width].reshape(
-                    count_ex, ex_rows, width
-                ),
+                partial_value.reshape(count_ex, ex_rows, width),
                 order,
                 position,
             )

time: 211 us -> 216 us (1.024)
  matrix products: 14.8 us -> 18.2 us
    dot_general x1 -> x2, matrix products: 8.14 us -> 11.6 us  [on_device(): jnp.dot(columns, proj[:, half * width:(half + 1) * width], preferred_elem...]
  transfers between devices with their start and end apart: 17 -> 17, of which waited for: 12 -> 12; matrix products, arithmetic and copies ran while one was open for 3% -> 5% of each run, Pallas kernels for 0% -> 0%
where the time goes in v6:
time: 216 us
  waiting for transfers between devices  104 us (48%)
  Pallas kernels  42.1 us (19%)
  starting transfers between devices  38.4 us (18%)
  matrix products  18.2 us (8%)
  local copies, waits for them, and re-layouts  7.44 us (3%)
  other arithmetic  4.07 us (2%)
    all_to_all x1, waiting for transfers between devices, on_device(): lax.all_to_all(grads, 'ex', split_axis=1, concat_axis=0, tiled=True)  77.4 us
    pallas_call x1, Pallas kernels, spd_solve(): pl.pallas_call(functools.partial(_solve_kernel, block=block), out_shape=j...  42.1 us
    ppermute x16, starting transfers between devices, partner(): lax.ppermute(array, axis, [(i, i ^ 1 << bit) for i in range(lax.axis_size...  30.8 us
    ppermute x16, waiting for transfers between devices, partner(): lax.ppermute(array, axis, [(i, i ^ 1 << bit) for i in range(lax.axis_size...  26.9 us
    dot_general x2, matrix products, on_device(): jnp.dot(columns, proj[:, half * width:(half + 1) * width], preferred_elem...  11.6 us
    all_to_all x1, starting transfers between devices, on_device(): lax.all_to_all(grads, 'ex', split_axis=1, concat_axis=0, tiled=True)  7.57 us
    all_to_all x1, local copies, waits for them, and re-layouts, on_device(): lax.all_to_all(grads, 'ex', split_axis=1, concat_axis=0, tiled=True)  4.71 us
    dot_general x1, matrix products, on_device(): kernel = jnp.dot(sketch_all, sketch_all.T, precision=lax.Precision.HIGHEST)  4.55 us
  transfers between devices with their start and end apart: 17, of which 12 were waited for; matrix products, arithmetic and copies ran while one was open for 5% of the time, Pallas kernels for 0%

profile of v6, /device:TPU:0, one launch (start us, length us, event | category | flops | bytes accessed | tf_op | source)
XLA Modules:
  0.0 215.7 jit_solution(15746057090256888033)
XLA Ops:
  0.6 4.7 %copy.43 = bf16[4,16,8,4096]{3,2,0,1:T(8,128)(2,1)} copy(bf16[4,16,8,4096]{3,2,1,0:T(8,128)(2,1)} %bitcast.94) | data formatting | bytes 8388608 | tf_op jit(solution)/shard_map/gradient_exchange/all_to_all | solution.py:139
  5.3 7.6 %all-to-all-start = ((bf16[32,16,4096]{2,0,1:T(8,128)(2,1)}), bf16[32,16,4096]{2,0,1:T(8,128)(2,1)}, u32[]{:S(2)}, u32[]{:S(2)}) async-start(bf16[32,16,4096]{2,0,1:T(8,128)(2,1)} %bitcast.93), calls=%async_computation | async-start | bytes 8388608 | tf_op jit(solution)/shard_map/gradient_exchange/all_to_all | solution.py:139
  13.1 77.4 %all-to-all-done = bf16[32,16,4096]{2,0,1:T(8,128)(2,1)} async-done(((bf16[32,16,4096]{2,0,1:T(8,128)(2,1)}), bf16[32,16,4096]{2,0,1:T(8,128)(2,1)}, u32[]{:S(2)}, u32[]{:S(2)}) %all-to-all-start) | async-done | bytes 4194336 | tf_op jit(solution)/shard_map/gradient_exchange/all_to_all | solution.py:139
  90.6 5.8 %fusion.1 = f32[2,2,2,2,32,512]{5,4,3,2,1,0:T(8,128)S(1)} fusion(bf16[2,2,2,2,32,4096]{5,4,3,2,1,0:T(8,128)(2,1)} %bitcast.1, bf16[4096,1024]{1,0:T(8,128)(2,1)} %param.5), kind=kOutput, calls=%fused_computation.4 | convolution fusion | flops 2147483648 | bytes 9437184 | tf_op jit(solution)/shard_map/partial_projection/dot_general | solution.py:145
  96.4 0.8 dynamic-slice_bitcast_fusion
  97.2 0.8 collective-permute-start.8
  98.0 5.8 %fusion.3 = f32[2,2,2,2,32,512]{5,4,3,2,1,0:T(8,128)S(1)} fusion(bf16[2,2,2,2,32,4096]{5,4,3,2,1,0:T(8,128)(2,1)} %bitcast.1, bf16[4096,1024]{1,0:T(8,128)(2,1)} %param.5), kind=kOutput, calls=%fused_computation.6 | convolution fusion | flops 2147483648 | bytes 9437184 | tf_op jit(solution)/shard_map/partial_projection/dot_general | solution.py:145
  103.8 0.8 dynamic-slice_bitcast_fusion.1
  104.7 1.5 convert_reduce_fusion
  106.5 14.8 %collective-permute-start.9 = (f32[2,2,32,512]{3,2,1,0:T(8,128)S(1)}, f32[2,2,32,512]{3,2,1,0:T(8,128)S(1)}, u32[]{:S(2)}, u32[]{:S(2)}) collective-permute-start(f32[2,2,32,512]{3,2,1,0:T(8,128)S(1)} %dynamic-slice_bitcast_fusion.2), channel_id=1, source_target_pairs={{0,4},{1,5},{2,6},{3,7},{4,0},{5,1},{6,2},{7,3},{8,12},{9,13},{10,... | collective-permute-start | bytes 786440 | tf_op jit(solution)/shard_map/sketch_reduce/ppermute | solution.py:93
  121.5 3.0 %collective-permute-start.1 = (f32[2,2,32,512]{3,2,1,0:T(8,128)S(1)}, f32[2,2,32,512]{3,2,1,0:T(8,128)S(1)}, u32[]{:S(2)}, u32[]{:S(2)}) collective-permute-start(f32[2,2,32,512]{3,2,1,0:T(8,128)S(1)} %dynamic-slice_bitcast_fusion.3), channel_id=1, source_target_pairs={{0,2},{1,3},{2,0},{3,1},{4,6},{5,7},{6,4},{7,5},{8,10},{9,11},{10,... | collective-permute-start | bytes 786440 | tf_op jit(solution)/shard_map/sketch_reduce/ppermute | solution.py:93
  124.5 3.3 %collective-permute-done.9 = f32[2,2,32,512]{3,2,1,0:T(8,128)S(1)} collective-permute-done((f32[2,2,32,512]{3,2,1,0:T(8,128)S(1)}, f32[2,2,32,512]{3,2,1,0:T(8,128)S(1)}, u32[]{:S(2)}, u32[]{:S(2)}) %collective-permute-start.9) | collective-permute-done | bytes 262176 | tf_op jit(solution)/shard_map/sketch_reduce/ppermute | solution.py:93
  127.9 3.3 %collective-permute-start.10 = (f32[2,32,512]{2,1,0:T(8,128)S(1)}, f32[2,32,512]{2,1,0:T(8,128)S(1)}, u32[]{:S(2)}, u32[]{:S(2)}) collective-permute-start(f32[2,32,512]{2,1,0:T(8,128)S(1)} %dynamic-slice_bitcast_fusion.4), channel_id=1, source_target_pairs={{0,2},{1,3},{2,0},{3,1},{4,6},{5,7},{6,4},{7,5},{8,10},{9,11},{10,... | collective-permute-start | bytes 393224 | tf_op jit(solution)/shard_map/sketch_reduce/ppermute | solution.py:93
  131.3 1.8 collective-permute-start.2
  133.1 1.6 collective-permute-done.10
  134.7 2.8 %collective-permute-start.11 = (f32[32,512]{1,0:T(8,128)S(1)}, f32[32,512]{1,0:T(8,128)S(1)}, u32[]{:S(2)}, u32[]{:S(2)}) collective-permute-start(f32[32,512]{1,0:T(8,128)S(1)} %dynamic-slice_bitcast_fusion.6), channel_id=1, source_target_pairs={{0,8},{1,9},{2,10},{3,11},{4,12},{5,13},{6,14},{7,15},{8,0},{9,1},... | collective-permute-start | bytes 196616 | tf_op jit(solution)/shard_map/sketch_reduce/ppermute | solution.py:93
  137.9 3.8 %collective-permute-done.11 = f32[32,512]{1,0:T(8,128)S(1)} collective-permute-done((f32[32,512]{1,0:T(8,128)S(1)}, f32[32,512]{1,0:T(8,128)S(1)}, u32[]{:S(2)}, u32[]{:S(2)}) %collective-permute-start.11) | collective-permute-done | bytes 65568 | tf_op jit(solution)/shard_map/sketch_reduce/ppermute | solution.py:93
  141.7 1.1 collective-permute-start.12
  142.9 3.4 %collective-permute-done.3 = f32[32,512]{1,0:T(8,128)S(1)} collective-permute-done((f32[32,512]{1,0:T(8,128)S(1)}, f32[32,512]{1,0:T(8,128)S(1)}, u32[]{:S(2)}, u32[]{:S(2)}) %collective-permute-start.3) | collective-permute-done | bytes 65568 | tf_op jit(solution)/shard_map/sketch_reduce/ppermute | solution.py:93
  146.3 1.3 collective-permute-done.12
  147.7 1.2 collective-permute-start.13
  148.9 2.7 %collective-permute-done.4 = f32[32,512]{1,0:T(8,128)S(1)} collective-permute-done((f32[32,512]{1,0:T(8,128)S(1)}, f32[32,512]{1,0:T(8,128)S(1)}, u32[]{:S(2)}, u32[]{:S(2)}) %collective-permute-start.4) | collective-permute-done | bytes 65568 | tf_op jit(solution)/shard_map/sketch_gather/ppermute | solution.py:93
  151.7 1.0 collective-permute-done.13
  152.8 1.1 collective-permute-start.14
  153.8 3.4 %collective-permute-done.5 = f32[2,32,512]{2,1,0:T(8,128)S(1)} collective-permute-done((f32[2,32,512]{2,1,0:T(8,128)S(1)}, f32[2,32,512]{2,1,0:T(8,128)S(1)}, u32[]{:S(2)}, u32[]{:S(2)}) %collective-permute-start.5) | collective-permute-done | bytes 131104 | tf_op jit(solution)/shard_map/sketch_gather/ppermute | solution.py:93
  157.6 2.4 %collective-permute-done.14 = f32[2,2,32,512]{3,2,0,1:T(8,128)S(1)} collective-permute-done((f32[2,2,32,512]{3,2,0,1:T(8,128)S(1)}, f32[2,2,32,512]{3,2,0,1:T(8,128)S(1)}, u32[]{:S(2)}, u32[]{:S(2)}) %collective-permute-start.14) | collective-permute-done | bytes 262176 | tf_op jit(solution)/shard_map/sketch_gather/ppermute | solution.py:93
  160.2 3.5 %collective-permute-done.6 = f32[2,2,32,512]{3,2,1,0:T(8,128)S(1)} collective-permute-done((f32[2,2,32,512]{3,2,1,0:T(8,128)S(1)}, f32[2,2,32,512]{3,2,1,0:T(8,128)S(1)}, u32[]{:S(2)}, u32[]{:S(2)}) %collective-permute-start.6) | collective-permute-done | bytes 262176 | tf_op jit(solution)/shard_map/sketch_gather/ppermute | solution.py:93
  163.7 0.8 pad_maximum_fusion.2
  164.6 0.7 pad.4.w_ref
  166.9 4.6 %select_add_fusion = (f32[512,512]{1,0:T(8,128)}, f32[512,512]{1,0:T(8,128)S(1)}) fusion(f32[512,512]{1,0:T(8,128)S(1)} %bitcast.95, f32[512,512]{1,0:T(8,128)S(1)} %bitcast.96), kind=kOutput, calls=%fused_computation.16 | convolution fusion | flops 3222798336 | bytes 4194304 | tf_op jit(solution)/shard_map/kernel_matrix/dot_general | solution.py:169
  171.4 42.1 %kernel_solve.1 = f32[512,128]{1,0:T(8,128)} custom-call(f32[512,512]{1,0:T(8,128)} %get-tuple-element.18.m_ref, f32[512,128]{1,0:T(8,128)} %pad.4.w_ref), custom_call_target="tpu_custom_call" | custom-call | tf_op jit(solution)/shard_map/kernel_solve/pallas_call | solution.py:84
  213.6 2.1 fusion.11
  (52 shorter events, 3.3 us)
Async XLA Ops:
  5.3 7.7 %copy-start.1 = (s32[24]{0:T(128)S(1)}, s32[24]{0:T(128)}, u32[]{:S(2)}) copy-start(s32[24]{0:T(128)} %param.7) | copy-start | bytes 292
  5.3 85.3 %all-to-all-start = ((bf16[32,16,4096]{2,0,1:T(8,128)(2,1)}), bf16[32,16,4096]{2,0,1:T(8,128)(2,1)}, u32[]{:S(2)}, u32[]{:S(2)}) async-start(bf16[32,16,4096]{2,0,1:T(8,128)(2,1)} %bitcast.93), calls=%async_computation | async-start | bytes 8388608 | tf_op jit(solution)/shard_map/gradient_exchange/all_to_all | solution.py:139
  97.2 7.4 %copy-start = (s32[24,128]{1,0:T(8,128)S(1)}, s32[24,128]{1,0:T(8,128)}, u32[]{:S(2)}) copy-start(s32[24,128]{1,0:T(8,128)} %param.6) | copy-start | bytes 36868
  97.2 9.2 %collective-permute-start.8 = (f32[2,2,2,32,512]{4,3,2,1,0:T(8,128)}, f32[2,2,2,32,512]{4,3,2,1,0:T(8,128)S(1)}, u32[]{:S(2)}, u32[]{:S(2)}) collective-permute-start(f32[2,2,2,32,512]{4,3,2,1,0:T(8,128)} %dynamic-slice_bitcast_fusion), channel_id=1, source_target_pairs={{0,1},{1,0},{2,3},{3,2},{4,5},{5,4},{6,7},{7,6},{8,9},{9,8},{10,11... | collective-permute-start | bytes 1572872 | tf_op jit(solution)/shard_map/sketch_reduce/ppermute | solution.py:93
  104.6 16.7 %collective-permute-start = (f32[2,2,2,32,512]{4,3,2,1,0:T(8,128)}, f32[2,2,2,32,512]{4,3,2,1,0:T(8,128)S(1)}, u32[]{:S(2)}, u32[]{:S(2)}) collective-permute-start(f32[2,2,2,32,512]{4,3,2,1,0:T(8,128)} %dynamic-slice_bitcast_fusion.1), channel_id=1, source_target_pairs={{0,1},{1,0},{2,3},{3,2},{4,5},{5,4},{6,7},{7,6},{8,9},{9,8},{10,11... | collective-permute-start | bytes 1572872 | tf_op jit(solution)/shard_map/sketch_reduce/ppermute | solution.py:93
  106.5 21.3 %collective-permute-start.9 = (f32[2,2,32,512]{3,2,1,0:T(8,128)S(1)}, f32[2,2,32,512]{3,2,1,0:T(8,128)S(1)}, u32[]{:S(2)}, u32[]{:S(2)}) collective-permute-start(f32[2,2,32,512]{3,2,1,0:T(8,128)S(1)} %dynamic-slice_bitcast_fusion.2), channel_id=1, source_target_pairs={{0,4},{1,5},{2,6},{3,7},{4,0},{5,1},{6,2},{7,3},{8,12},{9,13},{10,... | collective-permute-start | bytes 786440 | tf_op jit(solution)/shard_map/sketch_reduce/ppermute | solution.py:93
  121.5 9.7 %collective-permute-start.1 = (f32[2,2,32,512]{3,2,1,0:T(8,128)S(1)}, f32[2,2,32,512]{3,2,1,0:T(8,128)S(1)}, u32[]{:S(2)}, u32[]{:S(2)}) collective-permute-start(f32[2,2,32,512]{3,2,1,0:T(8,128)S(1)} %dynamic-slice_bitcast_fusion.3), channel_id=1, source_target_pairs={{0,2},{1,3},{2,0},{3,1},{4,6},{5,7},{6,4},{7,5},{8,10},{9,11},{10,... | collective-permute-start | bytes 786440 | tf_op jit(solution)/shard_map/sketch_reduce/ppermute | solution.py:93
  127.9 6.8 %collective-permute-start.10 = (f32[2,32,512]{2,1,0:T(8,128)S(1)}, f32[2,32,512]{2,1,0:T(8,128)S(1)}, u32[]{:S(2)}, u32[]{:S(2)}) collective-permute-start(f32[2,32,512]{2,1,0:T(8,128)S(1)} %dynamic-slice_bitcast_fusion.4), channel_id=1, source_target_pairs={{0,2},{1,3},{2,0},{3,1},{4,6},{5,7},{6,4},{7,5},{8,10},{9,11},{10,... | collective-permute-start | bytes 393224 | tf_op jit(solution)/shard_map/sketch_reduce/ppermute | solution.py:93
  131.3 6.3 %collective-permute-start.2 = (f32[2,32,512]{2,1,0:T(8,128)S(1)}, f32[2,32,512]{2,1,0:T(8,128)S(1)}, u32[]{:S(2)}, u32[]{:S(2)}) collective-permute-start(f32[2,32,512]{2,1,0:T(8,128)S(1)} %dynamic-slice_bitcast_fusion.5), channel_id=1, source_target_pairs={{0,4},{1,5},{2,6},{3,7},{4,0},{5,1},{6,2},{7,3},{8,12},{9,13},{10,... | collective-permute-start | bytes 393224 | tf_op jit(solution)/shard_map/sketch_reduce/ppermute | solution.py:93
  134.7 7.0 %collective-permute-start.11 = (f32[32,512]{1,0:T(8,128)S(1)}, f32[32,512]{1,0:T(8,128)S(1)}, u32[]{:S(2)}, u32[]{:S(2)}) collective-permute-start(f32[32,512]{1,0:T(8,128)S(1)} %dynamic-slice_bitcast_fusion.6), channel_id=1, source_target_pairs={{0,8},{1,9},{2,10},{3,11},{4,12},{5,13},{6,14},{7,15},{8,0},{9,1},... | collective-permute-start | bytes 196616 | tf_op jit(solution)/shard_map/sketch_reduce/ppermute | solution.py:93
  137.6 8.7 %collective-permute-start.3 = (f32[32,512]{1,0:T(8,128)S(1)}, f32[32,512]{1,0:T(8,128)S(1)}, u32[]{:S(2)}, u32[]{:S(2)}) collective-permute-start(f32[32,512]{1,0:T(8,128)S(1)} %dynamic-slice_bitcast_fusion.7), channel_id=1, source_target_pairs={{0,8},{1,9},{2,10},{3,11},{4,12},{5,13},{6,14},{7,15},{8,0},{9,1},... | collective-permute-start | bytes 196616 | tf_op jit(solution)/shard_map/sketch_reduce/ppermute | solution.py:93
  141.7 5.9 %collective-permute-start.12 = (f32[32,512]{1,0:T(8,128)S(1)}, f32[32,512]{1,0:T(8,128)S(1)}, u32[]{:S(2)}, u32[]{:S(2)}) collective-permute-start(f32[32,512]{1,0:T(8,128)S(1)} %bitcast_add_fusion.6), channel_id=1, source_target_pairs={{0,8},{1,9},{2,10},{3,11},{4,12},{5,13},{6,14},{7,15},{8,0},{9,1},... | collective-permute-start | bytes 196616 | tf_op jit(solution)/shard_map/sketch_gather/ppermute | solution.py:93
  146.3 5.3 %collective-permute-start.4 = (f32[32,512]{1,0:T(8,128)S(1)}, f32[32,512]{1,0:T(8,128)S(1)}, u32[]{:S(2)}, u32[]{:S(2)}) collective-permute-start(f32[32,512]{1,0:T(8,128)S(1)} %bitcast_add_fusion.7), channel_id=1, source_target_pairs={{0,8},{1,9},{2,10},{3,11},{4,12},{5,13},{6,14},{7,15},{8,0},{9,1},... | collective-permute-start | bytes 196616 | tf_op jit(solution)/shard_map/sketch_gather/ppermute | solution.py:93
  147.7 5.0 %collective-permute-start.13 = (f32[2,32,512]{2,1,0:T(8,128)S(1)}, f32[2,32,512]{2,1,0:T(8,128)S(1)}, u32[]{:S(2)}, u32[]{:S(2)}) collective-permute-start(f32[2,32,512]{2,1,0:T(8,128)S(1)} %pad_maximum_fusion.7), channel_id=1, source_target_pairs={{0,2},{1,3},{2,0},{3,1},{4,6},{5,7},{6,4},{7,5},{8,10},{9,11},{10,... | collective-permute-start | bytes 393224 | tf_op jit(solution)/shard_map/sketch_gather/ppermute | solution.py:93
  151.6 5.6 %collective-permute-start.5 = (f32[2,32,512]{2,1,0:T(8,128)S(1)}, f32[2,32,512]{2,1,0:T(8,128)S(1)}, u32[]{:S(2)}, u32[]{:S(2)}) collective-permute-start(f32[2,32,512]{2,1,0:T(8,128)S(1)} %pad_maximum_fusion.6), channel_id=1, source_target_pairs={{0,4},{1,5},{2,6},{3,7},{4,0},{5,1},{6,2},{7,3},{8,12},{9,13},{10,... | collective-permute-start | bytes 393224 | tf_op jit(solution)/shard_map/sketch_gather/ppermute | solution.py:93
  152.8 7.2 %collective-permute-start.14 = (f32[2,2,32,512]{3,2,0,1:T(8,128)S(1)}, f32[2,2,32,512]{3,2,0,1:T(8,128)S(1)}, u32[]{:S(2)}, u32[]{:S(2)}) collective-permute-start(f32[2,2,32,512]{3,2,0,1:T(8,128)S(1)} %pad_maximum_fusion.5), channel_id=1, source_target_pairs={{0,4},{1,5},{2,6},{3,7},{4,0},{5,1},{6,2},{7,3},{8,12},{9,13},{10,... | collective-permute-start | bytes 786440 | tf_op jit(solution)/shard_map/sketch_gather/ppermute | solution.py:93
  157.2 6.4 %collective-permute-start.6 = (f32[2,2,32,512]{3,2,1,0:T(8,128)S(1)}, f32[2,2,32,512]{3,2,1,0:T(8,128)S(1)}, u32[]{:S(2)}, u32[]{:S(2)}) collective-permute-start(f32[2,2,32,512]{3,2,1,0:T(8,128)S(1)} %pad_maximum_fusion.4), channel_id=1, source_target_pairs={{0,2},{1,3},{2,0},{3,1},{4,6},{5,7},{6,4},{7,5},{8,10},{9,11},{10,... | collective-permute-start | bytes 786440 | tf_op jit(solution)/shard_map/sketch_gather/ppermute | solution.py:93
  160.1 5.9 %collective-permute-start.15 = (f32[2,2,2,32,512]{4,3,0,2,1:T(8,128)S(1)}, f32[2,2,2,32,512]{4,3,0,2,1:T(8,128)S(1)}, u32[]{:S(2)}, u32[]{:S(2)}) collective-permute-start(f32[2,2,2,32,512]{4,3,0,2,1:T(8,128)S(1)} %pad_maximum_fusion.3), channel_id=1, source_target_pairs={{0,1},{1,0},{2,3},{3,2},{4,5},{5,4},{6,7},{7,6},{8,9},{9,8},{10,11... | collective-permute-start | bytes 1572872 | tf_op jit(solution)/shard_map/sketch_gather/ppermute | solution.py:93
  164.6 2.1 collective-permute-start.7

commit v7 on v5

--- a/solution.py
+++ b/solution.py
@@ -38,7 +38,12 @@
 
     def step(h, a):
         k = 4 * h
-        rows = [jnp.sum(jnp.where(sub == k + t, a, 0.0), axis=0, keepdims=True) for t in range(4)]
+        base = k - k % 8
+        tile = jnp.sum(
+            jnp.where((sub >= base) & (sub < base + 8), a, 0.0).reshape(size // 8, 8, size), axis=0)
+        in_tile = lax.broadcasted_iota(jnp.int32, (8, size), 0)
+        rows = [jnp.sum(jnp.where(in_tile == k % 8 + t, tile, 0.0), axis=0, keepdims=True)
+                for t in range(4)]
         cols = [jnp.sum(jnp.where(lane == k + t, a, 0.0), axis=1, keepdims=True) for t in range(4)]
         s0, s1 = pair_pivot(rows[0], rows[1], k)
         r2 = eliminate(rows[2], k, s0, s1)
@@ -65,17 +70,18 @@
     blocks = n // block
     for j in range(blocks):
         lo = j * block
-        inverse = _invert_block(a_ref[lo:lo + block, lo:lo + block])
-        pivot_rows = jnp.dot(inverse, a_ref[lo:lo + block, lo:], precision=HI,
+        hi = lo + block
+        inverse = _invert_block(a_ref[lo:hi, lo:hi])
+        pivot_rows = jnp.dot(inverse, a_ref[lo:hi, hi:], precision=HI,
                              preferred_element_type=jnp.float32)
         for i in range(blocks):
             if i == j:
                 continue
             r = i * block
-            a_ref[r:r + block, lo:] = a_ref[r:r + block, lo:] - jnp.dot(
-                a_ref[r:r + block, lo:lo + block], pivot_rows, precision=HI,
+            a_ref[r:r + block, hi:] = a_ref[r:r + block, hi:] - jnp.dot(
+                a_ref[r:r + block, lo:hi], pivot_rows, precision=HI,
                 preferred_element_type=jnp.float32)
-        a_ref[lo:lo + block, lo:] = pivot_rows
+        a_ref[lo:hi, hi:] = pivot_rows
     y_ref[...] = a_ref[:, n:]
 
 

time: 211 us -> 210 us (level)
  no operation moved by 1% of the time
where the time goes in v7:
time: 210 us; the launch traced here: 209 us
  waiting for transfers between devices  104 us (50%)
  Pallas kernels  40.1 us (19%)
  starting transfers between devices  38.2 us (18%)
  matrix products  14.8 us (7%)
  local copies, waits for them, and re-layouts  7.09 us (3%)
  other arithmetic  4.18 us (2%)
    all_to_all x1, waiting for transfers between devices, on_device(): lax.all_to_all(grads, 'ex', split_axis=1, concat_axis=0, tiled=True)  77.7 us
    pallas_call x1, Pallas kernels, spd_solve(): pl.pallas_call(functools.partial(_solve_kernel, block=block), out_shape=j...  40.1 us
    ppermute x16, starting transfers between devices, partner(): lax.ppermute(array, axis, [(i, i ^ 1 << bit) for i in range(lax.axis_size...  30.8 us
    ppermute x16, waiting for transfers between devices, partner(): lax.ppermute(array, axis, [(i, i ^ 1 << bit) for i in range(lax.axis_size...  26.3 us
    dot_general x1, matrix products, on_device(): partial_value = jnp.dot(columns, proj, preferred_element_type=jnp.float32)  8.14 us
    all_to_all x1, starting transfers between devices, on_device(): lax.all_to_all(grads, 'ex', split_axis=1, concat_axis=0, tiled=True)  7.44 us
    all_to_all x1, local copies, waits for them, and re-layouts, on_device(): lax.all_to_all(grads, 'ex', split_axis=1, concat_axis=0, tiled=True)  4.72 us
    dot_general x1, matrix products, on_device(): kernel = jnp.dot(sketch_all, sketch_all.T, precision=lax.Precision.HIGHEST)  4.55 us
  transfers between devices with their start and end apart: 17, of which 12 were waited for; matrix products, arithmetic and copies ran while one was open for 3% of the time, Pallas kernels for 0%

profile of v7, /device:TPU:0, one launch (start us, length us, event | category | flops | bytes accessed | tf_op | source)
XLA Modules:
  0.0 209.3 jit_solution(2224009474509464713)
XLA Ops:
  0.6 4.7 %copy.70 = bf16[4,16,8,4096]{3,2,0,1:T(8,128)(2,1)} copy(bf16[4,16,8,4096]{3,2,1,0:T(8,128)(2,1)} %bitcast.88) | data formatting | bytes 8388608 | tf_op jit(solution)/shard_map/gradient_exchange/all_to_all | solution.py:145
  5.3 7.4 %all-to-all-start = ((bf16[32,16,4096]{2,0,1:T(8,128)(2,1)}), bf16[32,16,4096]{2,0,1:T(8,128)(2,1)}, u32[]{:S(2)}, u32[]{:S(2)}) async-start(bf16[32,16,4096]{2,0,1:T(8,128)(2,1)} %bitcast.87), calls=%async_computation | async-start | bytes 8388608 | tf_op jit(solution)/shard_map/gradient_exchange/all_to_all | solution.py:145
  12.8 77.7 %all-to-all-done = bf16[32,16,4096]{2,0,1:T(8,128)(2,1)} async-done(((bf16[32,16,4096]{2,0,1:T(8,128)(2,1)}), bf16[32,16,4096]{2,0,1:T(8,128)(2,1)}, u32[]{:S(2)}, u32[]{:S(2)}) %all-to-all-start) | async-done | bytes 4194336 | tf_op jit(solution)/shard_map/gradient_exchange/all_to_all | solution.py:145
  90.5 8.1 %fusion.11 = f32[512,1024]{1,0:T(8,128)S(1)} fusion(bf16[512,4096]{1,0:T(8,128)(2,1)} %bitcast.1, bf16[4096,1024]{1,0:T(8,128)(2,1)} %param.5), kind=kOutput, calls=%fused_computation.63 | convolution fusion | flops 4294967296 | bytes 14680064 | tf_op jit(solution)/shard_map/partial_projection/dot_general | solution.py:147
  99.1 0.8 collective-permute-start.8
  100.1 0.9 copy.72
  101.1 1.5 convert_reduce_fusion
  102.9 14.7 %collective-permute-start.9 = (f32[2,2,32,512]{3,2,1,0:T(8,128)S(1)}, f32[2,2,32,512]{3,2,1,0:T(8,128)S(1)}, u32[]{:S(2)}, u32[]{:S(2)}) collective-permute-start(f32[2,2,32,512]{3,2,1,0:T(8,128)S(1)} %dynamic-slice_bitcast_fusion), channel_id=1, source_target_pairs={{0,4},{1,5},{2,6},{3,7},{4,0},{5,1},{6,2},{7,3},{8,12},{9,13},{10,... | collective-permute-start | bytes 786440 | tf_op jit(solution)/shard_map/sketch_reduce/ppermute | solution.py:99
  117.7 3.0 %collective-permute-start.1 = (f32[2,2,32,512]{3,2,1,0:T(8,128)S(1)}, f32[2,2,32,512]{3,2,1,0:T(8,128)S(1)}, u32[]{:S(2)}, u32[]{:S(2)}) collective-permute-start(f32[2,2,32,512]{3,2,1,0:T(8,128)S(1)} %dynamic-slice_bitcast_fusion.1), channel_id=1, source_target_pairs={{0,2},{1,3},{2,0},{3,1},{4,6},{5,7},{6,4},{7,5},{8,10},{9,11},{10,... | collective-permute-start | bytes 786440 | tf_op jit(solution)/shard_map/sketch_reduce/ppermute | solution.py:99
  120.7 3.5 %collective-permute-done.9 = f32[2,2,32,512]{3,2,1,0:T(8,128)S(1)} collective-permute-done((f32[2,2,32,512]{3,2,1,0:T(8,128)S(1)}, f32[2,2,32,512]{3,2,1,0:T(8,128)S(1)}, u32[]{:S(2)}, u32[]{:S(2)}) %collective-permute-start.9) | collective-permute-done | bytes 262176 | tf_op jit(solution)/shard_map/sketch_reduce/ppermute | solution.py:99
  124.3 3.2 %collective-permute-start.10 = (f32[2,32,512]{2,1,0:T(8,128)S(1)}, f32[2,32,512]{2,1,0:T(8,128)S(1)}, u32[]{:S(2)}, u32[]{:S(2)}) collective-permute-start(f32[2,32,512]{2,1,0:T(8,128)S(1)} %dynamic-slice_bitcast_fusion.2), channel_id=1, source_target_pairs={{0,2},{1,3},{2,0},{3,1},{4,6},{5,7},{6,4},{7,5},{8,10},{9,11},{10,... | collective-permute-start | bytes 393224 | tf_op jit(solution)/shard_map/sketch_reduce/ppermute | solution.py:99
  127.5 1.8 collective-permute-start.2
  129.3 1.6 collective-permute-done.10
  131.0 3.0 %collective-permute-start.11 = (f32[32,512]{1,0:T(8,128)S(1)}, f32[32,512]{1,0:T(8,128)S(1)}, u32[]{:S(2)}, u32[]{:S(2)}) collective-permute-start(f32[32,512]{1,0:T(8,128)S(1)} %dynamic-slice_bitcast_fusion.4), channel_id=1, source_target_pairs={{0,8},{1,9},{2,10},{3,11},{4,12},{5,13},{6,14},{7,15},{8,0},{9,1},... | collective-permute-start | bytes 196616 | tf_op jit(solution)/shard_map/sketch_reduce/ppermute | solution.py:99
  134.2 4.0 %collective-permute-done.11 = f32[32,512]{1,0:T(8,128)S(1)} collective-permute-done((f32[32,512]{1,0:T(8,128)S(1)}, f32[32,512]{1,0:T(8,128)S(1)}, u32[]{:S(2)}, u32[]{:S(2)}) %collective-permute-start.11) | collective-permute-done | bytes 65568 | tf_op jit(solution)/shard_map/sketch_reduce/ppermute | solution.py:99
  138.2 1.0 collective-permute-start.12
  139.3 2.5 %collective-permute-done.3 = f32[32,512]{1,0:T(8,128)S(1)} collective-permute-done((f32[32,512]{1,0:T(8,128)S(1)}, f32[32,512]{1,0:T(8,128)S(1)}, u32[]{:S(2)}, u32[]{:S(2)}) %collective-permute-start.3) | collective-permute-done | bytes 65568 | tf_op jit(solution)/shard_map/sketch_reduce/ppermute | solution.py:99
  141.9 2.3 %collective-permute-done.12 = f32[32,512]{1,0:T(8,128)S(1)} collective-permute-done((f32[32,512]{1,0:T(8,128)S(1)}, f32[32,512]{1,0:T(8,128)S(1)}, u32[]{:S(2)}, u32[]{:S(2)}) %collective-permute-start.12) | collective-permute-done | bytes 65568 | tf_op jit(solution)/shard_map/sketch_gather/ppermute | solution.py:99
  144.2 0.9 collective-permute-start.13
  145.1 2.5 %collective-permute-done.4 = f32[32,512]{1,0:T(8,128)S(1)} collective-permute-done((f32[32,512]{1,0:T(8,128)S(1)}, f32[32,512]{1,0:T(8,128)S(1)}, u32[]{:S(2)}, u32[]{:S(2)}) %collective-permute-start.4) | collective-permute-done | bytes 65568 | tf_op jit(solution)/shard_map/sketch_gather/ppermute | solution.py:99
  148.0 1.2 collective-permute-done.13
  149.3 0.6 collective-permute-start.14
  149.9 2.9 %collective-permute-done.5 = f32[2,32,512]{2,1,0:T(8,128)S(1)} collective-permute-done((f32[2,32,512]{2,1,0:T(8,128)S(1)}, f32[2,32,512]{2,1,0:T(8,128)S(1)}, u32[]{:S(2)}, u32[]{:S(2)}) %collective-permute-start.5) | collective-permute-done | bytes 131104 | tf_op jit(solution)/shard_map/sketch_gather/ppermute | solution.py:99
  152.8 0.9 collective-permute-start.6
  153.7 2.0 collective-permute-done.14
  155.9 3.4 %collective-permute-done.6 = f32[2,2,32,512]{3,2,1,0:T(8,128)S(1)} collective-permute-done((f32[2,2,32,512]{3,2,1,0:T(8,128)S(1)}, f32[2,2,32,512]{3,2,1,0:T(8,128)S(1)}, u32[]{:S(2)}, u32[]{:S(2)}) %collective-permute-start.6) | collective-permute-done | bytes 262176 | tf_op jit(solution)/shard_map/sketch_gather/ppermute | solution.py:99
  159.3 0.9 pad_maximum_fusion.2
  160.2 0.7 pad.4.w_ref
  161.0 0.7 pad_maximum_fusion.8
  162.5 4.5 %select_add_fusion = (f32[512,512]{1,0:T(8,128)}, f32[512,512]{1,0:T(8,128)S(1)}) fusion(f32[512,512]{1,0:T(8,128)S(1)} %bitcast.91, f32[512,512]{1,0:T(8,128)S(1)} %bitcast.92), kind=kOutput, calls=%fused_computation.10 | convolution fusion | flops 3222798336 | bytes 4194304 | tf_op jit(solution)/shard_map/kernel_matrix/dot_general | solution.py:174
  167.1 40.1 %kernel_solve.1 = f32[512,128]{1,0:T(8,128)} custom-call(f32[512,512]{1,0:T(8,128)} %get-tuple-element.24.m_ref, f32[512,128]{1,0:T(8,128)} %pad.4.w_ref), custom_call_target="tpu_custom_call" | custom-call | tf_op jit(solution)/shard_map/kernel_solve/pallas_call | solution.py:90
  207.1 2.1 %fusion.5 = f32[32,24]{0,1:T(8,128)} fusion(f32[512,128]{1,0:T(8,128)} %kernel_solve.1, f32[512,512]{1,0:T(8,128)S(1)} %get-tuple-element.25, s32[]{:T(128)S(6)} %select_n.227), kind=kOutput, calls=%fused_computation.22 | convolution fusion | flops 4718592 | bytes 330756 | tf_op jit(solution)/shard_map/dot_general | solution.py:181
  (53 shorter events, 3.1 us)
Async XLA Ops:
  5.3 85.1 %all-to-all-start = ((bf16[32,16,4096]{2,0,1:T(8,128)(2,1)}), bf16[32,16,4096]{2,0,1:T(8,128)(2,1)}, u32[]{:S(2)}, u32[]{:S(2)}) async-start(bf16[32,16,4096]{2,0,1:T(8,128)(2,1)} %bitcast.87), calls=%async_computation | async-start | bytes 8388608 | tf_op jit(solution)/shard_map/gradient_exchange/all_to_all | solution.py:145
  98.6 1.4 copy-start.1
  98.8 2.2 %copy-start = (s32[24,128]{1,0:T(8,128)S(1)}, s32[24,128]{1,0:T(8,128)}, u32[]{:S(2)}) copy-start(s32[24,128]{1,0:T(8,128)} %param.6) | copy-start | bytes 36868
  99.1 3.6 %collective-permute-start.8 = (f32[2,2,2,32,512]{4,3,2,0,1:T(8,128)S(1)}, f32[2,2,2,32,512]{4,3,2,0,1:T(8,128)S(1)}, u32[]{:S(2)}, u32[]{:S(2)}) collective-permute-start(f32[2,2,2,32,512]{4,3,2,0,1:T(8,128)S(1)} %bitcast.93), channel_id=1, source_target_pairs={{0,1},{1,0},{2,3},{3,2},{4,5},{5,4},{6,7},{7,6},{8,9},{9,8},{10,11... | collective-permute-start | bytes 1572872 | tf_op jit(solution)/shard_map/sketch_reduce/ppermute | solution.py:99
  100.9 16.7 %collective-permute-start = (f32[2,2,2,32,512]{4,3,1,0,2:T(8,128)}, f32[2,2,2,32,512]{4,3,1,0,2:T(8,128)S(1)}, u32[]{:S(2)}, u32[]{:S(2)}) collective-permute-start(f32[2,2,2,32,512]{4,3,1,0,2:T(8,128)} %bitcast.86), channel_id=1, source_target_pairs={{0,1},{1,0},{2,3},{3,2},{4,5},{5,4},{6,7},{7,6},{8,9},{9,8},{10,11... | collective-permute-start | bytes 1572872 | tf_op jit(solution)/shard_map/sketch_reduce/ppermute | solution.py:99
  102.9 21.3 %collective-permute-start.9 = (f32[2,2,32,512]{3,2,1,0:T(8,128)S(1)}, f32[2,2,32,512]{3,2,1,0:T(8,128)S(1)}, u32[]{:S(2)}, u32[]{:S(2)}) collective-permute-start(f32[2,2,32,512]{3,2,1,0:T(8,128)S(1)} %dynamic-slice_bitcast_fusion), channel_id=1, source_target_pairs={{0,4},{1,5},{2,6},{3,7},{4,0},{5,1},{6,2},{7,3},{8,12},{9,13},{10,... | collective-permute-start | bytes 786440 | tf_op jit(solution)/shard_map/sketch_reduce/ppermute | solution.py:99
  117.7 9.7 %collective-permute-start.1 = (f32[2,2,32,512]{3,2,1,0:T(8,128)S(1)}, f32[2,2,32,512]{3,2,1,0:T(8,128)S(1)}, u32[]{:S(2)}, u32[]{:S(2)}) collective-permute-start(f32[2,2,32,512]{3,2,1,0:T(8,128)S(1)} %dynamic-slice_bitcast_fusion.1), channel_id=1, source_target_pairs={{0,2},{1,3},{2,0},{3,1},{4,6},{5,7},{6,4},{7,5},{8,10},{9,11},{10,... | collective-permute-start | bytes 786440 | tf_op jit(solution)/shard_map/sketch_reduce/ppermute | solution.py:99
  124.3 6.7 %collective-permute-start.10 = (f32[2,32,512]{2,1,0:T(8,128)S(1)}, f32[2,32,512]{2,1,0:T(8,128)S(1)}, u32[]{:S(2)}, u32[]{:S(2)}) collective-permute-start(f32[2,32,512]{2,1,0:T(8,128)S(1)} %dynamic-slice_bitcast_fusion.2), channel_id=1, source_target_pairs={{0,2},{1,3},{2,0},{3,1},{4,6},{5,7},{6,4},{7,5},{8,10},{9,11},{10,... | collective-permute-start | bytes 393224 | tf_op jit(solution)/shard_map/sketch_reduce/ppermute | solution.py:99
  127.5 6.4 %collective-permute-start.2 = (f32[2,32,512]{2,1,0:T(8,128)S(1)}, f32[2,32,512]{2,1,0:T(8,128)S(1)}, u32[]{:S(2)}, u32[]{:S(2)}) collective-permute-start(f32[2,32,512]{2,1,0:T(8,128)S(1)} %dynamic-slice_bitcast_fusion.3), channel_id=1, source_target_pairs={{0,4},{1,5},{2,6},{3,7},{4,0},{5,1},{6,2},{7,3},{8,12},{9,13},{10,... | collective-permute-start | bytes 393224 | tf_op jit(solution)/shard_map/sketch_reduce/ppermute | solution.py:99
  131.0 7.2 %collective-permute-start.11 = (f32[32,512]{1,0:T(8,128)S(1)}, f32[32,512]{1,0:T(8,128)S(1)}, u32[]{:S(2)}, u32[]{:S(2)}) collective-permute-start(f32[32,512]{1,0:T(8,128)S(1)} %dynamic-slice_bitcast_fusion.4), channel_id=1, source_target_pairs={{0,8},{1,9},{2,10},{3,11},{4,12},{5,13},{6,14},{7,15},{8,0},{9,1},... | collective-permute-start | bytes 196616 | tf_op jit(solution)/shard_map/sketch_reduce/ppermute | solution.py:99
  134.0 7.8 %collective-permute-start.3 = (f32[32,512]{1,0:T(8,128)S(1)}, f32[32,512]{1,0:T(8,128)S(1)}, u32[]{:S(2)}, u32[]{:S(2)}) collective-permute-start(f32[32,512]{1,0:T(8,128)S(1)} %dynamic-slice_bitcast_fusion.5), channel_id=1, source_target_pairs={{0,8},{1,9},{2,10},{3,11},{4,12},{5,13},{6,14},{7,15},{8,0},{9,1},... | collective-permute-start | bytes 196616 | tf_op jit(solution)/shard_map/sketch_reduce/ppermute | solution.py:99
  138.2 5.9 %collective-permute-start.12 = (f32[32,512]{1,0:T(8,128)S(1)}, f32[32,512]{1,0:T(8,128)S(1)}, u32[]{:S(2)}, u32[]{:S(2)}) collective-permute-start(f32[32,512]{1,0:T(8,128)S(1)} %bitcast_add_fusion.6), channel_id=1, source_target_pairs={{0,8},{1,9},{2,10},{3,11},{4,12},{5,13},{6,14},{7,15},{8,0},{9,1},... | collective-permute-start | bytes 196616 | tf_op jit(solution)/shard_map/sketch_gather/ppermute | solution.py:99
  141.8 5.8 %collective-permute-start.4 = (f32[32,512]{1,0:T(8,128)S(1)}, f32[32,512]{1,0:T(8,128)S(1)}, u32[]{:S(2)}, u32[]{:S(2)}) collective-permute-start(f32[32,512]{1,0:T(8,128)S(1)} %bitcast_add_fusion.7), channel_id=1, source_target_pairs={{0,8},{1,9},{2,10},{3,11},{4,12},{5,13},{6,14},{7,15},{8,0},{9,1},... | collective-permute-start | bytes 196616 | tf_op jit(solution)/shard_map/sketch_gather/ppermute | solution.py:99
  144.2 5.0 %collective-permute-start.13 = (f32[2,32,512]{2,1,0:T(8,128)S(1)}, f32[2,32,512]{2,1,0:T(8,128)S(1)}, u32[]{:S(2)}, u32[]{:S(2)}) collective-permute-start(f32[2,32,512]{2,1,0:T(8,128)S(1)} %pad_maximum_fusion.7), channel_id=1, source_target_pairs={{0,2},{1,3},{2,0},{3,1},{4,6},{5,7},{6,4},{7,5},{8,10},{9,11},{10,... | collective-permute-start | bytes 393224 | tf_op jit(solution)/shard_map/sketch_gather/ppermute | solution.py:99
  147.7 5.1 %collective-permute-start.5 = (f32[2,32,512]{2,1,0:T(8,128)S(1)}, f32[2,32,512]{2,1,0:T(8,128)S(1)}, u32[]{:S(2)}, u32[]{:S(2)}) collective-permute-start(f32[2,32,512]{2,1,0:T(8,128)S(1)} %pad_maximum_fusion.6), channel_id=1, source_target_pairs={{0,4},{1,5},{2,6},{3,7},{4,0},{5,1},{6,2},{7,3},{8,12},{9,13},{10,... | collective-permute-start | bytes 393224 | tf_op jit(solution)/shard_map/sketch_gather/ppermute | solution.py:99
  149.3 6.4 %collective-permute-start.14 = (f32[2,2,32,512]{3,2,0,1:T(8,128)S(1)}, f32[2,2,32,512]{3,2,0,1:T(8,128)S(1)}, u32[]{:S(2)}, u32[]{:S(2)}) collective-permute-start(f32[2,2,32,512]{3,2,0,1:T(8,128)S(1)} %pad_maximum_fusion.5), channel_id=1, source_target_pairs={{0,4},{1,5},{2,6},{3,7},{4,0},{5,1},{6,2},{7,3},{8,12},{9,13},{10,... | collective-permute-start | bytes 786440 | tf_op jit(solution)/shard_map/sketch_gather/ppermute | solution.py:99
  152.8 6.4 %collective-permute-start.6 = (f32[2,2,32,512]{3,2,1,0:T(8,128)S(1)}, f32[2,2,32,512]{3,2,1,0:T(8,128)S(1)}, u32[]{:S(2)}, u32[]{:S(2)}) collective-permute-start(f32[2,2,32,512]{3,2,1,0:T(8,128)S(1)} %pad_maximum_fusion.4), channel_id=1, source_target_pairs={{0,2},{1,3},{2,0},{3,1},{4,6},{5,7},{6,4},{7,5},{8,10},{9,11},{10,... | collective-permute-start | bytes 786440 | tf_op jit(solution)/shard_map/sketch_gather/ppermute | solution.py:99
  155.8 5.8 %collective-permute-start.15 = (f32[2,2,2,32,512]{4,3,0,2,1:T(8,128)S(1)}, f32[2,2,2,32,512]{4,3,0,2,1:T(8,128)S(1)}, u32[]{:S(2)}, u32[]{:S(2)}) collective-permute-start(f32[2,2,2,32,512]{4,3,0,2,1:T(8,128)S(1)} %pad_maximum_fusion.3), channel_id=1, source_target_pairs={{0,1},{1,0},{2,3},{3,2},{4,5},{5,4},{6,7},{7,6},{8,9},{9,8},{10,11... | collective-permute-start | bytes 1572872 | tf_op jit(solution)/shard_map/sketch_gather/ppermute | solution.py:99
  160.2 2.1 %collective-permute-start.7 = (f32[2,2,2,32,512]{4,3,2,1,0:T(8,128)}, f32[2,2,2,32,512]{4,3,2,1,0:T(8,128)S(1)}, u32[]{:S(2)}, u32[]{:S(2)}) collective-permute-start(f32[2,2,2,32,512]{4,3,2,1,0:T(8,128)} %pad_maximum_fusion.2), channel_id=1, source_target_pairs={{0,1},{1,0},{2,3},{3,2},{4,5},{5,4},{6,7},{7,6},{8,9},{9,8},{10,11... | collective-permute-start | bytes 1572872 | tf_op jit(solution)/shard_map/sketch_gather/ppermute | solution.py:99

commit v8 on v7

--- a/solution.py
+++ b/solution.py
@@ -129,9 +129,10 @@
 
 def bit_orders(bits):
     first = list(range(bits))
-    if bits < 3:
+    if bits < 4:
         return [first]
-    return [first, [0, 2, 1] + list(range(3, bits))]
+    rest = list(range(4, bits))
+    return [[0, 1, 2, 3] + rest, [0, 2, 1, 3] + rest, [0, 1, 3, 2] + rest, [0, 2, 3, 1] + rest]
 
 
 def on_device(grads, proj, target_ids, target_counts):

time: 210 us -> 206 us (0.981)
  waiting for transfers between devices: 104 us -> 84.7 us
  starting transfers between devices: 38.2 us -> 54.9 us
    ppermute x16 -> x32, waiting for transfers between devices: 26.3 us -> 8.92 us  [partner(): lax.ppermute(array, axis, [(i, i ^ 1 << bit) for i in range(lax.axis_size...]
    ppermute x16 -> x32, starting transfers between devices: 30.8 us -> 47.4 us  [partner(): lax.ppermute(array, axis, [(i, i ^ 1 << bit) for i in range(lax.axis_size...]
  transfers between devices with their start and end apart: 17 -> 33, of which waited for: 12 -> 12; matrix products, arithmetic and copies ran while one was open for 3% -> 2% of each run, Pallas kernels for 0% -> 0%
where the time goes in v8:
time: 206 us; the launch traced here: 205 us
  waiting for transfers between devices  84.7 us (41%)
  starting transfers between devices  54.9 us (27%)
  Pallas kernels  40.1 us (19%)
  matrix products  14.8 us (7%)
  local copies, waits for them, and re-layouts  6.19 us (3%)
  other arithmetic  3.24 us (2%)
    all_to_all x1, waiting for transfers between devices, on_device(): lax.all_to_all(grads, 'ex', split_axis=1, concat_axis=0, tiled=True)  75.8 us
    ppermute x32, starting transfers between devices, partner(): lax.ppermute(array, axis, [(i, i ^ 1 << bit) for i in range(lax.axis_size...  47.4 us
    pallas_call x1, Pallas kernels, spd_solve(): pl.pallas_call(functools.partial(_solve_kernel, block=block), out_shape=j...  40.1 us
    ppermute x32, waiting for transfers between devices, partner(): lax.ppermute(array, axis, [(i, i ^ 1 << bit) for i in range(lax.axis_size...  8.92 us
    dot_general x1, matrix products, on_device(): partial_value = jnp.dot(columns, proj, preferred_element_type=jnp.float32)  8.14 us
    all_to_all x1, starting transfers between devices, on_device(): lax.all_to_all(grads, 'ex', split_axis=1, concat_axis=0, tiled=True)  7.57 us
    all_to_all x1, local copies, waits for them, and re-layouts, on_device(): lax.all_to_all(grads, 'ex', split_axis=1, concat_axis=0, tiled=True)  4.71 us
    dot_general x1, matrix products, on_device(): kernel = jnp.dot(sketch_all, sketch_all.T, precision=lax.Precision.HIGHEST)  4.53 us
  transfers between devices with their start and end apart: 33, of which 12 were waited for; matrix products, arithmetic and copies ran while one was open for 2% of the time, Pallas kernels for 0%

profile of v8, /device:TPU:0, one launch (start us, length us, event | category | flops | bytes accessed | tf_op | source)
XLA Modules:
  0.0 205.2 jit_solution(2692794984993010038)
XLA Ops:
  0.6 4.7 %copy.115 = bf16[4,16,8,4096]{3,2,0,1:T(8,128)(2,1)} copy(bf16[4,16,8,4096]{3,2,1,0:T(8,128)(2,1)} %bitcast.162) | data formatting | bytes 8388608 | tf_op jit(solution)/shard_map/gradient_exchange/all_to_all | solution.py:146
  5.3 7.6 %all-to-all-start = ((bf16[32,16,4096]{2,0,1:T(8,128)(2,1)}), bf16[32,16,4096]{2,0,1:T(8,128)(2,1)}, u32[]{:S(2)}, u32[]{:S(2)}) async-start(bf16[32,16,4096]{2,0,1:T(8,128)(2,1)} %bitcast.161), calls=%async_computation | async-start | bytes 8388608 | tf_op jit(solution)/shard_map/gradient_exchange/all_to_all | solution.py:146
  13.0 1.6 convert_reduce_fusion
  14.8 75.8 %all-to-all-done = bf16[32,16,4096]{2,0,1:T(8,128)(2,1)} async-done(((bf16[32,16,4096]{2,0,1:T(8,128)(2,1)}), bf16[32,16,4096]{2,0,1:T(8,128)(2,1)}, u32[]{:S(2)}, u32[]{:S(2)}) %all-to-all-start) | async-done | bytes 4194336 | tf_op jit(solution)/shard_map/gradient_exchange/all_to_all | solution.py:146
  90.6 8.1 %fusion.15 = f32[512,1024]{1,0:T(8,128)S(1)} fusion(bf16[512,4096]{1,0:T(8,128)(2,1)} %bitcast.1, bf16[4096,1024]{1,0:T(8,128)(2,1)} %param.5), kind=kOutput, calls=%fused_computation.107 | convolution fusion | flops 4294967296 | bytes 14680064 | tf_op jit(solution)/shard_map/partial_projection/dot_general | solution.py:148
  99.0 0.8 collective-permute-start.24
  99.8 0.7 pad.4.w_ref
  101.6 14.7 %collective-permute-start.25 = (f32[2,2,32,256]{3,2,1,0:T(8,128)S(1)}, f32[2,2,32,256]{3,2,1,0:T(8,128)S(1)}, u32[]{:S(2)}, u32[]{:S(2)}) collective-permute-start(f32[2,2,32,256]{3,2,1,0:T(8,128)S(1)} %dynamic-slice_bitcast_fusion.2), channel_id=1, source_target_pairs={{0,4},{1,5},{2,6},{3,7},{4,0},{5,1},{6,2},{7,3},{8,12},{9,13},{10,... | collective-permute-start | bytes 393224 | tf_op jit(solution)/shard_map/sketch_reduce/ppermute | solution.py:99
  116.4 3.0 %collective-permute-start.17 = (f32[2,2,32,256]{3,2,1,0:T(8,128)S(1)}, f32[2,2,32,256]{3,2,1,0:T(8,128)S(1)}, u32[]{:S(2)}, u32[]{:S(2)}) collective-permute-start(f32[2,2,32,256]{3,2,1,0:T(8,128)S(1)} %dynamic-slice_bitcast_fusion.3), channel_id=1, source_target_pairs={{0,2},{1,3},{2,0},{3,1},{4,6},{5,7},{6,4},{7,5},{8,10},{9,11},{10,... | collective-permute-start | bytes 393224 | tf_op jit(solution)/shard_map/sketch_reduce/ppermute | solution.py:99
  120.4 5.1 %collective-permute-start.26 = (f32[2,32,256]{2,1,0:T(8,128)S(1)}, f32[2,32,256]{2,1,0:T(8,128)S(1)}, u32[]{:S(2)}, u32[]{:S(2)}) collective-permute-start(f32[2,32,256]{2,1,0:T(8,128)S(1)} %dynamic-slice_bitcast_fusion.6), channel_id=1, source_target_pairs={{0,8},{1,9},{2,10},{3,11},{4,12},{5,13},{6,14},{7,15},{8,0},{9,1},... | collective-permute-start | bytes 196616 | tf_op jit(solution)/shard_map/sketch_reduce/ppermute | solution.py:99
  125.9 1.3 collective-permute-start.10
  127.3 1.7 collective-permute-start.2
  128.9 1.6 collective-permute-done.26
  131.7 3.0 %collective-permute-start.11 = (f32[32,256]{1,0:T(8,128)S(1)}, f32[32,256]{1,0:T(8,128)S(1)}, u32[]{:S(2)}, u32[]{:S(2)}) collective-permute-start(f32[32,256]{1,0:T(8,128)S(1)} %dynamic-slice_bitcast_fusion.12), channel_id=1, source_target_pairs={{0,8},{1,9},{2,10},{3,11},{4,12},{5,13},{6,14},{7,15},{8,0},{9,1},... | collective-permute-start | bytes 98312 | tf_op jit(solution)/shard_map/sketch_reduce/ppermute | solution.py:99
  134.8 1.2 collective-permute-start.28
  136.1 2.1 %collective-permute-start.20 = (f32[32,256]{1,0:T(8,128)S(1)}, f32[32,256]{1,0:T(8,128)S(1)}, u32[]{:S(2)}, u32[]{:S(2)}) collective-permute-start(f32[32,256]{1,0:T(8,128)S(1)} %bitcast_add_fusion.13), channel_id=1, source_target_pairs={{0,4},{1,5},{2,6},{3,7},{4,0},{5,1},{6,2},{7,3},{8,12},{9,13},{10,... | collective-permute-start | bytes 98312 | tf_op jit(solution)/shard_map/sketch_gather/ppermute | solution.py:99
  138.1 1.8 collective-permute-start.12
  140.2 1.0 collective-permute-start.4
  141.2 0.7 pad_maximum_fusion.12
  141.9 2.0 collective-permute-start.29
  143.9 1.0 collective-permute-start.21
  145.0 0.9 collective-permute-start.13
  147.2 1.4 collective-permute-start.30
  148.6 1.1 collective-permute-done.21
  150.0 1.7 collective-permute-start.14
  152.2 0.9 collective-permute-done.30
  153.2 1.6 collective-permute-done.22
  155.6 1.2 collective-permute-done.6
  157.3 1.1 collective-permute-done.7
  158.5 4.5 %select_add_fusion = (f32[512,512]{1,0:T(8,128)}, f32[512,512]{1,0:T(8,128)S(1)}) fusion(f32[512,256]{1,0:T(8,128)S(1)} %bitcast.169, f32[512,256]{1,0:T(8,128)S(1)} %bitcast.170, f32[512,256]{1,0:T(8,128)S(1)} %bitcast.171, f32[512,256]{1,0:T(8,128)S(1)} %bitcast.172), kind=kOutput, calls=%fused_computation.12 | convolution fusion | flops 3223846912 | bytes 4194304 | tf_op jit(solution)/shard_map/kernel_matrix/dot_general | solution.py:175
  163.0 40.1 %kernel_solve.1 = f32[512,128]{1,0:T(8,128)} custom-call(f32[512,512]{1,0:T(8,128)} %get-tuple-element.42.m_ref, f32[512,128]{1,0:T(8,128)} %pad.4.w_ref), custom_call_target="tpu_custom_call" | custom-call | tf_op jit(solution)/shard_map/kernel_solve/pallas_call | solution.py:90
  203.1 2.1 %fusion.9 = f32[32,24]{0,1:T(8,128)} fusion(f32[512,128]{1,0:T(8,128)} %kernel_solve.1, f32[512,512]{1,0:T(8,128)S(1)} %get-tuple-element.43, s32[]{:T(128)S(6)} %select_n.381), kind=kOutput, calls=%fused_computation.18 | convolution fusion | flops 4718592 | bytes 330756 | tf_op jit(solution)/shard_map/dot_general | solution.py:182
  (119 shorter events, 7.8 us)
Async XLA Ops:
  5.3 85.3 %all-to-all-start = ((bf16[32,16,4096]{2,0,1:T(8,128)(2,1)}), bf16[32,16,4096]{2,0,1:T(8,128)(2,1)}, u32[]{:S(2)}, u32[]{:S(2)}) async-start(bf16[32,16,4096]{2,0,1:T(8,128)(2,1)} %bitcast.161), calls=%async_computation | async-start | bytes 8388608 | tf_op jit(solution)/shard_map/gradient_exchange/all_to_all | solution.py:146
  99.0 2.6 %collective-permute-start.24 = (f32[2,2,2,32,256]{4,3,2,1,0:T(8,128)S(1)}, f32[2,2,2,32,256]{4,3,2,1,0:T(8,128)S(1)}, u32[]{:S(2)}, u32[]{:S(2)}) collective-permute-start(f32[2,2,2,32,256]{4,3,2,1,0:T(8,128)S(1)} %dynamic-slice_bitcast_fusion), channel_id=1, source_target_pairs={{0,1},{1,0},{2,3},{3,2},{4,5},{5,4},{6,7},{7,6},{8,9},{9,8},{10,11... | collective-permute-start | bytes 786440 | tf_op jit(solution)/shard_map/sketch_reduce/ppermute | solution.py:99
  100.6 15.7 %collective-permute-start.16 = (f32[2,2,2,32,256]{4,3,2,1,0:T(8,128)S(1)}, f32[2,2,2,32,256]{4,3,2,1,0:T(8,128)S(1)}, u32[]{:S(2)}, u32[]{:S(2)}) collective-permute-start(f32[2,2,2,32,256]{4,3,2,1,0:T(8,128)S(1)} %dynamic-slice_bitcast_fusion.1), channel_id=1, source_target_pairs={{0,1},{1,0},{2,3},{3,2},{4,5},{5,4},{6,7},{7,6},{8,9},{9,8},{10,11... | collective-permute-start | bytes 786440 | tf_op jit(solution)/shard_map/sketch_reduce/ppermute | solution.py:99
  100.9 18.5 %collective-permute-start.8 = (f32[2,2,2,32,256]{4,3,2,0,1:T(8,128)S(1)}, f32[2,2,2,32,256]{4,3,2,0,1:T(8,128)S(1)}, u32[]{:S(2)}, u32[]{:S(2)}) collective-permute-start(f32[2,2,2,32,256]{4,3,2,0,1:T(8,128)S(1)} %bitcast.174), channel_id=1, source_target_pairs={{0,1},{1,0},{2,3},{3,2},{4,5},{5,4},{6,7},{7,6},{8,9},{9,8},{10,11... | collective-permute-start | bytes 786440 | tf_op jit(solution)/shard_map/sketch_reduce/ppermute | solution.py:99
  101.3 18.6 %collective-permute-start = (f32[2,2,2,32,256]{4,3,1,0,2:T(8,128)S(1)}, f32[2,2,2,32,256]{4,3,1,0,2:T(8,128)S(1)}, u32[]{:S(2)}, u32[]{:S(2)}) collective-permute-start(f32[2,2,2,32,256]{4,3,1,0,2:T(8,128)S(1)} %bitcast.173), channel_id=1, source_target_pairs={{0,1},{1,0},{2,3},{3,2},{4,5},{5,4},{6,7},{7,6},{8,9},{9,8},{10,11... | collective-permute-start | bytes 786440 | tf_op jit(solution)/shard_map/sketch_reduce/ppermute | solution.py:99
  101.6 18.7 %collective-permute-start.25 = (f32[2,2,32,256]{3,2,1,0:T(8,128)S(1)}, f32[2,2,32,256]{3,2,1,0:T(8,128)S(1)}, u32[]{:S(2)}, u32[]{:S(2)}) collective-permute-start(f32[2,2,32,256]{3,2,1,0:T(8,128)S(1)} %dynamic-slice_bitcast_fusion.2), channel_id=1, source_target_pairs={{0,4},{1,5},{2,6},{3,7},{4,0},{5,1},{6,2},{7,3},{8,12},{9,13},{10,... | collective-permute-start | bytes 393224 | tf_op jit(solution)/shard_map/sketch_reduce/ppermute | solution.py:99
  116.4 9.2 %collective-permute-start.17 = (f32[2,2,32,256]{3,2,1,0:T(8,128)S(1)}, f32[2,2,32,256]{3,2,1,0:T(8,128)S(1)}, u32[]{:S(2)}, u32[]{:S(2)}) collective-permute-start(f32[2,2,32,256]{3,2,1,0:T(8,128)S(1)} %dynamic-slice_bitcast_fusion.3), channel_id=1, source_target_pairs={{0,2},{1,3},{2,0},{3,1},{4,6},{5,7},{6,4},{7,5},{8,10},{9,11},{10,... | collective-permute-start | bytes 393224 | tf_op jit(solution)/shard_map/sketch_reduce/ppermute | solution.py:99
  119.5 6.4 %collective-permute-start.9 = (f32[2,2,32,256]{3,2,1,0:T(8,128)S(1)}, f32[2,2,32,256]{3,2,1,0:T(8,128)S(1)}, u32[]{:S(2)}, u32[]{:S(2)}) collective-permute-start(f32[2,2,32,256]{3,2,1,0:T(8,128)S(1)} %dynamic-slice_bitcast_fusion.4), channel_id=1, source_target_pairs={{0,4},{1,5},{2,6},{3,7},{4,0},{5,1},{6,2},{7,3},{8,12},{9,13},{10,... | collective-permute-start | bytes 393224 | tf_op jit(solution)/shard_map/sketch_reduce/ppermute | solution.py:99
  120.0 7.2 %collective-permute-start.1 = (f32[2,2,32,256]{3,2,1,0:T(8,128)S(1)}, f32[2,2,32,256]{3,2,1,0:T(8,128)S(1)}, u32[]{:S(2)}, u32[]{:S(2)}) collective-permute-start(f32[2,2,32,256]{3,2,1,0:T(8,128)S(1)} %dynamic-slice_bitcast_fusion.5), channel_id=1, source_target_pairs={{0,2},{1,3},{2,0},{3,1},{4,6},{5,7},{6,4},{7,5},{8,10},{9,11},{10,... | collective-permute-start | bytes 393224 | tf_op jit(solution)/shard_map/sketch_reduce/ppermute | solution.py:99
  120.4 10.2 %collective-permute-start.26 = (f32[2,32,256]{2,1,0:T(8,128)S(1)}, f32[2,32,256]{2,1,0:T(8,128)S(1)}, u32[]{:S(2)}, u32[]{:S(2)}) collective-permute-start(f32[2,32,256]{2,1,0:T(8,128)S(1)} %dynamic-slice_bitcast_fusion.6), channel_id=1, source_target_pairs={{0,8},{1,9},{2,10},{3,11},{4,12},{5,13},{6,14},{7,15},{8,0},{9,1},... | collective-permute-start | bytes 196616 | tf_op jit(solution)/shard_map/sketch_reduce/ppermute | solution.py:99
  125.6 6.0 %collective-permute-start.18 = (f32[2,32,256]{2,1,0:T(8,128)S(1)}, f32[2,32,256]{2,1,0:T(8,128)S(1)}, u32[]{:S(2)}, u32[]{:S(2)}) collective-permute-start(f32[2,32,256]{2,1,0:T(8,128)S(1)} %dynamic-slice_bitcast_fusion.7), channel_id=1, source_target_pairs={{0,8},{1,9},{2,10},{3,11},{4,12},{5,13},{6,14},{7,15},{8,0},{9,1},... | collective-permute-start | bytes 196616 | tf_op jit(solution)/shard_map/sketch_reduce/ppermute | solution.py:99
  125.9 5.7 %collective-permute-start.10 = (f32[2,32,256]{2,1,0:T(8,128)S(1)}, f32[2,32,256]{2,1,0:T(8,128)S(1)}, u32[]{:S(2)}, u32[]{:S(2)}) collective-permute-start(f32[2,32,256]{2,1,0:T(8,128)S(1)} %dynamic-slice_bitcast_fusion.8), channel_id=1, source_target_pairs={{0,2},{1,3},{2,0},{3,1},{4,6},{5,7},{6,4},{7,5},{8,10},{9,11},{10,... | collective-permute-start | bytes 196616 | tf_op jit(solution)/shard_map/sketch_reduce/ppermute | solution.py:99
  127.3 7.4 %collective-permute-start.2 = (f32[2,32,256]{2,1,0:T(8,128)S(1)}, f32[2,32,256]{2,1,0:T(8,128)S(1)}, u32[]{:S(2)}, u32[]{:S(2)}) collective-permute-start(f32[2,32,256]{2,1,0:T(8,128)S(1)} %dynamic-slice_bitcast_fusion.9), channel_id=1, source_target_pairs={{0,4},{1,5},{2,6},{3,7},{4,0},{5,1},{6,2},{7,3},{8,12},{9,13},{10,... | collective-permute-start | bytes 196616 | tf_op jit(solution)/shard_map/sketch_reduce/ppermute | solution.py:99
  130.6 4.2 %collective-permute-start.27 = (f32[32,256]{1,0:T(8,128)S(1)}, f32[32,256]{1,0:T(8,128)S(1)}, u32[]{:S(2)}, u32[]{:S(2)}) collective-permute-start(f32[32,256]{1,0:T(8,128)S(1)} %dynamic-slice_bitcast_fusion.10), channel_id=1, source_target_pairs={{0,2},{1,3},{2,0},{3,1},{4,6},{5,7},{6,4},{7,5},{8,10},{9,11},{10,... | collective-permute-start | bytes 98312 | tf_op jit(solution)/shard_map/sketch_reduce/ppermute | solution.py:99
  131.6 4.5 %collective-permute-start.19 = (f32[32,256]{1,0:T(8,128)S(1)}, f32[32,256]{1,0:T(8,128)S(1)}, u32[]{:S(2)}, u32[]{:S(2)}) collective-permute-start(f32[32,256]{1,0:T(8,128)S(1)} %dynamic-slice_bitcast_fusion.11), channel_id=1, source_target_pairs={{0,4},{1,5},{2,6},{3,7},{4,0},{5,1},{6,2},{7,3},{8,12},{9,13},{10,... | collective-permute-start | bytes 98312 | tf_op jit(solution)/shard_map/sketch_reduce/ppermute | solution.py:99
  131.7 6.4 %collective-permute-start.11 = (f32[32,256]{1,0:T(8,128)S(1)}, f32[32,256]{1,0:T(8,128)S(1)}, u32[]{:S(2)}, u32[]{:S(2)}) collective-permute-start(f32[32,256]{1,0:T(8,128)S(1)} %dynamic-slice_bitcast_fusion.12), channel_id=1, source_target_pairs={{0,8},{1,9},{2,10},{3,11},{4,12},{5,13},{6,14},{7,15},{8,0},{9,1},... | collective-permute-start | bytes 98312 | tf_op jit(solution)/shard_map/sketch_reduce/ppermute | solution.py:99
  134.7 5.5 %collective-permute-start.3 = (f32[32,256]{1,0:T(8,128)S(1)}, f32[32,256]{1,0:T(8,128)S(1)}, u32[]{:S(2)}, u32[]{:S(2)}) collective-permute-start(f32[32,256]{1,0:T(8,128)S(1)} %dynamic-slice_bitcast_fusion.13), channel_id=1, source_target_pairs={{0,8},{1,9},{2,10},{3,11},{4,12},{5,13},{6,14},{7,15},{8,0},{9,1},... | collective-permute-start | bytes 98312 | tf_op jit(solution)/shard_map/sketch_reduce/ppermute | solution.py:99
  134.8 7.0 %collective-permute-start.28 = (f32[32,256]{1,0:T(8,128)S(1)}, f32[32,256]{1,0:T(8,128)S(1)}, u32[]{:S(2)}, u32[]{:S(2)}) collective-permute-start(f32[32,256]{1,0:T(8,128)S(1)} %bitcast_add_fusion.12), channel_id=1, source_target_pairs={{0,2},{1,3},{2,0},{3,1},{4,6},{5,7},{6,4},{7,5},{8,10},{9,11},{10,... | collective-permute-start | bytes 98312 | tf_op jit(solution)/shard_map/sketch_gather/ppermute | solution.py:99
  136.1 7.9 %collective-permute-start.20 = (f32[32,256]{1,0:T(8,128)S(1)}, f32[32,256]{1,0:T(8,128)S(1)}, u32[]{:S(2)}, u32[]{:S(2)}) collective-permute-start(f32[32,256]{1,0:T(8,128)S(1)} %bitcast_add_fusion.13), channel_id=1, source_target_pairs={{0,4},{1,5},{2,6},{3,7},{4,0},{5,1},{6,2},{7,3},{8,12},{9,13},{10,... | collective-permute-start | bytes 98312 | tf_op jit(solution)/shard_map/sketch_gather/ppermute | solution.py:99
  138.1 6.8 %collective-permute-start.12 = (f32[32,256]{1,0:T(8,128)S(1)}, f32[32,256]{1,0:T(8,128)S(1)}, u32[]{:S(2)}, u32[]{:S(2)}) collective-permute-start(f32[32,256]{1,0:T(8,128)S(1)} %bitcast_add_fusion.14), channel_id=1, source_target_pairs={{0,8},{1,9},{2,10},{3,11},{4,12},{5,13},{6,14},{7,15},{8,0},{9,1},... | collective-permute-start | bytes 98312 | tf_op jit(solution)/shard_map/sketch_gather/ppermute | solution.py:99
  140.2 6.1 %collective-permute-start.4 = (f32[32,256]{1,0:T(8,128)S(1)}, f32[32,256]{1,0:T(8,128)S(1)}, u32[]{:S(2)}, u32[]{:S(2)}) collective-permute-start(f32[32,256]{1,0:T(8,128)S(1)} %bitcast_add_fusion.15), channel_id=1, source_target_pairs={{0,8},{1,9},{2,10},{3,11},{4,12},{5,13},{6,14},{7,15},{8,0},{9,1},... | collective-permute-start | bytes 98312 | tf_op jit(solution)/shard_map/sketch_gather/ppermute | solution.py:99
  141.9 5.3 %collective-permute-start.29 = (f32[2,32,256]{2,1,0:T(8,128)S(1)}, f32[2,32,256]{2,1,0:T(8,128)S(1)}, u32[]{:S(2)}, u32[]{:S(2)}) collective-permute-start(f32[2,32,256]{2,1,0:T(8,128)S(1)} %pad_maximum_fusion.16), channel_id=1, source_target_pairs={{0,8},{1,9},{2,10},{3,11},{4,12},{5,13},{6,14},{7,15},{8,0},{9,1},... | collective-permute-start | bytes 196616 | tf_op jit(solution)/shard_map/sketch_gather/ppermute | solution.py:99
  143.9 5.8 %collective-permute-start.21 = (f32[2,32,256]{2,1,0:T(8,128)S(1)}, f32[2,32,256]{2,1,0:T(8,128)S(1)}, u32[]{:S(2)}, u32[]{:S(2)}) collective-permute-start(f32[2,32,256]{2,1,0:T(8,128)S(1)} %pad_maximum_fusion.15), channel_id=1, source_target_pairs={{0,8},{1,9},{2,10},{3,11},{4,12},{5,13},{6,14},{7,15},{8,0},{9,1},... | collective-permute-start | bytes 196616 | tf_op jit(solution)/shard_map/sketch_gather/ppermute | solution.py:99
  145.0 4.9 %collective-permute-start.13 = (f32[2,32,256]{2,1,0:T(8,128)S(1)}, f32[2,32,256]{2,1,0:T(8,128)S(1)}, u32[]{:S(2)}, u32[]{:S(2)}) collective-permute-start(f32[2,32,256]{2,1,0:T(8,128)S(1)} %pad_maximum_fusion.14), channel_id=1, source_target_pairs={{0,2},{1,3},{2,0},{3,1},{4,6},{5,7},{6,4},{7,5},{8,10},{9,11},{10,... | collective-permute-start | bytes 196616 | tf_op jit(solution)/shard_map/sketch_gather/ppermute | solution.py:99
  146.3 5.4 %collective-permute-start.5 = (f32[2,32,256]{2,1,0:T(8,128)S(1)}, f32[2,32,256]{2,1,0:T(8,128)S(1)}, u32[]{:S(2)}, u32[]{:S(2)}) collective-permute-start(f32[2,32,256]{2,1,0:T(8,128)S(1)} %pad_maximum_fusion.13), channel_id=1, source_target_pairs={{0,4},{1,5},{2,6},{3,7},{4,0},{5,1},{6,2},{7,3},{8,12},{9,13},{10,... | collective-permute-start | bytes 196616 | tf_op jit(solution)/shard_map/sketch_gather/ppermute | solution.py:99
  147.2 5.9 %collective-permute-start.30 = (f32[2,2,32,256]{3,2,1,0:T(8,128)S(1)}, f32[2,2,32,256]{3,2,1,0:T(8,128)S(1)}, u32[]{:S(2)}, u32[]{:S(2)}) collective-permute-start(f32[2,2,32,256]{3,2,1,0:T(8,128)S(1)} %pad_maximum_fusion.11), channel_id=1, source_target_pairs={{0,4},{1,5},{2,6},{3,7},{4,0},{5,1},{6,2},{7,3},{8,12},{9,13},{10,... | collective-permute-start | bytes 393224 | tf_op jit(solution)/shard_map/sketch_gather/ppermute | solution.py:99
  149.8 5.0 %collective-permute-start.22 = (f32[2,2,32,256]{3,2,0,1:T(8,128)S(1)}, f32[2,2,32,256]{3,2,0,1:T(8,128)S(1)}, u32[]{:S(2)}, u32[]{:S(2)}) collective-permute-start(f32[2,2,32,256]{3,2,0,1:T(8,128)S(1)} %pad_maximum_fusion.10), channel_id=1, source_target_pairs={{0,2},{1,3},{2,0},{3,1},{4,6},{5,7},{6,4},{7,5},{8,10},{9,11},{10,... | collective-permute-start | bytes 393224 | tf_op jit(solution)/shard_map/sketch_gather/ppermute | solution.py:99
  150.0 5.1 %collective-permute-start.14 = (f32[2,2,32,256]{3,2,1,0:T(8,128)S(1)}, f32[2,2,32,256]{3,2,1,0:T(8,128)S(1)}, u32[]{:S(2)}, u32[]{:S(2)}) collective-permute-start(f32[2,2,32,256]{3,2,1,0:T(8,128)S(1)} %pad_maximum_fusion.9), channel_id=1, source_target_pairs={{0,4},{1,5},{2,6},{3,7},{4,0},{5,1},{6,2},{7,3},{8,12},{9,13},{10,... | collective-permute-start | bytes 393224 | tf_op jit(solution)/shard_map/sketch_gather/ppermute | solution.py:99
  151.7 5.0 %collective-permute-start.6 = (f32[2,2,32,256]{3,2,1,0:T(8,128)S(1)}, f32[2,2,32,256]{3,2,1,0:T(8,128)S(1)}, u32[]{:S(2)}, u32[]{:S(2)}) collective-permute-start(f32[2,2,32,256]{3,2,1,0:T(8,128)S(1)} %pad_maximum_fusion.8), channel_id=1, source_target_pairs={{0,2},{1,3},{2,0},{3,1},{4,6},{5,7},{6,4},{7,5},{8,10},{9,11},{10,... | collective-permute-start | bytes 393224 | tf_op jit(solution)/shard_map/sketch_gather/ppermute | solution.py:99
  153.2 3.7 %collective-permute-start.31 = (f32[2,2,2,32,256]{4,3,2,0,1:T(8,128)S(1)}, f32[2,2,2,32,256]{4,3,2,0,1:T(8,128)S(1)}, u32[]{:S(2)}, u32[]{:S(2)}) collective-permute-start(f32[2,2,2,32,256]{4,3,2,0,1:T(8,128)S(1)} %pad_maximum_fusion.7), channel_id=1, source_target_pairs={{0,1},{1,0},{2,3},{3,2},{4,5},{5,4},{6,7},{7,6},{8,9},{9,8},{10,11... | collective-permute-start | bytes 786440 | tf_op jit(solution)/shard_map/sketch_gather/ppermute | solution.py:99
  154.9 2.1 %collective-permute-start.23 = (f32[2,2,2,32,256]{4,3,2,0,1:T(8,128)S(1)}, f32[2,2,2,32,256]{4,3,2,0,1:T(8,128)S(1)}, u32[]{:S(2)}, u32[]{:S(2)}) collective-permute-start(f32[2,2,2,32,256]{4,3,2,0,1:T(8,128)S(1)} %pad_maximum_fusion.6), channel_id=1, source_target_pairs={{0,1},{1,0},{2,3},{3,2},{4,5},{5,4},{6,7},{7,6},{8,9},{9,8},{10,11... | collective-permute-start | bytes 786440 | tf_op jit(solution)/shard_map/sketch_gather/ppermute | solution.py:99
  155.1 2.1 %collective-permute-start.15 = (f32[2,2,2,32,256]{4,3,2,0,1:T(8,128)S(1)}, f32[2,2,2,32,256]{4,3,2,0,1:T(8,128)S(1)}, u32[]{:S(2)}, u32[]{:S(2)}) collective-permute-start(f32[2,2,2,32,256]{4,3,2,0,1:T(8,128)S(1)} %pad_maximum_fusion.5), channel_id=1, source_target_pairs={{0,1},{1,0},{2,3},{3,2},{4,5},{5,4},{6,7},{7,6},{8,9},{9,8},{10,11... | collective-permute-start | bytes 786440 | tf_op jit(solution)/shard_map/sketch_gather/ppermute | solution.py:99
  (3 other events, 16.9 us)

commit v9 on v8

--- a/solution.py
+++ b/solution.py
@@ -99,24 +99,23 @@
     return lax.ppermute(array, axis, [(i, i ^ 1 << bit) for i in range(lax.axis_size(axis))])
 
 
-def reduce_scatter(partial_value, order, position):
+def reduce_and_gather(partial_value, order, position):
     bits = len(order)
-    value = partial_value.reshape((2,) * bits + partial_value.shape[1:])
+    rows = partial_value.shape[1:]
+    value = partial_value.reshape((2,) * bits + rows)
     remaining = list(range(bits - 1, -1, -1))
-    for level in order:
+    for level in order[:-1]:
         axis = remaining.index(level)
         own_bit = position // 2**level % 2
         kept = lax.dynamic_index_in_dim(value, own_bit, axis=axis, keepdims=False)
         sent = lax.dynamic_index_in_dim(value, 1 - own_bit, axis=axis, keepdims=False)
         value = kept + partner(sent, "ex", level)
         remaining.remove(level)
-    return value
-
-
-def all_gather(block, order, position):
-    value = block
-    present = []
-    for level in reversed(order):
+    last = order[-1]
+    value = value + partner(value, "ex", last)
+    own = lax.dynamic_index_in_dim(value, position // 2**last % 2, axis=0, keepdims=False)
+    present = [last]
+    for level in reversed(order[:-1]):
         received = partner(value, "ex", level)
         high_side = position // 2**level % 2 == 1
         low = jnp.where(high_side, received, value)
@@ -124,7 +123,7 @@
         present.append(level)
         present.sort(reverse=True)
         value = jnp.stack([low, high], axis=present.index(level))
-    return value.reshape((-1,) + block.shape[1:])
+    return own, value.reshape((-1,) + rows[1:])
 
 
 def bit_orders(bits):
@@ -150,16 +149,15 @@
     width = sketch_width // len(orders)
     owned, gathered = [], []
     for half, order in enumerate(orders):
-        with jax.named_scope("sketch_reduce"):
-            part = reduce_scatter(
+        with jax.named_scope("sketch_reduce_gather"):
+            part, every = reduce_and_gather(
                 partial_value[:, half * width:(half + 1) * width].reshape(
                     count_ex, ex_rows, width
                 ),
                 order,
                 position,
             )
-        with jax.named_scope("sketch_gather"):
-            gathered.append(all_gather(part, order, position))
+        gathered.append(every)
         owned.append(part)
     sketch = jnp.concatenate(owned, axis=1)
     sketch_all = jnp.concatenate(gathered, axis=1)

time: 206 us -> 203 us (0.985)
  starting transfers between devices: 54.9 us -> 48 us
  waiting for transfers between devices: 84.7 us -> 89.1 us
    ppermute x32 -> x28, starting transfers between devices: 47.4 us -> 40.5 us  [partner(): lax.ppermute(array, axis, [(i, i ^ 1 << bit) for i in range(lax.axis_size...]
    ppermute x32 -> x28, waiting for transfers between devices: 8.92 us -> 13.3 us  [partner(): lax.ppermute(array, axis, [(i, i ^ 1 << bit) for i in range(lax.axis_size...]
  transfers between devices with their start and end apart: 33 -> 29, of which waited for: 12 -> 14; matrix products, arithmetic and copies ran while one was open for 2% -> 2% of each run, Pallas kernels for 0% -> 0%
where the time goes in v9:
time: 203 us
  waiting for transfers between devices  89.1 us (44%)
  starting transfers between devices  48 us (24%)
  Pallas kernels  40.1 us (20%)
  matrix products  14.8 us (7%)
  local copies, waits for them, and re-layouts  6.17 us (3%)
  other arithmetic  3.2 us (2%)
    all_to_all x1, waiting for transfers between devices, on_device(): lax.all_to_all(grads, 'ex', split_axis=1, concat_axis=0, tiled=True)  75.8 us
    ppermute x28, starting transfers between devices, partner(): lax.ppermute(array, axis, [(i, i ^ 1 << bit) for i in range(lax.axis_size...  40.5 us
    pallas_call x1, Pallas kernels, spd_solve(): pl.pallas_call(functools.partial(_solve_kernel, block=block), out_shape=j...  40.1 us
    ppermute x28, waiting for transfers between devices, partner(): lax.ppermute(array, axis, [(i, i ^ 1 << bit) for i in range(lax.axis_size...  13.3 us
    dot_general x1, matrix products, on_device(): partial_value = jnp.dot(columns, proj, preferred_element_type=jnp.float32)  8.14 us
    all_to_all x1, starting transfers between devices, on_device(): lax.all_to_all(grads, 'ex', split_axis=1, concat_axis=0, tiled=True)  7.57 us
    all_to_all x1, local copies, waits for them, and re-layouts, on_device(): lax.all_to_all(grads, 'ex', split_axis=1, concat_axis=0, tiled=True)  4.71 us
    dot_general x1, matrix products, on_device(): kernel = jnp.dot(sketch_all, sketch_all.T, precision=lax.Precision.HIGHEST)  4.51 us
  transfers between devices with their start and end apart: 29, of which 14 were waited for; matrix products, arithmetic and copies ran while one was open for 2% of the time, Pallas kernels for 0%

profile of v9, /device:TPU:0, one launch (start us, length us, event | category | flops | bytes accessed | tf_op | source)
XLA Modules:
  0.0 202.6 jit_solution(6283663219980743343)
XLA Ops:
  0.6 4.7 %copy.104 = bf16[4,16,8,4096]{3,2,0,1:T(8,128)(2,1)} copy(bf16[4,16,8,4096]{3,2,1,0:T(8,128)(2,1)} %bitcast.136) | data formatting | bytes 8388608 | tf_op jit(solution)/shard_map/gradient_exchange/all_to_all | solution.py:145
  5.3 7.6 %all-to-all-start = ((bf16[32,16,4096]{2,0,1:T(8,128)(2,1)}), bf16[32,16,4096]{2,0,1:T(8,128)(2,1)}, u32[]{:S(2)}, u32[]{:S(2)}) async-start(bf16[32,16,4096]{2,0,1:T(8,128)(2,1)} %bitcast.135), calls=%async_computation | async-start | bytes 8388608 | tf_op jit(solution)/shard_map/gradient_exchange/all_to_all | solution.py:145
  13.0 1.6 convert_reduce_fusion
  14.8 75.8 %all-to-all-done = bf16[32,16,4096]{2,0,1:T(8,128)(2,1)} async-done(((bf16[32,16,4096]{2,0,1:T(8,128)(2,1)}), bf16[32,16,4096]{2,0,1:T(8,128)(2,1)}, u32[]{:S(2)}, u32[]{:S(2)}) %all-to-all-start) | async-done | bytes 4194336 | tf_op jit(solution)/shard_map/gradient_exchange/all_to_all | solution.py:145
  90.6 8.1 %fusion.15 = f32[512,1024]{1,0:T(8,128)S(1)} fusion(bf16[512,4096]{1,0:T(8,128)(2,1)} %bitcast.1, bf16[4096,1024]{1,0:T(8,128)(2,1)} %param.5), kind=kOutput, calls=%fused_computation.91 | convolution fusion | flops 4294967296 | bytes 14680064 | tf_op jit(solution)/shard_map/partial_projection/dot_general | solution.py:147
  99.0 0.8 collective-permute-start.21
  99.8 0.7 pad.4.w_ref
  101.6 14.7 %collective-permute-start.22 = (f32[2,2,32,256]{3,2,1,0:T(8,128)S(1)}, f32[2,2,32,256]{3,2,1,0:T(8,128)S(1)}, u32[]{:S(2)}, u32[]{:S(2)}) collective-permute-start(f32[2,2,32,256]{3,2,1,0:T(8,128)S(1)} %dynamic-slice_bitcast_fusion.2), channel_id=1, source_target_pairs={{0,4},{1,5},{2,6},{3,7},{4,0},{5,1},{6,2},{7,3},{8,12},{9,13},{10,... | collective-permute-start | bytes 393224 | tf_op jit(solution)/shard_map/sketch_reduce_gather/ppermute | solution.py:99
  116.4 3.0 %collective-permute-start.15 = (f32[2,2,32,256]{3,2,1,0:T(8,128)S(1)}, f32[2,2,32,256]{3,2,1,0:T(8,128)S(1)}, u32[]{:S(2)}, u32[]{:S(2)}) collective-permute-start(f32[2,2,32,256]{3,2,1,0:T(8,128)S(1)} %dynamic-slice_bitcast_fusion.3), channel_id=1, source_target_pairs={{0,2},{1,3},{2,0},{3,1},{4,6},{5,7},{6,4},{7,5},{8,10},{9,11},{10,... | collective-permute-start | bytes 393224 | tf_op jit(solution)/shard_map/sketch_reduce_gather/ppermute | solution.py:99
  119.5 0.5 collective-permute-start.8
  120.4 5.1 %collective-permute-start.23 = (f32[2,32,256]{2,1,0:T(8,128)S(1)}, f32[2,32,256]{2,1,0:T(8,128)S(1)}, u32[]{:S(2)}, u32[]{:S(2)}) collective-permute-start(f32[2,32,256]{2,1,0:T(8,128)S(1)} %dynamic-slice_bitcast_fusion.6), channel_id=1, source_target_pairs={{0,8},{1,9},{2,10},{3,11},{4,12},{5,13},{6,14},{7,15},{8,0},{9,1},... | collective-permute-start | bytes 196616 | tf_op jit(solution)/shard_map/sketch_reduce_gather/ppermute | solution.py:99
  126.0 1.3 collective-permute-start.9
  127.3 1.7 collective-permute-start.2
  129.0 1.6 collective-permute-done.23
  131.7 3.0 %collective-permute-start.10 = (f32[2,32,256]{2,1,0:T(8,128)S(1)}, f32[2,32,256]{2,1,0:T(8,128)S(1)}, u32[]{:S(2)}, u32[]{:S(2)}) collective-permute-start(f32[2,32,256]{2,1,0:T(8,128)S(1)} %bitcast_add_fusion.10), channel_id=1, source_target_pairs={{0,8},{1,9},{2,10},{3,11},{4,12},{5,13},{6,14},{7,15},{8,0},{9,1},... | collective-permute-start | bytes 196616 | tf_op jit(solution)/shard_map/sketch_reduce_gather/ppermute | solution.py:99
  135.0 2.8 %collective-permute-start.25 = (f32[2,32,256]{2,1,0:T(8,128)S(1)}, f32[2,32,256]{2,1,0:T(8,128)S(1)}, u32[]{:S(2)}, u32[]{:S(2)}) collective-permute-start(f32[2,32,256]{2,1,0:T(8,128)S(1)} %add.178), channel_id=1, source_target_pairs={{0,8},{1,9},{2,10},{3,11},{4,12},{5,13},{6,14},{7,15},{8,0},{9,1},... | collective-permute-start | bytes 196616 | tf_op jit(solution)/shard_map/sketch_reduce_gather/ppermute | solution.py:99
  138.0 5.0 %collective-permute-done.10 = f32[2,32,256]{2,1,0:T(8,128)S(1)} collective-permute-done((f32[2,32,256]{2,1,0:T(8,128)S(1)}, f32[2,32,256]{2,1,0:T(8,128)S(1)}, u32[]{:S(2)}, u32[]{:S(2)}) %collective-permute-start.10) | collective-permute-done | bytes 65568 | tf_op jit(solution)/shard_map/sketch_reduce_gather/ppermute | solution.py:99
  143.0 0.7 collective-permute-start.11
  143.7 0.7 collective-permute-done.3
  144.5 0.7 pad_maximum_fusion.12
  145.6 1.7 collective-permute-start.26
  147.3 0.8 collective-permute-start.19
  148.1 0.6 collective-permute-start.12
  149.1 1.1 collective-permute-start.5
  150.1 1.8 collective-permute-done.26
  152.1 0.5 collective-permute-done.19
  152.7 0.6 collective-permute-done.12
  153.5 0.7 collective-permute-done.5
  155.1 0.7 collective-permute-done.6
  155.9 4.5 %select_add_fusion = (f32[512,512]{1,0:T(8,128)}, f32[512,512]{1,0:T(8,128)S(1)}) fusion(f32[512,256]{1,0:T(8,128)S(1)} %bitcast.143, f32[512,256]{1,0:T(8,128)S(1)} %bitcast.144, f32[512,256]{1,0:T(8,128)S(1)} %bitcast.145, f32[512,256]{1,0:T(8,128)S(1)} %bitcast.146), kind=kOutput, calls=%fused_computation.12 | convolution fusion | flops 3223846912 | bytes 4194304 | tf_op jit(solution)/shard_map/kernel_matrix/dot_general | solution.py:173
  160.4 40.1 %kernel_solve.1 = f32[512,128]{1,0:T(8,128)} custom-call(f32[512,512]{1,0:T(8,128)} %get-tuple-element.34.m_ref, f32[512,128]{1,0:T(8,128)} %pad.4.w_ref), custom_call_target="tpu_custom_call" | custom-call | tf_op jit(solution)/shard_map/kernel_solve/pallas_call | solution.py:90
  200.5 2.1 %fusion.9 = f32[32,24]{0,1:T(8,128)} fusion(f32[512,128]{1,0:T(8,128)} %kernel_solve.1, f32[512,512]{1,0:T(8,128)S(1)} %get-tuple-element.35, s32[]{:T(128)S(6)} %select_n.314), kind=kOutput, calls=%fused_computation.18 | convolution fusion | flops 4718592 | bytes 330756 | tf_op jit(solution)/shard_map/dot_general | solution.py:180
  (103 shorter events, 6.3 us)
Async XLA Ops:
  5.3 7.6 %copy-start.1 = (s32[24]{0:T(128)S(1)}, s32[24]{0:T(128)}, u32[]{:S(2)}) copy-start(s32[24]{0:T(128)} %param.7) | copy-start | bytes 292
  5.3 7.7 %copy-start = (s32[24,128]{1,0:T(8,128)S(1)}, s32[24,128]{1,0:T(8,128)}, u32[]{:S(2)}) copy-start(s32[24,128]{1,0:T(8,128)} %param.6) | copy-start | bytes 36868
  5.3 85.3 %all-to-all-start = ((bf16[32,16,4096]{2,0,1:T(8,128)(2,1)}), bf16[32,16,4096]{2,0,1:T(8,128)(2,1)}, u32[]{:S(2)}, u32[]{:S(2)}) async-start(bf16[32,16,4096]{2,0,1:T(8,128)(2,1)} %bitcast.135), calls=%async_computation | async-start | bytes 8388608 | tf_op jit(solution)/shard_map/gradient_exchange/all_to_all | solution.py:145
  99.0 2.6 %collective-permute-start.21 = (f32[2,2,2,32,256]{4,3,2,1,0:T(8,128)S(1)}, f32[2,2,2,32,256]{4,3,2,1,0:T(8,128)S(1)}, u32[]{:S(2)}, u32[]{:S(2)}) collective-permute-start(f32[2,2,2,32,256]{4,3,2,1,0:T(8,128)S(1)} %dynamic-slice_bitcast_fusion), channel_id=1, source_target_pairs={{0,1},{1,0},{2,3},{3,2},{4,5},{5,4},{6,7},{7,6},{8,9},{9,8},{10,11... | collective-permute-start | bytes 786440 | tf_op jit(solution)/shard_map/sketch_reduce_gather/ppermute | solution.py:99
  100.6 15.7 %collective-permute-start.14 = (f32[2,2,2,32,256]{4,3,2,1,0:T(8,128)S(1)}, f32[2,2,2,32,256]{4,3,2,1,0:T(8,128)S(1)}, u32[]{:S(2)}, u32[]{:S(2)}) collective-permute-start(f32[2,2,2,32,256]{4,3,2,1,0:T(8,128)S(1)} %dynamic-slice_bitcast_fusion.1), channel_id=1, source_target_pairs={{0,1},{1,0},{2,3},{3,2},{4,5},{5,4},{6,7},{7,6},{8,9},{9,8},{10,11... | collective-permute-start | bytes 786440 | tf_op jit(solution)/shard_map/sketch_reduce_gather/ppermute | solution.py:99
  100.9 18.5 %collective-permute-start.7 = (f32[2,2,2,32,256]{4,3,2,0,1:T(8,128)S(1)}, f32[2,2,2,32,256]{4,3,2,0,1:T(8,128)S(1)}, u32[]{:S(2)}, u32[]{:S(2)}) collective-permute-start(f32[2,2,2,32,256]{4,3,2,0,1:T(8,128)S(1)} %bitcast.148), channel_id=1, source_target_pairs={{0,1},{1,0},{2,3},{3,2},{4,5},{5,4},{6,7},{7,6},{8,9},{9,8},{10,11... | collective-permute-start | bytes 786440 | tf_op jit(solution)/shard_map/sketch_reduce_gather/ppermute | solution.py:99
  101.3 18.6 %collective-permute-start = (f32[2,2,2,32,256]{4,3,1,0,2:T(8,128)S(1)}, f32[2,2,2,32,256]{4,3,1,0,2:T(8,128)S(1)}, u32[]{:S(2)}, u32[]{:S(2)}) collective-permute-start(f32[2,2,2,32,256]{4,3,1,0,2:T(8,128)S(1)} %bitcast.147), channel_id=1, source_target_pairs={{0,1},{1,0},{2,3},{3,2},{4,5},{5,4},{6,7},{7,6},{8,9},{9,8},{10,11... | collective-permute-start | bytes 786440 | tf_op jit(solution)/shard_map/sketch_reduce_gather/ppermute | solution.py:99
  101.6 18.7 %collective-permute-start.22 = (f32[2,2,32,256]{3,2,1,0:T(8,128)S(1)}, f32[2,2,32,256]{3,2,1,0:T(8,128)S(1)}, u32[]{:S(2)}, u32[]{:S(2)}) collective-permute-start(f32[2,2,32,256]{3,2,1,0:T(8,128)S(1)} %dynamic-slice_bitcast_fusion.2), channel_id=1, source_target_pairs={{0,4},{1,5},{2,6},{3,7},{4,0},{5,1},{6,2},{7,3},{8,12},{9,13},{10,... | collective-permute-start | bytes 393224 | tf_op jit(solution)/shard_map/sketch_reduce_gather/ppermute | solution.py:99
  116.4 9.2 %collective-permute-start.15 = (f32[2,2,32,256]{3,2,1,0:T(8,128)S(1)}, f32[2,2,32,256]{3,2,1,0:T(8,128)S(1)}, u32[]{:S(2)}, u32[]{:S(2)}) collective-permute-start(f32[2,2,32,256]{3,2,1,0:T(8,128)S(1)} %dynamic-slice_bitcast_fusion.3), channel_id=1, source_target_pairs={{0,2},{1,3},{2,0},{3,1},{4,6},{5,7},{6,4},{7,5},{8,10},{9,11},{10,... | collective-permute-start | bytes 393224 | tf_op jit(solution)/shard_map/sketch_reduce_gather/ppermute | solution.py:99
  119.5 6.4 %collective-permute-start.8 = (f32[2,2,32,256]{3,2,1,0:T(8,128)S(1)}, f32[2,2,32,256]{3,2,1,0:T(8,128)S(1)}, u32[]{:S(2)}, u32[]{:S(2)}) collective-permute-start(f32[2,2,32,256]{3,2,1,0:T(8,128)S(1)} %dynamic-slice_bitcast_fusion.4), channel_id=1, source_target_pairs={{0,4},{1,5},{2,6},{3,7},{4,0},{5,1},{6,2},{7,3},{8,12},{9,13},{10,... | collective-permute-start | bytes 393224 | tf_op jit(solution)/shard_map/sketch_reduce_gather/ppermute | solution.py:99
  120.0 7.2 %collective-permute-start.1 = (f32[2,2,32,256]{3,2,1,0:T(8,128)S(1)}, f32[2,2,32,256]{3,2,1,0:T(8,128)S(1)}, u32[]{:S(2)}, u32[]{:S(2)}) collective-permute-start(f32[2,2,32,256]{3,2,1,0:T(8,128)S(1)} %dynamic-slice_bitcast_fusion.5), channel_id=1, source_target_pairs={{0,2},{1,3},{2,0},{3,1},{4,6},{5,7},{6,4},{7,5},{8,10},{9,11},{10,... | collective-permute-start | bytes 393224 | tf_op jit(solution)/shard_map/sketch_reduce_gather/ppermute | solution.py:99
  120.4 10.2 %collective-permute-start.23 = (f32[2,32,256]{2,1,0:T(8,128)S(1)}, f32[2,32,256]{2,1,0:T(8,128)S(1)}, u32[]{:S(2)}, u32[]{:S(2)}) collective-permute-start(f32[2,32,256]{2,1,0:T(8,128)S(1)} %dynamic-slice_bitcast_fusion.6), channel_id=1, source_target_pairs={{0,8},{1,9},{2,10},{3,11},{4,12},{5,13},{6,14},{7,15},{8,0},{9,1},... | collective-permute-start | bytes 196616 | tf_op jit(solution)/shard_map/sketch_reduce_gather/ppermute | solution.py:99
  125.6 6.0 %collective-permute-start.16 = (f32[2,32,256]{2,1,0:T(8,128)S(1)}, f32[2,32,256]{2,1,0:T(8,128)S(1)}, u32[]{:S(2)}, u32[]{:S(2)}) collective-permute-start(f32[2,32,256]{2,1,0:T(8,128)S(1)} %dynamic-slice_bitcast_fusion.7), channel_id=1, source_target_pairs={{0,8},{1,9},{2,10},{3,11},{4,12},{5,13},{6,14},{7,15},{8,0},{9,1},... | collective-permute-start | bytes 196616 | tf_op jit(solution)/shard_map/sketch_reduce_gather/ppermute | solution.py:99
  126.0 5.7 %collective-permute-start.9 = (f32[2,32,256]{2,1,0:T(8,128)S(1)}, f32[2,32,256]{2,1,0:T(8,128)S(1)}, u32[]{:S(2)}, u32[]{:S(2)}) collective-permute-start(f32[2,32,256]{2,1,0:T(8,128)S(1)} %dynamic-slice_bitcast_fusion.8), channel_id=1, source_target_pairs={{0,2},{1,3},{2,0},{3,1},{4,6},{5,7},{6,4},{7,5},{8,10},{9,11},{10,... | collective-permute-start | bytes 196616 | tf_op jit(solution)/shard_map/sketch_reduce_gather/ppermute | solution.py:99
  127.3 7.3 %collective-permute-start.2 = (f32[2,32,256]{2,1,0:T(8,128)S(1)}, f32[2,32,256]{2,1,0:T(8,128)S(1)}, u32[]{:S(2)}, u32[]{:S(2)}) collective-permute-start(f32[2,32,256]{2,1,0:T(8,128)S(1)} %dynamic-slice_bitcast_fusion.9), channel_id=1, source_target_pairs={{0,4},{1,5},{2,6},{3,7},{4,0},{5,1},{6,2},{7,3},{8,12},{9,13},{10,... | collective-permute-start | bytes 196616 | tf_op jit(solution)/shard_map/sketch_reduce_gather/ppermute | solution.py:99
  130.6 4.3 %collective-permute-start.24 = (f32[2,32,256]{2,1,0:T(8,128)S(1)}, f32[2,32,256]{2,1,0:T(8,128)S(1)}, u32[]{:S(2)}, u32[]{:S(2)}) collective-permute-start(f32[2,32,256]{2,1,0:T(8,128)S(1)} %bitcast_add_fusion.8), channel_id=1, source_target_pairs={{0,2},{1,3},{2,0},{3,1},{4,6},{5,7},{6,4},{7,5},{8,10},{9,11},{10,... | collective-permute-start | bytes 196616 | tf_op jit(solution)/shard_map/sketch_reduce_gather/ppermute | solution.py:99
  131.6 6.2 %collective-permute-start.17 = (f32[2,32,256]{2,1,0:T(8,128)S(1)}, f32[2,32,256]{2,1,0:T(8,128)S(1)}, u32[]{:S(2)}, u32[]{:S(2)}) collective-permute-start(f32[2,32,256]{2,1,0:T(8,128)S(1)} %bitcast_add_fusion.9), channel_id=1, source_target_pairs={{0,4},{1,5},{2,6},{3,7},{4,0},{5,1},{6,2},{7,3},{8,12},{9,13},{10,... | collective-permute-start | bytes 196616 | tf_op jit(solution)/shard_map/sketch_reduce_gather/ppermute | solution.py:99
  131.7 11.3 %collective-permute-start.10 = (f32[2,32,256]{2,1,0:T(8,128)S(1)}, f32[2,32,256]{2,1,0:T(8,128)S(1)}, u32[]{:S(2)}, u32[]{:S(2)}) collective-permute-start(f32[2,32,256]{2,1,0:T(8,128)S(1)} %bitcast_add_fusion.10), channel_id=1, source_target_pairs={{0,8},{1,9},{2,10},{3,11},{4,12},{5,13},{6,14},{7,15},{8,0},{9,1},... | collective-permute-start | bytes 196616 | tf_op jit(solution)/shard_map/sketch_reduce_gather/ppermute | solution.py:99
  134.6 9.8 %collective-permute-start.3 = (f32[2,32,256]{2,1,0:T(8,128)S(1)}, f32[2,32,256]{2,1,0:T(8,128)S(1)}, u32[]{:S(2)}, u32[]{:S(2)}) collective-permute-start(f32[2,32,256]{2,1,0:T(8,128)S(1)} %bitcast_add_fusion.11), channel_id=1, source_target_pairs={{0,8},{1,9},{2,10},{3,11},{4,12},{5,13},{6,14},{7,15},{8,0},{9,1},... | collective-permute-start | bytes 196616 | tf_op jit(solution)/shard_map/sketch_reduce_gather/ppermute | solution.py:99
  135.0 10.6 %collective-permute-start.25 = (f32[2,32,256]{2,1,0:T(8,128)S(1)}, f32[2,32,256]{2,1,0:T(8,128)S(1)}, u32[]{:S(2)}, u32[]{:S(2)}) collective-permute-start(f32[2,32,256]{2,1,0:T(8,128)S(1)} %add.178), channel_id=1, source_target_pairs={{0,8},{1,9},{2,10},{3,11},{4,12},{5,13},{6,14},{7,15},{8,0},{9,1},... | collective-permute-start | bytes 196616 | tf_op jit(solution)/shard_map/sketch_reduce_gather/ppermute | solution.py:99
  137.7 9.6 %collective-permute-start.18 = (f32[2,32,256]{2,1,0:T(8,128)S(1)}, f32[2,32,256]{2,1,0:T(8,128)S(1)}, u32[]{:S(2)}, u32[]{:S(2)}) collective-permute-start(f32[2,32,256]{2,1,0:T(8,128)S(1)} %add.174), channel_id=1, source_target_pairs={{0,8},{1,9},{2,10},{3,11},{4,12},{5,13},{6,14},{7,15},{8,0},{9,1},... | collective-permute-start | bytes 196616 | tf_op jit(solution)/shard_map/sketch_reduce_gather/ppermute | solution.py:99
  143.0 5.1 %collective-permute-start.11 = (f32[2,32,256]{2,1,0:T(8,128)S(1)}, f32[2,32,256]{2,1,0:T(8,128)S(1)}, u32[]{:S(2)}, u32[]{:S(2)}) collective-permute-start(f32[2,32,256]{2,1,0:T(8,128)S(1)} %add.167), channel_id=1, source_target_pairs={{0,2},{1,3},{2,0},{3,1},{4,6},{5,7},{6,4},{7,5},{8,10},{9,11},{10,... | collective-permute-start | bytes 196616 | tf_op jit(solution)/shard_map/sketch_reduce_gather/ppermute | solution.py:99
  144.4 4.6 %collective-permute-start.4 = (f32[2,32,256]{2,1,0:T(8,128)S(1)}, f32[2,32,256]{2,1,0:T(8,128)S(1)}, u32[]{:S(2)}, u32[]{:S(2)}) collective-permute-start(f32[2,32,256]{2,1,0:T(8,128)S(1)} %add.163), channel_id=1, source_target_pairs={{0,4},{1,5},{2,6},{3,7},{4,0},{5,1},{6,2},{7,3},{8,12},{9,13},{10,... | collective-permute-start | bytes 196616 | tf_op jit(solution)/shard_map/sketch_reduce_gather/ppermute | solution.py:99
  145.6 6.3 %collective-permute-start.26 = (f32[2,2,32,256]{3,2,0,1:T(8,128)S(1)}, f32[2,2,32,256]{3,2,0,1:T(8,128)S(1)}, u32[]{:S(2)}, u32[]{:S(2)}) collective-permute-start(f32[2,2,32,256]{3,2,0,1:T(8,128)S(1)} %pad_maximum_fusion.11), channel_id=1, source_target_pairs={{0,4},{1,5},{2,6},{3,7},{4,0},{5,1},{6,2},{7,3},{8,12},{9,13},{10,... | collective-permute-start | bytes 393224 | tf_op jit(solution)/shard_map/sketch_reduce_gather/ppermute | solution.py:99
  147.3 5.2 %collective-permute-start.19 = (f32[2,2,32,256]{3,2,1,0:T(8,128)S(1)}, f32[2,2,32,256]{3,2,1,0:T(8,128)S(1)}, u32[]{:S(2)}, u32[]{:S(2)}) collective-permute-start(f32[2,2,32,256]{3,2,1,0:T(8,128)S(1)} %pad_maximum_fusion.10), channel_id=1, source_target_pairs={{0,2},{1,3},{2,0},{3,1},{4,6},{5,7},{6,4},{7,5},{8,10},{9,11},{10,... | collective-permute-start | bytes 393224 | tf_op jit(solution)/shard_map/sketch_reduce_gather/ppermute | solution.py:99
  148.1 5.2 %collective-permute-start.12 = (f32[2,2,32,256]{3,2,0,1:T(8,128)S(1)}, f32[2,2,32,256]{3,2,0,1:T(8,128)S(1)}, u32[]{:S(2)}, u32[]{:S(2)}) collective-permute-start(f32[2,2,32,256]{3,2,0,1:T(8,128)S(1)} %pad_maximum_fusion.9), channel_id=1, source_target_pairs={{0,4},{1,5},{2,6},{3,7},{4,0},{5,1},{6,2},{7,3},{8,12},{9,13},{10,... | collective-permute-start | bytes 393224 | tf_op jit(solution)/shard_map/sketch_reduce_gather/ppermute | solution.py:99
  149.1 5.0 %collective-permute-start.5 = (f32[2,2,32,256]{3,2,1,0:T(8,128)S(1)}, f32[2,2,32,256]{3,2,1,0:T(8,128)S(1)}, u32[]{:S(2)}, u32[]{:S(2)}) collective-permute-start(f32[2,2,32,256]{3,2,1,0:T(8,128)S(1)} %pad_maximum_fusion.8), channel_id=1, source_target_pairs={{0,2},{1,3},{2,0},{3,1},{4,6},{5,7},{6,4},{7,5},{8,10},{9,11},{10,... | collective-permute-start | bytes 393224 | tf_op jit(solution)/shard_map/sketch_reduce_gather/ppermute | solution.py:99
  152.0 2.3 %collective-permute-start.27 = (f32[2,2,2,32,256]{4,3,1,0,2:T(8,128)S(1)}, f32[2,2,2,32,256]{4,3,1,0,2:T(8,128)S(1)}, u32[]{:S(2)}, u32[]{:S(2)}) collective-permute-start(f32[2,2,2,32,256]{4,3,1,0,2:T(8,128)S(1)} %pad_maximum_fusion.7), channel_id=1, source_target_pairs={{0,1},{1,0},{2,3},{3,2},{4,5},{5,4},{6,7},{7,6},{8,9},{9,8},{10,11... | collective-permute-start | bytes 786440 | tf_op jit(solution)/shard_map/sketch_reduce_gather/ppermute | solution.py:99
  152.6 1.8 collective-permute-start.20
  153.4 1.6 collective-permute-start.13
  154.2 1.6 collective-permute-start.6

commit v10 on v9

--- a/solution.py
+++ b/solution.py
@@ -36,31 +36,30 @@
         kept = jnp.where((lane_row == k) | (lane_row == k + 1), 0.0, row)
         return kept - f0 * scaled0 - f1 * scaled1
 
+    in_tile = lax.broadcasted_iota(jnp.int32, (8, size), 0)
+    tile_lane = lax.broadcasted_iota(jnp.int32, (8, size), 1)
+
     def step(h, a):
-        k = 4 * h
-        base = k - k % 8
-        tile = jnp.sum(
-            jnp.where((sub >= base) & (sub < base + 8), a, 0.0).reshape(size // 8, 8, size), axis=0)
-        in_tile = lax.broadcasted_iota(jnp.int32, (8, size), 0)
-        rows = [jnp.sum(jnp.where(in_tile == k % 8 + t, tile, 0.0), axis=0, keepdims=True)
-                for t in range(4)]
-        cols = [jnp.sum(jnp.where(lane == k + t, a, 0.0), axis=1, keepdims=True) for t in range(4)]
-        s0, s1 = pair_pivot(rows[0], rows[1], k)
-        r2 = eliminate(rows[2], k, s0, s1)
-        r3 = eliminate(rows[3], k, s0, s1)
-        s2, s3 = pair_pivot(r2, r3, k + 2)
-        s0 = eliminate(s0, k + 2, s2, s3)
-        s1 = eliminate(s1, k + 2, s2, s3)
-        slab = (s0, s1, s2, s3)
-        pivot_rows = (sub_col >= k) & (sub_col < k + 4)
-        a = jnp.where((lane >= k) & (lane < k + 4), 0.0, a)
-        for t in range(4):
-            a = a - jnp.where(pivot_rows, 0.0, cols[t]) * slab[t]
-        for t in range(4):
-            a = jnp.where(sub == k + t, slab[t], a)
-        return a
-
-    return lax.fori_loop(0, size // 4, step, block)
+        k = 8 * h
+        in_rows = (sub >= k) & (sub < k + 8)
+        tile = jnp.sum(jnp.where(in_rows, a, 0.0).reshape(size // 8, 8, size), axis=0)
+        cols = [jnp.sum(jnp.where(lane == k + t, a, 0.0), axis=1, keepdims=True) for t in range(8)]
+        for u in range(4):
+            p = k + 2 * u
+            first = jnp.sum(jnp.where(in_tile == 2 * u, tile, 0.0), axis=0, keepdims=True)
+            second = jnp.sum(jnp.where(in_tile == 2 * u + 1, tile, 0.0), axis=0, keepdims=True)
+            s_first, s_second = pair_pivot(first, second, p)
+            f0 = jnp.sum(jnp.where(tile_lane == p, tile, 0.0), axis=1, keepdims=True)
+            f1 = jnp.sum(jnp.where(tile_lane == p + 1, tile, 0.0), axis=1, keepdims=True)
+            tile = jnp.where((tile_lane == p) | (tile_lane == p + 1), 0.0, tile) - f0 * s_first - f1 * s_second
+            tile = jnp.where(in_tile == 2 * u, s_first, jnp.where(in_tile == 2 * u + 1, s_second, tile))
+        slab = [jnp.sum(jnp.where(in_tile == t, tile, 0.0), axis=0, keepdims=True) for t in range(8)]
+        a = jnp.where((lane >= k) & (lane < k + 8), 0.0, a)
+        for t in range(8):
+            a = a - jnp.where(in_rows, 0.0, cols[t]) * slab[t]
+        return jnp.where(in_rows, jnp.tile(tile, (size // 8, 1)), a)
+
+    return lax.fori_loop(0, size // 8, step, block)
 
 
 def _solve_kernel(m_ref, w_ref, y_ref, a_ref, *, block):

time: 203 us -> 199 us (0.980)
  Pallas kernels: 40.1 us -> 36.2 us
    pallas_call x1, Pallas kernels: 40.1 us -> 36.2 us  [spd_solve(): pl.pallas_call(functools.partial(_solve_kernel, block=block), out_shape=j...]
where the time goes in v10:
time: 199 us
  waiting for transfers between devices  89.1 us (45%)
  starting transfers between devices  48 us (24%)
  Pallas kernels  36.2 us (18%)
  matrix products  14.8 us (7%)
  local copies, waits for them, and re-layouts  6.17 us (3%)
  other arithmetic  3.2 us (2%)
    all_to_all x1, waiting for transfers between devices, on_device(): lax.all_to_all(grads, 'ex', split_axis=1, concat_axis=0, tiled=True)  75.8 us
    ppermute x28, starting transfers between devices, partner(): lax.ppermute(array, axis, [(i, i ^ 1 << bit) for i in range(lax.axis_size...  40.5 us
    pallas_call x1, Pallas kernels, spd_solve(): pl.pallas_call(functools.partial(_solve_kernel, block=block), out_shape=j...  36.2 us
    ppermute x28, waiting for transfers between devices, partner(): lax.ppermute(array, axis, [(i, i ^ 1 << bit) for i in range(lax.axis_size...  13.3 us
    dot_general x1, matrix products, on_device(): partial_value = jnp.dot(columns, proj, preferred_element_type=jnp.float32)  8.14 us
    all_to_all x1, starting transfers between devices, on_device(): lax.all_to_all(grads, 'ex', split_axis=1, concat_axis=0, tiled=True)  7.57 us
    all_to_all x1, local copies, waits for them, and re-layouts, on_device(): lax.all_to_all(grads, 'ex', split_axis=1, concat_axis=0, tiled=True)  4.71 us
    dot_general x1, matrix products, on_device(): kernel = jnp.dot(sketch_all, sketch_all.T, precision=lax.Precision.HIGHEST)  4.51 us
  transfers between devices with their start and end apart: 29, of which 14 were waited for; matrix products, arithmetic and copies ran while one was open for 2% of the time, Pallas kernels for 0%

profile of v10, /device:TPU:0, one launch (start us, length us, event | category | flops | bytes accessed | tf_op | source)
XLA Modules:
  0.0 198.7 jit_solution(17992882997637988994)
XLA Ops:
  0.6 4.7 %copy.104 = bf16[4,16,8,4096]{3,2,0,1:T(8,128)(2,1)} copy(bf16[4,16,8,4096]{3,2,1,0:T(8,128)(2,1)} %bitcast.136) | data formatting | bytes 8388608 | tf_op jit(solution)/shard_map/gradient_exchange/all_to_all | solution.py:144
  5.3 7.6 %all-to-all-start = ((bf16[32,16,4096]{2,0,1:T(8,128)(2,1)}), bf16[32,16,4096]{2,0,1:T(8,128)(2,1)}, u32[]{:S(2)}, u32[]{:S(2)}) async-start(bf16[32,16,4096]{2,0,1:T(8,128)(2,1)} %bitcast.135), calls=%async_computation | async-start | bytes 8388608 | tf_op jit(solution)/shard_map/gradient_exchange/all_to_all | solution.py:144
  13.0 1.6 convert_reduce_fusion
  14.8 75.8 %all-to-all-done = bf16[32,16,4096]{2,0,1:T(8,128)(2,1)} async-done(((bf16[32,16,4096]{2,0,1:T(8,128)(2,1)}), bf16[32,16,4096]{2,0,1:T(8,128)(2,1)}, u32[]{:S(2)}, u32[]{:S(2)}) %all-to-all-start) | async-done | bytes 4194336 | tf_op jit(solution)/shard_map/gradient_exchange/all_to_all | solution.py:144
  90.6 8.1 %fusion.15 = f32[512,1024]{1,0:T(8,128)S(1)} fusion(bf16[512,4096]{1,0:T(8,128)(2,1)} %bitcast.1, bf16[4096,1024]{1,0:T(8,128)(2,1)} %param.5), kind=kOutput, calls=%fused_computation.91 | convolution fusion | flops 4294967296 | bytes 14680064 | tf_op jit(solution)/shard_map/partial_projection/dot_general | solution.py:146
  99.0 0.8 collective-permute-start.21
  99.8 0.7 pad.4.w_ref
  101.6 14.7 %collective-permute-start.22 = (f32[2,2,32,256]{3,2,1,0:T(8,128)S(1)}, f32[2,2,32,256]{3,2,1,0:T(8,128)S(1)}, u32[]{:S(2)}, u32[]{:S(2)}) collective-permute-start(f32[2,2,32,256]{3,2,1,0:T(8,128)S(1)} %dynamic-slice_bitcast_fusion.2), channel_id=1, source_target_pairs={{0,4},{1,5},{2,6},{3,7},{4,0},{5,1},{6,2},{7,3},{8,12},{9,13},{10,... | collective-permute-start | bytes 393224 | tf_op jit(solution)/shard_map/sketch_reduce_gather/ppermute | solution.py:98
  116.4 3.0 %collective-permute-start.15 = (f32[2,2,32,256]{3,2,1,0:T(8,128)S(1)}, f32[2,2,32,256]{3,2,1,0:T(8,128)S(1)}, u32[]{:S(2)}, u32[]{:S(2)}) collective-permute-start(f32[2,2,32,256]{3,2,1,0:T(8,128)S(1)} %dynamic-slice_bitcast_fusion.3), channel_id=1, source_target_pairs={{0,2},{1,3},{2,0},{3,1},{4,6},{5,7},{6,4},{7,5},{8,10},{9,11},{10,... | collective-permute-start | bytes 393224 | tf_op jit(solution)/shard_map/sketch_reduce_gather/ppermute | solution.py:98
  119.5 0.5 collective-permute-start.8
  120.4 5.1 %collective-permute-start.23 = (f32[2,32,256]{2,1,0:T(8,128)S(1)}, f32[2,32,256]{2,1,0:T(8,128)S(1)}, u32[]{:S(2)}, u32[]{:S(2)}) collective-permute-start(f32[2,32,256]{2,1,0:T(8,128)S(1)} %dynamic-slice_bitcast_fusion.6), channel_id=1, source_target_pairs={{0,8},{1,9},{2,10},{3,11},{4,12},{5,13},{6,14},{7,15},{8,0},{9,1},... | collective-permute-start | bytes 196616 | tf_op jit(solution)/shard_map/sketch_reduce_gather/ppermute | solution.py:98
  126.0 1.3 collective-permute-start.9
  127.3 1.7 collective-permute-start.2
  129.0 1.6 collective-permute-done.23
  131.7 3.0 %collective-permute-start.10 = (f32[2,32,256]{2,1,0:T(8,128)S(1)}, f32[2,32,256]{2,1,0:T(8,128)S(1)}, u32[]{:S(2)}, u32[]{:S(2)}) collective-permute-start(f32[2,32,256]{2,1,0:T(8,128)S(1)} %bitcast_add_fusion.10), channel_id=1, source_target_pairs={{0,8},{1,9},{2,10},{3,11},{4,12},{5,13},{6,14},{7,15},{8,0},{9,1},... | collective-permute-start | bytes 196616 | tf_op jit(solution)/shard_map/sketch_reduce_gather/ppermute | solution.py:98
  135.0 2.8 %collective-permute-start.25 = (f32[2,32,256]{2,1,0:T(8,128)S(1)}, f32[2,32,256]{2,1,0:T(8,128)S(1)}, u32[]{:S(2)}, u32[]{:S(2)}) collective-permute-start(f32[2,32,256]{2,1,0:T(8,128)S(1)} %add.178), channel_id=1, source_target_pairs={{0,8},{1,9},{2,10},{3,11},{4,12},{5,13},{6,14},{7,15},{8,0},{9,1},... | collective-permute-start | bytes 196616 | tf_op jit(solution)/shard_map/sketch_reduce_gather/ppermute | solution.py:98
  138.0 5.0 %collective-permute-done.10 = f32[2,32,256]{2,1,0:T(8,128)S(1)} collective-permute-done((f32[2,32,256]{2,1,0:T(8,128)S(1)}, f32[2,32,256]{2,1,0:T(8,128)S(1)}, u32[]{:S(2)}, u32[]{:S(2)}) %collective-permute-start.10) | collective-permute-done | bytes 65568 | tf_op jit(solution)/shard_map/sketch_reduce_gather/ppermute | solution.py:98
  143.0 0.7 collective-permute-start.11
  143.7 0.7 collective-permute-done.3
  144.5 0.7 pad_maximum_fusion.12
  145.6 1.7 collective-permute-start.26
  147.3 0.8 collective-permute-start.19
  148.1 0.6 collective-permute-start.12
  149.1 1.1 collective-permute-start.5
  150.1 1.8 collective-permute-done.26
  152.1 0.5 collective-permute-done.19
  152.7 0.6 collective-permute-done.12
  153.5 0.7 collective-permute-done.5
  155.1 0.7 collective-permute-done.6
  155.9 4.5 %select_add_fusion = (f32[512,512]{1,0:T(8,128)}, f32[512,512]{1,0:T(8,128)S(1)}) fusion(f32[512,256]{1,0:T(8,128)S(1)} %bitcast.143, f32[512,256]{1,0:T(8,128)S(1)} %bitcast.144, f32[512,256]{1,0:T(8,128)S(1)} %bitcast.145, f32[512,256]{1,0:T(8,128)S(1)} %bitcast.146), kind=kOutput, calls=%fused_computation.12 | convolution fusion | flops 3223846912 | bytes 4194304 | tf_op jit(solution)/shard_map/kernel_matrix/dot_general | solution.py:172
  160.4 36.2 %kernel_solve.1 = f32[512,128]{1,0:T(8,128)} custom-call(f32[512,512]{1,0:T(8,128)} %get-tuple-element.34.m_ref, f32[512,128]{1,0:T(8,128)} %pad.4.w_ref), custom_call_target="tpu_custom_call" | custom-call | tf_op jit(solution)/shard_map/kernel_solve/pallas_call | solution.py:89
  196.6 2.1 %fusion.9 = f32[32,24]{0,1:T(8,128)} fusion(f32[512,128]{1,0:T(8,128)} %kernel_solve.1, f32[512,512]{1,0:T(8,128)S(1)} %get-tuple-element.35, s32[]{:T(128)S(6)} %select_n.314), kind=kOutput, calls=%fused_computation.18 | convolution fusion | flops 4718592 | bytes 330756 | tf_op jit(solution)/shard_map/dot_general | solution.py:179
  (103 shorter events, 6.3 us)
Async XLA Ops:
  5.3 7.6 %copy-start.1 = (s32[24]{0:T(128)S(1)}, s32[24]{0:T(128)}, u32[]{:S(2)}) copy-start(s32[24]{0:T(128)} %param.7) | copy-start | bytes 292
  5.3 7.7 %copy-start = (s32[24,128]{1,0:T(8,128)S(1)}, s32[24,128]{1,0:T(8,128)}, u32[]{:S(2)}) copy-start(s32[24,128]{1,0:T(8,128)} %param.6) | copy-start | bytes 36868
  5.3 85.3 %all-to-all-start = ((bf16[32,16,4096]{2,0,1:T(8,128)(2,1)}), bf16[32,16,4096]{2,0,1:T(8,128)(2,1)}, u32[]{:S(2)}, u32[]{:S(2)}) async-start(bf16[32,16,4096]{2,0,1:T(8,128)(2,1)} %bitcast.135), calls=%async_computation | async-start | bytes 8388608 | tf_op jit(solution)/shard_map/gradient_exchange/all_to_all | solution.py:144
  99.0 2.6 %collective-permute-start.21 = (f32[2,2,2,32,256]{4,3,2,1,0:T(8,128)S(1)}, f32[2,2,2,32,256]{4,3,2,1,0:T(8,128)S(1)}, u32[]{:S(2)}, u32[]{:S(2)}) collective-permute-start(f32[2,2,2,32,256]{4,3,2,1,0:T(8,128)S(1)} %dynamic-slice_bitcast_fusion), channel_id=1, source_target_pairs={{0,1},{1,0},{2,3},{3,2},{4,5},{5,4},{6,7},{7,6},{8,9},{9,8},{10,11... | collective-permute-start | bytes 786440 | tf_op jit(solution)/shard_map/sketch_reduce_gather/ppermute | solution.py:98
  100.6 15.7 %collective-permute-start.14 = (f32[2,2,2,32,256]{4,3,2,1,0:T(8,128)S(1)}, f32[2,2,2,32,256]{4,3,2,1,0:T(8,128)S(1)}, u32[]{:S(2)}, u32[]{:S(2)}) collective-permute-start(f32[2,2,2,32,256]{4,3,2,1,0:T(8,128)S(1)} %dynamic-slice_bitcast_fusion.1), channel_id=1, source_target_pairs={{0,1},{1,0},{2,3},{3,2},{4,5},{5,4},{6,7},{7,6},{8,9},{9,8},{10,11... | collective-permute-start | bytes 786440 | tf_op jit(solution)/shard_map/sketch_reduce_gather/ppermute | solution.py:98
  100.9 18.5 %collective-permute-start.7 = (f32[2,2,2,32,256]{4,3,2,0,1:T(8,128)S(1)}, f32[2,2,2,32,256]{4,3,2,0,1:T(8,128)S(1)}, u32[]{:S(2)}, u32[]{:S(2)}) collective-permute-start(f32[2,2,2,32,256]{4,3,2,0,1:T(8,128)S(1)} %bitcast.148), channel_id=1, source_target_pairs={{0,1},{1,0},{2,3},{3,2},{4,5},{5,4},{6,7},{7,6},{8,9},{9,8},{10,11... | collective-permute-start | bytes 786440 | tf_op jit(solution)/shard_map/sketch_reduce_gather/ppermute | solution.py:98
  101.3 18.6 %collective-permute-start = (f32[2,2,2,32,256]{4,3,1,0,2:T(8,128)S(1)}, f32[2,2,2,32,256]{4,3,1,0,2:T(8,128)S(1)}, u32[]{:S(2)}, u32[]{:S(2)}) collective-permute-start(f32[2,2,2,32,256]{4,3,1,0,2:T(8,128)S(1)} %bitcast.147), channel_id=1, source_target_pairs={{0,1},{1,0},{2,3},{3,2},{4,5},{5,4},{6,7},{7,6},{8,9},{9,8},{10,11... | collective-permute-start | bytes 786440 | tf_op jit(solution)/shard_map/sketch_reduce_gather/ppermute | solution.py:98
  101.6 18.7 %collective-permute-start.22 = (f32[2,2,32,256]{3,2,1,0:T(8,128)S(1)}, f32[2,2,32,256]{3,2,1,0:T(8,128)S(1)}, u32[]{:S(2)}, u32[]{:S(2)}) collective-permute-start(f32[2,2,32,256]{3,2,1,0:T(8,128)S(1)} %dynamic-slice_bitcast_fusion.2), channel_id=1, source_target_pairs={{0,4},{1,5},{2,6},{3,7},{4,0},{5,1},{6,2},{7,3},{8,12},{9,13},{10,... | collective-permute-start | bytes 393224 | tf_op jit(solution)/shard_map/sketch_reduce_gather/ppermute | solution.py:98
  116.4 9.2 %collective-permute-start.15 = (f32[2,2,32,256]{3,2,1,0:T(8,128)S(1)}, f32[2,2,32,256]{3,2,1,0:T(8,128)S(1)}, u32[]{:S(2)}, u32[]{:S(2)}) collective-permute-start(f32[2,2,32,256]{3,2,1,0:T(8,128)S(1)} %dynamic-slice_bitcast_fusion.3), channel_id=1, source_target_pairs={{0,2},{1,3},{2,0},{3,1},{4,6},{5,7},{6,4},{7,5},{8,10},{9,11},{10,... | collective-permute-start | bytes 393224 | tf_op jit(solution)/shard_map/sketch_reduce_gather/ppermute | solution.py:98
  119.5 6.4 %collective-permute-start.8 = (f32[2,2,32,256]{3,2,1,0:T(8,128)S(1)}, f32[2,2,32,256]{3,2,1,0:T(8,128)S(1)}, u32[]{:S(2)}, u32[]{:S(2)}) collective-permute-start(f32[2,2,32,256]{3,2,1,0:T(8,128)S(1)} %dynamic-slice_bitcast_fusion.4), channel_id=1, source_target_pairs={{0,4},{1,5},{2,6},{3,7},{4,0},{5,1},{6,2},{7,3},{8,12},{9,13},{10,... | collective-permute-start | bytes 393224 | tf_op jit(solution)/shard_map/sketch_reduce_gather/ppermute | solution.py:98
  120.0 7.2 %collective-permute-start.1 = (f32[2,2,32,256]{3,2,1,0:T(8,128)S(1)}, f32[2,2,32,256]{3,2,1,0:T(8,128)S(1)}, u32[]{:S(2)}, u32[]{:S(2)}) collective-permute-start(f32[2,2,32,256]{3,2,1,0:T(8,128)S(1)} %dynamic-slice_bitcast_fusion.5), channel_id=1, source_target_pairs={{0,2},{1,3},{2,0},{3,1},{4,6},{5,7},{6,4},{7,5},{8,10},{9,11},{10,... | collective-permute-start | bytes 393224 | tf_op jit(solution)/shard_map/sketch_reduce_gather/ppermute | solution.py:98
  120.4 10.2 %collective-permute-start.23 = (f32[2,32,256]{2,1,0:T(8,128)S(1)}, f32[2,32,256]{2,1,0:T(8,128)S(1)}, u32[]{:S(2)}, u32[]{:S(2)}) collective-permute-start(f32[2,32,256]{2,1,0:T(8,128)S(1)} %dynamic-slice_bitcast_fusion.6), channel_id=1, source_target_pairs={{0,8},{1,9},{2,10},{3,11},{4,12},{5,13},{6,14},{7,15},{8,0},{9,1},... | collective-permute-start | bytes 196616 | tf_op jit(solution)/shard_map/sketch_reduce_gather/ppermute | solution.py:98
  125.6 6.0 %collective-permute-start.16 = (f32[2,32,256]{2,1,0:T(8,128)S(1)}, f32[2,32,256]{2,1,0:T(8,128)S(1)}, u32[]{:S(2)}, u32[]{:S(2)}) collective-permute-start(f32[2,32,256]{2,1,0:T(8,128)S(1)} %dynamic-slice_bitcast_fusion.7), channel_id=1, source_target_pairs={{0,8},{1,9},{2,10},{3,11},{4,12},{5,13},{6,14},{7,15},{8,0},{9,1},... | collective-permute-start | bytes 196616 | tf_op jit(solution)/shard_map/sketch_reduce_gather/ppermute | solution.py:98
  126.0 5.7 %collective-permute-start.9 = (f32[2,32,256]{2,1,0:T(8,128)S(1)}, f32[2,32,256]{2,1,0:T(8,128)S(1)}, u32[]{:S(2)}, u32[]{:S(2)}) collective-permute-start(f32[2,32,256]{2,1,0:T(8,128)S(1)} %dynamic-slice_bitcast_fusion.8), channel_id=1, source_target_pairs={{0,2},{1,3},{2,0},{3,1},{4,6},{5,7},{6,4},{7,5},{8,10},{9,11},{10,... | collective-permute-start | bytes 196616 | tf_op jit(solution)/shard_map/sketch_reduce_gather/ppermute | solution.py:98
  127.3 7.3 %collective-permute-start.2 = (f32[2,32,256]{2,1,0:T(8,128)S(1)}, f32[2,32,256]{2,1,0:T(8,128)S(1)}, u32[]{:S(2)}, u32[]{:S(2)}) collective-permute-start(f32[2,32,256]{2,1,0:T(8,128)S(1)} %dynamic-slice_bitcast_fusion.9), channel_id=1, source_target_pairs={{0,4},{1,5},{2,6},{3,7},{4,0},{5,1},{6,2},{7,3},{8,12},{9,13},{10,... | collective-permute-start | bytes 196616 | tf_op jit(solution)/shard_map/sketch_reduce_gather/ppermute | solution.py:98
  130.6 4.3 %collective-permute-start.24 = (f32[2,32,256]{2,1,0:T(8,128)S(1)}, f32[2,32,256]{2,1,0:T(8,128)S(1)}, u32[]{:S(2)}, u32[]{:S(2)}) collective-permute-start(f32[2,32,256]{2,1,0:T(8,128)S(1)} %bitcast_add_fusion.8), channel_id=1, source_target_pairs={{0,2},{1,3},{2,0},{3,1},{4,6},{5,7},{6,4},{7,5},{8,10},{9,11},{10,... | collective-permute-start | bytes 196616 | tf_op jit(solution)/shard_map/sketch_reduce_gather/ppermute | solution.py:98
  131.6 6.2 %collective-permute-start.17 = (f32[2,32,256]{2,1,0:T(8,128)S(1)}, f32[2,32,256]{2,1,0:T(8,128)S(1)}, u32[]{:S(2)}, u32[]{:S(2)}) collective-permute-start(f32[2,32,256]{2,1,0:T(8,128)S(1)} %bitcast_add_fusion.9), channel_id=1, source_target_pairs={{0,4},{1,5},{2,6},{3,7},{4,0},{5,1},{6,2},{7,3},{8,12},{9,13},{10,... | collective-permute-start | bytes 196616 | tf_op jit(solution)/shard_map/sketch_reduce_gather/ppermute | solution.py:98
  131.7 11.3 %collective-permute-start.10 = (f32[2,32,256]{2,1,0:T(8,128)S(1)}, f32[2,32,256]{2,1,0:T(8,128)S(1)}, u32[]{:S(2)}, u32[]{:S(2)}) collective-permute-start(f32[2,32,256]{2,1,0:T(8,128)S(1)} %bitcast_add_fusion.10), channel_id=1, source_target_pairs={{0,8},{1,9},{2,10},{3,11},{4,12},{5,13},{6,14},{7,15},{8,0},{9,1},... | collective-permute-start | bytes 196616 | tf_op jit(solution)/shard_map/sketch_reduce_gather/ppermute | solution.py:98
  134.6 9.8 %collective-permute-start.3 = (f32[2,32,256]{2,1,0:T(8,128)S(1)}, f32[2,32,256]{2,1,0:T(8,128)S(1)}, u32[]{:S(2)}, u32[]{:S(2)}) collective-permute-start(f32[2,32,256]{2,1,0:T(8,128)S(1)} %bitcast_add_fusion.11), channel_id=1, source_target_pairs={{0,8},{1,9},{2,10},{3,11},{4,12},{5,13},{6,14},{7,15},{8,0},{9,1},... | collective-permute-start | bytes 196616 | tf_op jit(solution)/shard_map/sketch_reduce_gather/ppermute | solution.py:98
  135.0 10.6 %collective-permute-start.25 = (f32[2,32,256]{2,1,0:T(8,128)S(1)}, f32[2,32,256]{2,1,0:T(8,128)S(1)}, u32[]{:S(2)}, u32[]{:S(2)}) collective-permute-start(f32[2,32,256]{2,1,0:T(8,128)S(1)} %add.178), channel_id=1, source_target_pairs={{0,8},{1,9},{2,10},{3,11},{4,12},{5,13},{6,14},{7,15},{8,0},{9,1},... | collective-permute-start | bytes 196616 | tf_op jit(solution)/shard_map/sketch_reduce_gather/ppermute | solution.py:98
  137.7 9.6 %collective-permute-start.18 = (f32[2,32,256]{2,1,0:T(8,128)S(1)}, f32[2,32,256]{2,1,0:T(8,128)S(1)}, u32[]{:S(2)}, u32[]{:S(2)}) collective-permute-start(f32[2,32,256]{2,1,0:T(8,128)S(1)} %add.174), channel_id=1, source_target_pairs={{0,8},{1,9},{2,10},{3,11},{4,12},{5,13},{6,14},{7,15},{8,0},{9,1},... | collective-permute-start | bytes 196616 | tf_op jit(solution)/shard_map/sketch_reduce_gather/ppermute | solution.py:98
  143.0 5.1 %collective-permute-start.11 = (f32[2,32,256]{2,1,0:T(8,128)S(1)}, f32[2,32,256]{2,1,0:T(8,128)S(1)}, u32[]{:S(2)}, u32[]{:S(2)}) collective-permute-start(f32[2,32,256]{2,1,0:T(8,128)S(1)} %add.167), channel_id=1, source_target_pairs={{0,2},{1,3},{2,0},{3,1},{4,6},{5,7},{6,4},{7,5},{8,10},{9,11},{10,... | collective-permute-start | bytes 196616 | tf_op jit(solution)/shard_map/sketch_reduce_gather/ppermute | solution.py:98
  144.4 4.6 %collective-permute-start.4 = (f32[2,32,256]{2,1,0:T(8,128)S(1)}, f32[2,32,256]{2,1,0:T(8,128)S(1)}, u32[]{:S(2)}, u32[]{:S(2)}) collective-permute-start(f32[2,32,256]{2,1,0:T(8,128)S(1)} %add.163), channel_id=1, source_target_pairs={{0,4},{1,5},{2,6},{3,7},{4,0},{5,1},{6,2},{7,3},{8,12},{9,13},{10,... | collective-permute-start | bytes 196616 | tf_op jit(solution)/shard_map/sketch_reduce_gather/ppermute | solution.py:98
  145.6 6.3 %collective-permute-start.26 = (f32[2,2,32,256]{3,2,0,1:T(8,128)S(1)}, f32[2,2,32,256]{3,2,0,1:T(8,128)S(1)}, u32[]{:S(2)}, u32[]{:S(2)}) collective-permute-start(f32[2,2,32,256]{3,2,0,1:T(8,128)S(1)} %pad_maximum_fusion.11), channel_id=1, source_target_pairs={{0,4},{1,5},{2,6},{3,7},{4,0},{5,1},{6,2},{7,3},{8,12},{9,13},{10,... | collective-permute-start | bytes 393224 | tf_op jit(solution)/shard_map/sketch_reduce_gather/ppermute | solution.py:98
  147.3 5.2 %collective-permute-start.19 = (f32[2,2,32,256]{3,2,1,0:T(8,128)S(1)}, f32[2,2,32,256]{3,2,1,0:T(8,128)S(1)}, u32[]{:S(2)}, u32[]{:S(2)}) collective-permute-start(f32[2,2,32,256]{3,2,1,0:T(8,128)S(1)} %pad_maximum_fusion.10), channel_id=1, source_target_pairs={{0,2},{1,3},{2,0},{3,1},{4,6},{5,7},{6,4},{7,5},{8,10},{9,11},{10,... | collective-permute-start | bytes 393224 | tf_op jit(solution)/shard_map/sketch_reduce_gather/ppermute | solution.py:98
  148.1 5.2 %collective-permute-start.12 = (f32[2,2,32,256]{3,2,0,1:T(8,128)S(1)}, f32[2,2,32,256]{3,2,0,1:T(8,128)S(1)}, u32[]{:S(2)}, u32[]{:S(2)}) collective-permute-start(f32[2,2,32,256]{3,2,0,1:T(8,128)S(1)} %pad_maximum_fusion.9), channel_id=1, source_target_pairs={{0,4},{1,5},{2,6},{3,7},{4,0},{5,1},{6,2},{7,3},{8,12},{9,13},{10,... | collective-permute-start | bytes 393224 | tf_op jit(solution)/shard_map/sketch_reduce_gather/ppermute | solution.py:98
  149.1 5.0 %collective-permute-start.5 = (f32[2,2,32,256]{3,2,1,0:T(8,128)S(1)}, f32[2,2,32,256]{3,2,1,0:T(8,128)S(1)}, u32[]{:S(2)}, u32[]{:S(2)}) collective-permute-start(f32[2,2,32,256]{3,2,1,0:T(8,128)S(1)} %pad_maximum_fusion.8), channel_id=1, source_target_pairs={{0,2},{1,3},{2,0},{3,1},{4,6},{5,7},{6,4},{7,5},{8,10},{9,11},{10,... | collective-permute-start | bytes 393224 | tf_op jit(solution)/shard_map/sketch_reduce_gather/ppermute | solution.py:98
  152.0 2.3 %collective-permute-start.27 = (f32[2,2,2,32,256]{4,3,1,0,2:T(8,128)S(1)}, f32[2,2,2,32,256]{4,3,1,0,2:T(8,128)S(1)}, u32[]{:S(2)}, u32[]{:S(2)}) collective-permute-start(f32[2,2,2,32,256]{4,3,1,0,2:T(8,128)S(1)} %pad_maximum_fusion.7), channel_id=1, source_target_pairs={{0,1},{1,0},{2,3},{3,2},{4,5},{5,4},{6,7},{7,6},{8,9},{9,8},{10,11... | collective-permute-start | bytes 786440 | tf_op jit(solution)/shard_map/sketch_reduce_gather/ppermute | solution.py:98
  152.6 1.8 collective-permute-start.20
  153.4 1.6 collective-permute-start.13
  154.2 1.6 collective-permute-start.6

commit v11 on v10

--- a/solution.py
+++ b/solution.py
@@ -98,12 +98,13 @@
     return lax.ppermute(array, axis, [(i, i ^ 1 << bit) for i in range(lax.axis_size(axis))])
 
 
-def reduce_and_gather(partial_value, order, position):
+def reduce_and_gather(first_kept, first_sent, order, position):
     bits = len(order)
-    rows = partial_value.shape[1:]
-    value = partial_value.reshape((2,) * bits + rows)
-    remaining = list(range(bits - 1, -1, -1))
-    for level in order[:-1]:
+    rows = first_kept.shape[1:]
+    value = first_kept.reshape((2,) * (bits - 1) + rows) + partner(
+        first_sent.reshape((2,) * (bits - 1) + rows), "ex", order[0])
+    remaining = [level for level in range(bits - 1, -1, -1) if level != order[0]]
+    for level in order[1:-1]:
         axis = remaining.index(level)
         own_bit = position // 2**level % 2
         kept = lax.dynamic_index_in_dim(value, own_bit, axis=axis, keepdims=False)
@@ -142,17 +143,25 @@
     sketch_width = proj.shape[1]
     with jax.named_scope("gradient_exchange"):
         columns = lax.all_to_all(grads, "ex", split_axis=1, concat_axis=0, tiled=True)
+    by_low_bit = columns.reshape(count_ex // 2, 2, ex_rows, columns.shape[1])
+    own_low = position % 2
     with jax.named_scope("partial_projection"):
-        partial_value = jnp.dot(columns, proj, preferred_element_type=jnp.float32)
+        sent_value = jnp.dot(
+            lax.dynamic_index_in_dim(by_low_bit, 1 - own_low, axis=1, keepdims=False), proj,
+            preferred_element_type=jnp.float32,
+        )
+        kept_value = jnp.dot(
+            lax.dynamic_index_in_dim(by_low_bit, own_low, axis=1, keepdims=False), proj,
+            preferred_element_type=jnp.float32,
+        )
     orders = bit_orders(bits)
     width = sketch_width // len(orders)
     owned, gathered = [], []
     for half, order in enumerate(orders):
         with jax.named_scope("sketch_reduce_gather"):
             part, every = reduce_and_gather(
-                partial_value[:, half * width:(half + 1) * width].reshape(
-                    count_ex, ex_rows, width
-                ),
+                kept_value[..., half * width:(half + 1) * width],
+                sent_value[..., half * width:(half + 1) * width],
                 order,
                 position,
             )

time: 199 us -> 203 us (1.020)
  matrix products: 14.8 us -> 19.3 us
  waiting for transfers between devices: 89.1 us -> 86.6 us
    dot_general x1 -> x2, matrix products: 8.14 us -> 12.7 us  [the longest x1 6.34 us: on_device(): jnp.dot(lax.dynamic_index_in_dim(by_low_bit, 1 - own_low, axis=1, keepdim...]
  transfers between devices with their start and end apart: 29 -> 29, of which waited for: 14 -> 13; matrix products, arithmetic and copies ran while one was open for 2% -> 5% of each run, Pallas kernels for 0% -> 0%
where the time goes in v11:
time: 203 us; the launch traced here: 202 us
  waiting for transfers between devices  86.6 us (43%)
  starting transfers between devices  49.3 us (24%)
  Pallas kernels  36.3 us (18%)
  matrix products  19.3 us (10%)
  local copies, waits for them, and re-layouts  6.09 us (3%)
  other arithmetic  3.2 us (2%)
    all_to_all x1, waiting for transfers between devices, on_device(): lax.all_to_all(grads, 'ex', split_axis=1, concat_axis=0, tiled=True)  74.9 us
    ppermute x28, starting transfers between devices, partner(): lax.ppermute(array, axis, [(i, i ^ 1 << bit) for i in range(lax.axis_size...  41.8 us
    pallas_call x1, Pallas kernels, spd_solve(): pl.pallas_call(functools.partial(_solve_kernel, block=block), out_shape=j...  36.3 us
    ppermute x28, waiting for transfers between devices, partner(): lax.ppermute(array, axis, [(i, i ^ 1 << bit) for i in range(lax.axis_size...  11.6 us
    all_to_all x1, starting transfers between devices, on_device(): lax.all_to_all(grads, 'ex', split_axis=1, concat_axis=0, tiled=True)  7.57 us
    dot_general x1, matrix products, on_device(): jnp.dot(lax.dynamic_index_in_dim(by_low_bit, 1 - own_low, axis=1, keepdim...  6.34 us
    dot_general x1, matrix products, on_device(): jnp.dot(lax.dynamic_index_in_dim(by_low_bit, own_low, axis=1, keepdims=Fa...  6.34 us
    all_to_all x1, local copies, waits for them, and re-layouts, on_device(): lax.all_to_all(grads, 'ex', split_axis=1, concat_axis=0, tiled=True)  4.71 us
  transfers between devices with their start and end apart: 29, of which 13 were waited for; matrix products, arithmetic and copies ran while one was open for 5% of the time, Pallas kernels for 0%

profile of v11, /device:TPU:0, one launch (start us, length us, event | category | flops | bytes accessed | tf_op | source)
XLA Modules:
  0.0 202.2 jit_solution(6697974554139053091)
XLA Ops:
  0.6 4.7 %copy.98 = bf16[4,16,8,4096]{3,2,0,1:T(8,128)(2,1)} copy(bf16[4,16,8,4096]{3,2,1,0:T(8,128)(2,1)} %bitcast.131) | data formatting | bytes 8388608 | tf_op jit(solution)/shard_map/gradient_exchange/all_to_all | solution.py:145
  5.3 7.6 %all-to-all-start = ((bf16[32,16,4096]{2,0,1:T(8,128)(2,1)}), bf16[32,16,4096]{2,0,1:T(8,128)(2,1)}, u32[]{:S(2)}, u32[]{:S(2)}) async-start(bf16[32,16,4096]{2,0,1:T(8,128)(2,1)} %bitcast.130), calls=%async_computation | async-start | bytes 8388608 | tf_op jit(solution)/shard_map/gradient_exchange/all_to_all | solution.py:145
  13.1 1.6 convert_reduce_fusion
  14.9 0.7 pad.4.w_ref
  15.7 74.9 %all-to-all-done = bf16[32,16,4096]{2,0,1:T(8,128)(2,1)} async-done(((bf16[32,16,4096]{2,0,1:T(8,128)(2,1)}), bf16[32,16,4096]{2,0,1:T(8,128)(2,1)}, u32[]{:S(2)}, u32[]{:S(2)}) %all-to-all-start) | async-done | bytes 4194336 | tf_op jit(solution)/shard_map/gradient_exchange/all_to_all | solution.py:145
  90.6 6.3 %fusion = f32[8,32,1024]{2,1,0:T(8,128)S(1)} fusion(bf16[4096,1024]{1,0:T(8,128)(2,1)} %param.5, bf16[8,2,32,4096]{3,2,1,0:T(8,128)(2,1)} %bitcast.1, s32[]{:T(128)S(6)} %select_n.262), kind=kOutput, calls=%fused_computation | convolution fusion | flops 2147483648 | bytes 11534340 | tf_op jit(solution)/shard_map/partial_projection/dot_general | solution.py:149
  97.1 0.8 collective-permute-start.21
  97.9 6.3 %fusion.2 = f32[8,32,1024]{2,1,0:T(8,128)S(1)} fusion(bf16[4096,1024]{1,0:T(8,128)(2,1)} %param.5, bf16[8,2,32,4096]{3,2,1,0:T(8,128)(2,1)} %bitcast.1, s32[]{:T(128)S(6)} %select_n.261), kind=kOutput, calls=%fused_computation.2 | convolution fusion | flops 2147483648 | bytes 11534340 | tf_op jit(solution)/shard_map/partial_projection/dot_general | solution.py:153
  104.4 0.6 collective-permute-start.7
  105.2 14.8 %collective-permute-start.22 = (f32[2,2,32,256]{3,2,1,0:T(8,128)S(1)}, f32[2,2,32,256]{3,2,1,0:T(8,128)S(1)}, u32[]{:S(2)}, u32[]{:S(2)}) collective-permute-start(f32[2,2,32,256]{3,2,1,0:T(8,128)S(1)} %dynamic-slice_bitcast_fusion), channel_id=1, source_target_pairs={{0,4},{1,5},{2,6},{3,7},{4,0},{5,1},{6,2},{7,3},{8,12},{9,13},{10,... | collective-permute-start | bytes 393224 | tf_op jit(solution)/shard_map/sketch_reduce_gather/ppermute | solution.py:98
  120.1 3.0 %collective-permute-start.15 = (f32[2,2,32,256]{3,2,1,0:T(8,128)S(1)}, f32[2,2,32,256]{3,2,1,0:T(8,128)S(1)}, u32[]{:S(2)}, u32[]{:S(2)}) collective-permute-start(f32[2,2,32,256]{3,2,1,0:T(8,128)S(1)} %dynamic-slice_bitcast_fusion.1), channel_id=1, source_target_pairs={{0,2},{1,3},{2,0},{3,1},{4,6},{5,7},{6,4},{7,5},{8,10},{9,11},{10,... | collective-permute-start | bytes 393224 | tf_op jit(solution)/shard_map/sketch_reduce_gather/ppermute | solution.py:98
  124.1 5.2 %collective-permute-start.23 = (f32[2,32,256]{2,1,0:T(8,128)S(1)}, f32[2,32,256]{2,1,0:T(8,128)S(1)}, u32[]{:S(2)}, u32[]{:S(2)}) collective-permute-start(f32[2,32,256]{2,1,0:T(8,128)S(1)} %dynamic-slice_bitcast_fusion.4), channel_id=1, source_target_pairs={{0,8},{1,9},{2,10},{3,11},{4,12},{5,13},{6,14},{7,15},{8,0},{9,1},... | collective-permute-start | bytes 196616 | tf_op jit(solution)/shard_map/sketch_reduce_gather/ppermute | solution.py:98
  129.6 1.4 collective-permute-start.9
  131.1 1.5 collective-permute-start.2
  132.7 1.6 collective-permute-done.23
  135.2 3.1 %collective-permute-start.10 = (f32[2,32,256]{2,1,0:T(8,128)S(1)}, f32[2,32,256]{2,1,0:T(8,128)S(1)}, u32[]{:S(2)}, u32[]{:S(2)}) collective-permute-start(f32[2,32,256]{2,1,0:T(8,128)S(1)} %bitcast_add_fusion.6), channel_id=1, source_target_pairs={{0,8},{1,9},{2,10},{3,11},{4,12},{5,13},{6,14},{7,15},{8,0},{9,1},... | collective-permute-start | bytes 196616 | tf_op jit(solution)/shard_map/sketch_reduce_gather/ppermute | solution.py:98
  138.6 2.8 %collective-permute-start.25 = (f32[2,32,256]{2,1,0:T(8,128)S(1)}, f32[2,32,256]{2,1,0:T(8,128)S(1)}, u32[]{:S(2)}, u32[]{:S(2)}) collective-permute-start(f32[2,32,256]{2,1,0:T(8,128)S(1)} %add.169), channel_id=1, source_target_pairs={{0,8},{1,9},{2,10},{3,11},{4,12},{5,13},{6,14},{7,15},{8,0},{9,1},... | collective-permute-start | bytes 196616 | tf_op jit(solution)/shard_map/sketch_reduce_gather/ppermute | solution.py:98
  141.7 4.5 %collective-permute-done.10 = f32[2,32,256]{2,1,0:T(8,128)S(1)} collective-permute-done((f32[2,32,256]{2,1,0:T(8,128)S(1)}, f32[2,32,256]{2,1,0:T(8,128)S(1)}, u32[]{:S(2)}, u32[]{:S(2)}) %collective-permute-start.10) | collective-permute-done | bytes 65568 | tf_op jit(solution)/shard_map/sketch_reduce_gather/ppermute | solution.py:98
  146.2 1.1 collective-permute-start.11
  147.7 0.7 pad_maximum_fusion.12
  148.7 1.8 collective-permute-start.26
  150.5 1.1 collective-permute-start.19
  151.7 0.7 collective-permute-start.12
  152.4 1.3 collective-permute-start.5
  153.8 1.0 collective-permute-done.26
  154.8 1.1 collective-permute-done.19
  156.1 0.6 collective-permute-done.12
  156.9 0.6 collective-permute-done.5
  158.5 0.6 collective-permute-done.6
  159.2 4.5 %select_add_fusion = (f32[512,512]{1,0:T(8,128)}, f32[512,512]{1,0:T(8,128)S(1)}) fusion(f32[512,256]{1,0:T(8,128)S(1)} %bitcast.138, f32[512,256]{1,0:T(8,128)S(1)} %bitcast.139, f32[512,256]{1,0:T(8,128)S(1)} %bitcast.140, f32[512,256]{1,0:T(8,128)S(1)} %bitcast.141), kind=kOutput, calls=%fused_computation.20 | convolution fusion | flops 3223846912 | bytes 4194304 | tf_op jit(solution)/shard_map/kernel_matrix/dot_general | solution.py:181
  163.7 36.3 %kernel_solve.1 = f32[512,128]{1,0:T(8,128)} custom-call(f32[512,512]{1,0:T(8,128)} %get-tuple-element.34.m_ref, f32[512,128]{1,0:T(8,128)} %pad.4.w_ref), custom_call_target="tpu_custom_call" | custom-call | tf_op jit(solution)/shard_map/kernel_solve/pallas_call | solution.py:89
  200.1 2.1 %fusion.17 = f32[32,24]{0,1:T(8,128)} fusion(f32[512,128]{1,0:T(8,128)} %kernel_solve.1, f32[512,512]{1,0:T(8,128)S(1)} %get-tuple-element.35, s32[]{:T(128)S(6)} %select_n.298), kind=kOutput, calls=%fused_computation.26 | convolution fusion | flops 4718592 | bytes 330756 | tf_op jit(solution)/shard_map/dot_general | solution.py:188
  (102 shorter events, 5.8 us)
Async XLA Ops:
  5.3 7.7 %copy-start.1 = (s32[24]{0:T(128)S(1)}, s32[24]{0:T(128)}, u32[]{:S(2)}) copy-start(s32[24]{0:T(128)} %param.7) | copy-start | bytes 292
  5.3 7.8 %copy-start = (s32[24,128]{1,0:T(8,128)S(1)}, s32[24,128]{1,0:T(8,128)}, u32[]{:S(2)}) copy-start(s32[24,128]{1,0:T(8,128)} %param.6) | copy-start | bytes 36868
  5.3 85.3 %all-to-all-start = ((bf16[32,16,4096]{2,0,1:T(8,128)(2,1)}), bf16[32,16,4096]{2,0,1:T(8,128)(2,1)}, u32[]{:S(2)}, u32[]{:S(2)}) async-start(bf16[32,16,4096]{2,0,1:T(8,128)(2,1)} %bitcast.130), calls=%async_computation | async-start | bytes 8388608 | tf_op jit(solution)/shard_map/gradient_exchange/all_to_all | solution.py:145
  97.1 8.1 %collective-permute-start.21 = (f32[2,2,2,32,256]{4,3,2,1,0:T(8,128)S(1)}, f32[2,2,2,32,256]{4,3,2,1,0:T(8,128)S(1)}, u32[]{:S(2)}, u32[]{:S(2)}) collective-permute-start(f32[2,2,2,32,256]{4,3,2,1,0:T(8,128)S(1)} %bitcast.143), channel_id=1, source_target_pairs={{0,1},{1,0},{2,3},{3,2},{4,5},{5,4},{6,7},{7,6},{8,9},{9,8},{10,11... | collective-permute-start | bytes 786440 | tf_op jit(solution)/shard_map/sketch_reduce_gather/ppermute | solution.py:98
  104.3 15.8 %collective-permute-start.14 = (f32[2,2,2,32,256]{4,3,2,1,0:T(8,128)S(1)}, f32[2,2,2,32,256]{4,3,2,1,0:T(8,128)S(1)}, u32[]{:S(2)}, u32[]{:S(2)}) collective-permute-start(f32[2,2,2,32,256]{4,3,2,1,0:T(8,128)S(1)} %bitcast.142), channel_id=1, source_target_pairs={{0,1},{1,0},{2,3},{3,2},{4,5},{5,4},{6,7},{7,6},{8,9},{9,8},{10,11... | collective-permute-start | bytes 786440 | tf_op jit(solution)/shard_map/sketch_reduce_gather/ppermute | solution.py:98
  104.4 18.7 %collective-permute-start.7 = (f32[2,2,2,32,256]{4,3,2,0,1:T(8,128)S(1)}, f32[2,2,2,32,256]{4,3,2,0,1:T(8,128)S(1)}, u32[]{:S(2)}, u32[]{:S(2)}) collective-permute-start(f32[2,2,2,32,256]{4,3,2,0,1:T(8,128)S(1)} %copy.83), channel_id=1, source_target_pairs={{0,1},{1,0},{2,3},{3,2},{4,5},{5,4},{6,7},{7,6},{8,9},{9,8},{10,11... | collective-permute-start | bytes 786440 | tf_op jit(solution)/shard_map/sketch_reduce_gather/ppermute | solution.py:98
  105.1 18.6 %collective-permute-start = (f32[2,2,2,32,256]{4,3,1,0,2:T(8,128)S(1)}, f32[2,2,2,32,256]{4,3,1,0,2:T(8,128)S(1)}, u32[]{:S(2)}, u32[]{:S(2)}) collective-permute-start(f32[2,2,2,32,256]{4,3,1,0,2:T(8,128)S(1)} %copy.76), channel_id=1, source_target_pairs={{0,1},{1,0},{2,3},{3,2},{4,5},{5,4},{6,7},{7,6},{8,9},{9,8},{10,11... | collective-permute-start | bytes 786440 | tf_op jit(solution)/shard_map/sketch_reduce_gather/ppermute | solution.py:98
  105.2 18.8 %collective-permute-start.22 = (f32[2,2,32,256]{3,2,1,0:T(8,128)S(1)}, f32[2,2,32,256]{3,2,1,0:T(8,128)S(1)}, u32[]{:S(2)}, u32[]{:S(2)}) collective-permute-start(f32[2,2,32,256]{3,2,1,0:T(8,128)S(1)} %dynamic-slice_bitcast_fusion), channel_id=1, source_target_pairs={{0,4},{1,5},{2,6},{3,7},{4,0},{5,1},{6,2},{7,3},{8,12},{9,13},{10,... | collective-permute-start | bytes 393224 | tf_op jit(solution)/shard_map/sketch_reduce_gather/ppermute | solution.py:98
  120.1 9.2 %collective-permute-start.15 = (f32[2,2,32,256]{3,2,1,0:T(8,128)S(1)}, f32[2,2,32,256]{3,2,1,0:T(8,128)S(1)}, u32[]{:S(2)}, u32[]{:S(2)}) collective-permute-start(f32[2,2,32,256]{3,2,1,0:T(8,128)S(1)} %dynamic-slice_bitcast_fusion.1), channel_id=1, source_target_pairs={{0,2},{1,3},{2,0},{3,1},{4,6},{5,7},{6,4},{7,5},{8,10},{9,11},{10,... | collective-permute-start | bytes 393224 | tf_op jit(solution)/shard_map/sketch_reduce_gather/ppermute | solution.py:98
  123.2 6.4 %collective-permute-start.8 = (f32[2,2,32,256]{3,2,1,0:T(8,128)S(1)}, f32[2,2,32,256]{3,2,1,0:T(8,128)S(1)}, u32[]{:S(2)}, u32[]{:S(2)}) collective-permute-start(f32[2,2,32,256]{3,2,1,0:T(8,128)S(1)} %dynamic-slice_bitcast_fusion.2), channel_id=1, source_target_pairs={{0,4},{1,5},{2,6},{3,7},{4,0},{5,1},{6,2},{7,3},{8,12},{9,13},{10,... | collective-permute-start | bytes 393224 | tf_op jit(solution)/shard_map/sketch_reduce_gather/ppermute | solution.py:98
  123.7 7.4 %collective-permute-start.1 = (f32[2,2,32,256]{3,2,1,0:T(8,128)S(1)}, f32[2,2,32,256]{3,2,1,0:T(8,128)S(1)}, u32[]{:S(2)}, u32[]{:S(2)}) collective-permute-start(f32[2,2,32,256]{3,2,1,0:T(8,128)S(1)} %dynamic-slice_bitcast_fusion.3), channel_id=1, source_target_pairs={{0,2},{1,3},{2,0},{3,1},{4,6},{5,7},{6,4},{7,5},{8,10},{9,11},{10,... | collective-permute-start | bytes 393224 | tf_op jit(solution)/shard_map/sketch_reduce_gather/ppermute | solution.py:98
  124.1 10.2 %collective-permute-start.23 = (f32[2,32,256]{2,1,0:T(8,128)S(1)}, f32[2,32,256]{2,1,0:T(8,128)S(1)}, u32[]{:S(2)}, u32[]{:S(2)}) collective-permute-start(f32[2,32,256]{2,1,0:T(8,128)S(1)} %dynamic-slice_bitcast_fusion.4), channel_id=1, source_target_pairs={{0,8},{1,9},{2,10},{3,11},{4,12},{5,13},{6,14},{7,15},{8,0},{9,1},... | collective-permute-start | bytes 196616 | tf_op jit(solution)/shard_map/sketch_reduce_gather/ppermute | solution.py:98
  129.3 5.8 %collective-permute-start.16 = (f32[2,32,256]{2,1,0:T(8,128)S(1)}, f32[2,32,256]{2,1,0:T(8,128)S(1)}, u32[]{:S(2)}, u32[]{:S(2)}) collective-permute-start(f32[2,32,256]{2,1,0:T(8,128)S(1)} %dynamic-slice_bitcast_fusion.5), channel_id=1, source_target_pairs={{0,8},{1,9},{2,10},{3,11},{4,12},{5,13},{6,14},{7,15},{8,0},{9,1},... | collective-permute-start | bytes 196616 | tf_op jit(solution)/shard_map/sketch_reduce_gather/ppermute | solution.py:98
  129.6 5.6 %collective-permute-start.9 = (f32[2,32,256]{2,1,0:T(8,128)S(1)}, f32[2,32,256]{2,1,0:T(8,128)S(1)}, u32[]{:S(2)}, u32[]{:S(2)}) collective-permute-start(f32[2,32,256]{2,1,0:T(8,128)S(1)} %dynamic-slice_bitcast_fusion.6), channel_id=1, source_target_pairs={{0,2},{1,3},{2,0},{3,1},{4,6},{5,7},{6,4},{7,5},{8,10},{9,11},{10,... | collective-permute-start | bytes 196616 | tf_op jit(solution)/shard_map/sketch_reduce_gather/ppermute | solution.py:98
  131.1 7.2 %collective-permute-start.2 = (f32[2,32,256]{2,1,0:T(8,128)S(1)}, f32[2,32,256]{2,1,0:T(8,128)S(1)}, u32[]{:S(2)}, u32[]{:S(2)}) collective-permute-start(f32[2,32,256]{2,1,0:T(8,128)S(1)} %dynamic-slice_bitcast_fusion.7), channel_id=1, source_target_pairs={{0,4},{1,5},{2,6},{3,7},{4,0},{5,1},{6,2},{7,3},{8,12},{9,13},{10,... | collective-permute-start | bytes 196616 | tf_op jit(solution)/shard_map/sketch_reduce_gather/ppermute | solution.py:98
  134.3 4.3 %collective-permute-start.24 = (f32[2,32,256]{2,1,0:T(8,128)S(1)}, f32[2,32,256]{2,1,0:T(8,128)S(1)}, u32[]{:S(2)}, u32[]{:S(2)}) collective-permute-start(f32[2,32,256]{2,1,0:T(8,128)S(1)} %bitcast_add_fusion.4), channel_id=1, source_target_pairs={{0,2},{1,3},{2,0},{3,1},{4,6},{5,7},{6,4},{7,5},{8,10},{9,11},{10,... | collective-permute-start | bytes 196616 | tf_op jit(solution)/shard_map/sketch_reduce_gather/ppermute | solution.py:98
  135.1 6.3 %collective-permute-start.17 = (f32[2,32,256]{2,1,0:T(8,128)S(1)}, f32[2,32,256]{2,1,0:T(8,128)S(1)}, u32[]{:S(2)}, u32[]{:S(2)}) collective-permute-start(f32[2,32,256]{2,1,0:T(8,128)S(1)} %bitcast_add_fusion.5), channel_id=1, source_target_pairs={{0,4},{1,5},{2,6},{3,7},{4,0},{5,1},{6,2},{7,3},{8,12},{9,13},{10,... | collective-permute-start | bytes 196616 | tf_op jit(solution)/shard_map/sketch_reduce_gather/ppermute | solution.py:98
  135.2 11.0 %collective-permute-start.10 = (f32[2,32,256]{2,1,0:T(8,128)S(1)}, f32[2,32,256]{2,1,0:T(8,128)S(1)}, u32[]{:S(2)}, u32[]{:S(2)}) collective-permute-start(f32[2,32,256]{2,1,0:T(8,128)S(1)} %bitcast_add_fusion.6), channel_id=1, source_target_pairs={{0,8},{1,9},{2,10},{3,11},{4,12},{5,13},{6,14},{7,15},{8,0},{9,1},... | collective-permute-start | bytes 196616 | tf_op jit(solution)/shard_map/sketch_reduce_gather/ppermute | solution.py:98
  138.4 9.3 %collective-permute-start.3 = (f32[2,32,256]{2,1,0:T(8,128)S(1)}, f32[2,32,256]{2,1,0:T(8,128)S(1)}, u32[]{:S(2)}, u32[]{:S(2)}) collective-permute-start(f32[2,32,256]{2,1,0:T(8,128)S(1)} %bitcast_add_fusion.7), channel_id=1, source_target_pairs={{0,8},{1,9},{2,10},{3,11},{4,12},{5,13},{6,14},{7,15},{8,0},{9,1},... | collective-permute-start | bytes 196616 | tf_op jit(solution)/shard_map/sketch_reduce_gather/ppermute | solution.py:98
  138.6 10.1 %collective-permute-start.25 = (f32[2,32,256]{2,1,0:T(8,128)S(1)}, f32[2,32,256]{2,1,0:T(8,128)S(1)}, u32[]{:S(2)}, u32[]{:S(2)}) collective-permute-start(f32[2,32,256]{2,1,0:T(8,128)S(1)} %add.169), channel_id=1, source_target_pairs={{0,8},{1,9},{2,10},{3,11},{4,12},{5,13},{6,14},{7,15},{8,0},{9,1},... | collective-permute-start | bytes 196616 | tf_op jit(solution)/shard_map/sketch_reduce_gather/ppermute | solution.py:98
  141.4 9.1 %collective-permute-start.18 = (f32[2,32,256]{2,1,0:T(8,128)S(1)}, f32[2,32,256]{2,1,0:T(8,128)S(1)}, u32[]{:S(2)}, u32[]{:S(2)}) collective-permute-start(f32[2,32,256]{2,1,0:T(8,128)S(1)} %add.165), channel_id=1, source_target_pairs={{0,8},{1,9},{2,10},{3,11},{4,12},{5,13},{6,14},{7,15},{8,0},{9,1},... | collective-permute-start | bytes 196616 | tf_op jit(solution)/shard_map/sketch_reduce_gather/ppermute | solution.py:98
  146.2 5.4 %collective-permute-start.11 = (f32[2,32,256]{2,1,0:T(8,128)S(1)}, f32[2,32,256]{2,1,0:T(8,128)S(1)}, u32[]{:S(2)}, u32[]{:S(2)}) collective-permute-start(f32[2,32,256]{2,1,0:T(8,128)S(1)} %add.158), channel_id=1, source_target_pairs={{0,2},{1,3},{2,0},{3,1},{4,6},{5,7},{6,4},{7,5},{8,10},{9,11},{10,... | collective-permute-start | bytes 196616 | tf_op jit(solution)/shard_map/sketch_reduce_gather/ppermute | solution.py:98
  147.6 4.8 %collective-permute-start.4 = (f32[2,32,256]{2,1,0:T(8,128)S(1)}, f32[2,32,256]{2,1,0:T(8,128)S(1)}, u32[]{:S(2)}, u32[]{:S(2)}) collective-permute-start(f32[2,32,256]{2,1,0:T(8,128)S(1)} %add.154), channel_id=1, source_target_pairs={{0,4},{1,5},{2,6},{3,7},{4,0},{5,1},{6,2},{7,3},{8,12},{9,13},{10,... | collective-permute-start | bytes 196616 | tf_op jit(solution)/shard_map/sketch_reduce_gather/ppermute | solution.py:98
  148.7 6.0 %collective-permute-start.26 = (f32[2,2,32,256]{3,2,0,1:T(8,128)S(1)}, f32[2,2,32,256]{3,2,0,1:T(8,128)S(1)}, u32[]{:S(2)}, u32[]{:S(2)}) collective-permute-start(f32[2,2,32,256]{3,2,0,1:T(8,128)S(1)} %pad_maximum_fusion.11), channel_id=1, source_target_pairs={{0,4},{1,5},{2,6},{3,7},{4,0},{5,1},{6,2},{7,3},{8,12},{9,13},{10,... | collective-permute-start | bytes 393224 | tf_op jit(solution)/shard_map/sketch_reduce_gather/ppermute | solution.py:98
  150.5 5.5 %collective-permute-start.19 = (f32[2,2,32,256]{3,2,1,0:T(8,128)S(1)}, f32[2,2,32,256]{3,2,1,0:T(8,128)S(1)}, u32[]{:S(2)}, u32[]{:S(2)}) collective-permute-start(f32[2,2,32,256]{3,2,1,0:T(8,128)S(1)} %pad_maximum_fusion.10), channel_id=1, source_target_pairs={{0,2},{1,3},{2,0},{3,1},{4,6},{5,7},{6,4},{7,5},{8,10},{9,11},{10,... | collective-permute-start | bytes 393224 | tf_op jit(solution)/shard_map/sketch_reduce_gather/ppermute | solution.py:98
  151.7 5.0 %collective-permute-start.12 = (f32[2,2,32,256]{3,2,0,1:T(8,128)S(1)}, f32[2,2,32,256]{3,2,0,1:T(8,128)S(1)}, u32[]{:S(2)}, u32[]{:S(2)}) collective-permute-start(f32[2,2,32,256]{3,2,0,1:T(8,128)S(1)} %pad_maximum_fusion.9), channel_id=1, source_target_pairs={{0,4},{1,5},{2,6},{3,7},{4,0},{5,1},{6,2},{7,3},{8,12},{9,13},{10,... | collective-permute-start | bytes 393224 | tf_op jit(solution)/shard_map/sketch_reduce_gather/ppermute | solution.py:98
  152.4 5.0 %collective-permute-start.5 = (f32[2,2,32,256]{3,2,1,0:T(8,128)S(1)}, f32[2,2,32,256]{3,2,1,0:T(8,128)S(1)}, u32[]{:S(2)}, u32[]{:S(2)}) collective-permute-start(f32[2,2,32,256]{3,2,1,0:T(8,128)S(1)} %pad_maximum_fusion.8), channel_id=1, source_target_pairs={{0,2},{1,3},{2,0},{3,1},{4,6},{5,7},{6,4},{7,5},{8,10},{9,11},{10,... | collective-permute-start | bytes 393224 | tf_op jit(solution)/shard_map/sketch_reduce_gather/ppermute | solution.py:98
  154.8 2.8 %collective-permute-start.27 = (f32[2,2,2,32,256]{4,3,1,0,2:T(8,128)S(1)}, f32[2,2,2,32,256]{4,3,1,0,2:T(8,128)S(1)}, u32[]{:S(2)}, u32[]{:S(2)}) collective-permute-start(f32[2,2,2,32,256]{4,3,1,0,2:T(8,128)S(1)} %pad_maximum_fusion.7), channel_id=1, source_target_pairs={{0,1},{1,0},{2,3},{3,2},{4,5},{5,4},{6,7},{7,6},{8,9},{9,8},{10,11... | collective-permute-start | bytes 786440 | tf_op jit(solution)/shard_map/sketch_reduce_gather/ppermute | solution.py:98
  156.0 1.7 collective-permute-start.20
  156.8 1.6 collective-permute-start.13
  157.5 1.6 collective-permute-start.6

commit v12 on v10

--- a/solution.py
+++ b/solution.py
@@ -175,8 +175,9 @@
             lanes = -(-weight.shape[0] // 128) * 128
             rhs = jnp.pad(weight.T, ((0, 0), (0, lanes - weight.shape[0])))
             coeffs = spd_solve(system, rhs, block=min(128, examples))[:, : weight.shape[0]]
-        own_kernel = lax.dynamic_slice_in_dim(kernel, position * ex_rows, ex_rows, axis=0)
-        scores = jnp.dot(own_kernel, coeffs, precision=lax.Precision.HIGHEST)
+        own_weight = lax.dynamic_slice_in_dim(weight.T, position * ex_rows, ex_rows, axis=0)
+        own_coeffs = lax.dynamic_slice_in_dim(coeffs, position * ex_rows, ex_rows, axis=0)
+        scores = jnp.float32(examples) * (own_weight - 0.1 * own_coeffs)
     else:
         with jax.named_scope("gram_solve"):
             gram_matrix = jnp.dot(sketch_all.T, sketch_all, precision=lax.Precision.HIGHEST)

time: 199 us -> 198 us (level)
  matrix products: 14.8 us -> 12.7 us
    dot_general x1 -> x0, matrix products: 2.11 us -> none  [on_device(): scores = jnp.dot(own_kernel, coeffs, precision=lax.Precision.HIGHEST)]
where the time goes in v12:
time: 198 us
  waiting for transfers between devices  89.1 us (45%)
  starting transfers between devices  48 us (24%)
  Pallas kernels  36.2 us (18%)
  matrix products  12.7 us (6%)
  local copies, waits for them, and re-layouts  6.84 us (3%)
  other arithmetic  3.95 us (2%)
    all_to_all x1, waiting for transfers between devices, on_device(): lax.all_to_all(grads, 'ex', split_axis=1, concat_axis=0, tiled=True)  75.8 us
    ppermute x28, starting transfers between devices, partner(): lax.ppermute(array, axis, [(i, i ^ 1 << bit) for i in range(lax.axis_size...  40.5 us
    pallas_call x1, Pallas kernels, spd_solve(): pl.pallas_call(functools.partial(_solve_kernel, block=block), out_shape=j...  36.2 us
    ppermute x28, waiting for transfers between devices, partner(): lax.ppermute(array, axis, [(i, i ^ 1 << bit) for i in range(lax.axis_size...  13.3 us
    dot_general x1, matrix products, on_device(): partial_value = jnp.dot(columns, proj, preferred_element_type=jnp.float32)  8.14 us
    all_to_all x1, starting transfers between devices, on_device(): lax.all_to_all(grads, 'ex', split_axis=1, concat_axis=0, tiled=True)  7.57 us
    all_to_all x1, local copies, waits for them, and re-layouts, on_device(): lax.all_to_all(grads, 'ex', split_axis=1, concat_axis=0, tiled=True)  4.72 us
    dot_general x1, matrix products, on_device(): kernel = jnp.dot(sketch_all, sketch_all.T, precision=lax.Precision.HIGHEST)  4.53 us
  transfers between devices with their start and end apart: 29, of which 14 were waited for; matrix products, arithmetic and copies ran while one was open for 2% of the time, Pallas kernels for 0%

profile of v12, /device:TPU:0, one launch (start us, length us, event | category | flops | bytes accessed | tf_op | source)
XLA Modules:
  0.0 198.0 jit_solution(5992517944577413418)
XLA Ops:
  0.6 4.7 %copy.90 = bf16[4,16,8,4096]{3,2,0,1:T(8,128)(2,1)} copy(bf16[4,16,8,4096]{3,2,1,0:T(8,128)(2,1)} %bitcast.141) | data formatting | bytes 8388608 | tf_op jit(solution)/shard_map/gradient_exchange/all_to_all | solution.py:144
  5.3 7.6 %all-to-all-start = ((bf16[32,16,4096]{2,0,1:T(8,128)(2,1)}), bf16[32,16,4096]{2,0,1:T(8,128)(2,1)}, u32[]{:S(2)}, u32[]{:S(2)}) async-start(bf16[32,16,4096]{2,0,1:T(8,128)(2,1)} %bitcast.140), calls=%async_computation | async-start | bytes 8388608 | tf_op jit(solution)/shard_map/gradient_exchange/all_to_all | solution.py:144
  13.1 1.6 convert_reduce_fusion
  14.8 75.8 %all-to-all-done = bf16[32,16,4096]{2,0,1:T(8,128)(2,1)} async-done(((bf16[32,16,4096]{2,0,1:T(8,128)(2,1)}), bf16[32,16,4096]{2,0,1:T(8,128)(2,1)}, u32[]{:S(2)}, u32[]{:S(2)}) %all-to-all-start) | async-done | bytes 4194336 | tf_op jit(solution)/shard_map/gradient_exchange/all_to_all | solution.py:144
  90.6 8.1 %fusion.14 = f32[512,1024]{1,0:T(8,128)S(1)} fusion(bf16[512,4096]{1,0:T(8,128)(2,1)} %bitcast.2, bf16[4096,1024]{1,0:T(8,128)(2,1)} %param.5), kind=kOutput, calls=%fused_computation.89 | convolution fusion | flops 4294967296 | bytes 14680064 | tf_op jit(solution)/shard_map/partial_projection/dot_general | solution.py:146
  99.0 0.8 collective-permute-start.21
  99.8 0.7 pad.4.w_ref
  101.6 14.7 %collective-permute-start.22 = (f32[2,2,32,256]{3,2,1,0:T(8,128)S(1)}, f32[2,2,32,256]{3,2,1,0:T(8,128)S(1)}, u32[]{:S(2)}, u32[]{:S(2)}) collective-permute-start(f32[2,2,32,256]{3,2,1,0:T(8,128)S(1)} %dynamic-slice_bitcast_fusion.2), channel_id=1, source_target_pairs={{0,4},{1,5},{2,6},{3,7},{4,0},{5,1},{6,2},{7,3},{8,12},{9,13},{10,... | collective-permute-start | bytes 393224 | tf_op jit(solution)/shard_map/sketch_reduce_gather/ppermute | solution.py:98
  116.4 3.0 %collective-permute-start.15 = (f32[2,2,32,256]{3,2,1,0:T(8,128)S(1)}, f32[2,2,32,256]{3,2,1,0:T(8,128)S(1)}, u32[]{:S(2)}, u32[]{:S(2)}) collective-permute-start(f32[2,2,32,256]{3,2,1,0:T(8,128)S(1)} %dynamic-slice_bitcast_fusion.3), channel_id=1, source_target_pairs={{0,2},{1,3},{2,0},{3,1},{4,6},{5,7},{6,4},{7,5},{8,10},{9,11},{10,... | collective-permute-start | bytes 393224 | tf_op jit(solution)/shard_map/sketch_reduce_gather/ppermute | solution.py:98
  120.4 5.1 %collective-permute-start.23 = (f32[2,32,256]{2,1,0:T(8,128)S(1)}, f32[2,32,256]{2,1,0:T(8,128)S(1)}, u32[]{:S(2)}, u32[]{:S(2)}) collective-permute-start(f32[2,32,256]{2,1,0:T(8,128)S(1)} %dynamic-slice_bitcast_fusion.6), channel_id=1, source_target_pairs={{0,8},{1,9},{2,10},{3,11},{4,12},{5,13},{6,14},{7,15},{8,0},{9,1},... | collective-permute-start | bytes 196616 | tf_op jit(solution)/shard_map/sketch_reduce_gather/ppermute | solution.py:98
  125.9 1.3 collective-permute-start.9
  127.3 1.7 collective-permute-start.2
  128.9 1.6 collective-permute-done.23
  131.7 3.0 %collective-permute-start.10 = (f32[2,32,256]{2,1,0:T(8,128)S(1)}, f32[2,32,256]{2,1,0:T(8,128)S(1)}, u32[]{:S(2)}, u32[]{:S(2)}) collective-permute-start(f32[2,32,256]{2,1,0:T(8,128)S(1)} %bitcast_add_fusion.10), channel_id=1, source_target_pairs={{0,8},{1,9},{2,10},{3,11},{4,12},{5,13},{6,14},{7,15},{8,0},{9,1},... | collective-permute-start | bytes 196616 | tf_op jit(solution)/shard_map/sketch_reduce_gather/ppermute | solution.py:98
  134.9 2.8 %collective-permute-start.25 = (f32[2,32,256]{2,1,0:T(8,128)S(1)}, f32[2,32,256]{2,1,0:T(8,128)S(1)}, u32[]{:S(2)}, u32[]{:S(2)}) collective-permute-start(f32[2,32,256]{2,1,0:T(8,128)S(1)} %add.180), channel_id=1, source_target_pairs={{0,8},{1,9},{2,10},{3,11},{4,12},{5,13},{6,14},{7,15},{8,0},{9,1},... | collective-permute-start | bytes 196616 | tf_op jit(solution)/shard_map/sketch_reduce_gather/ppermute | solution.py:98
  138.0 5.0 %collective-permute-done.10 = f32[2,32,256]{2,1,0:T(8,128)S(1)} collective-permute-done((f32[2,32,256]{2,1,0:T(8,128)S(1)}, f32[2,32,256]{2,1,0:T(8,128)S(1)}, u32[]{:S(2)}, u32[]{:S(2)}) %collective-permute-start.10) | collective-permute-done | bytes 65568 | tf_op jit(solution)/shard_map/sketch_reduce_gather/ppermute | solution.py:98
  143.0 0.7 collective-permute-start.11
  143.7 0.7 collective-permute-done.3
  144.5 0.7 pad_maximum_fusion.12
  145.6 1.7 collective-permute-start.26
  147.3 0.8 collective-permute-start.19
  148.1 0.6 collective-permute-start.12
  149.1 1.1 collective-permute-start.5
  150.1 1.8 collective-permute-done.26
  152.1 0.5 collective-permute-done.19
  152.7 0.6 collective-permute-done.12
  153.5 0.7 collective-permute-done.5
  155.1 0.7 collective-permute-done.6
  155.9 4.5 %select_add_fusion.m_ref = f32[512,512]{1,0:T(8,128)} fusion(f32[512,256]{1,0:T(8,128)S(1)} %bitcast.148, f32[512,256]{1,0:T(8,128)S(1)} %bitcast.149, f32[512,256]{1,0:T(8,128)S(1)} %bitcast.150, f32[512,256]{1,0:T(8,128)S(1)} %bitcast.151), kind=kOutput, calls=%fused_computation.12 | convolution fusion | flops 3223846912 | bytes 3145728 | tf_op jit(solution)/shard_map/kernel_matrix/dot_general | solution.py:172
  160.4 36.2 %kernel_solve.1 = f32[512,128]{1,0:T(8,128)} custom-call(f32[512,512]{1,0:T(8,128)} %select_add_fusion.m_ref, f32[512,128]{1,0:T(8,128)} %pad.4.w_ref), custom_call_target="tpu_custom_call" | custom-call | tf_op jit(solution)/shard_map/kernel_solve/pallas_call | solution.py:89
  196.6 0.7 fusion.11
  197.3 0.7 copy.83
  (105 shorter events, 6.8 us)
Async XLA Ops:
  5.3 7.6 %copy-start.1 = (s32[24]{0:T(128)S(1)}, s32[24]{0:T(128)}, u32[]{:S(2)}) copy-start(s32[24]{0:T(128)} %param.7) | copy-start | bytes 292
  5.3 7.7 %copy-start = (s32[24,128]{1,0:T(8,128)S(1)}, s32[24,128]{1,0:T(8,128)}, u32[]{:S(2)}) copy-start(s32[24,128]{1,0:T(8,128)} %param.6) | copy-start | bytes 36868
  5.3 85.3 %all-to-all-start = ((bf16[32,16,4096]{2,0,1:T(8,128)(2,1)}), bf16[32,16,4096]{2,0,1:T(8,128)(2,1)}, u32[]{:S(2)}, u32[]{:S(2)}) async-start(bf16[32,16,4096]{2,0,1:T(8,128)(2,1)} %bitcast.140), calls=%async_computation | async-start | bytes 8388608 | tf_op jit(solution)/shard_map/gradient_exchange/all_to_all | solution.py:144
  99.0 2.6 %collective-permute-start.21 = (f32[2,2,2,32,256]{4,3,2,1,0:T(8,128)S(1)}, f32[2,2,2,32,256]{4,3,2,1,0:T(8,128)S(1)}, u32[]{:S(2)}, u32[]{:S(2)}) collective-permute-start(f32[2,2,2,32,256]{4,3,2,1,0:T(8,128)S(1)} %dynamic-slice_bitcast_fusion), channel_id=1, source_target_pairs={{0,1},{1,0},{2,3},{3,2},{4,5},{5,4},{6,7},{7,6},{8,9},{9,8},{10,11... | collective-permute-start | bytes 786440 | tf_op jit(solution)/shard_map/sketch_reduce_gather/ppermute | solution.py:98
  100.6 15.7 %collective-permute-start.14 = (f32[2,2,2,32,256]{4,3,2,1,0:T(8,128)S(1)}, f32[2,2,2,32,256]{4,3,2,1,0:T(8,128)S(1)}, u32[]{:S(2)}, u32[]{:S(2)}) collective-permute-start(f32[2,2,2,32,256]{4,3,2,1,0:T(8,128)S(1)} %dynamic-slice_bitcast_fusion.1), channel_id=1, source_target_pairs={{0,1},{1,0},{2,3},{3,2},{4,5},{5,4},{6,7},{7,6},{8,9},{9,8},{10,11... | collective-permute-start | bytes 786440 | tf_op jit(solution)/shard_map/sketch_reduce_gather/ppermute | solution.py:98
  100.9 18.5 %collective-permute-start.7 = (f32[2,2,2,32,256]{4,3,2,0,1:T(8,128)S(1)}, f32[2,2,2,32,256]{4,3,2,0,1:T(8,128)S(1)}, u32[]{:S(2)}, u32[]{:S(2)}) collective-permute-start(f32[2,2,2,32,256]{4,3,2,0,1:T(8,128)S(1)} %bitcast.154), channel_id=1, source_target_pairs={{0,1},{1,0},{2,3},{3,2},{4,5},{5,4},{6,7},{7,6},{8,9},{9,8},{10,11... | collective-permute-start | bytes 786440 | tf_op jit(solution)/shard_map/sketch_reduce_gather/ppermute | solution.py:98
  101.3 18.6 %collective-permute-start = (f32[2,2,2,32,256]{4,3,1,0,2:T(8,128)S(1)}, f32[2,2,2,32,256]{4,3,1,0,2:T(8,128)S(1)}, u32[]{:S(2)}, u32[]{:S(2)}) collective-permute-start(f32[2,2,2,32,256]{4,3,1,0,2:T(8,128)S(1)} %bitcast.153), channel_id=1, source_target_pairs={{0,1},{1,0},{2,3},{3,2},{4,5},{5,4},{6,7},{7,6},{8,9},{9,8},{10,11... | collective-permute-start | bytes 786440 | tf_op jit(solution)/shard_map/sketch_reduce_gather/ppermute | solution.py:98
  101.6 18.7 %collective-permute-start.22 = (f32[2,2,32,256]{3,2,1,0:T(8,128)S(1)}, f32[2,2,32,256]{3,2,1,0:T(8,128)S(1)}, u32[]{:S(2)}, u32[]{:S(2)}) collective-permute-start(f32[2,2,32,256]{3,2,1,0:T(8,128)S(1)} %dynamic-slice_bitcast_fusion.2), channel_id=1, source_target_pairs={{0,4},{1,5},{2,6},{3,7},{4,0},{5,1},{6,2},{7,3},{8,12},{9,13},{10,... | collective-permute-start | bytes 393224 | tf_op jit(solution)/shard_map/sketch_reduce_gather/ppermute | solution.py:98
  116.4 9.2 %collective-permute-start.15 = (f32[2,2,32,256]{3,2,1,0:T(8,128)S(1)}, f32[2,2,32,256]{3,2,1,0:T(8,128)S(1)}, u32[]{:S(2)}, u32[]{:S(2)}) collective-permute-start(f32[2,2,32,256]{3,2,1,0:T(8,128)S(1)} %dynamic-slice_bitcast_fusion.3), channel_id=1, source_target_pairs={{0,2},{1,3},{2,0},{3,1},{4,6},{5,7},{6,4},{7,5},{8,10},{9,11},{10,... | collective-permute-start | bytes 393224 | tf_op jit(solution)/shard_map/sketch_reduce_gather/ppermute | solution.py:98
  119.5 6.4 %collective-permute-start.8 = (f32[2,2,32,256]{3,2,1,0:T(8,128)S(1)}, f32[2,2,32,256]{3,2,1,0:T(8,128)S(1)}, u32[]{:S(2)}, u32[]{:S(2)}) collective-permute-start(f32[2,2,32,256]{3,2,1,0:T(8,128)S(1)} %dynamic-slice_bitcast_fusion.4), channel_id=1, source_target_pairs={{0,4},{1,5},{2,6},{3,7},{4,0},{5,1},{6,2},{7,3},{8,12},{9,13},{10,... | collective-permute-start | bytes 393224 | tf_op jit(solution)/shard_map/sketch_reduce_gather/ppermute | solution.py:98
  120.0 7.2 %collective-permute-start.1 = (f32[2,2,32,256]{3,2,1,0:T(8,128)S(1)}, f32[2,2,32,256]{3,2,1,0:T(8,128)S(1)}, u32[]{:S(2)}, u32[]{:S(2)}) collective-permute-start(f32[2,2,32,256]{3,2,1,0:T(8,128)S(1)} %dynamic-slice_bitcast_fusion.5), channel_id=1, source_target_pairs={{0,2},{1,3},{2,0},{3,1},{4,6},{5,7},{6,4},{7,5},{8,10},{9,11},{10,... | collective-permute-start | bytes 393224 | tf_op jit(solution)/shard_map/sketch_reduce_gather/ppermute | solution.py:98
  120.4 10.2 %collective-permute-start.23 = (f32[2,32,256]{2,1,0:T(8,128)S(1)}, f32[2,32,256]{2,1,0:T(8,128)S(1)}, u32[]{:S(2)}, u32[]{:S(2)}) collective-permute-start(f32[2,32,256]{2,1,0:T(8,128)S(1)} %dynamic-slice_bitcast_fusion.6), channel_id=1, source_target_pairs={{0,8},{1,9},{2,10},{3,11},{4,12},{5,13},{6,14},{7,15},{8,0},{9,1},... | collective-permute-start | bytes 196616 | tf_op jit(solution)/shard_map/sketch_reduce_gather/ppermute | solution.py:98
  125.6 6.0 %collective-permute-start.16 = (f32[2,32,256]{2,1,0:T(8,128)S(1)}, f32[2,32,256]{2,1,0:T(8,128)S(1)}, u32[]{:S(2)}, u32[]{:S(2)}) collective-permute-start(f32[2,32,256]{2,1,0:T(8,128)S(1)} %dynamic-slice_bitcast_fusion.7), channel_id=1, source_target_pairs={{0,8},{1,9},{2,10},{3,11},{4,12},{5,13},{6,14},{7,15},{8,0},{9,1},... | collective-permute-start | bytes 196616 | tf_op jit(solution)/shard_map/sketch_reduce_gather/ppermute | solution.py:98
  125.9 5.7 %collective-permute-start.9 = (f32[2,32,256]{2,1,0:T(8,128)S(1)}, f32[2,32,256]{2,1,0:T(8,128)S(1)}, u32[]{:S(2)}, u32[]{:S(2)}) collective-permute-start(f32[2,32,256]{2,1,0:T(8,128)S(1)} %dynamic-slice_bitcast_fusion.8), channel_id=1, source_target_pairs={{0,2},{1,3},{2,0},{3,1},{4,6},{5,7},{6,4},{7,5},{8,10},{9,11},{10,... | collective-permute-start | bytes 196616 | tf_op jit(solution)/shard_map/sketch_reduce_gather/ppermute | solution.py:98
  127.3 7.3 %collective-permute-start.2 = (f32[2,32,256]{2,1,0:T(8,128)S(1)}, f32[2,32,256]{2,1,0:T(8,128)S(1)}, u32[]{:S(2)}, u32[]{:S(2)}) collective-permute-start(f32[2,32,256]{2,1,0:T(8,128)S(1)} %dynamic-slice_bitcast_fusion.9), channel_id=1, source_target_pairs={{0,4},{1,5},{2,6},{3,7},{4,0},{5,1},{6,2},{7,3},{8,12},{9,13},{10,... | collective-permute-start | bytes 196616 | tf_op jit(solution)/shard_map/sketch_reduce_gather/ppermute | solution.py:98
  130.6 4.3 %collective-permute-start.24 = (f32[2,32,256]{2,1,0:T(8,128)S(1)}, f32[2,32,256]{2,1,0:T(8,128)S(1)}, u32[]{:S(2)}, u32[]{:S(2)}) collective-permute-start(f32[2,32,256]{2,1,0:T(8,128)S(1)} %bitcast_add_fusion.8), channel_id=1, source_target_pairs={{0,2},{1,3},{2,0},{3,1},{4,6},{5,7},{6,4},{7,5},{8,10},{9,11},{10,... | collective-permute-start | bytes 196616 | tf_op jit(solution)/shard_map/sketch_reduce_gather/ppermute | solution.py:98
  131.5 6.2 %collective-permute-start.17 = (f32[2,32,256]{2,1,0:T(8,128)S(1)}, f32[2,32,256]{2,1,0:T(8,128)S(1)}, u32[]{:S(2)}, u32[]{:S(2)}) collective-permute-start(f32[2,32,256]{2,1,0:T(8,128)S(1)} %bitcast_add_fusion.9), channel_id=1, source_target_pairs={{0,4},{1,5},{2,6},{3,7},{4,0},{5,1},{6,2},{7,3},{8,12},{9,13},{10,... | collective-permute-start | bytes 196616 | tf_op jit(solution)/shard_map/sketch_reduce_gather/ppermute | solution.py:98
  131.7 11.3 %collective-permute-start.10 = (f32[2,32,256]{2,1,0:T(8,128)S(1)}, f32[2,32,256]{2,1,0:T(8,128)S(1)}, u32[]{:S(2)}, u32[]{:S(2)}) collective-permute-start(f32[2,32,256]{2,1,0:T(8,128)S(1)} %bitcast_add_fusion.10), channel_id=1, source_target_pairs={{0,8},{1,9},{2,10},{3,11},{4,12},{5,13},{6,14},{7,15},{8,0},{9,1},... | collective-permute-start | bytes 196616 | tf_op jit(solution)/shard_map/sketch_reduce_gather/ppermute | solution.py:98
  134.6 9.8 %collective-permute-start.3 = (f32[2,32,256]{2,1,0:T(8,128)S(1)}, f32[2,32,256]{2,1,0:T(8,128)S(1)}, u32[]{:S(2)}, u32[]{:S(2)}) collective-permute-start(f32[2,32,256]{2,1,0:T(8,128)S(1)} %bitcast_add_fusion.11), channel_id=1, source_target_pairs={{0,8},{1,9},{2,10},{3,11},{4,12},{5,13},{6,14},{7,15},{8,0},{9,1},... | collective-permute-start | bytes 196616 | tf_op jit(solution)/shard_map/sketch_reduce_gather/ppermute | solution.py:98
  134.9 10.6 %collective-permute-start.25 = (f32[2,32,256]{2,1,0:T(8,128)S(1)}, f32[2,32,256]{2,1,0:T(8,128)S(1)}, u32[]{:S(2)}, u32[]{:S(2)}) collective-permute-start(f32[2,32,256]{2,1,0:T(8,128)S(1)} %add.180), channel_id=1, source_target_pairs={{0,8},{1,9},{2,10},{3,11},{4,12},{5,13},{6,14},{7,15},{8,0},{9,1},... | collective-permute-start | bytes 196616 | tf_op jit(solution)/shard_map/sketch_reduce_gather/ppermute | solution.py:98
  137.7 9.6 %collective-permute-start.18 = (f32[2,32,256]{2,1,0:T(8,128)S(1)}, f32[2,32,256]{2,1,0:T(8,128)S(1)}, u32[]{:S(2)}, u32[]{:S(2)}) collective-permute-start(f32[2,32,256]{2,1,0:T(8,128)S(1)} %add.176), channel_id=1, source_target_pairs={{0,8},{1,9},{2,10},{3,11},{4,12},{5,13},{6,14},{7,15},{8,0},{9,1},... | collective-permute-start | bytes 196616 | tf_op jit(solution)/shard_map/sketch_reduce_gather/ppermute | solution.py:98
  143.0 5.1 %collective-permute-start.11 = (f32[2,32,256]{2,1,0:T(8,128)S(1)}, f32[2,32,256]{2,1,0:T(8,128)S(1)}, u32[]{:S(2)}, u32[]{:S(2)}) collective-permute-start(f32[2,32,256]{2,1,0:T(8,128)S(1)} %add.169), channel_id=1, source_target_pairs={{0,2},{1,3},{2,0},{3,1},{4,6},{5,7},{6,4},{7,5},{8,10},{9,11},{10,... | collective-permute-start | bytes 196616 | tf_op jit(solution)/shard_map/sketch_reduce_gather/ppermute | solution.py:98
  144.4 4.6 %collective-permute-start.4 = (f32[2,32,256]{2,1,0:T(8,128)S(1)}, f32[2,32,256]{2,1,0:T(8,128)S(1)}, u32[]{:S(2)}, u32[]{:S(2)}) collective-permute-start(f32[2,32,256]{2,1,0:T(8,128)S(1)} %add.165), channel_id=1, source_target_pairs={{0,4},{1,5},{2,6},{3,7},{4,0},{5,1},{6,2},{7,3},{8,12},{9,13},{10,... | collective-permute-start | bytes 196616 | tf_op jit(solution)/shard_map/sketch_reduce_gather/ppermute | solution.py:98
  145.6 6.3 %collective-permute-start.26 = (f32[2,2,32,256]{3,2,0,1:T(8,128)S(1)}, f32[2,2,32,256]{3,2,0,1:T(8,128)S(1)}, u32[]{:S(2)}, u32[]{:S(2)}) collective-permute-start(f32[2,2,32,256]{3,2,0,1:T(8,128)S(1)} %pad_maximum_fusion.11), channel_id=1, source_target_pairs={{0,4},{1,5},{2,6},{3,7},{4,0},{5,1},{6,2},{7,3},{8,12},{9,13},{10,... | collective-permute-start | bytes 393224 | tf_op jit(solution)/shard_map/sketch_reduce_gather/ppermute | solution.py:98
  147.3 5.2 %collective-permute-start.19 = (f32[2,2,32,256]{3,2,1,0:T(8,128)S(1)}, f32[2,2,32,256]{3,2,1,0:T(8,128)S(1)}, u32[]{:S(2)}, u32[]{:S(2)}) collective-permute-start(f32[2,2,32,256]{3,2,1,0:T(8,128)S(1)} %pad_maximum_fusion.10), channel_id=1, source_target_pairs={{0,2},{1,3},{2,0},{3,1},{4,6},{5,7},{6,4},{7,5},{8,10},{9,11},{10,... | collective-permute-start | bytes 393224 | tf_op jit(solution)/shard_map/sketch_reduce_gather/ppermute | solution.py:98
  148.1 5.2 %collective-permute-start.12 = (f32[2,2,32,256]{3,2,0,1:T(8,128)S(1)}, f32[2,2,32,256]{3,2,0,1:T(8,128)S(1)}, u32[]{:S(2)}, u32[]{:S(2)}) collective-permute-start(f32[2,2,32,256]{3,2,0,1:T(8,128)S(1)} %pad_maximum_fusion.9), channel_id=1, source_target_pairs={{0,4},{1,5},{2,6},{3,7},{4,0},{5,1},{6,2},{7,3},{8,12},{9,13},{10,... | collective-permute-start | bytes 393224 | tf_op jit(solution)/shard_map/sketch_reduce_gather/ppermute | solution.py:98
  149.1 5.0 %collective-permute-start.5 = (f32[2,2,32,256]{3,2,1,0:T(8,128)S(1)}, f32[2,2,32,256]{3,2,1,0:T(8,128)S(1)}, u32[]{:S(2)}, u32[]{:S(2)}) collective-permute-start(f32[2,2,32,256]{3,2,1,0:T(8,128)S(1)} %pad_maximum_fusion.8), channel_id=1, source_target_pairs={{0,2},{1,3},{2,0},{3,1},{4,6},{5,7},{6,4},{7,5},{8,10},{9,11},{10,... | collective-permute-start | bytes 393224 | tf_op jit(solution)/shard_map/sketch_reduce_gather/ppermute | solution.py:98
  152.0 2.3 %collective-permute-start.27 = (f32[2,2,2,32,256]{4,3,1,0,2:T(8,128)S(1)}, f32[2,2,2,32,256]{4,3,1,0,2:T(8,128)S(1)}, u32[]{:S(2)}, u32[]{:S(2)}) collective-permute-start(f32[2,2,2,32,256]{4,3,1,0,2:T(8,128)S(1)} %pad_maximum_fusion.7), channel_id=1, source_target_pairs={{0,1},{1,0},{2,3},{3,2},{4,5},{5,4},{6,7},{7,6},{8,9},{9,8},{10,11... | collective-permute-start | bytes 786440 | tf_op jit(solution)/shard_map/sketch_reduce_gather/ppermute | solution.py:98
  152.6 1.8 collective-permute-start.20
  153.4 1.6 collective-permute-start.13
  154.2 1.6 collective-permute-start.6

commit v13 on v12

--- a/solution.py
+++ b/solution.py
@@ -98,12 +98,11 @@
     return lax.ppermute(array, axis, [(i, i ^ 1 << bit) for i in range(lax.axis_size(axis))])
 
 
-def reduce_and_gather(partial_value, order, position):
+def reduce_and_gather(value, order, position):
     bits = len(order)
-    rows = partial_value.shape[1:]
-    value = partial_value.reshape((2,) * bits + rows)
-    remaining = list(range(bits - 1, -1, -1))
-    for level in order[:-1]:
+    rows = value.shape[bits - 1:]
+    remaining = [level for level in range(bits - 1, -1, -1) if level != order[0]]
+    for level in order[1:-1]:
         axis = remaining.index(level)
         own_bit = position // 2**level % 2
         kept = lax.dynamic_index_in_dim(value, own_bit, axis=axis, keepdims=False)
@@ -140,10 +139,22 @@
     ex_rows = grads.shape[0]
     examples = ex_rows * count_ex
     sketch_width = proj.shape[1]
+    chips = count_ex // 2
+    own_low = position % 2
+    block_rows = proj.shape[0]
+    with jax.named_scope("projection_pair"):
+        sibling = partner(proj, "ex", 0)
+        low_rows = jnp.where(own_low == 0, proj, sibling)
+        high_rows = jnp.where(own_low == 0, sibling, proj)
     with jax.named_scope("gradient_exchange"):
-        columns = lax.all_to_all(grads, "ex", split_axis=1, concat_axis=0, tiled=True)
+        columns = lax.all_to_all(
+            grads, "ex", split_axis=1, concat_axis=0, tiled=True,
+            axis_index_groups=[[2 * chip + core for chip in range(chips)] for core in range(2)],
+        )
     with jax.named_scope("partial_projection"):
-        partial_value = jnp.dot(columns, proj, preferred_element_type=jnp.float32)
+        partial_value = jnp.dot(
+            columns[:, :block_rows], low_rows, preferred_element_type=jnp.float32
+        ) + jnp.dot(columns[:, block_rows:], high_rows, preferred_element_type=jnp.float32)
     orders = bit_orders(bits)
     width = sketch_width // len(orders)
     owned, gathered = [], []
@@ -151,7 +162,7 @@
         with jax.named_scope("sketch_reduce_gather"):
             part, every = reduce_and_gather(
                 partial_value[:, half * width:(half + 1) * width].reshape(
-                    count_ex, ex_rows, width
+                    (2,) * (bits - 1) + (ex_rows, width)
                 ),
                 order,
                 position,

time: 198 us -> 200 us (1.010)
  starting transfers between devices: 48 us -> 29.9 us
  waiting for transfers between devices: 89.1 us -> 105 us
  matrix products: 12.7 us -> 17.3 us
    ppermute x28 -> x25, starting transfers between devices: 40.5 us -> 22.9 us  [partner(): lax.ppermute(array, axis, [(i, i ^ 1 << bit) for i in range(lax.axis_size...]
    all_to_all x1, waiting for transfers between devices: 75.8 us -> 91.3 us  [on_device(): lax.all_to_all(grads, 'ex', split_axis=1, concat_axis=0, tiled=True, axis...]
    dot_general x1 -> x2, matrix products: 8.14 us -> 12.7 us  [the longest x1 6.37 us: on_device(): jnp.dot(columns[:, :block_rows], low_rows, preferred_element_type=jnp.flo...]
    ppermute x28 -> x25, waiting for transfers between devices: 13.3 us -> 13.9 us  [partner(): lax.ppermute(array, axis, [(i, i ^ 1 << bit) for i in range(lax.axis_size...]
  transfers between devices with their start and end apart: 29 -> 26, of which waited for: 14 -> 14; matrix products, arithmetic and copies ran while one was open for 2% -> 4% of each run, Pallas kernels for 0% -> 0%
where the time goes in v13:
time: 200 us
  waiting for transfers between devices  105 us (52%)
  Pallas kernels  36.3 us (18%)
  starting transfers between devices  29.9 us (15%)
  matrix products  17.3 us (9%)
  local copies, waits for them, and re-layouts  6.42 us (3%)
  other arithmetic  3.8 us (2%)
    all_to_all x1, waiting for transfers between devices, on_device(): lax.all_to_all(grads, 'ex', split_axis=1, concat_axis=0, tiled=True, axis...  91.3 us
    pallas_call x1, Pallas kernels, spd_solve(): pl.pallas_call(functools.partial(_solve_kernel, block=block), out_shape=j...  36.3 us
    ppermute x25, starting transfers between devices, partner(): lax.ppermute(array, axis, [(i, i ^ 1 << bit) for i in range(lax.axis_size...  22.9 us
    ppermute x25, waiting for transfers between devices, partner(): lax.ppermute(array, axis, [(i, i ^ 1 << bit) for i in range(lax.axis_size...  13.9 us
    all_to_all x1, starting transfers between devices, on_device(): lax.all_to_all(grads, 'ex', split_axis=1, concat_axis=0, tiled=True, axis...  6.98 us
    dot_general x1, matrix products, on_device(): jnp.dot(columns[:, :block_rows], low_rows, preferred_element_type=jnp.flo...  6.37 us
    dot_general x1, matrix products, on_device(): jnp.dot(columns[:, block_rows:], high_rows, preferred_element_type=jnp.fl...  6.37 us
    all_to_all x1, local copies, waits for them, and re-layouts, on_device(): lax.all_to_all(grads, 'ex', split_axis=1, concat_axis=0, tiled=True, axis...  4.55 us
  transfers between devices with their start and end apart: 26, of which 14 were waited for; matrix products, arithmetic and copies ran while one was open for 4% of the time, Pallas kernels for 0%

profile of v13, /device:TPU:0, one launch (start us, length us, event | category | flops | bytes accessed | tf_op | source)
XLA Modules:
  0.0 200.1 jit_solution(13920679090007541319)
XLA Ops:
  1.1 4.6 %copy.86 = bf16[4,8,8,8192]{3,2,0,1:T(8,128)(2,1)} copy(bf16[4,8,8,8192]{3,2,1,0:T(8,128)(2,1)} %bitcast.131) | data formatting | bytes 8388608 | tf_op jit(solution)/shard_map/gradient_exchange/all_to_all | solution.py:150
  5.7 7.0 %all-to-all-start = ((bf16[32,8,8192]{2,0,1:T(8,128)(2,1)}), bf16[32,8,8192]{2,0,1:T(8,128)(2,1)}, u32[]{:S(2)}, u32[]{:S(2)}) async-start(bf16[32,8,8192]{2,0,1:T(8,128)(2,1)} %bitcast.130), calls=%async_computation | async-start | bytes 8388608 | tf_op jit(solution)/shard_map/gradient_exchange/all_to_all | solution.py:150
  12.8 1.6 convert_reduce_fusion
  14.5 0.7 pad.4.w_ref
  15.3 91.3 %all-to-all-done = bf16[32,8,8192]{2,0,1:T(8,128)(2,1)} async-done(((bf16[32,8,8192]{2,0,1:T(8,128)(2,1)}), bf16[32,8,8192]{2,0,1:T(8,128)(2,1)}, u32[]{:S(2)}, u32[]{:S(2)}) %all-to-all-start) | async-done | bytes 4194336 | tf_op jit(solution)/shard_map/gradient_exchange/all_to_all | solution.py:150
  106.6 6.4 %fusion = f32[1024,256]{0,1:T(8,128)S(1)} fusion(bf16[4096,1024]{1,0:T(8,128)(2,1)} %collective-permute-done, bf16[4096,1024]{1,0:T(8,128)(2,1)} %param.5, pred[]{:T(512)S(6)} %eq.72, bf16[256,8192]{1,0:T(8,128)(2,1)} %bitcast.2), kind=kOutput, calls=%fused_computation | convolution fusion | flops 2151677952 | bytes 19922944 | tf_op jit(solution)/shard_map/partial_projection/dot_general | solution.py:157
  113.0 6.4 %fusion.22 = f32[256,1024]{1,0:T(8,128)S(1)} fusion(f32[1024,256]{0,1:T(8,128)S(1)} %fusion, bf16[4096,1024]{1,0:T(8,128)(2,1)} %param.5, bf16[4096,1024]{1,0:T(8,128)(2,1)} %collective-permute-done, pred[]{:T(512)S(6)} %eq.72, bf16[256,8192]{1,0:T(8,128)(2,1)} %bitcast.2), kind=kOutput, calls=%fused_computation.21 | convolution fusion | flops 2151940096 | bytes 20971520 | tf_op jit(solution)/shard_map/partial_projection/dot_general | solution.py:155
  119.6 1.5 collective-permute-start.13
  121.7 2.1 %collective-permute-start.19 = (f32[2,2,32,256]{3,2,1,0:T(8,128)S(1)}, f32[2,2,32,256]{3,2,1,0:T(8,128)S(1)}, u32[]{:S(2)}, u32[]{:S(2)}) collective-permute-start(f32[2,2,32,256]{3,2,1,0:T(8,128)S(1)} %dynamic-slice_bitcast_fusion), channel_id=1, source_target_pairs={{0,4},{1,5},{2,6},{3,7},{4,0},{5,1},{6,2},{7,3},{8,12},{9,13},{10,... | collective-permute-start | bytes 393224 | tf_op jit(solution)/shard_map/sketch_reduce_gather/ppermute | solution.py:98
  123.8 2.0 %collective-permute-done.7 = f32[2,2,32,256]{3,2,1,0:T(8,128)S(1)} collective-permute-done((f32[2,2,32,256]{3,2,1,0:T(8,128)S(1)}, f32[2,2,32,256]{3,2,1,0:T(8,128)S(1)}, u32[]{:S(2)}, u32[]{:S(2)}) %collective-permute-start.7) | collective-permute-done | bytes 131104 | tf_op jit(solution)/shard_map/sketch_reduce_gather/ppermute | solution.py:98
  125.9 1.5 collective-permute-start.8
  127.5 1.6 collective-permute-start.14
  129.1 0.8 collective-permute-start.2
  129.9 1.8 collective-permute-start.20
  131.7 1.2 collective-permute-start.9
  133.0 2.2 %collective-permute-done.14 = f32[2,32,256]{2,1,0:T(8,128)S(1)} collective-permute-done((f32[2,32,256]{2,1,0:T(8,128)S(1)}, f32[2,32,256]{2,1,0:T(8,128)S(1)}, u32[]{:S(2)}, u32[]{:S(2)}) %collective-permute-start.14) | collective-permute-done | bytes 65568 | tf_op jit(solution)/shard_map/sketch_reduce_gather/ppermute | solution.py:98
  135.3 1.3 collective-permute-start.3
  136.6 2.1 %collective-permute-done.20 = f32[2,32,256]{2,1,0:T(8,128)S(1)} collective-permute-done((f32[2,32,256]{2,1,0:T(8,128)S(1)}, f32[2,32,256]{2,1,0:T(8,128)S(1)}, u32[]{:S(2)}, u32[]{:S(2)}) %collective-permute-start.20) | collective-permute-done | bytes 65568 | tf_op jit(solution)/shard_map/sketch_reduce_gather/ppermute | solution.py:98
  138.8 0.9 collective-permute-start.21
  139.8 1.1 collective-permute-start.10
  140.9 0.9 collective-permute-done.15
  142.0 2.9 %collective-permute-start.4 = (f32[2,32,256]{2,1,0:T(8,128)S(1)}, f32[2,32,256]{2,1,0:T(8,128)S(1)}, u32[]{:S(2)}, u32[]{:S(2)}) collective-permute-start(f32[2,32,256]{2,1,0:T(8,128)S(1)} %add.141), channel_id=1, source_target_pairs={{0,4},{1,5},{2,6},{3,7},{4,0},{5,1},{6,2},{7,3},{8,12},{9,13},{10,... | collective-permute-start | bytes 196616 | tf_op jit(solution)/shard_map/sketch_reduce_gather/ppermute | solution.py:98
  145.8 2.0 %collective-permute-start.11 = (f32[2,2,32,256]{3,2,0,1:T(8,128)S(1)}, f32[2,2,32,256]{3,2,0,1:T(8,128)S(1)}, u32[]{:S(2)}, u32[]{:S(2)}) collective-permute-start(f32[2,2,32,256]{3,2,0,1:T(8,128)S(1)} %pad_maximum_fusion.9), channel_id=1, source_target_pairs={{0,4},{1,5},{2,6},{3,7},{4,0},{5,1},{6,2},{7,3},{8,12},{9,13},{10,... | collective-permute-start | bytes 393224 | tf_op jit(solution)/shard_map/sketch_reduce_gather/ppermute | solution.py:98
  149.1 1.4 collective-permute-start.5
  152.1 1.3 collective-permute-done.17
  153.5 1.3 collective-permute-done.5
  154.9 1.0 collective-permute-done.23
  156.4 1.2 collective-permute-done.24
  157.8 4.5 %select_add_fusion.m_ref = f32[512,512]{1,0:T(8,128)} fusion(f32[512,256]{1,0:T(8,128)S(1)} %bitcast.142, f32[512,256]{1,0:T(8,128)S(1)} %bitcast.141, f32[512,256]{1,0:T(8,128)S(1)} %bitcast.140, f32[512,256]{1,0:T(8,128)S(1)} %bitcast.143), kind=kOutput, calls=%fused_computation.22 | convolution fusion | flops 3223846912 | bytes 3145728 | tf_op jit(solution)/shard_map/kernel_matrix/dot_general | solution.py:183
  162.4 36.3 %kernel_solve.1 = f32[512,128]{1,0:T(8,128)} custom-call(f32[512,512]{1,0:T(8,128)} %select_add_fusion.m_ref, f32[512,128]{1,0:T(8,128)} %pad.4.w_ref), custom_call_target="tpu_custom_call" | custom-call | tf_op jit(solution)/shard_map/kernel_solve/pallas_call | solution.py:89
  198.7 0.7 fusion.29
  199.4 0.7 copy.79
  (91 shorter events, 6.5 us)
Async XLA Ops:
  0.6 106.0 %collective-permute-start = (bf16[4096,1024]{1,0:T(8,128)(2,1)}, bf16[4096,1024]{1,0:T(8,128)(2,1)}, u32[]{:S(2)}, u32[]{:S(2)}) collective-permute-start(bf16[4096,1024]{1,0:T(8,128)(2,1)} %param.5), channel_id=1, source_target_pairs={{0,1},{1,0},{2,3},{3,2},{4,5},{5,4},{6,7},{7,6},{8,9},{9,8},{10,11... | collective-permute-start | bytes 25165832 | tf_op jit(solution)/shard_map/projection_pair/ppermute | solution.py:98
  5.7 7.0 %copy-start.1 = (s32[24]{0:T(128)S(1)}, s32[24]{0:T(128)}, u32[]{:S(2)}) copy-start(s32[24]{0:T(128)} %param.7) | copy-start | bytes 292
  5.7 7.1 %copy-start = (s32[24,128]{1,0:T(8,128)S(1)}, s32[24,128]{1,0:T(8,128)}, u32[]{:S(2)}) copy-start(s32[24,128]{1,0:T(8,128)} %param.6) | copy-start | bytes 36868
  5.7 100.9 %all-to-all-start = ((bf16[32,8,8192]{2,0,1:T(8,128)(2,1)}), bf16[32,8,8192]{2,0,1:T(8,128)(2,1)}, u32[]{:S(2)}, u32[]{:S(2)}) async-start(bf16[32,8,8192]{2,0,1:T(8,128)(2,1)} %bitcast.130), calls=%async_computation | async-start | bytes 8388608 | tf_op jit(solution)/shard_map/gradient_exchange/all_to_all | solution.py:150
  119.5 6.3 %collective-permute-start.7 = (f32[2,2,32,256]{3,2,1,0:T(8,128)S(1)}, f32[2,2,32,256]{3,2,1,0:T(8,128)S(1)}, u32[]{:S(2)}, u32[]{:S(2)}) collective-permute-start(f32[2,2,32,256]{3,2,1,0:T(8,128)S(1)} %dynamic-slice_bitcast_fusion.2), channel_id=1, source_target_pairs={{0,4},{1,5},{2,6},{3,7},{4,0},{5,1},{6,2},{7,3},{8,12},{9,13},{10,... | collective-permute-start | bytes 393224 | tf_op jit(solution)/shard_map/sketch_reduce_gather/ppermute | solution.py:98
  119.6 7.8 %collective-permute-start.13 = (f32[2,2,32,256]{3,2,1,0:T(8,128)S(1)}, f32[2,2,32,256]{3,2,1,0:T(8,128)S(1)}, u32[]{:S(2)}, u32[]{:S(2)}) collective-permute-start(f32[2,2,32,256]{3,2,1,0:T(8,128)S(1)} %dynamic-slice_bitcast_fusion.1), channel_id=1, source_target_pairs={{0,2},{1,3},{2,0},{3,1},{4,6},{5,7},{6,4},{7,5},{8,10},{9,11},{10,... | collective-permute-start | bytes 393224 | tf_op jit(solution)/shard_map/sketch_reduce_gather/ppermute | solution.py:98
  121.2 7.9 %collective-permute-start.1 = (f32[2,2,32,256]{3,2,1,0:T(8,128)S(1)}, f32[2,2,32,256]{3,2,1,0:T(8,128)S(1)}, u32[]{:S(2)}, u32[]{:S(2)}) collective-permute-start(f32[2,2,32,256]{3,2,1,0:T(8,128)S(1)} %dynamic-slice_bitcast_fusion.3), channel_id=1, source_target_pairs={{0,2},{1,3},{2,0},{3,1},{4,6},{5,7},{6,4},{7,5},{8,10},{9,11},{10,... | collective-permute-start | bytes 393224 | tf_op jit(solution)/shard_map/sketch_reduce_gather/ppermute | solution.py:98
  121.7 8.1 %collective-permute-start.19 = (f32[2,2,32,256]{3,2,1,0:T(8,128)S(1)}, f32[2,2,32,256]{3,2,1,0:T(8,128)S(1)}, u32[]{:S(2)}, u32[]{:S(2)}) collective-permute-start(f32[2,2,32,256]{3,2,1,0:T(8,128)S(1)} %dynamic-slice_bitcast_fusion), channel_id=1, source_target_pairs={{0,4},{1,5},{2,6},{3,7},{4,0},{5,1},{6,2},{7,3},{8,12},{9,13},{10,... | collective-permute-start | bytes 393224 | tf_op jit(solution)/shard_map/sketch_reduce_gather/ppermute | solution.py:98
  125.9 5.8 %collective-permute-start.8 = (f32[2,32,256]{2,1,0:T(8,128)S(1)}, f32[2,32,256]{2,1,0:T(8,128)S(1)}, u32[]{:S(2)}, u32[]{:S(2)}) collective-permute-start(f32[2,32,256]{2,1,0:T(8,128)S(1)} %dynamic-slice_bitcast_fusion.6), channel_id=1, source_target_pairs={{0,2},{1,3},{2,0},{3,1},{4,6},{5,7},{6,4},{7,5},{8,10},{9,11},{10,... | collective-permute-start | bytes 196616 | tf_op jit(solution)/shard_map/sketch_reduce_gather/ppermute | solution.py:98
  127.5 7.7 %collective-permute-start.14 = (f32[2,32,256]{2,1,0:T(8,128)S(1)}, f32[2,32,256]{2,1,0:T(8,128)S(1)}, u32[]{:S(2)}, u32[]{:S(2)}) collective-permute-start(f32[2,32,256]{2,1,0:T(8,128)S(1)} %dynamic-slice_bitcast_fusion.5), channel_id=1, source_target_pairs={{0,8},{1,9},{2,10},{3,11},{4,12},{5,13},{6,14},{7,15},{8,0},{9,1},... | collective-permute-start | bytes 196616 | tf_op jit(solution)/shard_map/sketch_reduce_gather/ppermute | solution.py:98
  129.1 6.2 %collective-permute-start.2 = (f32[2,32,256]{2,1,0:T(8,128)S(1)}, f32[2,32,256]{2,1,0:T(8,128)S(1)}, u32[]{:S(2)}, u32[]{:S(2)}) collective-permute-start(f32[2,32,256]{2,1,0:T(8,128)S(1)} %dynamic-slice_bitcast_fusion.7), channel_id=1, source_target_pairs={{0,4},{1,5},{2,6},{3,7},{4,0},{5,1},{6,2},{7,3},{8,12},{9,13},{10,... | collective-permute-start | bytes 196616 | tf_op jit(solution)/shard_map/sketch_reduce_gather/ppermute | solution.py:98
  129.9 8.9 %collective-permute-start.20 = (f32[2,32,256]{2,1,0:T(8,128)S(1)}, f32[2,32,256]{2,1,0:T(8,128)S(1)}, u32[]{:S(2)}, u32[]{:S(2)}) collective-permute-start(f32[2,32,256]{2,1,0:T(8,128)S(1)} %dynamic-slice_bitcast_fusion.4), channel_id=1, source_target_pairs={{0,8},{1,9},{2,10},{3,11},{4,12},{5,13},{6,14},{7,15},{8,0},{9,1},... | collective-permute-start | bytes 196616 | tf_op jit(solution)/shard_map/sketch_reduce_gather/ppermute | solution.py:98
  131.7 8.1 %collective-permute-start.9 = (f32[2,32,256]{2,1,0:T(8,128)S(1)}, f32[2,32,256]{2,1,0:T(8,128)S(1)}, u32[]{:S(2)}, u32[]{:S(2)}) collective-permute-start(f32[2,32,256]{2,1,0:T(8,128)S(1)} %bitcast_add_fusion.6), channel_id=1, source_target_pairs={{0,8},{1,9},{2,10},{3,11},{4,12},{5,13},{6,14},{7,15},{8,0},{9,1},... | collective-permute-start | bytes 196616 | tf_op jit(solution)/shard_map/sketch_reduce_gather/ppermute | solution.py:98
  135.2 6.6 %collective-permute-start.15 = (f32[2,32,256]{2,1,0:T(8,128)S(1)}, f32[2,32,256]{2,1,0:T(8,128)S(1)}, u32[]{:S(2)}, u32[]{:S(2)}) collective-permute-start(f32[2,32,256]{2,1,0:T(8,128)S(1)} %bitcast_add_fusion.5), channel_id=1, source_target_pairs={{0,4},{1,5},{2,6},{3,7},{4,0},{5,1},{6,2},{7,3},{8,12},{9,13},{10,... | collective-permute-start | bytes 196616 | tf_op jit(solution)/shard_map/sketch_reduce_gather/ppermute | solution.py:98
  135.3 6.6 %collective-permute-start.3 = (f32[2,32,256]{2,1,0:T(8,128)S(1)}, f32[2,32,256]{2,1,0:T(8,128)S(1)}, u32[]{:S(2)}, u32[]{:S(2)}) collective-permute-start(f32[2,32,256]{2,1,0:T(8,128)S(1)} %bitcast_add_fusion.7), channel_id=1, source_target_pairs={{0,8},{1,9},{2,10},{3,11},{4,12},{5,13},{6,14},{7,15},{8,0},{9,1},... | collective-permute-start | bytes 196616 | tf_op jit(solution)/shard_map/sketch_reduce_gather/ppermute | solution.py:98
  138.8 6.1 %collective-permute-start.21 = (f32[2,32,256]{2,1,0:T(8,128)S(1)}, f32[2,32,256]{2,1,0:T(8,128)S(1)}, u32[]{:S(2)}, u32[]{:S(2)}) collective-permute-start(f32[2,32,256]{2,1,0:T(8,128)S(1)} %bitcast_add_fusion.4), channel_id=1, source_target_pairs={{0,2},{1,3},{2,0},{3,1},{4,6},{5,7},{6,4},{7,5},{8,10},{9,11},{10,... | collective-permute-start | bytes 196616 | tf_op jit(solution)/shard_map/sketch_reduce_gather/ppermute | solution.py:98
  139.8 5.9 %collective-permute-start.10 = (f32[2,32,256]{2,1,0:T(8,128)S(1)}, f32[2,32,256]{2,1,0:T(8,128)S(1)}, u32[]{:S(2)}, u32[]{:S(2)}) collective-permute-start(f32[2,32,256]{2,1,0:T(8,128)S(1)} %add.144), channel_id=1, source_target_pairs={{0,2},{1,3},{2,0},{3,1},{4,6},{5,7},{6,4},{7,5},{8,10},{9,11},{10,... | collective-permute-start | bytes 196616 | tf_op jit(solution)/shard_map/sketch_reduce_gather/ppermute | solution.py:98
  141.8 6.5 %collective-permute-start.16 = (f32[2,32,256]{2,1,0:T(8,128)S(1)}, f32[2,32,256]{2,1,0:T(8,128)S(1)}, u32[]{:S(2)}, u32[]{:S(2)}) collective-permute-start(f32[2,32,256]{2,1,0:T(8,128)S(1)} %add.150), channel_id=1, source_target_pairs={{0,8},{1,9},{2,10},{3,11},{4,12},{5,13},{6,14},{7,15},{8,0},{9,1},... | collective-permute-start | bytes 196616 | tf_op jit(solution)/shard_map/sketch_reduce_gather/ppermute | solution.py:98
  142.0 7.1 %collective-permute-start.4 = (f32[2,32,256]{2,1,0:T(8,128)S(1)}, f32[2,32,256]{2,1,0:T(8,128)S(1)}, u32[]{:S(2)}, u32[]{:S(2)}) collective-permute-start(f32[2,32,256]{2,1,0:T(8,128)S(1)} %add.141), channel_id=1, source_target_pairs={{0,4},{1,5},{2,6},{3,7},{4,0},{5,1},{6,2},{7,3},{8,12},{9,13},{10,... | collective-permute-start | bytes 196616 | tf_op jit(solution)/shard_map/sketch_reduce_gather/ppermute | solution.py:98
  144.9 6.0 %collective-permute-start.22 = (f32[2,32,256]{2,1,0:T(8,128)S(1)}, f32[2,32,256]{2,1,0:T(8,128)S(1)}, u32[]{:S(2)}, u32[]{:S(2)}) collective-permute-start(f32[2,32,256]{2,1,0:T(8,128)S(1)} %add.153), channel_id=1, source_target_pairs={{0,8},{1,9},{2,10},{3,11},{4,12},{5,13},{6,14},{7,15},{8,0},{9,1},... | collective-permute-start | bytes 196616 | tf_op jit(solution)/shard_map/sketch_reduce_gather/ppermute | solution.py:98
  145.8 6.2 %collective-permute-start.11 = (f32[2,2,32,256]{3,2,0,1:T(8,128)S(1)}, f32[2,2,32,256]{3,2,0,1:T(8,128)S(1)}, u32[]{:S(2)}, u32[]{:S(2)}) collective-permute-start(f32[2,2,32,256]{3,2,0,1:T(8,128)S(1)} %pad_maximum_fusion.9), channel_id=1, source_target_pairs={{0,4},{1,5},{2,6},{3,7},{4,0},{5,1},{6,2},{7,3},{8,12},{9,13},{10,... | collective-permute-start | bytes 393224 | tf_op jit(solution)/shard_map/sketch_reduce_gather/ppermute | solution.py:98
  148.3 5.0 %collective-permute-start.17 = (f32[2,2,32,256]{3,2,1,0:T(8,128)S(1)}, f32[2,2,32,256]{3,2,1,0:T(8,128)S(1)}, u32[]{:S(2)}, u32[]{:S(2)}) collective-permute-start(f32[2,2,32,256]{3,2,1,0:T(8,128)S(1)} %pad_maximum_fusion.10), channel_id=1, source_target_pairs={{0,2},{1,3},{2,0},{3,1},{4,6},{5,7},{6,4},{7,5},{8,10},{9,11},{10,... | collective-permute-start | bytes 393224 | tf_op jit(solution)/shard_map/sketch_reduce_gather/ppermute | solution.py:98
  149.1 5.7 %collective-permute-start.5 = (f32[2,2,32,256]{3,2,1,0:T(8,128)S(1)}, f32[2,2,32,256]{3,2,1,0:T(8,128)S(1)}, u32[]{:S(2)}, u32[]{:S(2)}) collective-permute-start(f32[2,2,32,256]{3,2,1,0:T(8,128)S(1)} %pad_maximum_fusion.8), channel_id=1, source_target_pairs={{0,2},{1,3},{2,0},{3,1},{4,6},{5,7},{6,4},{7,5},{8,10},{9,11},{10,... | collective-permute-start | bytes 393224 | tf_op jit(solution)/shard_map/sketch_reduce_gather/ppermute | solution.py:98
  150.9 5.0 %collective-permute-start.23 = (f32[2,2,32,256]{3,2,0,1:T(8,128)S(1)}, f32[2,2,32,256]{3,2,0,1:T(8,128)S(1)}, u32[]{:S(2)}, u32[]{:S(2)}) collective-permute-start(f32[2,2,32,256]{3,2,0,1:T(8,128)S(1)} %pad_maximum_fusion.11), channel_id=1, source_target_pairs={{0,4},{1,5},{2,6},{3,7},{4,0},{5,1},{6,2},{7,3},{8,12},{9,13},{10,... | collective-permute-start | bytes 393224 | tf_op jit(solution)/shard_map/sketch_reduce_gather/ppermute | solution.py:98
  152.0 4.1 %collective-permute-start.12 = (f32[2,2,2,32,256]{4,3,0,2,1:T(8,128)S(1)}, f32[2,2,2,32,256]{4,3,0,2,1:T(8,128)S(1)}, u32[]{:S(2)}, u32[]{:S(2)}) collective-permute-start(f32[2,2,2,32,256]{4,3,0,2,1:T(8,128)S(1)} %pad_maximum_fusion.5), channel_id=1, source_target_pairs={{0,1},{1,0},{2,3},{3,2},{4,5},{5,4},{6,7},{7,6},{8,9},{9,8},{10,11... | collective-permute-start | bytes 786440 | tf_op jit(solution)/shard_map/sketch_reduce_gather/ppermute | solution.py:98
  153.4 2.8 %collective-permute-start.18 = (f32[2,2,2,32,256]{4,3,1,0,2:T(8,128)S(1)}, f32[2,2,2,32,256]{4,3,1,0,2:T(8,128)S(1)}, u32[]{:S(2)}, u32[]{:S(2)}) collective-permute-start(f32[2,2,2,32,256]{4,3,1,0,2:T(8,128)S(1)} %pad_maximum_fusion.6), channel_id=1, source_target_pairs={{0,1},{1,0},{2,3},{3,2},{4,5},{5,4},{6,7},{7,6},{8,9},{9,8},{10,11... | collective-permute-start | bytes 786440 | tf_op jit(solution)/shard_map/sketch_reduce_gather/ppermute | solution.py:98
  154.8 2.9 %collective-permute-start.6 = (f32[2,2,2,32,256]{4,3,2,1,0:T(8,128)S(1)}, f32[2,2,2,32,256]{4,3,2,1,0:T(8,128)S(1)}, u32[]{:S(2)}, u32[]{:S(2)}) collective-permute-start(f32[2,2,2,32,256]{4,3,2,1,0:T(8,128)S(1)} %pad_maximum_fusion.4), channel_id=1, source_target_pairs={{0,1},{1,0},{2,3},{3,2},{4,5},{5,4},{6,7},{7,6},{8,9},{9,8},{10,11... | collective-permute-start | bytes 786440 | tf_op jit(solution)/shard_map/sketch_reduce_gather/ppermute | solution.py:98
  156.0 1.6 collective-permute-start.24

commit v14 on v13

--- a/solution.py
+++ b/solution.py
@@ -151,6 +151,7 @@
             grads, "ex", split_axis=1, concat_axis=0, tiled=True,
             axis_index_groups=[[2 * chip + core for chip in range(chips)] for core in range(2)],
         )
+    columns, low_rows, high_rows = lax.optimization_barrier((columns, low_rows, high_rows))
     with jax.named_scope("partial_projection"):
         partial_value = jnp.dot(
             columns[:, :block_rows], low_rows, preferred_element_type=jnp.float32

time: 200 us -> 198 us (0.990)
  other arithmetic: 3.8 us -> 15.2 us
  waiting for transfers between devices: 105 us -> 94.3 us
  matrix products: 17.3 us -> 14.9 us
    all_to_all x1, waiting for transfers between devices: 91.3 us -> 79.9 us  [on_device(): lax.all_to_all(grads, 'ex', split_axis=1, concat_axis=0, tiled=True, axis...]
    select_n x0 -> x1, other arithmetic: none -> 11.4 us  [on_device(): high_rows = jnp.where(own_low == 0, sibling, proj)]
    dot_general x1, matrix products: 6.37 us -> 3.92 us  [on_device(): jnp.dot(columns[:, :block_rows], low_rows, preferred_element_type=jnp.flo...]
  transfers between devices with their start and end apart: 26 -> 26, of which waited for: 14 -> 12; matrix products, arithmetic and copies ran while one was open for 4% -> 10% of each run, Pallas kernels for 0% -> 0%
where the time goes in v14:
time: 198 us
  waiting for transfers between devices  94.3 us (48%)
  Pallas kernels  36.3 us (18%)
  starting transfers between devices  29.2 us (15%)
  other arithmetic  15.2 us (8%)
  matrix products  14.9 us (8%)
  local copies, waits for them, and re-layouts  6.47 us (3%)
    all_to_all x1, waiting for transfers between devices, on_device(): lax.all_to_all(grads, 'ex', split_axis=1, concat_axis=0, tiled=True, axis...  79.9 us
    pallas_call x1, Pallas kernels, spd_solve(): pl.pallas_call(functools.partial(_solve_kernel, block=block), out_shape=j...  36.3 us
    ppermute x25, starting transfers between devices, partner(): lax.ppermute(array, axis, [(i, i ^ 1 << bit) for i in range(lax.axis_size...  22.2 us
    ppermute x25, waiting for transfers between devices, partner(): lax.ppermute(array, axis, [(i, i ^ 1 << bit) for i in range(lax.axis_size...  14.4 us
    select_n x1, other arithmetic, on_device(): high_rows = jnp.where(own_low == 0, sibling, proj)  11.4 us
    all_to_all x1, starting transfers between devices, on_device(): lax.all_to_all(grads, 'ex', split_axis=1, concat_axis=0, tiled=True, axis...  6.98 us
    dot_general x1, matrix products, on_device(): jnp.dot(columns[:, block_rows:], high_rows, preferred_element_type=jnp.fl...  6.48 us
    all_to_all x1, local copies, waits for them, and re-layouts, on_device(): lax.all_to_all(grads, 'ex', split_axis=1, concat_axis=0, tiled=True, axis...  4.61 us
  transfers between devices with their start and end apart: 26, of which 12 were waited for; matrix products, arithmetic and copies ran while one was open for 10% of the time, Pallas kernels for 0%

profile of v14, /device:TPU:0, one launch (start us, length us, event | category | flops | bytes accessed | tf_op | source)
XLA Modules:
  0.0 197.6 jit_solution(17717056578083854843)
XLA Ops:
  1.1 4.6 %copy.86 = bf16[4,8,8,8192]{3,2,0,1:T(8,128)(2,1)} copy(bf16[4,8,8,8192]{3,2,1,0:T(8,128)(2,1)} %bitcast.131) | data formatting | bytes 8388608 | tf_op jit(solution)/shard_map/gradient_exchange/all_to_all | solution.py:150
  5.8 7.0 %all-to-all-start = ((bf16[32,8,8192]{2,0,1:T(8,128)(2,1)}), bf16[32,8,8192]{2,0,1:T(8,128)(2,1)}, u32[]{:S(2)}, u32[]{:S(2)}) async-start(bf16[32,8,8192]{2,0,1:T(8,128)(2,1)} %bitcast.130), calls=%async_computation | async-start | bytes 8388608 | tf_op jit(solution)/shard_map/gradient_exchange/all_to_all | solution.py:150
  12.8 1.6 convert_reduce_fusion
  14.6 0.7 pad.4.w_ref
  15.4 11.4 %broadcast_select_fusion = (bf16[4096,1024]{1,0:T(8,128)(2,1)}, bf16[4096,1024]{1,0:T(8,128)(2,1)}) fusion(bf16[4096,1024]{1,0:T(8,128)(2,1)} %collective-permute-done, bf16[4096,1024]{1,0:T(8,128)(2,1)} %param.5, pred[]{:T(512)S(6)} %eq.72), kind=kLoop, calls=%fused_computation | loop fusion | flops 8388608 | bytes 33554432 | tf_op jit(solution)/shard_map/projection_pair/jit(_where)/select_n | solution.py:148
  26.8 79.9 %all-to-all-done = bf16[32,8,8192]{2,0,1:T(8,128)(2,1)} async-done(((bf16[32,8,8192]{2,0,1:T(8,128)(2,1)}), bf16[32,8,8192]{2,0,1:T(8,128)(2,1)}, u32[]{:S(2)}, u32[]{:S(2)}) %all-to-all-start) | async-done | bytes 4194336 | tf_op jit(solution)/shard_map/gradient_exchange/all_to_all | solution.py:150
  106.7 6.5 %fusion.9 = f32[256,1024]{1,0:T(8,128)S(1)} fusion(bf16[4096,1024]{1,0:T(8,128)(2,1)} %get-tuple-element.7, bf16[256,8192]{1,0:T(8,128)(2,1)} %bitcast.2), kind=kOutput, calls=%fused_computation.14 | convolution fusion | flops 2147483648 | bytes 11534336 | tf_op jit(solution)/shard_map/partial_projection/dot_general | solution.py:158
  113.2 3.9 %fusion.13 = f32[256,1024]{1,0:T(8,128)S(1)} fusion(f32[256,1024]{1,0:T(8,128)S(1)} %fusion.9, bf16[4096,1024]{1,0:T(8,128)(2,1)S(1)} %copy-done, bf16[256,8192]{1,0:T(8,128)(2,1)} %bitcast.2), kind=kOutput, calls=%fused_computation.18 | convolution fusion | flops 2147745792 | bytes 12582912 | tf_op jit(solution)/shard_map/partial_projection/dot_general | solution.py:156
  117.2 1.5 collective-permute-start.1
  119.5 2.1 %collective-permute-start.19 = (f32[2,2,32,256]{3,2,1,0:T(8,128)S(1)}, f32[2,2,32,256]{3,2,1,0:T(8,128)S(1)}, u32[]{:S(2)}, u32[]{:S(2)}) collective-permute-start(f32[2,2,32,256]{3,2,1,0:T(8,128)S(1)} %dynamic-slice_bitcast_fusion), channel_id=1, source_target_pairs={{0,4},{1,5},{2,6},{3,7},{4,0},{5,1},{6,2},{7,3},{8,12},{9,13},{10,... | collective-permute-start | bytes 393224 | tf_op jit(solution)/shard_map/sketch_reduce_gather/ppermute | solution.py:98
  121.6 1.9 collective-permute-done.1
  123.6 1.7 collective-permute-done.7
  126.0 1.5 collective-permute-start.14
  127.5 1.6 collective-permute-start.20
  129.1 1.5 collective-permute-start.3
  130.6 1.6 collective-permute-start.9
  132.2 3.8 %collective-permute-done.14 = f32[2,32,256]{2,1,0:T(8,128)S(1)} collective-permute-done((f32[2,32,256]{2,1,0:T(8,128)S(1)}, f32[2,32,256]{2,1,0:T(8,128)S(1)}, u32[]{:S(2)}, u32[]{:S(2)}) %collective-permute-start.14) | collective-permute-done | bytes 65568 | tf_op jit(solution)/shard_map/sketch_reduce_gather/ppermute | solution.py:98
  136.1 1.5 collective-permute-done.20
  137.6 1.2 collective-permute-start.21
  138.8 1.0 collective-permute-start.4
  140.4 2.0 %collective-permute-start.16 = (f32[2,32,256]{2,1,0:T(8,128)S(1)}, f32[2,32,256]{2,1,0:T(8,128)S(1)}, u32[]{:S(2)}, u32[]{:S(2)}) collective-permute-start(f32[2,32,256]{2,1,0:T(8,128)S(1)} %add.146), channel_id=1, source_target_pairs={{0,8},{1,9},{2,10},{3,11},{4,12},{5,13},{6,14},{7,15},{8,0},{9,1},... | collective-permute-start | bytes 196616 | tf_op jit(solution)/shard_map/sketch_reduce_gather/ppermute | solution.py:98
  142.5 1.0 collective-permute-start.22
  144.2 1.6 collective-permute-start.5
  145.8 1.2 collective-permute-start.11
  147.1 0.9 collective-permute-start.17
  148.4 0.7 collective-permute-start.23
  149.4 1.5 collective-permute-done.11
  151.0 1.1 collective-permute-done.17
  152.3 1.2 collective-permute-done.23
  153.9 1.2 collective-permute-done.24
  155.3 4.5 %select_add_fusion.m_ref = f32[512,512]{1,0:T(8,128)} fusion(f32[512,256]{1,0:T(8,128)S(1)} %bitcast.142, f32[512,256]{1,0:T(8,128)S(1)} %bitcast.141, f32[512,256]{1,0:T(8,128)S(1)} %bitcast.140, f32[512,256]{1,0:T(8,128)S(1)} %bitcast.143), kind=kOutput, calls=%fused_computation.19 | convolution fusion | flops 3223846912 | bytes 3145728 | tf_op jit(solution)/shard_map/kernel_matrix/dot_general | solution.py:184
  159.9 36.3 %kernel_solve.1 = f32[512,128]{1,0:T(8,128)} custom-call(f32[512,512]{1,0:T(8,128)} %select_add_fusion.m_ref, f32[512,128]{1,0:T(8,128)} %pad.4.w_ref), custom_call_target="tpu_custom_call" | custom-call | tf_op jit(solution)/shard_map/kernel_solve/pallas_call | solution.py:89
  (94 shorter events, 6.8 us)
Async XLA Ops:
  0.6 14.7 %collective-permute-start = (bf16[4096,1024]{1,0:T(8,128)(2,1)}, bf16[4096,1024]{1,0:T(8,128)(2,1)}, u32[]{:S(2)}, u32[]{:S(2)}) collective-permute-start(bf16[4096,1024]{1,0:T(8,128)(2,1)} %param.5), channel_id=1, source_target_pairs={{0,1},{1,0},{2,3},{3,2},{4,5},{5,4},{6,7},{7,6},{8,9},{9,8},{10,11... | collective-permute-start | bytes 25165832 | tf_op jit(solution)/shard_map/projection_pair/ppermute | solution.py:98
  5.8 7.0 %copy-start.2 = (s32[24]{0:T(128)S(1)}, s32[24]{0:T(128)}, u32[]{:S(2)}) copy-start(s32[24]{0:T(128)} %param.7) | copy-start | bytes 292
  5.8 7.1 %copy-start.1 = (s32[24,128]{1,0:T(8,128)S(1)}, s32[24,128]{1,0:T(8,128)}, u32[]{:S(2)}) copy-start(s32[24,128]{1,0:T(8,128)} %param.6) | copy-start | bytes 36868
  5.8 100.9 %all-to-all-start = ((bf16[32,8,8192]{2,0,1:T(8,128)(2,1)}), bf16[32,8,8192]{2,0,1:T(8,128)(2,1)}, u32[]{:S(2)}, u32[]{:S(2)}) async-start(bf16[32,8,8192]{2,0,1:T(8,128)(2,1)} %bitcast.130), calls=%async_computation | async-start | bytes 8388608 | tf_op jit(solution)/shard_map/gradient_exchange/all_to_all | solution.py:150
  106.7 6.5 %copy-start = (bf16[4096,1024]{1,0:T(8,128)(2,1)S(1)}, bf16[4096,1024]{1,0:T(8,128)(2,1)}, u32[]{:S(2)}) copy-start(bf16[4096,1024]{1,0:T(8,128)(2,1)} %get-tuple-element.6) | copy-start | bytes 25165828
  117.2 6.3 %collective-permute-start.1 = (f32[2,2,32,256]{3,2,1,0:T(8,128)S(1)}, f32[2,2,32,256]{3,2,1,0:T(8,128)S(1)}, u32[]{:S(2)}, u32[]{:S(2)}) collective-permute-start(f32[2,2,32,256]{3,2,1,0:T(8,128)S(1)} %dynamic-slice_bitcast_fusion.3), channel_id=1, source_target_pairs={{0,2},{1,3},{2,0},{3,1},{4,6},{5,7},{6,4},{7,5},{8,10},{9,11},{10,... | collective-permute-start | bytes 393224 | tf_op jit(solution)/shard_map/sketch_reduce_gather/ppermute | solution.py:98
  118.8 6.5 %collective-permute-start.7 = (f32[2,2,32,256]{3,2,1,0:T(8,128)S(1)}, f32[2,2,32,256]{3,2,1,0:T(8,128)S(1)}, u32[]{:S(2)}, u32[]{:S(2)}) collective-permute-start(f32[2,2,32,256]{3,2,1,0:T(8,128)S(1)} %dynamic-slice_bitcast_fusion.2), channel_id=1, source_target_pairs={{0,4},{1,5},{2,6},{3,7},{4,0},{5,1},{6,2},{7,3},{8,12},{9,13},{10,... | collective-permute-start | bytes 393224 | tf_op jit(solution)/shard_map/sketch_reduce_gather/ppermute | solution.py:98
  118.9 7.1 %collective-permute-start.13 = (f32[2,2,32,256]{3,2,1,0:T(8,128)S(1)}, f32[2,2,32,256]{3,2,1,0:T(8,128)S(1)}, u32[]{:S(2)}, u32[]{:S(2)}) collective-permute-start(f32[2,2,32,256]{3,2,1,0:T(8,128)S(1)} %dynamic-slice_bitcast_fusion.1), channel_id=1, source_target_pairs={{0,2},{1,3},{2,0},{3,1},{4,6},{5,7},{6,4},{7,5},{8,10},{9,11},{10,... | collective-permute-start | bytes 393224 | tf_op jit(solution)/shard_map/sketch_reduce_gather/ppermute | solution.py:98
  119.5 8.0 %collective-permute-start.19 = (f32[2,2,32,256]{3,2,1,0:T(8,128)S(1)}, f32[2,2,32,256]{3,2,1,0:T(8,128)S(1)}, u32[]{:S(2)}, u32[]{:S(2)}) collective-permute-start(f32[2,2,32,256]{3,2,1,0:T(8,128)S(1)} %dynamic-slice_bitcast_fusion), channel_id=1, source_target_pairs={{0,4},{1,5},{2,6},{3,7},{4,0},{5,1},{6,2},{7,3},{8,12},{9,13},{10,... | collective-permute-start | bytes 393224 | tf_op jit(solution)/shard_map/sketch_reduce_gather/ppermute | solution.py:98
  123.5 5.6 %collective-permute-start.2 = (f32[2,32,256]{2,1,0:T(8,128)S(1)}, f32[2,32,256]{2,1,0:T(8,128)S(1)}, u32[]{:S(2)}, u32[]{:S(2)}) collective-permute-start(f32[2,32,256]{2,1,0:T(8,128)S(1)} %dynamic-slice_bitcast_fusion.7), channel_id=1, source_target_pairs={{0,4},{1,5},{2,6},{3,7},{4,0},{5,1},{6,2},{7,3},{8,12},{9,13},{10,... | collective-permute-start | bytes 196616 | tf_op jit(solution)/shard_map/sketch_reduce_gather/ppermute | solution.py:98
  125.3 5.3 %collective-permute-start.8 = (f32[2,32,256]{2,1,0:T(8,128)S(1)}, f32[2,32,256]{2,1,0:T(8,128)S(1)}, u32[]{:S(2)}, u32[]{:S(2)}) collective-permute-start(f32[2,32,256]{2,1,0:T(8,128)S(1)} %dynamic-slice_bitcast_fusion.6), channel_id=1, source_target_pairs={{0,2},{1,3},{2,0},{3,1},{4,6},{5,7},{6,4},{7,5},{8,10},{9,11},{10,... | collective-permute-start | bytes 196616 | tf_op jit(solution)/shard_map/sketch_reduce_gather/ppermute | solution.py:98
  126.0 10.0 %collective-permute-start.14 = (f32[2,32,256]{2,1,0:T(8,128)S(1)}, f32[2,32,256]{2,1,0:T(8,128)S(1)}, u32[]{:S(2)}, u32[]{:S(2)}) collective-permute-start(f32[2,32,256]{2,1,0:T(8,128)S(1)} %dynamic-slice_bitcast_fusion.5), channel_id=1, source_target_pairs={{0,8},{1,9},{2,10},{3,11},{4,12},{5,13},{6,14},{7,15},{8,0},{9,1},... | collective-permute-start | bytes 196616 | tf_op jit(solution)/shard_map/sketch_reduce_gather/ppermute | solution.py:98
  127.5 10.1 %collective-permute-start.20 = (f32[2,32,256]{2,1,0:T(8,128)S(1)}, f32[2,32,256]{2,1,0:T(8,128)S(1)}, u32[]{:S(2)}, u32[]{:S(2)}) collective-permute-start(f32[2,32,256]{2,1,0:T(8,128)S(1)} %dynamic-slice_bitcast_fusion.4), channel_id=1, source_target_pairs={{0,8},{1,9},{2,10},{3,11},{4,12},{5,13},{6,14},{7,15},{8,0},{9,1},... | collective-permute-start | bytes 196616 | tf_op jit(solution)/shard_map/sketch_reduce_gather/ppermute | solution.py:98
  129.1 9.7 %collective-permute-start.3 = (f32[2,32,256]{2,1,0:T(8,128)S(1)}, f32[2,32,256]{2,1,0:T(8,128)S(1)}, u32[]{:S(2)}, u32[]{:S(2)}) collective-permute-start(f32[2,32,256]{2,1,0:T(8,128)S(1)} %bitcast_add_fusion.7), channel_id=1, source_target_pairs={{0,8},{1,9},{2,10},{3,11},{4,12},{5,13},{6,14},{7,15},{8,0},{9,1},... | collective-permute-start | bytes 196616 | tf_op jit(solution)/shard_map/sketch_reduce_gather/ppermute | solution.py:98
  130.6 9.2 %collective-permute-start.9 = (f32[2,32,256]{2,1,0:T(8,128)S(1)}, f32[2,32,256]{2,1,0:T(8,128)S(1)}, u32[]{:S(2)}, u32[]{:S(2)}) collective-permute-start(f32[2,32,256]{2,1,0:T(8,128)S(1)} %bitcast_add_fusion.6), channel_id=1, source_target_pairs={{0,8},{1,9},{2,10},{3,11},{4,12},{5,13},{6,14},{7,15},{8,0},{9,1},... | collective-permute-start | bytes 196616 | tf_op jit(solution)/shard_map/sketch_reduce_gather/ppermute | solution.py:98
  136.0 4.4 %collective-permute-start.15 = (f32[2,32,256]{2,1,0:T(8,128)S(1)}, f32[2,32,256]{2,1,0:T(8,128)S(1)}, u32[]{:S(2)}, u32[]{:S(2)}) collective-permute-start(f32[2,32,256]{2,1,0:T(8,128)S(1)} %bitcast_add_fusion.5), channel_id=1, source_target_pairs={{0,4},{1,5},{2,6},{3,7},{4,0},{5,1},{6,2},{7,3},{8,12},{9,13},{10,... | collective-permute-start | bytes 196616 | tf_op jit(solution)/shard_map/sketch_reduce_gather/ppermute | solution.py:98
  137.6 4.8 %collective-permute-start.21 = (f32[2,32,256]{2,1,0:T(8,128)S(1)}, f32[2,32,256]{2,1,0:T(8,128)S(1)}, u32[]{:S(2)}, u32[]{:S(2)}) collective-permute-start(f32[2,32,256]{2,1,0:T(8,128)S(1)} %bitcast_add_fusion.4), channel_id=1, source_target_pairs={{0,2},{1,3},{2,0},{3,1},{4,6},{5,7},{6,4},{7,5},{8,10},{9,11},{10,... | collective-permute-start | bytes 196616 | tf_op jit(solution)/shard_map/sketch_reduce_gather/ppermute | solution.py:98
  138.8 5.4 %collective-permute-start.4 = (f32[2,32,256]{2,1,0:T(8,128)S(1)}, f32[2,32,256]{2,1,0:T(8,128)S(1)}, u32[]{:S(2)}, u32[]{:S(2)}) collective-permute-start(f32[2,32,256]{2,1,0:T(8,128)S(1)} %add.137), channel_id=1, source_target_pairs={{0,4},{1,5},{2,6},{3,7},{4,0},{5,1},{6,2},{7,3},{8,12},{9,13},{10,... | collective-permute-start | bytes 196616 | tf_op jit(solution)/shard_map/sketch_reduce_gather/ppermute | solution.py:98
  139.8 6.0 %collective-permute-start.10 = (f32[2,32,256]{2,1,0:T(8,128)S(1)}, f32[2,32,256]{2,1,0:T(8,128)S(1)}, u32[]{:S(2)}, u32[]{:S(2)}) collective-permute-start(f32[2,32,256]{2,1,0:T(8,128)S(1)} %add.140), channel_id=1, source_target_pairs={{0,2},{1,3},{2,0},{3,1},{4,6},{5,7},{6,4},{7,5},{8,10},{9,11},{10,... | collective-permute-start | bytes 196616 | tf_op jit(solution)/shard_map/sketch_reduce_gather/ppermute | solution.py:98
  140.4 6.6 %collective-permute-start.16 = (f32[2,32,256]{2,1,0:T(8,128)S(1)}, f32[2,32,256]{2,1,0:T(8,128)S(1)}, u32[]{:S(2)}, u32[]{:S(2)}) collective-permute-start(f32[2,32,256]{2,1,0:T(8,128)S(1)} %add.146), channel_id=1, source_target_pairs={{0,8},{1,9},{2,10},{3,11},{4,12},{5,13},{6,14},{7,15},{8,0},{9,1},... | collective-permute-start | bytes 196616 | tf_op jit(solution)/shard_map/sketch_reduce_gather/ppermute | solution.py:98
  142.5 5.9 %collective-permute-start.22 = (f32[2,32,256]{2,1,0:T(8,128)S(1)}, f32[2,32,256]{2,1,0:T(8,128)S(1)}, u32[]{:S(2)}, u32[]{:S(2)}) collective-permute-start(f32[2,32,256]{2,1,0:T(8,128)S(1)} %add.149), channel_id=1, source_target_pairs={{0,8},{1,9},{2,10},{3,11},{4,12},{5,13},{6,14},{7,15},{8,0},{9,1},... | collective-permute-start | bytes 196616 | tf_op jit(solution)/shard_map/sketch_reduce_gather/ppermute | solution.py:98
  144.2 5.0 %collective-permute-start.5 = (f32[2,2,32,256]{3,2,1,0:T(8,128)S(1)}, f32[2,2,32,256]{3,2,1,0:T(8,128)S(1)}, u32[]{:S(2)}, u32[]{:S(2)}) collective-permute-start(f32[2,2,32,256]{3,2,1,0:T(8,128)S(1)} %pad_maximum_fusion.8), channel_id=1, source_target_pairs={{0,2},{1,3},{2,0},{3,1},{4,6},{5,7},{6,4},{7,5},{8,10},{9,11},{10,... | collective-permute-start | bytes 393224 | tf_op jit(solution)/shard_map/sketch_reduce_gather/ppermute | solution.py:98
  145.8 5.0 %collective-permute-start.11 = (f32[2,2,32,256]{3,2,0,1:T(8,128)S(1)}, f32[2,2,32,256]{3,2,0,1:T(8,128)S(1)}, u32[]{:S(2)}, u32[]{:S(2)}) collective-permute-start(f32[2,2,32,256]{3,2,0,1:T(8,128)S(1)} %pad_maximum_fusion.9), channel_id=1, source_target_pairs={{0,4},{1,5},{2,6},{3,7},{4,0},{5,1},{6,2},{7,3},{8,12},{9,13},{10,... | collective-permute-start | bytes 393224 | tf_op jit(solution)/shard_map/sketch_reduce_gather/ppermute | solution.py:98
  147.1 5.0 %collective-permute-start.17 = (f32[2,2,32,256]{3,2,1,0:T(8,128)S(1)}, f32[2,2,32,256]{3,2,1,0:T(8,128)S(1)}, u32[]{:S(2)}, u32[]{:S(2)}) collective-permute-start(f32[2,2,32,256]{3,2,1,0:T(8,128)S(1)} %pad_maximum_fusion.10), channel_id=1, source_target_pairs={{0,2},{1,3},{2,0},{3,1},{4,6},{5,7},{6,4},{7,5},{8,10},{9,11},{10,... | collective-permute-start | bytes 393224 | tf_op jit(solution)/shard_map/sketch_reduce_gather/ppermute | solution.py:98
  148.4 5.0 %collective-permute-start.23 = (f32[2,2,32,256]{3,2,0,1:T(8,128)S(1)}, f32[2,2,32,256]{3,2,0,1:T(8,128)S(1)}, u32[]{:S(2)}, u32[]{:S(2)}) collective-permute-start(f32[2,2,32,256]{3,2,0,1:T(8,128)S(1)} %pad_maximum_fusion.11), channel_id=1, source_target_pairs={{0,4},{1,5},{2,6},{3,7},{4,0},{5,1},{6,2},{7,3},{8,12},{9,13},{10,... | collective-permute-start | bytes 393224 | tf_op jit(solution)/shard_map/sketch_reduce_gather/ppermute | solution.py:98
  149.3 5.9 %collective-permute-start.6 = (f32[2,2,2,32,256]{4,3,2,1,0:T(8,128)S(1)}, f32[2,2,2,32,256]{4,3,2,1,0:T(8,128)S(1)}, u32[]{:S(2)}, u32[]{:S(2)}) collective-permute-start(f32[2,2,2,32,256]{4,3,2,1,0:T(8,128)S(1)} %pad_maximum_fusion.4), channel_id=1, source_target_pairs={{0,1},{1,0},{2,3},{3,2},{4,5},{5,4},{6,7},{7,6},{8,9},{9,8},{10,11... | collective-permute-start | bytes 786440 | tf_op jit(solution)/shard_map/sketch_reduce_gather/ppermute | solution.py:98
  150.9 2.6 %collective-permute-start.12 = (f32[2,2,2,32,256]{4,3,0,2,1:T(8,128)S(1)}, f32[2,2,2,32,256]{4,3,0,2,1:T(8,128)S(1)}, u32[]{:S(2)}, u32[]{:S(2)}) collective-permute-start(f32[2,2,2,32,256]{4,3,0,2,1:T(8,128)S(1)} %pad_maximum_fusion.5), channel_id=1, source_target_pairs={{0,1},{1,0},{2,3},{3,2},{4,5},{5,4},{6,7},{7,6},{8,9},{9,8},{10,11... | collective-permute-start | bytes 786440 | tf_op jit(solution)/shard_map/sketch_reduce_gather/ppermute | solution.py:98
  152.2 1.6 collective-permute-start.18
  153.5 1.6 collective-permute-start.24

commit v15 on v12

--- a/solution.py
+++ b/solution.py
@@ -130,7 +130,9 @@
     if bits < 4:
         return [first]
     rest = list(range(4, bits))
-    return [[0, 1, 2, 3] + rest, [0, 2, 1, 3] + rest, [0, 1, 3, 2] + rest, [0, 2, 3, 1] + rest]
+    return [order + rest for order in (
+        [0, 1, 2, 3], [0, 2, 1, 3], [0, 1, 3, 2], [0, 2, 3, 1],
+        [0, 3, 1, 2], [0, 3, 2, 1], [0, 1, 2, 3], [0, 2, 1, 3])]
 
 
 def on_device(grads, proj, target_ids, target_counts):

time: 198 us -> 220 us (1.11)
  starting transfers between devices: 48 us -> 76.7 us
  waiting for transfers between devices: 89.1 us -> 81.8 us
    ppermute x28 -> x56, starting transfers between devices: 40.5 us -> 69.1 us  [partner(): lax.ppermute(array, axis, [(i, i ^ 1 << bit) for i in range(lax.axis_size...]
    ppermute x28 -> x56, waiting for transfers between devices: 13.3 us -> 6.9 us  [partner(): lax.ppermute(array, axis, [(i, i ^ 1 << bit) for i in range(lax.axis_size...]
  transfers between devices with their start and end apart: 29 -> 57, of which waited for: 14 -> 8; matrix products, arithmetic and copies ran while one was open for 2% -> 2% of each run, Pallas kernels for 0% -> 0%
where the time goes in v15:
time: 220 us
  waiting for transfers between devices  81.8 us (37%)
  starting transfers between devices  76.7 us (35%)
  Pallas kernels  36.2 us (16%)
  matrix products  12.8 us (6%)
  local copies, waits for them, and re-layouts  7.18 us (3%)
  other arithmetic  3.38 us (2%)
    all_to_all x1, waiting for transfers between devices, on_device(): lax.all_to_all(grads, 'ex', split_axis=1, concat_axis=0, tiled=True)  74.9 us
    ppermute x56, starting transfers between devices, partner(): lax.ppermute(array, axis, [(i, i ^ 1 << bit) for i in range(lax.axis_size...  69.1 us
    pallas_call x1, Pallas kernels, spd_solve(): pl.pallas_call(functools.partial(_solve_kernel, block=block), out_shape=j...  36.2 us
    dot_general x1, matrix products, on_device(): partial_value = jnp.dot(columns, proj, preferred_element_type=jnp.float32)  8.33 us
    all_to_all x1, starting transfers between devices, on_device(): lax.all_to_all(grads, 'ex', split_axis=1, concat_axis=0, tiled=True)  7.57 us
    ppermute x56, waiting for transfers between devices, partner(): lax.ppermute(array, axis, [(i, i ^ 1 << bit) for i in range(lax.axis_size...  6.9 us
    all_to_all x1, local copies, waits for them, and re-layouts, on_device(): lax.all_to_all(grads, 'ex', split_axis=1, concat_axis=0, tiled=True)  4.72 us
    dot_general x1, matrix products, on_device(): kernel = jnp.dot(sketch_all, sketch_all.T, precision=lax.Precision.HIGHEST)  4.52 us
  transfers between devices with their start and end apart: 57, of which 8 were waited for; matrix products, arithmetic and copies ran while one was open for 2% of the time, Pallas kernels for 0%

profile of v15, /device:TPU:0, one launch (start us, length us, event | category | flops | bytes accessed | tf_op | source)
XLA Modules:
  0.0 220.0 jit_solution(1885702004867115759)
XLA Ops:
  0.6 4.7 %copy.199 = bf16[4,16,8,4096]{3,2,0,1:T(8,128)(2,1)} copy(bf16[4,16,8,4096]{3,2,1,0:T(8,128)(2,1)} %bitcast.259) | data formatting | bytes 8388608 | tf_op jit(solution)/shard_map/gradient_exchange/all_to_all | solution.py:146
  5.4 7.6 %all-to-all-start = ((bf16[32,16,4096]{2,0,1:T(8,128)(2,1)}), bf16[32,16,4096]{2,0,1:T(8,128)(2,1)}, u32[]{:S(2)}, u32[]{:S(2)}) async-start(bf16[32,16,4096]{2,0,1:T(8,128)(2,1)} %bitcast.258), calls=%async_computation | async-start | bytes 8388608 | tf_op jit(solution)/shard_map/gradient_exchange/all_to_all | solution.py:146
  13.2 1.6 convert_reduce_fusion
  15.7 74.9 %all-to-all-done = bf16[32,16,4096]{2,0,1:T(8,128)(2,1)} async-done(((bf16[32,16,4096]{2,0,1:T(8,128)(2,1)}), bf16[32,16,4096]{2,0,1:T(8,128)(2,1)}, u32[]{:S(2)}, u32[]{:S(2)}) %all-to-all-start) | async-done | bytes 4194336 | tf_op jit(solution)/shard_map/gradient_exchange/all_to_all | solution.py:146
  90.6 8.3 %fusion.5 = f32[512,1024]{1,0:T(8,128)S(1)} fusion(bf16[512,4096]{1,0:T(8,128)(2,1)} %bitcast.2, bf16[4096,1024]{1,0:T(8,128)(2,1)} %param.5), kind=kOutput, calls=%fused_computation.157 | convolution fusion | flops 4294967296 | bytes 14680064 | tf_op jit(solution)/shard_map/partial_projection/dot_general | solution.py:148
  102.3 6.2 %collective-permute-start.1 = (f32[2,2,32,128]{3,2,1,0:T(8,128)S(1)}, f32[2,2,32,128]{3,2,1,0:T(8,128)S(1)}, u32[]{:S(2)}, u32[]{:S(2)}) collective-permute-start(f32[2,2,32,128]{3,2,1,0:T(8,128)S(1)} %dynamic-slice_bitcast_fusion.11), channel_id=1, source_target_pairs={{0,2},{1,3},{2,0},{3,1},{4,6},{5,7},{6,4},{7,5},{8,10},{9,11},{10,... | collective-permute-start | bytes 196616 | tf_op jit(solution)/shard_map/sketch_reduce_gather/ppermute | solution.py:98
  108.6 11.6 %collective-permute-start.8 = (f32[2,2,32,128]{3,2,1,0:T(8,128)S(1)}, f32[2,2,32,128]{3,2,1,0:T(8,128)S(1)}, u32[]{:S(2)}, u32[]{:S(2)}) collective-permute-start(f32[2,2,32,128]{3,2,1,0:T(8,128)S(1)} %dynamic-slice_bitcast_fusion.10), channel_id=1, source_target_pairs={{0,4},{1,5},{2,6},{3,7},{4,0},{5,1},{6,2},{7,3},{8,12},{9,13},{10,... | collective-permute-start | bytes 196616 | tf_op jit(solution)/shard_map/sketch_reduce_gather/ppermute | solution.py:98
  120.6 3.9 %collective-permute-start.29 = (f32[2,2,32,128]{3,2,1,0:T(8,128)S(1)}, f32[2,2,32,128]{3,2,1,0:T(8,128)S(1)}, u32[]{:S(2)}, u32[]{:S(2)}) collective-permute-start(f32[2,2,32,128]{3,2,1,0:T(8,128)S(1)} %dynamic-slice_bitcast_fusion.7), channel_id=1, source_target_pairs={{0,8},{1,9},{2,10},{3,11},{4,12},{5,13},{6,14},{7,15},{8,0},{9,1},... | collective-permute-start | bytes 196616 | tf_op jit(solution)/shard_map/sketch_reduce_gather/ppermute | solution.py:98
  124.6 1.1 collective-permute-start.43
  125.8 2.1 collective-permute-start.50
  128.5 2.1 collective-permute-start.9
  130.6 1.5 collective-permute-start.16
  132.1 1.6 collective-permute-start.23
  133.8 1.2 collective-permute-start.30
  135.6 1.6 collective-permute-start.44
  138.2 1.5 collective-permute-start.3
  139.7 1.6 collective-permute-start.10
  141.6 1.4 collective-permute-start.24
  143.0 1.6 collective-permute-start.31
  145.6 1.5 collective-permute-start.45
  147.1 1.6 collective-permute-start.52
  150.6 2.4 %collective-permute-start.18 = (f32[2,32,128]{2,1,0:T(8,128)S(1)}, f32[2,32,128]{2,1,0:T(8,128)S(1)}, u32[]{:S(2)}, u32[]{:S(2)}) collective-permute-start(f32[2,32,128]{2,1,0:T(8,128)S(1)} %add.281), channel_id=1, source_target_pairs={{0,8},{1,9},{2,10},{3,11},{4,12},{5,13},{6,14},{7,15},{8,0},{9,1},... | collective-permute-start | bytes 98312 | tf_op jit(solution)/shard_map/sketch_reduce_gather/ppermute | solution.py:98
  153.7 1.1 collective-permute-start.32
  154.8 1.4 collective-permute-start.39
  159.3 1.4 collective-permute-start.12
  160.7 1.2 collective-permute-start.19
  163.7 3.2 %collective-permute-done.47 = f32[2,2,32,128]{3,2,1,0:T(8,128)S(1)} collective-permute-done((f32[2,2,32,128]{3,2,1,0:T(8,128)S(1)}, f32[2,2,32,128]{3,2,1,0:T(8,128)S(1)}, u32[]{:S(2)}, u32[]{:S(2)}) %collective-permute-start.47) | collective-permute-done | bytes 65568 | tf_op jit(solution)/shard_map/sketch_reduce_gather/ppermute | solution.py:98
  166.9 2.3 %collective-permute-start.33 = (f32[2,2,32,128]{3,2,0,1:T(8,128)S(1)}, f32[2,2,32,128]{3,2,0,1:T(8,128)S(1)}, u32[]{:S(2)}, u32[]{:S(2)}) collective-permute-start(f32[2,2,32,128]{3,2,0,1:T(8,128)S(1)} %pad_maximum_fusion.20), channel_id=1, source_target_pairs={{0,8},{1,9},{2,10},{3,11},{4,12},{5,13},{6,14},{7,15},{8,0},{9,1},... | collective-permute-start | bytes 196616 | tf_op jit(solution)/shard_map/sketch_reduce_gather/ppermute | solution.py:98
  169.9 1.6 collective-permute-start.54
  172.4 2.3 %collective-permute-done.40 = f32[2,2,32,128]{3,2,0,1:T(8,128)S(1)} collective-permute-done((f32[2,2,32,128]{3,2,0,1:T(8,128)S(1)}, f32[2,2,32,128]{3,2,0,1:T(8,128)S(1)}, u32[]{:S(2)}, u32[]{:S(2)}) %collective-permute-start.40) | collective-permute-done | bytes 65568 | tf_op jit(solution)/shard_map/sketch_reduce_gather/ppermute | solution.py:98
  177.9 4.5 %fusion.1.m_ref = f32[512,512]{1,0:T(8,128)} fusion(f32[512,1024]{1,0:T(8,128)S(1)} %constant_dynamic-update-slice_fusion), kind=kOutput, calls=%fused_computation.5 | convolution fusion | flops 3222274048 | bytes 3145728 | tf_op jit(solution)/shard_map/kernel_matrix/dot_general | solution.py:174
  182.4 36.2 %kernel_solve.1 = f32[512,128]{1,0:T(8,128)} custom-call(f32[512,512]{1,0:T(8,128)} %fusion.1.m_ref, f32[512,128]{1,0:T(8,128)} %pad.4.w_ref), custom_call_target="tpu_custom_call" | custom-call | tf_op jit(solution)/shard_map/kernel_solve/pallas_call | solution.py:89
  (233 shorter events, 21.4 us)
Async XLA Ops:
  5.4 85.3 %all-to-all-start = ((bf16[32,16,4096]{2,0,1:T(8,128)(2,1)}), bf16[32,16,4096]{2,0,1:T(8,128)(2,1)}, u32[]{:S(2)}, u32[]{:S(2)}) async-start(bf16[32,16,4096]{2,0,1:T(8,128)(2,1)} %bitcast.258), calls=%async_computation | async-start | bytes 8388608 | tf_op jit(solution)/shard_map/gradient_exchange/all_to_all | solution.py:146
  100.8 7.8 %collective-permute-start.28 = (f32[2,2,2,32,128]{4,3,2,1,0:T(8,128)S(1)}, f32[2,2,2,32,128]{4,3,2,1,0:T(8,128)S(1)}, u32[]{:S(2)}, u32[]{:S(2)}) collective-permute-start(f32[2,2,2,32,128]{4,3,2,1,0:T(8,128)S(1)} %dynamic-slice_bitcast_fusion.1), channel_id=1, source_target_pairs={{0,1},{1,0},{2,3},{3,2},{4,5},{5,4},{6,7},{7,6},{8,9},{9,8},{10,11... | collective-permute-start | bytes 393224 | tf_op jit(solution)/shard_map/sketch_reduce_gather/ppermute | solution.py:98
  101.5 18.8 %collective-permute-start.35 = (f32[2,2,2,32,128]{4,3,2,1,0:T(8,128)S(1)}, f32[2,2,2,32,128]{4,3,2,1,0:T(8,128)S(1)}, u32[]{:S(2)}, u32[]{:S(2)}) collective-permute-start(f32[2,2,2,32,128]{4,3,2,1,0:T(8,128)S(1)} %dynamic-slice_bitcast_fusion), channel_id=1, source_target_pairs={{0,1},{1,0},{2,3},{3,2},{4,5},{5,4},{6,7},{7,6},{8,9},{9,8},{10,11... | collective-permute-start | bytes 393224 | tf_op jit(solution)/shard_map/sketch_reduce_gather/ppermute | solution.py:98
  101.6 18.8 %collective-permute-start.42 = (f32[2,2,2,32,128]{4,3,1,0,2:T(8,128)S(1)}, f32[2,2,2,32,128]{4,3,1,0,2:T(8,128)S(1)}, u32[]{:S(2)}, u32[]{:S(2)}) collective-permute-start(f32[2,2,2,32,128]{4,3,1,0,2:T(8,128)S(1)} %bitcast.282), channel_id=1, source_target_pairs={{0,1},{1,0},{2,3},{3,2},{4,5},{5,4},{6,7},{7,6},{8,9},{9,8},{10,11... | collective-permute-start | bytes 393224 | tf_op jit(solution)/shard_map/sketch_reduce_gather/ppermute | solution.py:98
  102.2 18.4 %collective-permute-start.49 = (f32[2,2,2,32,128]{4,3,2,0,1:T(8,128)S(1)}, f32[2,2,2,32,128]{4,3,2,0,1:T(8,128)S(1)}, u32[]{:S(2)}, u32[]{:S(2)}) collective-permute-start(f32[2,2,2,32,128]{4,3,2,0,1:T(8,128)S(1)} %bitcast.281), channel_id=1, source_target_pairs={{0,1},{1,0},{2,3},{3,2},{4,5},{5,4},{6,7},{7,6},{8,9},{9,8},{10,11... | collective-permute-start | bytes 393224 | tf_op jit(solution)/shard_map/sketch_reduce_gather/ppermute | solution.py:98
  102.3 22.2 %collective-permute-start.1 = (f32[2,2,32,128]{3,2,1,0:T(8,128)S(1)}, f32[2,2,32,128]{3,2,1,0:T(8,128)S(1)}, u32[]{:S(2)}, u32[]{:S(2)}) collective-permute-start(f32[2,2,32,128]{3,2,1,0:T(8,128)S(1)} %dynamic-slice_bitcast_fusion.11), channel_id=1, source_target_pairs={{0,2},{1,3},{2,0},{3,1},{4,6},{5,7},{6,4},{7,5},{8,10},{9,11},{10,... | collective-permute-start | bytes 196616 | tf_op jit(solution)/shard_map/sketch_reduce_gather/ppermute | solution.py:98
  108.6 16.0 %collective-permute-start.8 = (f32[2,2,32,128]{3,2,1,0:T(8,128)S(1)}, f32[2,2,32,128]{3,2,1,0:T(8,128)S(1)}, u32[]{:S(2)}, u32[]{:S(2)}) collective-permute-start(f32[2,2,32,128]{3,2,1,0:T(8,128)S(1)} %dynamic-slice_bitcast_fusion.10), channel_id=1, source_target_pairs={{0,4},{1,5},{2,6},{3,7},{4,0},{5,1},{6,2},{7,3},{8,12},{9,13},{10,... | collective-permute-start | bytes 196616 | tf_op jit(solution)/shard_map/sketch_reduce_gather/ppermute | solution.py:98
  120.4 7.5 %collective-permute-start.22 = (f32[2,2,32,128]{3,2,1,0:T(8,128)S(1)}, f32[2,2,32,128]{3,2,1,0:T(8,128)S(1)}, u32[]{:S(2)}, u32[]{:S(2)}) collective-permute-start(f32[2,2,32,128]{3,2,1,0:T(8,128)S(1)} %dynamic-slice_bitcast_fusion.8), channel_id=1, source_target_pairs={{0,4},{1,5},{2,6},{3,7},{4,0},{5,1},{6,2},{7,3},{8,12},{9,13},{10,... | collective-permute-start | bytes 196616 | tf_op jit(solution)/shard_map/sketch_reduce_gather/ppermute | solution.py:98
  120.6 7.9 %collective-permute-start.29 = (f32[2,2,32,128]{3,2,1,0:T(8,128)S(1)}, f32[2,2,32,128]{3,2,1,0:T(8,128)S(1)}, u32[]{:S(2)}, u32[]{:S(2)}) collective-permute-start(f32[2,2,32,128]{3,2,1,0:T(8,128)S(1)} %dynamic-slice_bitcast_fusion.7), channel_id=1, source_target_pairs={{0,8},{1,9},{2,10},{3,11},{4,12},{5,13},{6,14},{7,15},{8,0},{9,1},... | collective-permute-start | bytes 196616 | tf_op jit(solution)/shard_map/sketch_reduce_gather/ppermute | solution.py:98
  124.5 6.1 %collective-permute-start.36 = (f32[2,2,32,128]{3,2,1,0:T(8,128)S(1)}, f32[2,2,32,128]{3,2,1,0:T(8,128)S(1)}, u32[]{:S(2)}, u32[]{:S(2)}) collective-permute-start(f32[2,2,32,128]{3,2,1,0:T(8,128)S(1)} %dynamic-slice_bitcast_fusion.6), channel_id=1, source_target_pairs={{0,8},{1,9},{2,10},{3,11},{4,12},{5,13},{6,14},{7,15},{8,0},{9,1},... | collective-permute-start | bytes 196616 | tf_op jit(solution)/shard_map/sketch_reduce_gather/ppermute | solution.py:98
  124.6 7.5 %collective-permute-start.43 = (f32[2,2,32,128]{3,2,1,0:T(8,128)S(1)}, f32[2,2,32,128]{3,2,1,0:T(8,128)S(1)}, u32[]{:S(2)}, u32[]{:S(2)}) collective-permute-start(f32[2,2,32,128]{3,2,1,0:T(8,128)S(1)} %dynamic-slice_bitcast_fusion.5), channel_id=1, source_target_pairs={{0,2},{1,3},{2,0},{3,1},{4,6},{5,7},{6,4},{7,5},{8,10},{9,11},{10,... | collective-permute-start | bytes 196616 | tf_op jit(solution)/shard_map/sketch_reduce_gather/ppermute | solution.py:98
  125.8 7.9 %collective-permute-start.50 = (f32[2,2,32,128]{3,2,1,0:T(8,128)S(1)}, f32[2,2,32,128]{3,2,1,0:T(8,128)S(1)}, u32[]{:S(2)}, u32[]{:S(2)}) collective-permute-start(f32[2,2,32,128]{3,2,1,0:T(8,128)S(1)} %dynamic-slice_bitcast_fusion.4), channel_id=1, source_target_pairs={{0,4},{1,5},{2,6},{3,7},{4,0},{5,1},{6,2},{7,3},{8,12},{9,13},{10,... | collective-permute-start | bytes 196616 | tf_op jit(solution)/shard_map/sketch_reduce_gather/ppermute | solution.py:98
  128.0 7.1 %collective-permute-start.2 = (f32[2,32,128]{2,1,0:T(8,128)S(1)}, f32[2,32,128]{2,1,0:T(8,128)S(1)}, u32[]{:S(2)}, u32[]{:S(2)}) collective-permute-start(f32[2,32,128]{2,1,0:T(8,128)S(1)} %dynamic-slice_bitcast_fusion.19), channel_id=1, source_target_pairs={{0,4},{1,5},{2,6},{3,7},{4,0},{5,1},{6,2},{7,3},{8,12},{9,13},{10,... | collective-permute-start | bytes 98312 | tf_op jit(solution)/shard_map/sketch_reduce_gather/ppermute | solution.py:98
  128.5 7.1 %collective-permute-start.9 = (f32[2,32,128]{2,1,0:T(8,128)S(1)}, f32[2,32,128]{2,1,0:T(8,128)S(1)}, u32[]{:S(2)}, u32[]{:S(2)}) collective-permute-start(f32[2,32,128]{2,1,0:T(8,128)S(1)} %dynamic-slice_bitcast_fusion.18), channel_id=1, source_target_pairs={{0,2},{1,3},{2,0},{3,1},{4,6},{5,7},{6,4},{7,5},{8,10},{9,11},{10,... | collective-permute-start | bytes 98312 | tf_op jit(solution)/shard_map/sketch_reduce_gather/ppermute | solution.py:98
  130.6 6.6 %collective-permute-start.16 = (f32[2,32,128]{2,1,0:T(8,128)S(1)}, f32[2,32,128]{2,1,0:T(8,128)S(1)}, u32[]{:S(2)}, u32[]{:S(2)}) collective-permute-start(f32[2,32,128]{2,1,0:T(8,128)S(1)} %dynamic-slice_bitcast_fusion.17), channel_id=1, source_target_pairs={{0,8},{1,9},{2,10},{3,11},{4,12},{5,13},{6,14},{7,15},{8,0},{9,1},... | collective-permute-start | bytes 98312 | tf_op jit(solution)/shard_map/sketch_reduce_gather/ppermute | solution.py:98
  132.1 6.0 %collective-permute-start.23 = (f32[2,32,128]{2,1,0:T(8,128)S(1)}, f32[2,32,128]{2,1,0:T(8,128)S(1)}, u32[]{:S(2)}, u32[]{:S(2)}) collective-permute-start(f32[2,32,128]{2,1,0:T(8,128)S(1)} %dynamic-slice_bitcast_fusion.16), channel_id=1, source_target_pairs={{0,8},{1,9},{2,10},{3,11},{4,12},{5,13},{6,14},{7,15},{8,0},{9,1},... | collective-permute-start | bytes 98312 | tf_op jit(solution)/shard_map/sketch_reduce_gather/ppermute | solution.py:98
  135.0 6.2 %collective-permute-start.37 = (f32[2,32,128]{2,1,0:T(8,128)S(1)}, f32[2,32,128]{2,1,0:T(8,128)S(1)}, u32[]{:S(2)}, u32[]{:S(2)}) collective-permute-start(f32[2,32,128]{2,1,0:T(8,128)S(1)} %dynamic-slice_bitcast_fusion.14), channel_id=1, source_target_pairs={{0,4},{1,5},{2,6},{3,7},{4,0},{5,1},{6,2},{7,3},{8,12},{9,13},{10,... | collective-permute-start | bytes 98312 | tf_op jit(solution)/shard_map/sketch_reduce_gather/ppermute | solution.py:98
  135.6 6.1 %collective-permute-start.44 = (f32[2,32,128]{2,1,0:T(8,128)S(1)}, f32[2,32,128]{2,1,0:T(8,128)S(1)}, u32[]{:S(2)}, u32[]{:S(2)}) collective-permute-start(f32[2,32,128]{2,1,0:T(8,128)S(1)} %dynamic-slice_bitcast_fusion.13), channel_id=1, source_target_pairs={{0,4},{1,5},{2,6},{3,7},{4,0},{5,1},{6,2},{7,3},{8,12},{9,13},{10,... | collective-permute-start | bytes 98312 | tf_op jit(solution)/shard_map/sketch_reduce_gather/ppermute | solution.py:98
  138.2 6.5 %collective-permute-start.3 = (f32[2,32,128]{2,1,0:T(8,128)S(1)}, f32[2,32,128]{2,1,0:T(8,128)S(1)}, u32[]{:S(2)}, u32[]{:S(2)}) collective-permute-start(f32[2,32,128]{2,1,0:T(8,128)S(1)} %bitcast_add_fusion.23), channel_id=1, source_target_pairs={{0,8},{1,9},{2,10},{3,11},{4,12},{5,13},{6,14},{7,15},{8,0},{9,1},... | collective-permute-start | bytes 98312 | tf_op jit(solution)/shard_map/sketch_reduce_gather/ppermute | solution.py:98
  139.7 6.0 %collective-permute-start.10 = (f32[2,32,128]{2,1,0:T(8,128)S(1)}, f32[2,32,128]{2,1,0:T(8,128)S(1)}, u32[]{:S(2)}, u32[]{:S(2)}) collective-permute-start(f32[2,32,128]{2,1,0:T(8,128)S(1)} %bitcast_add_fusion.22), channel_id=1, source_target_pairs={{0,8},{1,9},{2,10},{3,11},{4,12},{5,13},{6,14},{7,15},{8,0},{9,1},... | collective-permute-start | bytes 98312 | tf_op jit(solution)/shard_map/sketch_reduce_gather/ppermute | solution.py:98
  141.6 7.1 %collective-permute-start.24 = (f32[2,32,128]{2,1,0:T(8,128)S(1)}, f32[2,32,128]{2,1,0:T(8,128)S(1)}, u32[]{:S(2)}, u32[]{:S(2)}) collective-permute-start(f32[2,32,128]{2,1,0:T(8,128)S(1)} %bitcast_add_fusion.20), channel_id=1, source_target_pairs={{0,2},{1,3},{2,0},{3,1},{4,6},{5,7},{6,4},{7,5},{8,10},{9,11},{10,... | collective-permute-start | bytes 98312 | tf_op jit(solution)/shard_map/sketch_reduce_gather/ppermute | solution.py:98
  143.0 6.5 %collective-permute-start.31 = (f32[2,32,128]{2,1,0:T(8,128)S(1)}, f32[2,32,128]{2,1,0:T(8,128)S(1)}, u32[]{:S(2)}, u32[]{:S(2)}) collective-permute-start(f32[2,32,128]{2,1,0:T(8,128)S(1)} %bitcast_add_fusion.19), channel_id=1, source_target_pairs={{0,4},{1,5},{2,6},{3,7},{4,0},{5,1},{6,2},{7,3},{8,12},{9,13},{10,... | collective-permute-start | bytes 98312 | tf_op jit(solution)/shard_map/sketch_reduce_gather/ppermute | solution.py:98
  144.7 5.9 %collective-permute-start.38 = (f32[2,32,128]{2,1,0:T(8,128)S(1)}, f32[2,32,128]{2,1,0:T(8,128)S(1)}, u32[]{:S(2)}, u32[]{:S(2)}) collective-permute-start(f32[2,32,128]{2,1,0:T(8,128)S(1)} %bitcast_add_fusion.18), channel_id=1, source_target_pairs={{0,2},{1,3},{2,0},{3,1},{4,6},{5,7},{6,4},{7,5},{8,10},{9,11},{10,... | collective-permute-start | bytes 98312 | tf_op jit(solution)/shard_map/sketch_reduce_gather/ppermute | solution.py:98
  145.6 7.3 %collective-permute-start.45 = (f32[2,32,128]{2,1,0:T(8,128)S(1)}, f32[2,32,128]{2,1,0:T(8,128)S(1)}, u32[]{:S(2)}, u32[]{:S(2)}) collective-permute-start(f32[2,32,128]{2,1,0:T(8,128)S(1)} %bitcast_add_fusion.17), channel_id=1, source_target_pairs={{0,8},{1,9},{2,10},{3,11},{4,12},{5,13},{6,14},{7,15},{8,0},{9,1},... | collective-permute-start | bytes 98312 | tf_op jit(solution)/shard_map/sketch_reduce_gather/ppermute | solution.py:98
  147.1 6.5 %collective-permute-start.52 = (f32[2,32,128]{2,1,0:T(8,128)S(1)}, f32[2,32,128]{2,1,0:T(8,128)S(1)}, u32[]{:S(2)}, u32[]{:S(2)}) collective-permute-start(f32[2,32,128]{2,1,0:T(8,128)S(1)} %bitcast_add_fusion.16), channel_id=1, source_target_pairs={{0,8},{1,9},{2,10},{3,11},{4,12},{5,13},{6,14},{7,15},{8,0},{9,1},... | collective-permute-start | bytes 98312 | tf_op jit(solution)/shard_map/sketch_reduce_gather/ppermute | solution.py:98
  148.7 6.1 %collective-permute-start.4 = (f32[2,32,128]{2,1,0:T(8,128)S(1)}, f32[2,32,128]{2,1,0:T(8,128)S(1)}, u32[]{:S(2)}, u32[]{:S(2)}) collective-permute-start(f32[2,32,128]{2,1,0:T(8,128)S(1)} %add.270), channel_id=1, source_target_pairs={{0,4},{1,5},{2,6},{3,7},{4,0},{5,1},{6,2},{7,3},{8,12},{9,13},{10,... | collective-permute-start | bytes 98312 | tf_op jit(solution)/shard_map/sketch_reduce_gather/ppermute | solution.py:98
  149.5 6.7 %collective-permute-start.11 = (f32[2,32,128]{2,1,0:T(8,128)S(1)}, f32[2,32,128]{2,1,0:T(8,128)S(1)}, u32[]{:S(2)}, u32[]{:S(2)}) collective-permute-start(f32[2,32,128]{2,1,0:T(8,128)S(1)} %add.274), channel_id=1, source_target_pairs={{0,2},{1,3},{2,0},{3,1},{4,6},{5,7},{6,4},{7,5},{8,10},{9,11},{10,... | collective-permute-start | bytes 98312 | tf_op jit(solution)/shard_map/sketch_reduce_gather/ppermute | solution.py:98
  150.6 6.5 %collective-permute-start.18 = (f32[2,32,128]{2,1,0:T(8,128)S(1)}, f32[2,32,128]{2,1,0:T(8,128)S(1)}, u32[]{:S(2)}, u32[]{:S(2)}) collective-permute-start(f32[2,32,128]{2,1,0:T(8,128)S(1)} %add.281), channel_id=1, source_target_pairs={{0,8},{1,9},{2,10},{3,11},{4,12},{5,13},{6,14},{7,15},{8,0},{9,1},... | collective-permute-start | bytes 98312 | tf_op jit(solution)/shard_map/sketch_reduce_gather/ppermute | solution.py:98
  158.1 11.1 %collective-permute-start.5 = (f32[2,2,32,128]{3,2,1,0:T(8,128)S(1)}, f32[2,2,32,128]{3,2,1,0:T(8,128)S(1)}, u32[]{:S(2)}, u32[]{:S(2)}) collective-permute-start(f32[2,2,32,128]{3,2,1,0:T(8,128)S(1)} %pad_maximum_fusion.16), channel_id=1, source_target_pairs={{0,2},{1,3},{2,0},{3,1},{4,6},{5,7},{6,4},{7,5},{8,10},{9,11},{10,... | collective-permute-start | bytes 196616 | tf_op jit(solution)/shard_map/sketch_reduce_gather/ppermute | solution.py:98
  159.3 10.7 %collective-permute-start.12 = (f32[2,2,32,128]{3,2,0,1:T(8,128)S(1)}, f32[2,2,32,128]{3,2,0,1:T(8,128)S(1)}, u32[]{:S(2)}, u32[]{:S(2)}) collective-permute-start(f32[2,2,32,128]{3,2,0,1:T(8,128)S(1)} %pad_maximum_fusion.17), channel_id=1, source_target_pairs={{0,4},{1,5},{2,6},{3,7},{4,0},{5,1},{6,2},{7,3},{8,12},{9,13},{10,... | collective-permute-start | bytes 196616 | tf_op jit(solution)/shard_map/sketch_reduce_gather/ppermute | solution.py:98
  160.7 10.9 %collective-permute-start.19 = (f32[2,2,32,128]{3,2,1,0:T(8,128)S(1)}, f32[2,2,32,128]{3,2,1,0:T(8,128)S(1)}, u32[]{:S(2)}, u32[]{:S(2)}) collective-permute-start(f32[2,2,32,128]{3,2,1,0:T(8,128)S(1)} %pad_maximum_fusion.18), channel_id=1, source_target_pairs={{0,2},{1,3},{2,0},{3,1},{4,6},{5,7},{6,4},{7,5},{8,10},{9,11},{10,... | collective-permute-start | bytes 196616 | tf_op jit(solution)/shard_map/sketch_reduce_gather/ppermute | solution.py:98
  161.9 9.8 %collective-permute-start.26 = (f32[2,2,32,128]{3,2,0,1:T(8,128)S(1)}, f32[2,2,32,128]{3,2,0,1:T(8,128)S(1)}, u32[]{:S(2)}, u32[]{:S(2)}) collective-permute-start(f32[2,2,32,128]{3,2,0,1:T(8,128)S(1)} %pad_maximum_fusion.19), channel_id=1, source_target_pairs={{0,4},{1,5},{2,6},{3,7},{4,0},{5,1},{6,2},{7,3},{8,12},{9,13},{10,... | collective-permute-start | bytes 196616 | tf_op jit(solution)/shard_map/sketch_reduce_gather/ppermute | solution.py:98
  (28 other events, 130.0 us)

commit v16 on v12

--- a/solution.py
+++ b/solution.py
@@ -130,7 +130,7 @@
     if bits < 4:
         return [first]
     rest = list(range(4, bits))
-    return [[0, 1, 2, 3] + rest, [0, 2, 1, 3] + rest, [0, 1, 3, 2] + rest, [0, 2, 3, 1] + rest]
+    return [[0, 1, 2, 3] + rest, [0, 2, 1, 3] + rest, [0, 1, 2, 3] + rest, [0, 2, 1, 3] + rest]
 
 
 def on_device(grads, proj, target_ids, target_counts):

time: 198 us -> 196 us (0.990)
  waiting for transfers between devices: 89.1 us -> 85 us
  starting transfers between devices: 48 us -> 50.1 us
    ppermute x28, waiting for transfers between devices: 13.3 us -> 10 us  [partner(): lax.ppermute(array, axis, [(i, i ^ 1 << bit) for i in range(lax.axis_size...]
    ppermute x28, starting transfers between devices: 40.5 us -> 42.6 us  [partner(): lax.ppermute(array, axis, [(i, i ^ 1 << bit) for i in range(lax.axis_size...]
  transfers between devices with their start and end apart: 29 -> 29, of which waited for: 14 -> 13; matrix products, arithmetic and copies ran while one was open for 2% -> 2% of each run, Pallas kernels for 0% -> 0%
where the time goes in v16:
time: 196 us
  waiting for transfers between devices  85 us (43%)
  starting transfers between devices  50.1 us (26%)
  Pallas kernels  36.2 us (18%)
  matrix products  12.7 us (6%)
  local copies, waits for them, and re-layouts  6.89 us (4%)
  other arithmetic  3.94 us (2%)
    all_to_all x1, waiting for transfers between devices, on_device(): lax.all_to_all(grads, 'ex', split_axis=1, concat_axis=0, tiled=True)  75 us
    ppermute x28, starting transfers between devices, partner(): lax.ppermute(array, axis, [(i, i ^ 1 << bit) for i in range(lax.axis_size...  42.6 us
    pallas_call x1, Pallas kernels, spd_solve(): pl.pallas_call(functools.partial(_solve_kernel, block=block), out_shape=j...  36.2 us
    ppermute x28, waiting for transfers between devices, partner(): lax.ppermute(array, axis, [(i, i ^ 1 << bit) for i in range(lax.axis_size...  10 us
    dot_general x1, matrix products, on_device(): partial_value = jnp.dot(columns, proj, preferred_element_type=jnp.float32)  8.14 us
    all_to_all x1, starting transfers between devices, on_device(): lax.all_to_all(grads, 'ex', split_axis=1, concat_axis=0, tiled=True)  7.57 us
    all_to_all x1, local copies, waits for them, and re-layouts, on_device(): lax.all_to_all(grads, 'ex', split_axis=1, concat_axis=0, tiled=True)  4.71 us
    dot_general x1, matrix products, on_device(): kernel = jnp.dot(sketch_all, sketch_all.T, precision=lax.Precision.HIGHEST)  4.53 us
  transfers between devices with their start and end apart: 29, of which 13 were waited for; matrix products, arithmetic and copies ran while one was open for 2% of the time, Pallas kernels for 0%

profile of v16, /device:TPU:0, one launch (start us, length us, event | category | flops | bytes accessed | tf_op | source)
XLA Modules:
  0.0 196.1 jit_solution(16715121683907855059)
XLA Ops:
  0.6 4.7 %copy.112 = bf16[4,16,8,4096]{3,2,0,1:T(8,128)(2,1)} copy(bf16[4,16,8,4096]{3,2,1,0:T(8,128)(2,1)} %bitcast.141) | data formatting | bytes 8388608 | tf_op jit(solution)/shard_map/gradient_exchange/all_to_all | solution.py:144
  5.3 7.6 %all-to-all-start = ((bf16[32,16,4096]{2,0,1:T(8,128)(2,1)}), bf16[32,16,4096]{2,0,1:T(8,128)(2,1)}, u32[]{:S(2)}, u32[]{:S(2)}) async-start(bf16[32,16,4096]{2,0,1:T(8,128)(2,1)} %bitcast.140), calls=%async_computation | async-start | bytes 8388608 | tf_op jit(solution)/shard_map/gradient_exchange/all_to_all | solution.py:144
  13.1 1.6 convert_reduce_fusion
  14.9 0.7 pad.4.w_ref
  15.6 75.0 %all-to-all-done = bf16[32,16,4096]{2,0,1:T(8,128)(2,1)} async-done(((bf16[32,16,4096]{2,0,1:T(8,128)(2,1)}), bf16[32,16,4096]{2,0,1:T(8,128)(2,1)}, u32[]{:S(2)}, u32[]{:S(2)}) %all-to-all-start) | async-done | bytes 4194336 | tf_op jit(solution)/shard_map/gradient_exchange/all_to_all | solution.py:144
  90.6 8.1 %fusion.14 = f32[512,1024]{1,0:T(8,128)S(1)} fusion(bf16[512,4096]{1,0:T(8,128)(2,1)} %bitcast.2, bf16[4096,1024]{1,0:T(8,128)(2,1)} %param.5), kind=kOutput, calls=%fused_computation.93 | convolution fusion | flops 4294967296 | bytes 14680064 | tf_op jit(solution)/shard_map/partial_projection/dot_general | solution.py:146
  99.0 0.8 collective-permute-start.21
  101.1 14.7 %collective-permute-start.22 = (f32[2,2,32,256]{3,2,1,0:T(8,128)S(1)}, f32[2,2,32,256]{3,2,1,0:T(8,128)S(1)}, u32[]{:S(2)}, u32[]{:S(2)}) collective-permute-start(f32[2,2,32,256]{3,2,1,0:T(8,128)S(1)} %dynamic-slice_bitcast_fusion), channel_id=1, source_target_pairs={{0,4},{1,5},{2,6},{3,7},{4,0},{5,1},{6,2},{7,3},{8,12},{9,13},{10,... | collective-permute-start | bytes 393224 | tf_op jit(solution)/shard_map/sketch_reduce_gather/ppermute | solution.py:98
  115.8 3.0 %collective-permute-start.15 = (f32[2,2,32,256]{3,2,1,0:T(8,128)S(1)}, f32[2,2,32,256]{3,2,1,0:T(8,128)S(1)}, u32[]{:S(2)}, u32[]{:S(2)}) collective-permute-start(f32[2,2,32,256]{3,2,1,0:T(8,128)S(1)} %dynamic-slice_bitcast_fusion.1), channel_id=1, source_target_pairs={{0,2},{1,3},{2,0},{3,1},{4,6},{5,7},{6,4},{7,5},{8,10},{9,11},{10,... | collective-permute-start | bytes 393224 | tf_op jit(solution)/shard_map/sketch_reduce_gather/ppermute | solution.py:98
  119.7 3.4 %collective-permute-start.23 = (f32[2,32,256]{2,1,0:T(8,128)S(1)}, f32[2,32,256]{2,1,0:T(8,128)S(1)}, u32[]{:S(2)}, u32[]{:S(2)}) collective-permute-start(f32[2,32,256]{2,1,0:T(8,128)S(1)} %dynamic-slice_bitcast_fusion.4), channel_id=1, source_target_pairs={{0,2},{1,3},{2,0},{3,1},{4,6},{5,7},{6,4},{7,5},{8,10},{9,11},{10,... | collective-permute-start | bytes 196616 | tf_op jit(solution)/shard_map/sketch_reduce_gather/ppermute | solution.py:98
  123.2 2.1 %collective-permute-start.16 = (f32[2,32,256]{2,1,0:T(8,128)S(1)}, f32[2,32,256]{2,1,0:T(8,128)S(1)}, u32[]{:S(2)}, u32[]{:S(2)}) collective-permute-start(f32[2,32,256]{2,1,0:T(8,128)S(1)} %dynamic-slice_bitcast_fusion.5), channel_id=1, source_target_pairs={{0,4},{1,5},{2,6},{3,7},{4,0},{5,1},{6,2},{7,3},{8,12},{9,13},{10,... | collective-permute-start | bytes 196616 | tf_op jit(solution)/shard_map/sketch_reduce_gather/ppermute | solution.py:98
  126.0 1.7 collective-permute-start.2
  127.7 2.1 %collective-permute-start.24 = (f32[2,32,256]{2,1,0:T(8,128)S(1)}, f32[2,32,256]{2,1,0:T(8,128)S(1)}, u32[]{:S(2)}, u32[]{:S(2)}) collective-permute-start(f32[2,32,256]{2,1,0:T(8,128)S(1)} %bitcast_add_fusion.8), channel_id=1, source_target_pairs={{0,8},{1,9},{2,10},{3,11},{4,12},{5,13},{6,14},{7,15},{8,0},{9,1},... | collective-permute-start | bytes 196616 | tf_op jit(solution)/shard_map/sketch_reduce_gather/ppermute | solution.py:98
  129.8 1.0 collective-permute-start.17
  130.8 2.1 %collective-permute-start.10 = (f32[2,32,256]{2,1,0:T(8,128)S(1)}, f32[2,32,256]{2,1,0:T(8,128)S(1)}, u32[]{:S(2)}, u32[]{:S(2)}) collective-permute-start(f32[2,32,256]{2,1,0:T(8,128)S(1)} %bitcast_add_fusion.10), channel_id=1, source_target_pairs={{0,8},{1,9},{2,10},{3,11},{4,12},{5,13},{6,14},{7,15},{8,0},{9,1},... | collective-permute-start | bytes 196616 | tf_op jit(solution)/shard_map/sketch_reduce_gather/ppermute | solution.py:98
  132.9 1.0 collective-permute-start.3
  133.9 3.8 %collective-permute-done.24 = f32[2,32,256]{2,1,0:T(8,128)S(1)} collective-permute-done((f32[2,32,256]{2,1,0:T(8,128)S(1)}, f32[2,32,256]{2,1,0:T(8,128)S(1)}, u32[]{:S(2)}, u32[]{:S(2)}) %collective-permute-start.24) | collective-permute-done | bytes 65568 | tf_op jit(solution)/shard_map/sketch_reduce_gather/ppermute | solution.py:98
  137.7 1.9 collective-permute-start.25
  140.0 0.8 collective-permute-done.10
  140.8 1.2 collective-permute-start.11
  142.0 1.3 collective-permute-start.4
  144.0 0.9 collective-permute-start.26
  144.9 1.2 collective-permute-start.19
  146.1 1.1 collective-permute-start.12
  147.2 1.2 collective-permute-start.5
  148.4 0.9 collective-permute-done.26
  150.1 1.1 collective-permute-done.12
  151.3 1.0 collective-permute-done.5
  152.9 1.0 collective-permute-done.6
  154.0 4.5 %select_add_fusion.m_ref = f32[512,512]{1,0:T(8,128)} fusion(f32[512,256]{1,0:T(8,128)S(1)} %bitcast.146, f32[512,256]{1,0:T(8,128)S(1)} %bitcast.147, f32[512,256]{1,0:T(8,128)S(1)} %bitcast.148, f32[512,256]{1,0:T(8,128)S(1)} %bitcast.149), kind=kOutput, calls=%fused_computation.12 | convolution fusion | flops 3223846912 | bytes 3145728 | tf_op jit(solution)/shard_map/kernel_matrix/dot_general | solution.py:172
  158.5 36.2 %kernel_solve.1 = f32[512,128]{1,0:T(8,128)} custom-call(f32[512,512]{1,0:T(8,128)} %select_add_fusion.m_ref, f32[512,128]{1,0:T(8,128)} %pad.4.w_ref), custom_call_target="tpu_custom_call" | custom-call | tf_op jit(solution)/shard_map/kernel_solve/pallas_call | solution.py:89
  194.7 0.7 fusion.11
  (106 shorter events, 6.7 us)
Async XLA Ops:
  5.3 7.7 %copy-start.1 = (s32[24]{0:T(128)S(1)}, s32[24]{0:T(128)}, u32[]{:S(2)}) copy-start(s32[24]{0:T(128)} %param.7) | copy-start | bytes 292
  5.3 7.8 %copy-start = (s32[24,128]{1,0:T(8,128)S(1)}, s32[24,128]{1,0:T(8,128)}, u32[]{:S(2)}) copy-start(s32[24,128]{1,0:T(8,128)} %param.6) | copy-start | bytes 36868
  5.3 85.3 %all-to-all-start = ((bf16[32,16,4096]{2,0,1:T(8,128)(2,1)}), bf16[32,16,4096]{2,0,1:T(8,128)(2,1)}, u32[]{:S(2)}, u32[]{:S(2)}) async-start(bf16[32,16,4096]{2,0,1:T(8,128)(2,1)} %bitcast.140), calls=%async_computation | async-start | bytes 8388608 | tf_op jit(solution)/shard_map/gradient_exchange/all_to_all | solution.py:144
  99.0 2.0 %collective-permute-start.21 = (f32[2,2,2,32,256]{4,3,2,0,1:T(8,128)S(1)}, f32[2,2,2,32,256]{4,3,2,0,1:T(8,128)S(1)}, u32[]{:S(2)}, u32[]{:S(2)}) collective-permute-start(f32[2,2,2,32,256]{4,3,2,0,1:T(8,128)S(1)} %bitcast.153), channel_id=1, source_target_pairs={{0,1},{1,0},{2,3},{3,2},{4,5},{5,4},{6,7},{7,6},{8,9},{9,8},{10,11... | collective-permute-start | bytes 786440 | tf_op jit(solution)/shard_map/sketch_reduce_gather/ppermute | solution.py:98
  99.9 15.9 %collective-permute-start.14 = (f32[2,2,2,32,256]{4,3,1,0,2:T(8,128)S(1)}, f32[2,2,2,32,256]{4,3,1,0,2:T(8,128)S(1)}, u32[]{:S(2)}, u32[]{:S(2)}) collective-permute-start(f32[2,2,2,32,256]{4,3,1,0,2:T(8,128)S(1)} %bitcast.152), channel_id=1, source_target_pairs={{0,1},{1,0},{2,3},{3,2},{4,5},{5,4},{6,7},{7,6},{8,9},{9,8},{10,11... | collective-permute-start | bytes 786440 | tf_op jit(solution)/shard_map/sketch_reduce_gather/ppermute | solution.py:98
  100.1 18.8 %collective-permute-start.7 = (f32[2,2,2,32,256]{4,3,2,0,1:T(8,128)S(1)}, f32[2,2,2,32,256]{4,3,2,0,1:T(8,128)S(1)}, u32[]{:S(2)}, u32[]{:S(2)}) collective-permute-start(f32[2,2,2,32,256]{4,3,2,0,1:T(8,128)S(1)} %bitcast.154), channel_id=1, source_target_pairs={{0,1},{1,0},{2,3},{3,2},{4,5},{5,4},{6,7},{7,6},{8,9},{9,8},{10,11... | collective-permute-start | bytes 786440 | tf_op jit(solution)/shard_map/sketch_reduce_gather/ppermute | solution.py:98
  100.7 18.6 %collective-permute-start = (f32[2,2,2,32,256]{4,3,1,0,2:T(8,128)S(1)}, f32[2,2,2,32,256]{4,3,1,0,2:T(8,128)S(1)}, u32[]{:S(2)}, u32[]{:S(2)}) collective-permute-start(f32[2,2,2,32,256]{4,3,1,0,2:T(8,128)S(1)} %bitcast.151), channel_id=1, source_target_pairs={{0,1},{1,0},{2,3},{3,2},{4,5},{5,4},{6,7},{7,6},{8,9},{9,8},{10,11... | collective-permute-start | bytes 786440 | tf_op jit(solution)/shard_map/sketch_reduce_gather/ppermute | solution.py:98
  101.1 18.6 %collective-permute-start.22 = (f32[2,2,32,256]{3,2,1,0:T(8,128)S(1)}, f32[2,2,32,256]{3,2,1,0:T(8,128)S(1)}, u32[]{:S(2)}, u32[]{:S(2)}) collective-permute-start(f32[2,2,32,256]{3,2,1,0:T(8,128)S(1)} %dynamic-slice_bitcast_fusion), channel_id=1, source_target_pairs={{0,4},{1,5},{2,6},{3,7},{4,0},{5,1},{6,2},{7,3},{8,12},{9,13},{10,... | collective-permute-start | bytes 393224 | tf_op jit(solution)/shard_map/sketch_reduce_gather/ppermute | solution.py:98
  115.8 7.3 %collective-permute-start.15 = (f32[2,2,32,256]{3,2,1,0:T(8,128)S(1)}, f32[2,2,32,256]{3,2,1,0:T(8,128)S(1)}, u32[]{:S(2)}, u32[]{:S(2)}) collective-permute-start(f32[2,2,32,256]{3,2,1,0:T(8,128)S(1)} %dynamic-slice_bitcast_fusion.1), channel_id=1, source_target_pairs={{0,2},{1,3},{2,0},{3,1},{4,6},{5,7},{6,4},{7,5},{8,10},{9,11},{10,... | collective-permute-start | bytes 393224 | tf_op jit(solution)/shard_map/sketch_reduce_gather/ppermute | solution.py:98
  118.9 6.3 %collective-permute-start.8 = (f32[2,2,32,256]{3,2,1,0:T(8,128)S(1)}, f32[2,2,32,256]{3,2,1,0:T(8,128)S(1)}, u32[]{:S(2)}, u32[]{:S(2)}) collective-permute-start(f32[2,2,32,256]{3,2,1,0:T(8,128)S(1)} %dynamic-slice_bitcast_fusion.2), channel_id=1, source_target_pairs={{0,4},{1,5},{2,6},{3,7},{4,0},{5,1},{6,2},{7,3},{8,12},{9,13},{10,... | collective-permute-start | bytes 393224 | tf_op jit(solution)/shard_map/sketch_reduce_gather/ppermute | solution.py:98
  119.4 6.6 %collective-permute-start.1 = (f32[2,2,32,256]{3,2,1,0:T(8,128)S(1)}, f32[2,2,32,256]{3,2,1,0:T(8,128)S(1)}, u32[]{:S(2)}, u32[]{:S(2)}) collective-permute-start(f32[2,2,32,256]{3,2,1,0:T(8,128)S(1)} %dynamic-slice_bitcast_fusion.3), channel_id=1, source_target_pairs={{0,2},{1,3},{2,0},{3,1},{4,6},{5,7},{6,4},{7,5},{8,10},{9,11},{10,... | collective-permute-start | bytes 393224 | tf_op jit(solution)/shard_map/sketch_reduce_gather/ppermute | solution.py:98
  119.7 8.0 %collective-permute-start.23 = (f32[2,32,256]{2,1,0:T(8,128)S(1)}, f32[2,32,256]{2,1,0:T(8,128)S(1)}, u32[]{:S(2)}, u32[]{:S(2)}) collective-permute-start(f32[2,32,256]{2,1,0:T(8,128)S(1)} %dynamic-slice_bitcast_fusion.4), channel_id=1, source_target_pairs={{0,2},{1,3},{2,0},{3,1},{4,6},{5,7},{6,4},{7,5},{8,10},{9,11},{10,... | collective-permute-start | bytes 196616 | tf_op jit(solution)/shard_map/sketch_reduce_gather/ppermute | solution.py:98
  123.2 6.6 %collective-permute-start.16 = (f32[2,32,256]{2,1,0:T(8,128)S(1)}, f32[2,32,256]{2,1,0:T(8,128)S(1)}, u32[]{:S(2)}, u32[]{:S(2)}) collective-permute-start(f32[2,32,256]{2,1,0:T(8,128)S(1)} %dynamic-slice_bitcast_fusion.5), channel_id=1, source_target_pairs={{0,4},{1,5},{2,6},{3,7},{4,0},{5,1},{6,2},{7,3},{8,12},{9,13},{10,... | collective-permute-start | bytes 196616 | tf_op jit(solution)/shard_map/sketch_reduce_gather/ppermute | solution.py:98
  125.3 5.5 %collective-permute-start.9 = (f32[2,32,256]{2,1,0:T(8,128)S(1)}, f32[2,32,256]{2,1,0:T(8,128)S(1)}, u32[]{:S(2)}, u32[]{:S(2)}) collective-permute-start(f32[2,32,256]{2,1,0:T(8,128)S(1)} %dynamic-slice_bitcast_fusion.6), channel_id=1, source_target_pairs={{0,2},{1,3},{2,0},{3,1},{4,6},{5,7},{6,4},{7,5},{8,10},{9,11},{10,... | collective-permute-start | bytes 196616 | tf_op jit(solution)/shard_map/sketch_reduce_gather/ppermute | solution.py:98
  126.0 6.9 %collective-permute-start.2 = (f32[2,32,256]{2,1,0:T(8,128)S(1)}, f32[2,32,256]{2,1,0:T(8,128)S(1)}, u32[]{:S(2)}, u32[]{:S(2)}) collective-permute-start(f32[2,32,256]{2,1,0:T(8,128)S(1)} %dynamic-slice_bitcast_fusion.7), channel_id=1, source_target_pairs={{0,4},{1,5},{2,6},{3,7},{4,0},{5,1},{6,2},{7,3},{8,12},{9,13},{10,... | collective-permute-start | bytes 196616 | tf_op jit(solution)/shard_map/sketch_reduce_gather/ppermute | solution.py:98
  127.7 9.9 %collective-permute-start.24 = (f32[2,32,256]{2,1,0:T(8,128)S(1)}, f32[2,32,256]{2,1,0:T(8,128)S(1)}, u32[]{:S(2)}, u32[]{:S(2)}) collective-permute-start(f32[2,32,256]{2,1,0:T(8,128)S(1)} %bitcast_add_fusion.8), channel_id=1, source_target_pairs={{0,8},{1,9},{2,10},{3,11},{4,12},{5,13},{6,14},{7,15},{8,0},{9,1},... | collective-permute-start | bytes 196616 | tf_op jit(solution)/shard_map/sketch_reduce_gather/ppermute | solution.py:98
  129.8 10.0 %collective-permute-start.17 = (f32[2,32,256]{2,1,0:T(8,128)S(1)}, f32[2,32,256]{2,1,0:T(8,128)S(1)}, u32[]{:S(2)}, u32[]{:S(2)}) collective-permute-start(f32[2,32,256]{2,1,0:T(8,128)S(1)} %bitcast_add_fusion.9), channel_id=1, source_target_pairs={{0,8},{1,9},{2,10},{3,11},{4,12},{5,13},{6,14},{7,15},{8,0},{9,1},... | collective-permute-start | bytes 196616 | tf_op jit(solution)/shard_map/sketch_reduce_gather/ppermute | solution.py:98
  130.8 10.0 %collective-permute-start.10 = (f32[2,32,256]{2,1,0:T(8,128)S(1)}, f32[2,32,256]{2,1,0:T(8,128)S(1)}, u32[]{:S(2)}, u32[]{:S(2)}) collective-permute-start(f32[2,32,256]{2,1,0:T(8,128)S(1)} %bitcast_add_fusion.10), channel_id=1, source_target_pairs={{0,8},{1,9},{2,10},{3,11},{4,12},{5,13},{6,14},{7,15},{8,0},{9,1},... | collective-permute-start | bytes 196616 | tf_op jit(solution)/shard_map/sketch_reduce_gather/ppermute | solution.py:98
  132.9 9.1 %collective-permute-start.3 = (f32[2,32,256]{2,1,0:T(8,128)S(1)}, f32[2,32,256]{2,1,0:T(8,128)S(1)}, u32[]{:S(2)}, u32[]{:S(2)}) collective-permute-start(f32[2,32,256]{2,1,0:T(8,128)S(1)} %bitcast_add_fusion.11), channel_id=1, source_target_pairs={{0,8},{1,9},{2,10},{3,11},{4,12},{5,13},{6,14},{7,15},{8,0},{9,1},... | collective-permute-start | bytes 196616 | tf_op jit(solution)/shard_map/sketch_reduce_gather/ppermute | solution.py:98
  137.7 6.3 %collective-permute-start.25 = (f32[2,32,256]{2,1,0:T(8,128)S(1)}, f32[2,32,256]{2,1,0:T(8,128)S(1)}, u32[]{:S(2)}, u32[]{:S(2)}) collective-permute-start(f32[2,32,256]{2,1,0:T(8,128)S(1)} %add.173), channel_id=1, source_target_pairs={{0,2},{1,3},{2,0},{3,1},{4,6},{5,7},{6,4},{7,5},{8,10},{9,11},{10,... | collective-permute-start | bytes 196616 | tf_op jit(solution)/shard_map/sketch_reduce_gather/ppermute | solution.py:98
  139.9 5.0 %collective-permute-start.18 = (f32[2,32,256]{2,1,0:T(8,128)S(1)}, f32[2,32,256]{2,1,0:T(8,128)S(1)}, u32[]{:S(2)}, u32[]{:S(2)}) collective-permute-start(f32[2,32,256]{2,1,0:T(8,128)S(1)} %add.169), channel_id=1, source_target_pairs={{0,4},{1,5},{2,6},{3,7},{4,0},{5,1},{6,2},{7,3},{8,12},{9,13},{10,... | collective-permute-start | bytes 196616 | tf_op jit(solution)/shard_map/sketch_reduce_gather/ppermute | solution.py:98
  140.8 5.3 %collective-permute-start.11 = (f32[2,32,256]{2,1,0:T(8,128)S(1)}, f32[2,32,256]{2,1,0:T(8,128)S(1)}, u32[]{:S(2)}, u32[]{:S(2)}) collective-permute-start(f32[2,32,256]{2,1,0:T(8,128)S(1)} %add.165), channel_id=1, source_target_pairs={{0,2},{1,3},{2,0},{3,1},{4,6},{5,7},{6,4},{7,5},{8,10},{9,11},{10,... | collective-permute-start | bytes 196616 | tf_op jit(solution)/shard_map/sketch_reduce_gather/ppermute | solution.py:98
  142.0 5.2 %collective-permute-start.4 = (f32[2,32,256]{2,1,0:T(8,128)S(1)}, f32[2,32,256]{2,1,0:T(8,128)S(1)}, u32[]{:S(2)}, u32[]{:S(2)}) collective-permute-start(f32[2,32,256]{2,1,0:T(8,128)S(1)} %add.161), channel_id=1, source_target_pairs={{0,4},{1,5},{2,6},{3,7},{4,0},{5,1},{6,2},{7,3},{8,12},{9,13},{10,... | collective-permute-start | bytes 196616 | tf_op jit(solution)/shard_map/sketch_reduce_gather/ppermute | solution.py:98
  144.0 5.3 %collective-permute-start.26 = (f32[2,2,32,256]{3,2,0,1:T(8,128)S(1)}, f32[2,2,32,256]{3,2,0,1:T(8,128)S(1)}, u32[]{:S(2)}, u32[]{:S(2)}) collective-permute-start(f32[2,2,32,256]{3,2,0,1:T(8,128)S(1)} %pad_maximum_fusion.11), channel_id=1, source_target_pairs={{0,4},{1,5},{2,6},{3,7},{4,0},{5,1},{6,2},{7,3},{8,12},{9,13},{10,... | collective-permute-start | bytes 393224 | tf_op jit(solution)/shard_map/sketch_reduce_gather/ppermute | solution.py:98
  144.9 5.0 %collective-permute-start.19 = (f32[2,2,32,256]{3,2,0,1:T(8,128)S(1)}, f32[2,2,32,256]{3,2,0,1:T(8,128)S(1)}, u32[]{:S(2)}, u32[]{:S(2)}) collective-permute-start(f32[2,2,32,256]{3,2,0,1:T(8,128)S(1)} %pad_maximum_fusion.10), channel_id=1, source_target_pairs={{0,2},{1,3},{2,0},{3,1},{4,6},{5,7},{6,4},{7,5},{8,10},{9,11},{10,... | collective-permute-start | bytes 393224 | tf_op jit(solution)/shard_map/sketch_reduce_gather/ppermute | solution.py:98
  146.1 5.0 %collective-permute-start.12 = (f32[2,2,32,256]{3,2,0,1:T(8,128)S(1)}, f32[2,2,32,256]{3,2,0,1:T(8,128)S(1)}, u32[]{:S(2)}, u32[]{:S(2)}) collective-permute-start(f32[2,2,32,256]{3,2,0,1:T(8,128)S(1)} %pad_maximum_fusion.9), channel_id=1, source_target_pairs={{0,4},{1,5},{2,6},{3,7},{4,0},{5,1},{6,2},{7,3},{8,12},{9,13},{10,... | collective-permute-start | bytes 393224 | tf_op jit(solution)/shard_map/sketch_reduce_gather/ppermute | solution.py:98
  147.2 5.0 %collective-permute-start.5 = (f32[2,2,32,256]{3,2,1,0:T(8,128)S(1)}, f32[2,2,32,256]{3,2,1,0:T(8,128)S(1)}, u32[]{:S(2)}, u32[]{:S(2)}) collective-permute-start(f32[2,2,32,256]{3,2,1,0:T(8,128)S(1)} %pad_maximum_fusion.8), channel_id=1, source_target_pairs={{0,2},{1,3},{2,0},{3,1},{4,6},{5,7},{6,4},{7,5},{8,10},{9,11},{10,... | collective-permute-start | bytes 393224 | tf_op jit(solution)/shard_map/sketch_reduce_gather/ppermute | solution.py:98
  149.4 3.0 %collective-permute-start.27 = (f32[2,2,2,32,256]{4,3,0,1,2:T(8,128)S(1)}, f32[2,2,2,32,256]{4,3,0,1,2:T(8,128)S(1)}, u32[]{:S(2)}, u32[]{:S(2)}) collective-permute-start(f32[2,2,2,32,256]{4,3,0,1,2:T(8,128)S(1)} %pad_maximum_fusion.7), channel_id=1, source_target_pairs={{0,1},{1,0},{2,3},{3,2},{4,5},{5,4},{6,7},{7,6},{8,9},{9,8},{10,11... | collective-permute-start | bytes 786440 | tf_op jit(solution)/shard_map/sketch_reduce_gather/ppermute | solution.py:98
  150.0 2.6 %collective-permute-start.20 = (f32[2,2,2,32,256]{4,3,0,1,2:T(8,128)S(1)}, f32[2,2,2,32,256]{4,3,0,1,2:T(8,128)S(1)}, u32[]{:S(2)}, u32[]{:S(2)}) collective-permute-start(f32[2,2,2,32,256]{4,3,0,1,2:T(8,128)S(1)} %pad_maximum_fusion.6), channel_id=1, source_target_pairs={{0,1},{1,0},{2,3},{3,2},{4,5},{5,4},{6,7},{7,6},{8,9},{9,8},{10,11... | collective-permute-start | bytes 786440 | tf_op jit(solution)/shard_map/sketch_reduce_gather/ppermute | solution.py:98
  151.2 1.6 collective-permute-start.13
  152.3 1.6 collective-permute-start.6

commit v17 on v16

--- a/solution.py
+++ b/solution.py
@@ -130,7 +130,7 @@
     if bits < 4:
         return [first]
     rest = list(range(4, bits))
-    return [[0, 1, 2, 3] + rest, [0, 2, 1, 3] + rest, [0, 1, 2, 3] + rest, [0, 2, 1, 3] + rest]
+    return [[0, 1, 2, 3] + rest, [0, 2, 1, 3] + rest]
 
 
 def on_device(grads, proj, target_ids, target_counts):

time: 196 us -> 202 us (1.031)
  waiting for transfers between devices: 85 us -> 102 us
  starting transfers between devices: 50.1 us -> 39.3 us
    ppermute x28 -> x14, waiting for transfers between devices: 10 us -> 24 us  [partner(): lax.ppermute(array, axis, [(i, i ^ 1 << bit) for i in range(lax.axis_size...]
    ppermute x28 -> x14, starting transfers between devices: 42.6 us -> 31.9 us  [partner(): lax.ppermute(array, axis, [(i, i ^ 1 << bit) for i in range(lax.axis_size...]
    all_to_all x1, waiting for transfers between devices: 75 us -> 77.7 us  [on_device(): lax.all_to_all(grads, 'ex', split_axis=1, concat_axis=0, tiled=True)]
  transfers between devices with their start and end apart: 29 -> 15, of which waited for: 13 -> 9; matrix products, arithmetic and copies ran while one was open for 2% -> 2% of each run, Pallas kernels for 0% -> 0%
where the time goes in v17:
time: 202 us
  waiting for transfers between devices  102 us (50%)
  starting transfers between devices  39.3 us (19%)
  Pallas kernels  36.2 us (18%)
  matrix products  12.7 us (6%)
  local copies, waits for them, and re-layouts  6.91 us (3%)
  other arithmetic  4.04 us (2%)
    all_to_all x1, waiting for transfers between devices, on_device(): lax.all_to_all(grads, 'ex', split_axis=1, concat_axis=0, tiled=True)  77.7 us
    pallas_call x1, Pallas kernels, spd_solve(): pl.pallas_call(functools.partial(_solve_kernel, block=block), out_shape=j...  36.2 us
    ppermute x14, starting transfers between devices, partner(): lax.ppermute(array, axis, [(i, i ^ 1 << bit) for i in range(lax.axis_size...  31.9 us
    ppermute x14, waiting for transfers between devices, partner(): lax.ppermute(array, axis, [(i, i ^ 1 << bit) for i in range(lax.axis_size...  24 us
    dot_general x1, matrix products, on_device(): partial_value = jnp.dot(columns, proj, preferred_element_type=jnp.float32)  8.14 us
    all_to_all x1, starting transfers between devices, on_device(): lax.all_to_all(grads, 'ex', split_axis=1, concat_axis=0, tiled=True)  7.44 us
    all_to_all x1, local copies, waits for them, and re-layouts, on_device(): lax.all_to_all(grads, 'ex', split_axis=1, concat_axis=0, tiled=True)  4.69 us
    dot_general x1, matrix products, on_device(): kernel = jnp.dot(sketch_all, sketch_all.T, precision=lax.Precision.HIGHEST)  4.53 us
  transfers between devices with their start and end apart: 15, of which 9 were waited for; matrix products, arithmetic and copies ran while one was open for 2% of the time, Pallas kernels for 0%

profile of v17, /device:TPU:0, one launch (start us, length us, event | category | flops | bytes accessed | tf_op | source)
XLA Modules:
  0.0 201.8 jit_solution(9242289468688801294)
XLA Ops:
  0.6 4.7 %copy.62 = bf16[4,16,8,4096]{3,2,0,1:T(8,128)(2,1)} copy(bf16[4,16,8,4096]{3,2,1,0:T(8,128)(2,1)} %bitcast.85) | data formatting | bytes 8388608 | tf_op jit(solution)/shard_map/gradient_exchange/all_to_all | solution.py:144
  5.3 7.4 %all-to-all-start = ((bf16[32,16,4096]{2,0,1:T(8,128)(2,1)}), bf16[32,16,4096]{2,0,1:T(8,128)(2,1)}, u32[]{:S(2)}, u32[]{:S(2)}) async-start(bf16[32,16,4096]{2,0,1:T(8,128)(2,1)} %bitcast.84), calls=%async_computation | async-start | bytes 8388608 | tf_op jit(solution)/shard_map/gradient_exchange/all_to_all | solution.py:144
  12.8 77.7 %all-to-all-done = bf16[32,16,4096]{2,0,1:T(8,128)(2,1)} async-done(((bf16[32,16,4096]{2,0,1:T(8,128)(2,1)}), bf16[32,16,4096]{2,0,1:T(8,128)(2,1)}, u32[]{:S(2)}, u32[]{:S(2)}) %all-to-all-start) | async-done | bytes 4194336 | tf_op jit(solution)/shard_map/gradient_exchange/all_to_all | solution.py:144
  90.4 8.1 %fusion.10 = f32[512,1024]{1,0:T(8,128)S(1)} fusion(bf16[512,4096]{1,0:T(8,128)(2,1)} %bitcast.2, bf16[4096,1024]{1,0:T(8,128)(2,1)} %param.5), kind=kOutput, calls=%fused_computation.53 | convolution fusion | flops 4294967296 | bytes 14680064 | tf_op jit(solution)/shard_map/partial_projection/dot_general | solution.py:146
  98.6 0.2 fusion.9
  98.8 0.3 constant_dynamic-slice_fusion.1
  99.1 0.8 collective-permute-start.7
  100.1 1.6 convert_reduce_fusion
  101.6 0.1 copy.43
  101.8 0.1 collective-permute-start
  102.1 14.8 %collective-permute-start.8 = (f32[2,2,32,512]{3,2,1,0:T(8,128)S(1)}, f32[2,2,32,512]{3,2,1,0:T(8,128)S(1)}, u32[]{:S(2)}, u32[]{:S(2)}) collective-permute-start(f32[2,2,32,512]{3,2,1,0:T(8,128)S(1)} %dynamic-slice_bitcast_fusion), channel_id=1, source_target_pairs={{0,4},{1,5},{2,6},{3,7},{4,0},{5,1},{6,2},{7,3},{8,12},{9,13},{10,... | collective-permute-start | bytes 786440 | tf_op jit(solution)/shard_map/sketch_reduce_gather/ppermute | solution.py:98
  117.0 3.0 %collective-permute-start.1 = (f32[2,2,32,512]{3,2,1,0:T(8,128)S(1)}, f32[2,2,32,512]{3,2,1,0:T(8,128)S(1)}, u32[]{:S(2)}, u32[]{:S(2)}) collective-permute-start(f32[2,2,32,512]{3,2,1,0:T(8,128)S(1)} %dynamic-slice_bitcast_fusion.1), channel_id=1, source_target_pairs={{0,2},{1,3},{2,0},{3,1},{4,6},{5,7},{6,4},{7,5},{8,10},{9,11},{10,... | collective-permute-start | bytes 786440 | tf_op jit(solution)/shard_map/sketch_reduce_gather/ppermute | solution.py:98
  120.0 3.4 %collective-permute-done.8 = f32[2,2,32,512]{3,2,1,0:T(8,128)S(1)} collective-permute-done((f32[2,2,32,512]{3,2,1,0:T(8,128)S(1)}, f32[2,2,32,512]{3,2,1,0:T(8,128)S(1)}, u32[]{:S(2)}, u32[]{:S(2)}) %collective-permute-start.8) | collective-permute-done | bytes 262176 | tf_op jit(solution)/shard_map/sketch_reduce_gather/ppermute | solution.py:98
  123.5 3.3 %collective-permute-start.9 = (f32[2,32,512]{2,1,0:T(8,128)S(1)}, f32[2,32,512]{2,1,0:T(8,128)S(1)}, u32[]{:S(2)}, u32[]{:S(2)}) collective-permute-start(f32[2,32,512]{2,1,0:T(8,128)S(1)} %dynamic-slice_bitcast_fusion.2), channel_id=1, source_target_pairs={{0,2},{1,3},{2,0},{3,1},{4,6},{5,7},{6,4},{7,5},{8,10},{9,11},{10,... | collective-permute-start | bytes 393224 | tf_op jit(solution)/shard_map/sketch_reduce_gather/ppermute | solution.py:98
  126.8 1.8 collective-permute-start.2
  128.6 1.6 collective-permute-done.9
  130.2 2.9 %collective-permute-start.10 = (f32[2,32,512]{2,1,0:T(8,128)S(1)}, f32[2,32,512]{2,1,0:T(8,128)S(1)}, u32[]{:S(2)}, u32[]{:S(2)}) collective-permute-start(f32[2,32,512]{2,1,0:T(8,128)S(1)} %bitcast_add_fusion.4), channel_id=1, source_target_pairs={{0,8},{1,9},{2,10},{3,11},{4,12},{5,13},{6,14},{7,15},{8,0},{9,1},... | collective-permute-start | bytes 393224 | tf_op jit(solution)/shard_map/sketch_reduce_gather/ppermute | solution.py:98
  133.1 2.6 %collective-permute-start.3 = (f32[2,32,512]{2,1,0:T(8,128)S(1)}, f32[2,32,512]{2,1,0:T(8,128)S(1)}, u32[]{:S(2)}, u32[]{:S(2)}) collective-permute-start(f32[2,32,512]{2,1,0:T(8,128)S(1)} %bitcast_add_fusion.5), channel_id=1, source_target_pairs={{0,8},{1,9},{2,10},{3,11},{4,12},{5,13},{6,14},{7,15},{8,0},{9,1},... | collective-permute-start | bytes 393224 | tf_op jit(solution)/shard_map/sketch_reduce_gather/ppermute | solution.py:98
  135.7 6.9 %collective-permute-done.10 = f32[2,32,512]{2,1,0:T(8,128)S(1)} collective-permute-done((f32[2,32,512]{2,1,0:T(8,128)S(1)}, f32[2,32,512]{2,1,0:T(8,128)S(1)}, u32[]{:S(2)}, u32[]{:S(2)}) %collective-permute-start.10) | collective-permute-done | bytes 131104 | tf_op jit(solution)/shard_map/sketch_reduce_gather/ppermute | solution.py:98
  142.6 1.0 collective-permute-start.11
  143.7 0.7 pad.4.w_ref
  144.6 3.1 %collective-permute-done.11 = f32[2,32,512]{2,1,0:T(8,128)S(1)} collective-permute-done((f32[2,32,512]{2,1,0:T(8,128)S(1)}, f32[2,32,512]{2,1,0:T(8,128)S(1)}, u32[]{:S(2)}, u32[]{:S(2)}) %collective-permute-start.11) | collective-permute-done | bytes 131104 | tf_op jit(solution)/shard_map/sketch_reduce_gather/ppermute | solution.py:98
  147.8 3.2 %collective-permute-done.4 = f32[2,32,512]{2,1,0:T(8,128)S(1)} collective-permute-done((f32[2,32,512]{2,1,0:T(8,128)S(1)}, f32[2,32,512]{2,1,0:T(8,128)S(1)}, u32[]{:S(2)}, u32[]{:S(2)}) %collective-permute-start.4) | collective-permute-done | bytes 131104 | tf_op jit(solution)/shard_map/sketch_reduce_gather/ppermute | solution.py:98
  151.0 1.3 collective-permute-start.5
  152.3 2.0 collective-permute-done.12
  154.5 2.9 %collective-permute-done.5 = f32[2,2,32,512]{3,2,1,0:T(8,128)S(1)} collective-permute-done((f32[2,2,32,512]{3,2,1,0:T(8,128)S(1)}, f32[2,2,32,512]{3,2,1,0:T(8,128)S(1)}, u32[]{:S(2)}, u32[]{:S(2)}) %collective-permute-start.5) | collective-permute-done | bytes 262176 | tf_op jit(solution)/shard_map/sketch_reduce_gather/ppermute | solution.py:98
  157.7 0.7 pad_maximum_fusion.6
  158.6 0.9 collective-permute-done.6
  159.8 4.5 %select_add_fusion.m_ref = f32[512,512]{1,0:T(8,128)} fusion(f32[512,512]{1,0:T(8,128)S(1)} %bitcast.88, f32[512,512]{1,0:T(8,128)S(1)} %bitcast.89), kind=kOutput, calls=%fused_computation.10 | convolution fusion | flops 3222798336 | bytes 3145728 | tf_op jit(solution)/shard_map/kernel_matrix/dot_general | solution.py:172
  164.3 36.2 %kernel_solve.1 = f32[512,128]{1,0:T(8,128)} custom-call(f32[512,512]{1,0:T(8,128)} %select_add_fusion.m_ref, f32[512,128]{1,0:T(8,128)} %pad.4.w_ref), custom_call_target="tpu_custom_call" | custom-call | tf_op jit(solution)/shard_map/kernel_solve/pallas_call | solution.py:89
  200.4 0.7 fusion.7
  201.2 0.7 copy.55
  (47 shorter events, 1.7 us)
Async XLA Ops:
  5.3 85.1 %all-to-all-start = ((bf16[32,16,4096]{2,0,1:T(8,128)(2,1)}), bf16[32,16,4096]{2,0,1:T(8,128)(2,1)}, u32[]{:S(2)}, u32[]{:S(2)}) async-start(bf16[32,16,4096]{2,0,1:T(8,128)(2,1)} %bitcast.84), calls=%async_computation | async-start | bytes 8388608 | tf_op jit(solution)/shard_map/gradient_exchange/all_to_all | solution.py:144
  98.6 1.4 copy-start.1
  98.6 1.4 copy-start
  99.1 2.9 %collective-permute-start.7 = (f32[2,2,2,32,512]{4,3,2,0,1:T(8,128)S(1)}, f32[2,2,2,32,512]{4,3,2,0,1:T(8,128)S(1)}, u32[]{:S(2)}, u32[]{:S(2)}) collective-permute-start(f32[2,2,2,32,512]{4,3,2,0,1:T(8,128)S(1)} %bitcast.90), channel_id=1, source_target_pairs={{0,1},{1,0},{2,3},{3,2},{4,5},{5,4},{6,7},{7,6},{8,9},{9,8},{10,11... | collective-permute-start | bytes 1572872 | tf_op jit(solution)/shard_map/sketch_reduce_gather/ppermute | solution.py:98
  101.8 15.1 %collective-permute-start = (f32[2,2,2,32,512]{4,3,1,0,2:T(8,128)S(1)}, f32[2,2,2,32,512]{4,3,1,0,2:T(8,128)S(1)}, u32[]{:S(2)}, u32[]{:S(2)}) collective-permute-start(f32[2,2,2,32,512]{4,3,1,0,2:T(8,128)S(1)} %bitcast.91), channel_id=1, source_target_pairs={{0,1},{1,0},{2,3},{3,2},{4,5},{5,4},{6,7},{7,6},{8,9},{9,8},{10,11... | collective-permute-start | bytes 1572872 | tf_op jit(solution)/shard_map/sketch_reduce_gather/ppermute | solution.py:98
  102.1 21.3 %collective-permute-start.8 = (f32[2,2,32,512]{3,2,1,0:T(8,128)S(1)}, f32[2,2,32,512]{3,2,1,0:T(8,128)S(1)}, u32[]{:S(2)}, u32[]{:S(2)}) collective-permute-start(f32[2,2,32,512]{3,2,1,0:T(8,128)S(1)} %dynamic-slice_bitcast_fusion), channel_id=1, source_target_pairs={{0,4},{1,5},{2,6},{3,7},{4,0},{5,1},{6,2},{7,3},{8,12},{9,13},{10,... | collective-permute-start | bytes 786440 | tf_op jit(solution)/shard_map/sketch_reduce_gather/ppermute | solution.py:98
  117.0 9.7 %collective-permute-start.1 = (f32[2,2,32,512]{3,2,1,0:T(8,128)S(1)}, f32[2,2,32,512]{3,2,1,0:T(8,128)S(1)}, u32[]{:S(2)}, u32[]{:S(2)}) collective-permute-start(f32[2,2,32,512]{3,2,1,0:T(8,128)S(1)} %dynamic-slice_bitcast_fusion.1), channel_id=1, source_target_pairs={{0,2},{1,3},{2,0},{3,1},{4,6},{5,7},{6,4},{7,5},{8,10},{9,11},{10,... | collective-permute-start | bytes 786440 | tf_op jit(solution)/shard_map/sketch_reduce_gather/ppermute | solution.py:98
  123.5 6.7 %collective-permute-start.9 = (f32[2,32,512]{2,1,0:T(8,128)S(1)}, f32[2,32,512]{2,1,0:T(8,128)S(1)}, u32[]{:S(2)}, u32[]{:S(2)}) collective-permute-start(f32[2,32,512]{2,1,0:T(8,128)S(1)} %dynamic-slice_bitcast_fusion.2), channel_id=1, source_target_pairs={{0,2},{1,3},{2,0},{3,1},{4,6},{5,7},{6,4},{7,5},{8,10},{9,11},{10,... | collective-permute-start | bytes 393224 | tf_op jit(solution)/shard_map/sketch_reduce_gather/ppermute | solution.py:98
  126.8 6.3 %collective-permute-start.2 = (f32[2,32,512]{2,1,0:T(8,128)S(1)}, f32[2,32,512]{2,1,0:T(8,128)S(1)}, u32[]{:S(2)}, u32[]{:S(2)}) collective-permute-start(f32[2,32,512]{2,1,0:T(8,128)S(1)} %dynamic-slice_bitcast_fusion.3), channel_id=1, source_target_pairs={{0,4},{1,5},{2,6},{3,7},{4,0},{5,1},{6,2},{7,3},{8,12},{9,13},{10,... | collective-permute-start | bytes 393224 | tf_op jit(solution)/shard_map/sketch_reduce_gather/ppermute | solution.py:98
  130.2 12.4 %collective-permute-start.10 = (f32[2,32,512]{2,1,0:T(8,128)S(1)}, f32[2,32,512]{2,1,0:T(8,128)S(1)}, u32[]{:S(2)}, u32[]{:S(2)}) collective-permute-start(f32[2,32,512]{2,1,0:T(8,128)S(1)} %bitcast_add_fusion.4), channel_id=1, source_target_pairs={{0,8},{1,9},{2,10},{3,11},{4,12},{5,13},{6,14},{7,15},{8,0},{9,1},... | collective-permute-start | bytes 393224 | tf_op jit(solution)/shard_map/sketch_reduce_gather/ppermute | solution.py:98
  133.1 11.3 %collective-permute-start.3 = (f32[2,32,512]{2,1,0:T(8,128)S(1)}, f32[2,32,512]{2,1,0:T(8,128)S(1)}, u32[]{:S(2)}, u32[]{:S(2)}) collective-permute-start(f32[2,32,512]{2,1,0:T(8,128)S(1)} %bitcast_add_fusion.5), channel_id=1, source_target_pairs={{0,8},{1,9},{2,10},{3,11},{4,12},{5,13},{6,14},{7,15},{8,0},{9,1},... | collective-permute-start | bytes 393224 | tf_op jit(solution)/shard_map/sketch_reduce_gather/ppermute | solution.py:98
  142.6 5.0 %collective-permute-start.11 = (f32[2,32,512]{2,1,0:T(8,128)S(1)}, f32[2,32,512]{2,1,0:T(8,128)S(1)}, u32[]{:S(2)}, u32[]{:S(2)}) collective-permute-start(f32[2,32,512]{2,1,0:T(8,128)S(1)} %add.113), channel_id=1, source_target_pairs={{0,2},{1,3},{2,0},{3,1},{4,6},{5,7},{6,4},{7,5},{8,10},{9,11},{10,... | collective-permute-start | bytes 393224 | tf_op jit(solution)/shard_map/sketch_reduce_gather/ppermute | solution.py:98
  144.5 6.5 %collective-permute-start.4 = (f32[2,32,512]{2,1,0:T(8,128)S(1)}, f32[2,32,512]{2,1,0:T(8,128)S(1)}, u32[]{:S(2)}, u32[]{:S(2)}) collective-permute-start(f32[2,32,512]{2,1,0:T(8,128)S(1)} %add.109), channel_id=1, source_target_pairs={{0,4},{1,5},{2,6},{3,7},{4,0},{5,1},{6,2},{7,3},{8,12},{9,13},{10,... | collective-permute-start | bytes 393224 | tf_op jit(solution)/shard_map/sketch_reduce_gather/ppermute | solution.py:98
  147.7 6.6 %collective-permute-start.12 = (f32[2,2,32,512]{3,2,1,0:T(8,128)S(1)}, f32[2,2,32,512]{3,2,1,0:T(8,128)S(1)}, u32[]{:S(2)}, u32[]{:S(2)}) collective-permute-start(f32[2,2,32,512]{3,2,1,0:T(8,128)S(1)} %pad_maximum_fusion.5), channel_id=1, source_target_pairs={{0,4},{1,5},{2,6},{3,7},{4,0},{5,1},{6,2},{7,3},{8,12},{9,13},{10,... | collective-permute-start | bytes 786440 | tf_op jit(solution)/shard_map/sketch_reduce_gather/ppermute | solution.py:98
  151.0 6.4 %collective-permute-start.5 = (f32[2,2,32,512]{3,2,1,0:T(8,128)S(1)}, f32[2,2,32,512]{3,2,1,0:T(8,128)S(1)}, u32[]{:S(2)}, u32[]{:S(2)}) collective-permute-start(f32[2,2,32,512]{3,2,1,0:T(8,128)S(1)} %pad_maximum_fusion.4), channel_id=1, source_target_pairs={{0,2},{1,3},{2,0},{3,1},{4,6},{5,7},{6,4},{7,5},{8,10},{9,11},{10,... | collective-permute-start | bytes 786440 | tf_op jit(solution)/shard_map/sketch_reduce_gather/ppermute | solution.py:98
  154.4 3.9 %collective-permute-start.13 = (f32[2,2,2,32,512]{4,3,2,1,0:T(8,128)S(1)}, f32[2,2,2,32,512]{4,3,2,1,0:T(8,128)S(1)}, u32[]{:S(2)}, u32[]{:S(2)}) collective-permute-start(f32[2,2,2,32,512]{4,3,2,1,0:T(8,128)S(1)} %pad_maximum_fusion.3), channel_id=1, source_target_pairs={{0,1},{1,0},{2,3},{3,2},{4,5},{5,4},{6,7},{7,6},{8,9},{9,8},{10,11... | collective-permute-start | bytes 1572872 | tf_op jit(solution)/shard_map/sketch_reduce_gather/ppermute | solution.py:98
  157.6 2.0 collective-permute-start.6
